TPU v7x, 32 devices: a whole 2x2x4 slice. The times are simulated.
32 devices in a mesh: groups: 2 (over y), sec: 4 (over x, core), plane: 4 (over z).
Axes of the slice: x: 2, y: 2, z: 4, core: 2. Of those that a mesh axis runs over, the one named last changes fastest.
Arguments:
- tokens: bfloat16 [16, 512, 1024], P(('groups', 'sec'), 'plane'), parts along dimension 0, may hold values from -8 to 8
- counts: int32 [16], P('groups'), parts along dimension 0, may hold values from 128 to 512, as said below
- region_ids: int32 [16, 512], P(('groups', 'sec'), 'plane'), parts along dimension 0, may hold values from 0 to 31
- norm_gains: float32 [2, 1024], replicated, may hold values from 0.1 to 1.9
- cross_qkv: bfloat16 [1024, 3072], P('plane'), may hold values from -2 to 2
- cross_out: bfloat16 [1024, 1024], P('plane'), may hold values from -0.1875 to 0.1875
- plane_qkv: bfloat16 [1024, 3072], P('plane'), may hold values from -2 to 2
- plane_out: bfloat16 [1024, 1024], P('plane'), may hold values from -0.1875 to 0.1875
Outputs:
- encoded: bfloat16 [16, 512, 1024], P(('groups', 'sec'), 'plane'), parts along dimension 0
- pooled: float32 [64, 1024], P(('groups', 'sec', 'plane')), parts along dimension 0
There are 2 independent parts, one for each index of `groups`. A program takes and returns all parts, laid end to end along the dimension named above; an argument that names none is the same for every part. Nothing has to cross between parts.
Inputs may be any that keep to these rules, and one draw needn't show every extreme that they name: `counts`: valid tissue tokens of each section; they are the first positions of the section.
All inputs are finite; a program needn't handle non-finite values.
Results may differ from a plain program's by a relative error of at most 0.009.
Values may be sent and summed in bfloat16 or wider, within the bound.
No kernel may reach another device: no remote copies, remote signals or barrier semaphores. Data moves between devices by JAX's collectives and lax.ppermute only.
A program may use at most 64 MiB of HBM per device.

v0:
```python
import math

import jax
import jax.numpy as jnp
from jax import lax
from jax.sharding import PartitionSpec as P

HEADS = 16
HEAD_DIM = 64
WINDOW = 128


negative_big = -1e30


def shifted_2(value, axis, by):
    peers = lax.axis_size(axis)
    pairs = [(i, i + by) for i in range(peers) if 0 <= i + by < peers]
    return lax.ppermute(value, axis, pairs)


def rms_norm(values, gain):
    wide = values.astype(jnp.float32)
    scaled = wide * lax.rsqrt(jnp.mean(wide * wide, axis=-1, keepdims=True) + 1e-06) * gain
    return scaled.astype(jnp.bfloat16)


def masked_softmax(scores, allowed):
    shifted = jnp.where(allowed, scores, negative_big)
    top = jnp.max(shifted, axis=-1, keepdims=True)
    expo = jnp.where(allowed, jnp.exp(shifted - top), 0.0)
    return (expo / jnp.sum(expo, axis=-1, keepdims=True)).astype(jnp.bfloat16)


def fold_product(inputs, weight_piece):
    return jnp.dot(inputs, weight_piece, preferred_element_type=jnp.float32)


def attend_items(pieces):
    packed_all, flags_all = pieces
    seq_len = packed_all.shape[2]
    block_len = 512
    score_scale = 1.0 / math.sqrt(HEAD_DIM)
    key_index = jnp.arange(seq_len, dtype=jnp.int32)

    def one_item(item_pair):
        packed, key_flag = item_pair
        key_rows = packed[:, HEAD_DIM : 2 * HEAD_DIM]
        value_rows = packed[:, 2 * HEAD_DIM :]
        key_alive = key_flag > 0.5
        query_blocks = packed[:, :HEAD_DIM].reshape(seq_len // block_len, block_len, HEAD_DIM)
        block_starts = jnp.arange(seq_len // block_len, dtype=jnp.int32) * block_len

        def one_block(block_pair):
            query_rows, offset = block_pair
            scores = (
                jnp.einsum("qd,kd->qk", query_rows, key_rows, preferred_element_type=jnp.float32)
                * score_scale
            )
            own_index = offset + jnp.arange(block_len, dtype=jnp.int32)
            allowed = key_alive[None, :] | (key_index[None, :] == own_index[:, None])
            attention = masked_softmax(scores, allowed)
            return jnp.dot(attention, value_rows, preferred_element_type=jnp.float32).astype(
                jnp.bfloat16
            )

        return lax.map(one_block, (query_blocks, block_starts)).reshape(seq_len, HEAD_DIM)

    return lax.map(one_item, (packed_all[0], flags_all[0]))[None]


def body(tokens, counts, region_ids, norm_gains, cross_qkv, cross_out, plane_qkv, plane_out):
    sec_block, tok_block, model_width = tokens.shape
    plane_count = lax.axis_size("plane")
    regions = 2 * lax.axis_size("sec") * plane_count
    positions = lax.axis_index("plane") * tok_block + jnp.arange(tok_block, dtype=jnp.int32)
    padded_counts = jnp.concatenate(
        [jnp.zeros((1,), jnp.int32), counts, jnp.zeros((1,), jnp.int32)]
    )
    near_counts = lax.dynamic_slice_in_dim(
        padded_counts, lax.axis_index("sec") * sec_block, sec_block + 2
    )
    near_valid = positions[None, :] < near_counts[:, None]
    own_valid = near_valid[1 : sec_block + 1]
    score_scale = 1.0 / math.sqrt(HEAD_DIM)
    normed = rms_norm(tokens, norm_gains[0])
    inputs = normed.reshape(-1, model_width)
    result = fold_product(inputs, lax.all_gather(cross_qkv, "plane", axis=0, tiled=True))
    projected = result.astype(jnp.bfloat16).reshape(sec_block, tok_block, 3 * model_width)
    own_kv = projected[:, :, model_width:]
    from_below = shifted_2(own_kv[sec_block - 1], "sec", 1)
    from_above = shifted_2(own_kv[0], "sec", -1)
    near_kv = jnp.concatenate([from_below[None], own_kv, from_above[None]], axis=0)
    queries = projected[:, :, :model_width]
    windows = tok_block // WINDOW
    query_win = queries.reshape(sec_block, windows, WINDOW, HEADS, HEAD_DIM)
    pair_win = near_kv.reshape(sec_block + 2, windows, WINDOW, 2, HEADS, HEAD_DIM)
    stacked = jnp.concatenate(
        [pair_win[0:sec_block], pair_win[1 : sec_block + 1], pair_win[2 : sec_block + 2]], axis=2
    )
    valid_win = near_valid.reshape(sec_block + 2, windows, WINDOW)
    valid_three = jnp.concatenate(
        [valid_win[0:sec_block], valid_win[1 : sec_block + 1], valid_win[2 : sec_block + 2]], axis=2
    )
    itself = jnp.arange(3 * WINDOW)[None, :] == jnp.arange(WINDOW)[:, None] + WINDOW
    scores = (
        jnp.einsum(
            "snqhd,snkhd->snhqk", query_win, stacked[:, :, :, 0], preferred_element_type=jnp.float32
        )
        * score_scale
    )
    allowed = valid_three[:, :, None, None, :] | itself[None, None, None]
    attention = masked_softmax(scores, allowed)
    context = jnp.einsum(
        "snhqk,snkhd->snqhd", attention, stacked[:, :, :, 1], preferred_element_type=jnp.float32
    )
    context = context.astype(jnp.bfloat16).reshape(-1, model_width)
    result = fold_product(context, lax.all_gather(cross_out, "plane", axis=0, tiled=True))
    after_cross = (tokens.reshape(-1, model_width).astype(jnp.float32) + result).astype(
        jnp.bfloat16
    )
    normed = rms_norm(after_cross, norm_gains[1])
    result = fold_product(normed, lax.all_gather(plane_qkv, "plane", axis=0, tiled=True))
    projected = result.astype(jnp.bfloat16).reshape(sec_block, tok_block, 3, HEADS, HEAD_DIM)
    per_device = sec_block * HEADS // plane_count
    heads_first = jnp.transpose(projected, (0, 3, 1, 2, 4)).reshape(
        plane_count, per_device, tok_block, 3 * HEAD_DIM
    )
    key_flags = jnp.broadcast_to(own_valid[:, None, :], (sec_block, HEADS, tok_block)).astype(
        jnp.bfloat16
    )
    key_flags = key_flags.reshape(plane_count, per_device, tok_block)
    attended = attend_items(
        (
            lax.all_to_all(heads_first, "plane", split_axis=0, concat_axis=2, tiled=True),
            lax.all_to_all(key_flags, "plane", split_axis=0, concat_axis=2, tiled=True),
        )
    )
    returned = lax.all_to_all(attended, "plane", split_axis=2, concat_axis=0, tiled=True)
    context = jnp.transpose(
        returned.reshape(sec_block, HEADS, tok_block, HEAD_DIM), (0, 2, 1, 3)
    ).reshape(-1, model_width)
    result = fold_product(context, lax.all_gather(plane_out, "plane", axis=0, tiled=True))
    encoded = (after_cross.astype(jnp.float32) + result).astype(jnp.bfloat16)
    labels = region_ids.reshape(-1)
    member = (jnp.arange(regions, dtype=jnp.int32)[:, None] == labels[None, :]) & own_valid.reshape(
        -1
    )[None, :]
    region_sum = jnp.dot(member.astype(jnp.bfloat16), encoded, preferred_element_type=jnp.float32)
    region_count = jnp.sum(member.astype(jnp.float32), axis=1)
    totals, counted = (
        lax.psum_scatter(region_sum, ("sec", "plane"), scatter_dimension=0, tiled=True),
        lax.psum_scatter(region_count, ("sec", "plane"), scatter_dimension=0, tiled=True),
    )
    pooled = totals / jnp.maximum(counted, 1.0)[:, None]
    return (encoded.reshape(sec_block, tok_block, model_width), pooled)


def solution(mesh):
    in_specs = (
        P(("groups", "sec"), "plane", None),
        P("groups"),
        P(("groups", "sec"), "plane"),
        P(),
        P("plane", None),
        P("plane", None),
        P("plane", None),
        P("plane", None),
    )
    out_specs = (P(("groups", "sec"), "plane", None), P(("groups", "sec", "plane"), None))
    return jax.shard_map(body, mesh=mesh, in_specs=in_specs, out_specs=out_specs, check_vma=False)
```

profile of v0, /device:TPU:0, one launch (start us, length us, event | category | flops | bytes accessed | tf_op | source)
XLA Modules:
  0.0 520.9 jit_solution(6824321501404920193)
XLA Ops:
  10.1 117.6 %all-gather.5.cloned.1.call-done = bf16[1024,3072]{1,0:T(8,128)(2,1)} async-done(((bf16[256,3072]{1,0:T(8,128)(2,1)}), bf16[1024,3072]{1,0:T(8,128)(2,1)}) %all-gather.5.cloned.1.call-update) | async-done | bytes 6291472 | tf_op jit(solution)/shard_map/all_gather | solution.py:88
  127.7 4.6 convolution_convert_fusion.2
  133.4 2.8 collective-permute-start
  137.2 1.3 collective-permute-start.1
  140.2 1.3 copy.58
  141.5 1.4 pad_maximum_fusion.2
  144.4 3.2 fusion.43
  147.7 1.8 fusion.22
  150.1 23.4 %all-gather.7.cloned.1.call-done = bf16[1024,1024]{1,0:T(8,128)(2,1)} async-done(((bf16[256,1024]{1,0:T(8,128)(2,1)}), bf16[1024,1024]{1,0:T(8,128)(2,1)}) %all-gather.7.cloned.1.call-update) | async-done | bytes 2097168 | tf_op jit(solution)/shard_map/all_gather | solution.py:118
  173.5 2.4 fusion.23
  175.9 113.2 %all-gather.9.cloned.1.call-done = bf16[1024,3072]{1,0:T(8,128)(2,1)} async-done(((bf16[256,3072]{1,0:T(8,128)(2,1)}), bf16[1024,3072]{1,0:T(8,128)(2,1)}) %all-gather.9.cloned.1.call-update) | async-done | bytes 6291472 | tf_op jit(solution)/shard_map/all_gather | solution.py:123
  289.1 5.8 %convolution_convert_fusion.1 = bf16[256,3072]{1,0:T(8,128)(2,1)} fusion(bf16[1024,3072]{1,0:T(8,128)(2,1)} %all-gather.9.cloned.1.call-done, bf16[256,1024]{1,0:T(8,128)(2,1)S(1)} %get-tuple-element.97, f32[1024]{0:T(1024)S(1)} %bitcast.126, f32[256]{0:T(256)S(1)} %add_rsqrt_fusion), kind=kOutput, calls=%fused_computation.23 | convolution fusion | flops 1612447744 | bytes 8393728 | tf_op jit(solution)/shard_map/dot_general | solution.py:36
  294.9 1.7 copy.60
  297.5 39.9 %all_to_all.45 = bf16[4,8,128,192]{2,3,1,0:T(8,128)(2,1)S(1)} all-to-all(bf16[4,8,128,192]{2,3,1,0:T(8,128)(2,1)S(1)} %bitcast.105), channel_id=1, replica_groups=mesh['groups'=2,'sec'=4,'plane'=4] {'plane'}, dimensions={0} | all-to-all | bytes 3145728 | tf_op jit(solution)/shard_map/all_to_all | solution.py:135
  338.0 3.2 all-to-all-start
  341.8 2.5 copy.69
  344.4 2.4 all-to-all-done
  346.8 16.5 %while.11 = (s32[]{:T(128)}, bf16[8,512,64]{1,2,0:T(8,128)(2,1)S(1)}, bf16[8,512]{1,0:T(8,128)(2,1)S(1)}, bf16[8,512,192]{2,1,0:T(8,128)(2,1)}, s32[]{:T(128)}) while((s32[]{:T(128)}, bf16[8,512,64]{1,2,0:T(8,128)(2,1)S(1)}, bf16[8,512]{1,0:T(8,128)(2,1)S(1)}, bf16[8,512,192]{2,1,0:T(8,128)(2,1)}, s32[]{:T(128)}) %tuple.56), condition=%wide.region_7.8_spmd.clone, body=%wide.region_4.7_spmd.clone.sunk | while | flops 71336448 | bytes 3945545 | solution.py:69
  364.2 1.6 reshape.161
  365.8 3.6 all-to-all-start.2
  370.8 51.4 %all-reduce.1 = f32[32]{0:T(128)S(1)} all-reduce(f32[32]{0:T(128)S(1)} %convert_reduce_fusion), channel_id=3, replica_groups=mesh['groups'=2,'sec'=4,'plane'=4] {'sec','plane'}, use_global_device_ids=true, to_apply=%region_10.11.clone | all-reduce | flops 32 | bytes 256
  424.5 2.3 fusion.19
  427.8 85.2 %all-reduce.4.cloned.1.call-done = f32[32,1024]{1,0:T(8,128)} async-done(((f32[32,1024]{1,0:T(8,128)}), f32[32,1024]{1,0:T(8,128)}) %all-reduce.4.cloned.1.call-update) | async-done | bytes 131088
  512.9 1.4 dynamic-slice_divide_fusion
  (108 shorter events, 31.8 us)
Async XLA Ops:
  7.2 2.3 copy-start.6
  7.2 2.5 copy-start
  7.2 2.7 copy-start.4
  7.2 120.5 %all-gather.5.cloned.1.call-start = ((), (), s32[]{:S(2)}) async-start(), calls=%async_computation.3 | async-start | bytes 7864320 | tf_op jit(solution)/shard_map/all_gather | solution.py:88
  7.9 165.5 %all-gather.7.cloned.1.call-start = ((), (), s32[]{:S(2)}) async-start(), calls=%async_computation.4 | async-start | bytes 2621440 | tf_op jit(solution)/shard_map/all_gather | solution.py:118
  8.7 280.5 %all-gather.9.cloned.1.call-start = ((), (), s32[]{:S(2)}) async-start(), calls=%async_computation.5 | async-start | bytes 7864320 | tf_op jit(solution)/shard_map/all_gather | solution.py:123
  133.4 8.2 %collective-permute-start = (bf16[128,2048]{0,1:T(8,128)(2,1)}, bf16[128,2048]{0,1:T(8,128)(2,1)}, u32[]{:S(2)}, u32[]{:S(2)}) collective-permute-start(bf16[128,2048]{0,1:T(8,128)(2,1)} %bitcast.121), channel_id=1, source_target_pairs={{0,4},{4,8},{8,12},{1,5},{5,9},{9,13},{2,6},{6,10},{10,14},{3,7},{... | collective-permute-start | bytes 1572872 | tf_op jit(solution)/shard_map/ppermute | solution.py:19
  137.2 4.4 collective-permute-start.1
  175.9 119.0 %copy-start.2 = (bf16[256,1024]{1,0:T(8,128)(2,1)}, bf16[256,1024]{1,0:T(8,128)(2,1)S(1)}, u32[]{:S(2)}) copy-start(bf16[256,1024]{1,0:T(8,128)(2,1)S(1)} %get-tuple-element.97) | copy-start | bytes 1572868
  338.0 8.8 %all-to-all-start = ((bf16[4,8,128]{2,1,0:T(8,128)(2,1)}), bf16[4,8,128]{2,1,0:T(8,128)(2,1)S(1)}, u32[]{:S(2)}, u32[]{:S(2)}) async-start(bf16[4,8,128]{2,1,0:T(8,128)(2,1)} %broadcast_in_dim.86), calls=%async_computation | async-start | bytes 16384 | tf_op jit(solution)/shard_map/all_to_all | solution.py:136
  341.2 83.2 %all-gather.11.cloned.1.call-start = ((), (), s32[]{:S(2)}) async-start(), calls=%async_computation.6 | async-start | bytes 2621440 | tf_op jit(solution)/shard_map/all_gather | solution.py:143
  363.3 6.1 %copy-start.7 = (u32[32]{0:T(128)S(1)}, u32[32]{0:T(128)}, u32[]{:S(2)}) copy-start(u32[32]{0:T(128)} %constant.80) | copy-start | bytes 388
  363.3 7.3 %copy-start.5 = (s32[2,128]{1,0:T(2,128)S(1)}, s32[2,128]{1,0:T(2,128)}, u32[]{:S(2)}) copy-start(s32[2,128]{1,0:T(2,128)} %param.12) | copy-start | bytes 3076
  365.8 58.7 %copy-start.3 = (bf16[256,1024]{1,0:T(8,128)(2,1)S(1)}, bf16[256,1024]{1,0:T(8,128)(2,1)}, u32[]{:S(2)}) copy-start(bf16[256,1024]{1,0:T(8,128)(2,1)} %copy-done.2) | copy-start | bytes 1572868
  365.8 56.4 %all-to-all-start.2 = ((bf16[4,2,32768]{2,1,0:T(2,128)(2,1)}), bf16[4,2,32768]{2,1,0:T(2,128)(2,1)S(1)}, u32[]{:S(2)}, u32[]{:S(2)}) async-start(bf16[4,2,32768]{2,1,0:T(2,128)(2,1)} %reshape.161), calls=%async_computation.2 | async-start | bytes 1048576 | tf_op jit(solution)/shard_map/all_to_all | solution.py:139
  369.4 143.5 %all-reduce.4.cloned.1.call-start = ((), (), s32[]{:S(2)}) async-start(), calls=%async_computation.7 | async-start | bytes 262144
  426.8 87.6 %copy-start.1 = (bf16[256,1024]{1,0:T(8,128)(2,1)}, bf16[256,1024]{1,0:T(8,128)(2,1)S(1)}, u32[]{:S(2)}) copy-start(bf16[256,1024]{1,0:T(8,128)(2,1)S(1)} %fusion.19) | copy-start | bytes 1572868
Sparse Core Ops, SparseCore 0:
  9.6 118.0 all-gather.4
  129.3 44.1 all-gather.6
  175.0 114.0 all-gather.8
  343.3 58.9 all-gather.10
  427.8 85.0 all-reduce.3
where the time goes:
time: 523 us; the launch traced here: 521 us
  waiting for transfers between devices  344 us (66%)
  blocking collectives  91.3 us (17%)
  matrix products  25.1 us (5%)
  local copies, waits for them, and re-layouts  24.3 us (5%)
  between operations  14.8 us (3%)
  starting transfers between devices  11.3 us (2%)
  other arithmetic  9.65 us (2%)
    all_gather x1, waiting for transfers between devices, body(): lax.all_gather(cross_qkv, 'plane', axis=0, tiled=True)  118 us
    all_gather x1, waiting for transfers between devices, body(): lax.all_gather(plane_qkv, 'plane', axis=0, tiled=True)  113 us
    unnamed x6, waiting for transfers between devices  87.6 us
    unnamed x1, blocking collectives  51.4 us
    all_to_all x1, blocking collectives, body(): lax.all_to_all(heads_first, 'plane', split_axis=0, concat_axis=2, tiled=T...  39.9 us
    all_gather x1, waiting for transfers between devices, body(): lax.all_gather(cross_out, 'plane', axis=0, tiled=True)  23.4 us
    dot_general x4, matrix products, fold_product(): return jnp.dot(inputs, weight_piece, preferred_element_type=jnp.float32)  15.1 us
  transfers between devices with their start and end apart: 9, of which 5 were waited for; matrix products, arithmetic and copies ran while one was open for 9% of the time, Pallas kernels for 0%

commit v1 on v0

--- a/solution.py
+++ b/solution.py
@@ -34,6 +34,38 @@
 
 def fold_product(inputs, weight_piece):
     return jnp.dot(inputs, weight_piece, preferred_element_type=jnp.float32)
+
+
+def gather_pieces(shard):
+    groups = lax.axis_size("groups")
+    sections = lax.axis_size("sec")
+    pair = 2 if sections % 2 == 0 else 1
+    width = shard.shape[1] // (groups * pair)
+    g = lax.axis_index("groups")
+    k = lax.axis_index("sec") % pair
+    own = g * pair + k
+    mine = lax.dynamic_slice_in_dim(shard, own * width, width, axis=1)
+    first = lax.all_gather(mine, "plane", axis=0, tiled=True)
+    by_group = [(own, first)]
+    for step in range(1, groups):
+        moved = [(i, (i + step) % groups) for i in range(groups)]
+        source = lax.rem(g - step + groups, groups)
+        by_group.append((source * pair + k, lax.ppermute(first, "groups", moved)))
+    held = list(by_group)
+    if pair == 2:
+        swap = [(i, i ^ 1) for i in range(sections)]
+        for piece, block in by_group:
+            held.append((piece - k + (1 - k), lax.ppermute(block, "sec", swap)))
+    return held, width
+
+
+def project(inputs, pieces):
+    held, width = pieces
+    out = jnp.zeros((inputs.shape[0], width * len(held)), jnp.float32)
+    for piece, block in held:
+        part = jnp.dot(inputs, block, preferred_element_type=jnp.float32)
+        out = lax.dynamic_update_slice_in_dim(out, part, piece * width, axis=1)
+    return out
 
 
 def attend_items(pieces):
@@ -83,9 +115,13 @@
     near_valid = positions[None, :] < near_counts[:, None]
     own_valid = near_valid[1 : sec_block + 1]
     score_scale = 1.0 / math.sqrt(HEAD_DIM)
+    cross_qkv_pieces = gather_pieces(cross_qkv)
+    cross_out_pieces = gather_pieces(cross_out)
+    plane_qkv_pieces = gather_pieces(plane_qkv)
+    plane_out_pieces = gather_pieces(plane_out)
     normed = rms_norm(tokens, norm_gains[0])
     inputs = normed.reshape(-1, model_width)
-    result = fold_product(inputs, lax.all_gather(cross_qkv, "plane", axis=0, tiled=True))
+    result = project(inputs, cross_qkv_pieces)
     projected = result.astype(jnp.bfloat16).reshape(sec_block, tok_block, 3 * model_width)
     own_kv = projected[:, :, model_width:]
     from_below = shifted_2(own_kv[sec_block - 1], "sec", 1)
@@ -115,12 +151,12 @@
         "snhqk,snkhd->snqhd", attention, stacked[:, :, :, 1], preferred_element_type=jnp.float32
     )
     context = context.astype(jnp.bfloat16).reshape(-1, model_width)
-    result = fold_product(context, lax.all_gather(cross_out, "plane", axis=0, tiled=True))
+    result = project(context, cross_out_pieces)
     after_cross = (tokens.reshape(-1, model_width).astype(jnp.float32) + result).astype(
         jnp.bfloat16
     )
     normed = rms_norm(after_cross, norm_gains[1])
-    result = fold_product(normed, lax.all_gather(plane_qkv, "plane", axis=0, tiled=True))
+    result = project(normed, plane_qkv_pieces)
     projected = result.astype(jnp.bfloat16).reshape(sec_block, tok_block, 3, HEADS, HEAD_DIM)
     per_device = sec_block * HEADS // plane_count
     heads_first = jnp.transpose(projected, (0, 3, 1, 2, 4)).reshape(
@@ -140,7 +176,7 @@
     context = jnp.transpose(
         returned.reshape(sec_block, HEADS, tok_block, HEAD_DIM), (0, 2, 1, 3)
     ).reshape(-1, model_width)
-    result = fold_product(context, lax.all_gather(plane_out, "plane", axis=0, tiled=True))
+    result = project(context, plane_out_pieces)
     encoded = (after_cross.astype(jnp.float32) + result).astype(jnp.bfloat16)
     labels = region_ids.reshape(-1)
     member = (jnp.arange(regions, dtype=jnp.int32)[:, None] == labels[None, :]) & own_valid.reshape(

time: 523 us -> 394 us (0.75)
  waiting for transfers between devices: 344 us -> 164 us
  blocking collectives: 91.3 us -> 116 us
  local copies, waits for them, and re-layouts: 24.3 us -> 33.5 us
  matrix products: 25.1 us -> 32.7 us
  starting transfers between devices: 11.3 us -> 17.5 us
    all_gather x4 -> x2, waiting for transfers between devices: 254 us -> 41.9 us  [gather_pieces(): first = lax.all_gather(mine, 'plane', axis=0, tiled=True)]
    all_gather x0 -> x2, blocking collectives: none -> 42 us  [gather_pieces(): first = lax.all_gather(mine, 'plane', axis=0, tiled=True)]
    ppermute x0 -> x12, waiting for transfers between devices: none -> 35.7 us  [the longest x4 35.7 us: gather_pieces(): by_group.append((source * pair + k, lax.ppermute(first, 'groups', moved)))]
    unnamed x1, blocking collectives: 51.4 us -> 33.8 us
    dot_general x4 -> x16, matrix products: 15.1 us -> 22.8 us  [project(): part = jnp.dot(inputs, block, preferred_element_type=jnp.float32)]
    ppermute x0 -> x12, starting transfers between devices: none -> 6.43 us  [the longest x4 3.5 us: gather_pieces(): by_group.append((source * pair + k, lax.ppermute(first, 'groups', moved)))]
    unnamed x6 -> x4, waiting for transfers between devices: 87.6 us -> 83.6 us
  transfers between devices with their start and end apart: 9 -> 19, of which waited for: 5 -> 6; matrix products, arithmetic and copies ran while one was open for 9% -> 13% of each run, Pallas kernels for 0% -> 0%
where the time goes in v1:
time: 394 us; the launch traced here: 391 us
  waiting for transfers between devices  164 us (42%)
  blocking collectives  116 us (29%)
  local copies, waits for them, and re-layouts  33.5 us (9%)
  matrix products  32.7 us (8%)
  starting transfers between devices  17.5 us (4%)
  between operations  15 us (4%)
  other arithmetic  12.9 us (3%)
    unnamed x4, waiting for transfers between devices  83.6 us
    all_gather x2, blocking collectives, gather_pieces(): first = lax.all_gather(mine, 'plane', axis=0, tiled=True)  42 us
    all_gather x2, waiting for transfers between devices, gather_pieces(): first = lax.all_gather(mine, 'plane', axis=0, tiled=True)  41.9 us
    all_to_all x1, blocking collectives, body(): lax.all_to_all(heads_first, 'plane', split_axis=0, concat_axis=2, tiled=T...  39.9 us
    ppermute x4, waiting for transfers between devices, gather_pieces(): by_group.append((source * pair + k, lax.ppermute(first, 'groups', moved)))  35.7 us
    unnamed x1, blocking collectives  33.8 us
    dot_general x16, matrix products, project(): part = jnp.dot(inputs, block, preferred_element_type=jnp.float32)  22.8 us
    unnamed x29, local copies, waits for them, and re-layouts  8.1 us
  transfers between devices with their start and end apart: 19, of which 6 were waited for; matrix products, arithmetic and copies ran while one was open for 13% of the time, Pallas kernels for 0%

profile of v1, /device:TPU:0, one launch (start us, length us, event | category | flops | bytes accessed | tf_op | source)
XLA Modules:
  0.0 391.4 jit_solution(481135209715958584)
XLA Ops:
  11.2 38.2 %all-gather.3.cloned.1.call-done = bf16[1024,768]{1,0:T(8,128)(2,1)} async-done(((bf16[256,768]{1,0:T(8,128)(2,1)}), bf16[1024,768]{1,0:T(8,128)(2,1)}) %all-gather.3.cloned.1.call-update) | async-done | bytes 1572880 | tf_op jit(solution)/shard_map/all_gather | solution.py:48
  51.8 19.5 %all_gather.13 = bf16[1024,256]{1,0:T(8,128)(2,1)} all-gather(bf16[256,256]{1,0:T(8,128)(2,1)S(1)} %constant_dynamic-slice_fusion.2), channel_id=1, replica_groups=mesh['groups'=2,'sec'=4,'plane'=4] {'plane'}, dimensions={0}, use_global_device_ids=true | all-gather | bytes 655360 | tf_op jit(solution)/shard_map/all_gather | solution.py:48
  72.5 14.5 %collective-permute-done = bf16[1024,768]{1,0:T(8,128)(2,1)} collective-permute-done((bf16[1024,768]{1,0:T(8,128)(2,1)}, bf16[1024,768]{1,0:T(8,128)(2,1)}, u32[]{:S(2)}, u32[]{:S(2)}) %collective-permute-start) | collective-permute-done | bytes 1572896 | tf_op jit(solution)/shard_map/ppermute | solution.py:53
  87.2 3.8 all-gather.5.cloned.1.call-done
  91.5 2.0 convolution_dynamic-update-slice_fusion.7
  97.5 2.0 convolution_dynamic-update-slice_fusion.4
  100.6 2.5 collective-permute-start.3
  109.5 21.2 %collective-permute-done.8 = bf16[1024,768]{1,0:T(8,128)(2,1)} collective-permute-done((bf16[1024,768]{1,0:T(8,128)(2,1)}, bf16[1024,768]{1,0:T(8,128)(2,1)}, u32[]{:S(2)}, u32[]{:S(2)}) %collective-permute-start.8) | collective-permute-done | bytes 1572896 | tf_op jit(solution)/shard_map/ppermute | solution.py:53
  131.2 2.7 pad_maximum_fusion.2
  133.9 2.4 copy.53
  137.6 2.0 pad_maximum_fusion
  140.7 3.2 fusion.56
  154.3 2.0 convolution_dynamic-update-slice_fusion.2
  156.4 2.0 convolution_dynamic-update-slice_fusion.1
  158.4 2.0 convolution_dynamic-update-slice_fusion
  162.0 39.9 %all_to_all.45 = bf16[4,8,128,192]{2,3,1,0:T(8,128)(2,1)S(1)} all-to-all(bf16[4,8,128,192]{2,3,1,0:T(8,128)(2,1)S(1)} %bitcast.141), channel_id=1, replica_groups=mesh['groups'=2,'sec'=4,'plane'=4] {'plane'}, dimensions={0} | all-to-all | bytes 3145728 | tf_op jit(solution)/shard_map/all_to_all | solution.py:171
  202.5 3.5 all-to-all-start
  206.0 2.6 copy.68
  208.6 2.7 all-to-all-done
  211.3 16.5 %while.11 = (s32[]{:T(128)}, bf16[8,512,64]{1,2,0:T(8,128)(2,1)S(1)}, bf16[8,512]{1,0:T(8,128)(2,1)S(1)}, bf16[8,512,192]{2,1,0:T(8,128)(2,1)}, s32[]{:T(128)}) while((s32[]{:T(128)}, bf16[8,512,64]{1,2,0:T(8,128)(2,1)S(1)}, bf16[8,512]{1,0:T(8,128)(2,1)S(1)}, bf16[8,512,192]{2,1,0:T(8,128)(2,1)}, s32[]{:T(128)}) %tuple.52), condition=%wide.region_7.8_spmd.clone, body=%wide.region_4.7_spmd.clone.sunk | while | flops 71336448 | bytes 3945545 | solution.py:101
  230.2 3.5 all-to-all-start.2
  234.6 22.5 %all_gather.15 = bf16[1024,256]{1,0:T(8,128)(2,1)S(1)} all-gather(bf16[256,256]{1,0:T(8,128)(2,1)S(1)} %constant_dynamic-slice_fusion), channel_id=1, replica_groups=mesh['groups'=2,'sec'=4,'plane'=4] {'plane'}, dimensions={0}, use_global_device_ids=true | all-gather | bytes 655360 | tf_op jit(solution)/shard_map/all_gather | solution.py:48
  259.9 33.8 %all-reduce.1 = f32[32]{0:T(128)S(1)} all-reduce(f32[32]{0:T(128)S(1)} %convert_reduce_fusion), channel_id=3, replica_groups=mesh['groups'=2,'sec'=4,'plane'=4] {'sec','plane'}, use_global_device_ids=true, to_apply=%region_10.11.clone | all-reduce | flops 32 | bytes 256
  299.9 83.5 %all-reduce.4.cloned.1.call-done = f32[32,1024]{1,0:T(8,128)} async-done(((f32[32,1024]{1,0:T(8,128)}), f32[32,1024]{1,0:T(8,128)}) %all-reduce.4.cloned.1.call-update) | async-done | bytes 131088
  (158 shorter events, 64.1 us)
Async XLA Ops:
  7.2 42.2 %all-gather.3.cloned.1.call-start = ((), (), s32[]{:S(2)}) async-start(), calls=%async_computation.3 | async-start | bytes 1966080 | tf_op jit(solution)/shard_map/all_gather | solution.py:48
  8.6 63.0 %copy-start.10 = (s32[8]{0:T(128)S(1)}, s32[8]{0:T(128)}, u32[]{:S(2)}) copy-start(s32[8]{0:T(128)} %param.11) | copy-start | bytes 100
  8.6 63.7 %copy-start.2 = (bf16[2,128,1024]{2,1,0:T(8,128)(2,1)S(1)}, bf16[2,128,1024]{2,1,0:T(8,128)(2,1)}, u32[]{:S(2)}) copy-start(bf16[2,128,1024]{2,1,0:T(8,128)(2,1)} %param.10) | copy-start | bytes 1572868
  9.4 77.7 %copy-start.7 = (f32[2,1024]{1,0:T(2,128)S(1)}, f32[2,1024]{1,0:T(2,128)}, u32[]{:S(2)}) copy-start(f32[2,1024]{1,0:T(2,128)} %param.13) | copy-start | bytes 24580
  9.4 81.6 %all-gather.5.cloned.1.call-start = ((), (), s32[]{:S(2)}) async-start(), calls=%async_computation.4 | async-start | bytes 1966080 | tf_op jit(solution)/shard_map/all_gather | solution.py:48
  49.4 37.6 %collective-permute-start = (bf16[1024,768]{1,0:T(8,128)(2,1)}, bf16[1024,768]{1,0:T(8,128)(2,1)}, u32[]{:S(2)}, u32[]{:S(2)}) collective-permute-start(bf16[1024,768]{1,0:T(8,128)(2,1)} %all-gather.3.cloned.1.call-done), channel_id=1, source_target_pairs={{0,16},{16,0},{1,17},{17,1},{2,18},{18,2},{3,19},{19,3},{4,20},{20... | collective-permute-start | bytes 4718600 | tf_op jit(solution)/shard_map/ppermute | solution.py:53
  71.3 33.5 %collective-permute-start.5 = (bf16[1024,256]{1,0:T(8,128)(2,1)}, bf16[1024,256]{1,0:T(8,128)(2,1)}, u32[]{:S(2)}, u32[]{:S(2)}) collective-permute-start(bf16[1024,256]{1,0:T(8,128)(2,1)} %all_gather.13), channel_id=1, source_target_pairs={{0,16},{16,0},{1,17},{17,1},{2,18},{18,2},{3,19},{19,3},{4,20},{20... | collective-permute-start | bytes 1572872 | tf_op jit(solution)/shard_map/ppermute | solution.py:53
  71.5 77.7 %collective-permute-start.6 = (bf16[1024,256]{1,0:T(8,128)(2,1)}, bf16[1024,256]{1,0:T(8,128)(2,1)}, u32[]{:S(2)}, u32[]{:S(2)}) collective-permute-start(bf16[1024,256]{1,0:T(8,128)(2,1)} %all_gather.13), channel_id=1, source_target_pairs={{0,4},{4,0},{8,12},{12,8},{1,5},{5,1},{9,13},{13,9},{2,6},{6,2},{1... | collective-permute-start | bytes 1572872 | tf_op jit(solution)/shard_map/ppermute | solution.py:58
  71.8 23.7 %collective-permute-start.1 = (bf16[1024,768]{1,0:T(8,128)(2,1)}, bf16[1024,768]{1,0:T(8,128)(2,1)}, u32[]{:S(2)}, u32[]{:S(2)}) collective-permute-start(bf16[1024,768]{1,0:T(8,128)(2,1)} %all-gather.3.cloned.1.call-done), channel_id=1, source_target_pairs={{0,4},{4,0},{8,12},{12,8},{1,5},{5,1},{9,13},{13,9},{2,6},{6,2},{1... | collective-permute-start | bytes 4718600 | tf_op jit(solution)/shard_map/ppermute | solution.py:58
  87.0 10.5 %collective-permute-start.2 = (bf16[1024,768]{1,0:T(8,128)(2,1)}, bf16[1024,768]{1,0:T(8,128)(2,1)}, u32[]{:S(2)}, u32[]{:S(2)}) collective-permute-start(bf16[1024,768]{1,0:T(8,128)(2,1)} %collective-permute-done), channel_id=1, source_target_pairs={{0,4},{4,0},{8,12},{12,8},{1,5},{5,1},{9,13},{13,9},{2,6},{6,2},{1... | collective-permute-start | bytes 4718600 | tf_op jit(solution)/shard_map/ppermute | solution.py:58
  91.0 39.7 %collective-permute-start.8 = (bf16[1024,768]{1,0:T(8,128)(2,1)}, bf16[1024,768]{1,0:T(8,128)(2,1)}, u32[]{:S(2)}, u32[]{:S(2)}) collective-permute-start(bf16[1024,768]{1,0:T(8,128)(2,1)} %all-gather.5.cloned.1.call-done), channel_id=1, source_target_pairs={{0,16},{16,0},{1,17},{17,1},{2,18},{18,2},{3,19},{19,3},{4,20},{20... | collective-permute-start | bytes 4718600 | tf_op jit(solution)/shard_map/ppermute | solution.py:53
  100.6 30.1 %collective-permute-start.3 = (bf16[128,2048]{1,0:T(8,128)(2,1)}, bf16[128,2048]{1,0:T(8,128)(2,1)}, u32[]{:S(2)}, u32[]{:S(2)}) collective-permute-start(bf16[128,2048]{1,0:T(8,128)(2,1)} %get-tuple-element.85), channel_id=1, source_target_pairs={{0,4},{4,8},{8,12},{1,5},{5,9},{9,13},{2,6},{6,10},{10,14},{3,7},{... | collective-permute-start | bytes 1572872 | tf_op jit(solution)/shard_map/ppermute | solution.py:19
  103.1 28.1 %collective-permute-start.4 = (bf16[128,2048]{1,0:T(8,128)(2,1)}, bf16[128,2048]{1,0:T(8,128)(2,1)}, u32[]{:S(2)}, u32[]{:S(2)}) collective-permute-start(bf16[128,2048]{1,0:T(8,128)(2,1)} %get-tuple-element.86), channel_id=1, source_target_pairs={{4,0},{8,4},{12,8},{5,1},{9,5},{13,9},{6,2},{10,6},{14,10},{7,3},{... | collective-permute-start | bytes 1572872 | tf_op jit(solution)/shard_map/ppermute | solution.py:19
  104.8 45.9 %collective-permute-start.7 = (bf16[1024,256]{1,0:T(8,128)(2,1)}, bf16[1024,256]{1,0:T(8,128)(2,1)}, u32[]{:S(2)}, u32[]{:S(2)}) collective-permute-start(bf16[1024,256]{1,0:T(8,128)(2,1)} %collective-permute-done.5), channel_id=1, source_target_pairs={{0,4},{4,0},{8,12},{12,8},{1,5},{5,1},{9,13},{13,9},{2,6},{6,2},{1... | collective-permute-start | bytes 1572872 | tf_op jit(solution)/shard_map/ppermute | solution.py:58
  130.7 25.7 %collective-permute-start.9 = (bf16[1024,768]{1,0:T(8,128)(2,1)}, bf16[1024,768]{1,0:T(8,128)(2,1)}, u32[]{:S(2)}, u32[]{:S(2)}) collective-permute-start(bf16[1024,768]{1,0:T(8,128)(2,1)} %all-gather.5.cloned.1.call-done), channel_id=1, source_target_pairs={{0,4},{4,0},{8,12},{12,8},{1,5},{5,1},{9,13},{13,9},{2,6},{6,2},{1... | collective-permute-start | bytes 4718600 | tf_op jit(solution)/shard_map/ppermute | solution.py:58
  130.7 27.7 %collective-permute-start.10 = (bf16[1024,768]{1,0:T(8,128)(2,1)}, bf16[1024,768]{1,0:T(8,128)(2,1)}, u32[]{:S(2)}, u32[]{:S(2)}) collective-permute-start(bf16[1024,768]{1,0:T(8,128)(2,1)} %collective-permute-done.8), channel_id=1, source_target_pairs={{0,4},{4,0},{8,12},{12,8},{1,5},{5,1},{9,13},{13,9},{2,6},{6,2},{1... | collective-permute-start | bytes 4718600 | tf_op jit(solution)/shard_map/ppermute | solution.py:58
  202.5 8.8 %all-to-all-start = ((bf16[4,8,128]{2,1,0:T(8,128)(2,1)}), bf16[4,8,128]{2,1,0:T(8,128)(2,1)S(1)}, u32[]{:S(2)}, u32[]{:S(2)}) async-start(bf16[4,8,128]{2,1,0:T(8,128)(2,1)} %broadcast_in_dim.86), calls=%async_computation | async-start | bytes 16384 | tf_op jit(solution)/shard_map/all_to_all | solution.py:172
  230.2 63.7 %all-to-all-start.2 = ((bf16[4,2,32768]{2,1,0:T(2,128)(2,1)}), bf16[4,2,32768]{2,1,0:T(2,128)(2,1)S(1)}, u32[]{:S(2)}, u32[]{:S(2)}) async-start(bf16[4,2,32768]{2,1,0:T(2,128)(2,1)} %reshape.161), calls=%async_computation.2 | async-start | bytes 1048576 | tf_op jit(solution)/shard_map/all_to_all | solution.py:175
  233.7 149.8 %all-reduce.4.cloned.1.call-start = ((), (), s32[]{:S(2)}) async-start(), calls=%async_computation.5 | async-start | bytes 262144
  257.1 36.6 %collective-permute-start.11 = (bf16[1024,256]{1,0:T(8,128)(2,1)S(1)}, bf16[1024,256]{1,0:T(8,128)(2,1)S(1)}, u32[]{:S(2)}, u32[]{:S(2)}) collective-permute-start(bf16[1024,256]{1,0:T(8,128)(2,1)S(1)} %all_gather.15), channel_id=1, source_target_pairs={{0,16},{16,0},{1,17},{17,1},{2,18},{18,2},{3,19},{19,3},{4,20},{20... | collective-permute-start | bytes 1572872 | tf_op jit(solution)/shard_map/ppermute | solution.py:53
  258.6 38.4 %collective-permute-start.12 = (bf16[1024,256]{1,0:T(8,128)(2,1)S(1)}, bf16[1024,256]{1,0:T(8,128)(2,1)}, u32[]{:S(2)}, u32[]{:S(2)}) collective-permute-start(bf16[1024,256]{1,0:T(8,128)(2,1)S(1)} %all_gather.15), channel_id=1, source_target_pairs={{0,4},{4,0},{8,12},{12,8},{1,5},{5,1},{9,13},{13,9},{2,6},{6,2},{1... | collective-permute-start | bytes 1572872 | tf_op jit(solution)/shard_map/ppermute | solution.py:58
  293.8 4.6 %collective-permute-start.13 = (bf16[1024,256]{1,0:T(8,128)(2,1)S(1)}, bf16[1024,256]{1,0:T(8,128)(2,1)S(1)}, u32[]{:S(2)}, u32[]{:S(2)}) collective-permute-start(bf16[1024,256]{1,0:T(8,128)(2,1)S(1)} %collective-permute-done.11), channel_id=1, source_target_pairs={{0,4},{4,0},{8,12},{12,8},{1,5},{5,1},{9,13},{13,9},{2,6},{6,2},{1... | collective-permute-start | bytes 1572872 | tf_op jit(solution)/shard_map/ppermute | solution.py:58
  298.4 86.4 %copy-start.1 = (bf16[256,3072]{1,0:T(8,128)(2,1)S(1)}, bf16[256,3072]{1,0:T(8,128)(2,1)}, u32[]{:S(2)}) copy-start(bf16[256,3072]{1,0:T(8,128)(2,1)} %param.14) | copy-start | bytes 4718596
  299.0 85.9 %copy-start.4 = (bf16[256,1024]{1,0:T(8,128)(2,1)}, bf16[256,1024]{1,0:T(8,128)(2,1)S(1)}, u32[]{:S(2)}) copy-start(bf16[256,1024]{1,0:T(8,128)(2,1)S(1)} %fusion.24) | copy-start | bytes 1572868
  (7 other events, 73.4 us)
Sparse Core Ops, SparseCore 0:
  9.6 39.7 all-gather.2
  51.5 39.4 all-gather.4
  300.0 83.4 all-reduce.3

commit v2 on v1

--- a/solution.py
+++ b/solution.py
@@ -36,15 +36,22 @@
     return jnp.dot(inputs, weight_piece, preferred_element_type=jnp.float32)
 
 
-def gather_pieces(shard):
+def gather_pieces(shards):
     groups = lax.axis_size("groups")
     sections = lax.axis_size("sec")
     pair = 2 if sections % 2 == 0 else 1
-    width = shard.shape[1] // (groups * pair)
+    count = groups * pair
+    widths = [shard.shape[1] // count for shard in shards]
     g = lax.axis_index("groups")
     k = lax.axis_index("sec") % pair
     own = g * pair + k
-    mine = lax.dynamic_slice_in_dim(shard, own * width, width, axis=1)
+    mine = jnp.concatenate(
+        [
+            lax.dynamic_slice_in_dim(shard, own * width, width, axis=1)
+            for shard, width in zip(shards, widths)
+        ],
+        axis=1,
+    )
     first = lax.all_gather(mine, "plane", axis=0, tiled=True)
     by_group = [(own, first)]
     for step in range(1, groups):
@@ -56,7 +63,12 @@
         swap = [(i, i ^ 1) for i in range(sections)]
         for piece, block in by_group:
             held.append((piece - k + (1 - k), lax.ppermute(block, "sec", swap)))
-    return held, width
+    results = []
+    offset = 0
+    for width in widths:
+        results.append(([(piece, block[:, offset : offset + width]) for piece, block in held], width))
+        offset += width
+    return results
 
 
 def project(inputs, pieces):
@@ -115,10 +127,9 @@
     near_valid = positions[None, :] < near_counts[:, None]
     own_valid = near_valid[1 : sec_block + 1]
     score_scale = 1.0 / math.sqrt(HEAD_DIM)
-    cross_qkv_pieces = gather_pieces(cross_qkv)
-    cross_out_pieces = gather_pieces(cross_out)
-    plane_qkv_pieces = gather_pieces(plane_qkv)
-    plane_out_pieces = gather_pieces(plane_out)
+    (cross_qkv_pieces,) = gather_pieces([cross_qkv])
+    (plane_qkv_pieces,) = gather_pieces([plane_qkv])
+    cross_out_pieces, plane_out_pieces = gather_pieces([cross_out, plane_out])
     normed = rms_norm(tokens, norm_gains[0])
     inputs = normed.reshape(-1, model_width)
     result = project(inputs, cross_qkv_pieces)
@@ -182,13 +193,27 @@
     member = (jnp.arange(regions, dtype=jnp.int32)[:, None] == labels[None, :]) & own_valid.reshape(
         -1
     )[None, :]
-    region_sum = jnp.dot(member.astype(jnp.bfloat16), encoded, preferred_element_type=jnp.float32)
-    region_count = jnp.sum(member.astype(jnp.float32), axis=1)
-    totals, counted = (
-        lax.psum_scatter(region_sum, ("sec", "plane"), scatter_dimension=0, tiled=True),
-        lax.psum_scatter(region_count, ("sec", "plane"), scatter_dimension=0, tiled=True),
-    )
-    pooled = totals / jnp.maximum(counted, 1.0)[:, None]
+    extended = jnp.concatenate([encoded, jnp.ones((encoded.shape[0], 128), jnp.bfloat16)], axis=1)
+    partial = jnp.dot(member.astype(jnp.bfloat16), extended, preferred_element_type=jnp.float32)
+    sections = lax.axis_size("sec")
+    width = partial.shape[1]
+    partial = partial.reshape(sections, plane_count, 2, width)
+    me_plane = lax.axis_index("plane")
+    gathered = lax.dynamic_index_in_dim(partial, me_plane, axis=1, keepdims=False)
+    for step in range(1, plane_count):
+        moved = [(i, (i + step) % plane_count) for i in range(plane_count)]
+        target = lax.rem(me_plane + step, plane_count)
+        block = lax.dynamic_index_in_dim(partial, target, axis=1, keepdims=False)
+        gathered = gathered + lax.ppermute(block, "plane", moved)
+    me_sec = lax.axis_index("sec")
+    totals = lax.dynamic_index_in_dim(gathered, me_sec, axis=0, keepdims=False)
+    for step in range(1, sections):
+        moved = [(i, (i + step) % sections) for i in range(sections)]
+        target = lax.rem(me_sec + step, sections)
+        block = lax.dynamic_index_in_dim(gathered, target, axis=0, keepdims=False)
+        totals = totals + lax.ppermute(block, "sec", moved)
+    counted = totals[:, model_width]
+    pooled = totals[:, :model_width] / jnp.maximum(counted, 1.0)[:, None]
     return (encoded.reshape(sec_block, tok_block, model_width), pooled)
 
 

time: 394 us -> 297 us (0.75)
  blocking collectives: 116 us -> 39.9 us
  waiting for transfers between devices: 164 us -> 137 us
  starting transfers between devices: 17.5 us -> 24.6 us
    unnamed x4 -> x3, waiting for transfers between devices: 83.6 us -> 0.05 us
    all_gather x2 -> x0, blocking collectives: 42 us -> none  [gather_pieces(): first = lax.all_gather(mine, 'plane', axis=0, tiled=True)]
    unnamed x1 -> x0, blocking collectives: 33.8 us -> none
    all_gather x2 -> x3, waiting for transfers between devices: 41.9 us -> 65.3 us  [gather_pieces(): first = lax.all_gather(mine, 'plane', axis=0, tiled=True)]
    ppermute x4 -> x3, waiting for transfers between devices: 35.7 us -> 52.5 us  [gather_pieces(): by_group.append((source * pair + k, lax.ppermute(first, 'groups', moved)))]
    all_to_all x1, waiting for transfers between devices: 0.01 us -> 12.9 us  [body(): lax.all_to_all(attended, 'plane', split_axis=2, concat_axis=0, tiled=True)]
    ppermute x0 -> x6, starting transfers between devices: none -> 6.82 us  [the longest x3 3.87 us: body(): gathered = gathered + lax.ppermute(block, 'plane', moved)]
    unnamed x29 -> x28, local copies, waits for them, and re-layouts: 8.1 us -> 7.47 us
  transfers between devices with their start and end apart: 19 -> 22, of which waited for: 6 -> 11; matrix products, arithmetic and copies ran while one was open for 13% -> 15% of each run, Pallas kernels for 0% -> 0%
where the time goes in v2:
time: 297 us; the launch traced here: 296 us
  waiting for transfers between devices  137 us (46%)
  blocking collectives  39.9 us (13%)
  matrix products  33.9 us (11%)
  local copies, waits for them, and re-layouts  32.3 us (11%)
  starting transfers between devices  24.6 us (8%)
  between operations  14.5 us (5%)
  other arithmetic  12.8 us (4%)
    all_gather x3, waiting for transfers between devices, gather_pieces(): first = lax.all_gather(mine, 'plane', axis=0, tiled=True)  65.3 us
    ppermute x3, waiting for transfers between devices, gather_pieces(): by_group.append((source * pair + k, lax.ppermute(first, 'groups', moved)))  52.5 us
    all_to_all x1, blocking collectives, body(): lax.all_to_all(heads_first, 'plane', split_axis=0, concat_axis=2, tiled=T...  39.9 us
    dot_general x16, matrix products, project(): part = jnp.dot(inputs, block, preferred_element_type=jnp.float32)  24.6 us
    all_to_all x1, waiting for transfers between devices, body(): lax.all_to_all(attended, 'plane', split_axis=2, concat_axis=0, tiled=True)  12.9 us
    squeeze x8, local copies, waits for them, and re-layouts, attend_items(): return lax.map(one_item, (packed_all[0], flags_all[0]))[None]  7.76 us
    unnamed x28, local copies, waits for them, and re-layouts  7.47 us
  transfers between devices with their start and end apart: 22, of which 11 were waited for; matrix products, arithmetic and copies ran while one was open for 15% of the time, Pallas kernels for 0%

profile of v2, /device:TPU:0, one launch (start us, length us, event | category | flops | bytes accessed | tf_op | source)
XLA Modules:
  0.0 295.6 jit_solution(5493600042261658552)
XLA Ops:
  13.1 36.3 %all-gather.4.cloned.1.call-done = bf16[1024,768]{1,0:T(8,128)(2,1)} async-done(((bf16[256,768]{1,0:T(8,128)(2,1)}), bf16[1024,768]{1,0:T(8,128)(2,1)}) %all-gather.4.cloned.1.call-update) | async-done | bytes 1572880 | tf_op jit(solution)/shard_map/all_gather | solution.py:55
  51.4 34.3 %collective-permute-done = bf16[1024,768]{1,0:T(8,128)(2,1)} collective-permute-done((bf16[1024,768]{1,0:T(8,128)(2,1)}, bf16[1024,768]{1,0:T(8,128)(2,1)}, u32[]{:S(2)}, u32[]{:S(2)}) %collective-permute-start) | collective-permute-done | bytes 1572896 | tf_op jit(solution)/shard_map/ppermute | solution.py:60
  87.5 29.0 %all-gather.8.cloned.1.call-done = bf16[1024,768]{1,0:T(8,128)(2,1)} async-done(((bf16[256,768]{1,0:T(8,128)(2,1)}), bf16[1024,768]{1,0:T(8,128)(2,1)}) %all-gather.8.cloned.1.call-update) | async-done | bytes 1572880 | tf_op jit(solution)/shard_map/all_gather | solution.py:55
  118.8 2.0 convolution_dynamic-update-slice_fusion.6
  120.8 2.0 convolution_dynamic-update-slice_fusion.5
  122.8 2.0 convolution_dynamic-update-slice_fusion.4
  125.9 2.2 collective-permute-start.3
  129.8 2.0 collective-permute-start.6
  134.8 18.1 %collective-permute-done.8 = bf16[1024,768]{1,0:T(8,128)(2,1)} collective-permute-done((bf16[1024,768]{1,0:T(8,128)(2,1)}, bf16[1024,768]{1,0:T(8,128)(2,1)}, u32[]{:S(2)}, u32[]{:S(2)}) %collective-permute-start.8) | collective-permute-done | bytes 1572896 | tf_op jit(solution)/shard_map/ppermute | solution.py:60
  153.4 2.7 pad_maximum_fusion.2
  156.2 2.3 copy.37
  159.9 2.0 pad_maximum_fusion
  162.9 3.2 %fusion.71 = (f32[2,16,128]{2,1,0:T(8,128)S(1)}, f32[2,16,128,384]{3,2,1,0:T(8,128)S(1)}) fusion(f32[2,16,128,384]{3,2,1,0:T(8,128)S(1)} %fusion.18, pred[2,128,384]{2,1,0:T(8,128)(4,1)S(1)} %broadcast_or_fusion), kind=kOutput, calls=%fused_computation.133 | output fusion | flops 11010431 | bytes 12697600 | tf_op jit(solution)/shard_map/sub | solution.py:31
  176.5 2.0 convolution_dynamic-update-slice_fusion.2
  178.6 2.0 convolution_dynamic-update-slice_fusion.1
  180.7 2.0 convolution_dynamic-update-slice_fusion
  184.2 39.9 %all_to_all.45 = bf16[4,8,128,192]{2,3,1,0:T(8,128)(2,1)S(1)} all-to-all(bf16[4,8,128,192]{2,3,1,0:T(8,128)(2,1)S(1)} %bitcast.155), channel_id=1, replica_groups=mesh['groups'=2,'sec'=4,'plane'=4] {'plane'}, dimensions={0} | all-to-all | bytes 3145728 | tf_op jit(solution)/shard_map/all_to_all | solution.py:182
  224.7 3.5 %all-to-all-start = ((bf16[4,8,128]{2,1,0:T(8,128)(2,1)}), bf16[4,8,128]{2,1,0:T(8,128)(2,1)S(1)}, u32[]{:S(2)}, u32[]{:S(2)}) async-start(bf16[4,8,128]{2,1,0:T(8,128)(2,1)} %broadcast_in_dim.87), calls=%async_computation | async-start | bytes 16384 | tf_op jit(solution)/shard_map/all_to_all | solution.py:183
  228.2 2.6 copy.52
  230.8 2.7 all-to-all-done
  233.5 16.5 %while.11 = (s32[]{:T(128)}, bf16[8,512,64]{1,2,0:T(8,128)(2,1)S(1)}, bf16[8,512]{1,0:T(8,128)(2,1)S(1)}, bf16[8,512,192]{2,1,0:T(8,128)(2,1)}, s32[]{:T(128)}) while((s32[]{:T(128)}, bf16[8,512,64]{1,2,0:T(8,128)(2,1)S(1)}, bf16[8,512]{1,0:T(8,128)(2,1)S(1)}, bf16[8,512,192]{2,1,0:T(8,128)(2,1)}, s32[]{:T(128)}) %tuple.56), condition=%wide.region_7.8_spmd.clone, body=%wide.region_4.7_spmd.clone.sunk | while | flops 71336448 | bytes 3945545 | solution.py:113
  252.4 3.5 %all-to-all-start.2 = ((bf16[4,2,32768]{2,1,0:T(2,128)(2,1)}), bf16[4,2,32768]{2,1,0:T(2,128)(2,1)S(1)}, u32[]{:S(2)}, u32[]{:S(2)}) async-start(bf16[4,2,32768]{2,1,0:T(2,128)(2,1)} %reshape.163), calls=%async_computation.2 | async-start | bytes 1048576 | tf_op jit(solution)/shard_map/all_to_all | solution.py:186
  255.9 12.9 %all-to-all-done.2 = bf16[4,2,32768]{2,1,0:T(2,128)(2,1)S(1)} async-done(((bf16[4,2,32768]{2,1,0:T(2,128)(2,1)}), bf16[4,2,32768]{2,1,0:T(2,128)(2,1)S(1)}, u32[]{:S(2)}, u32[]{:S(2)}) %all-to-all-start.2) | async-done | bytes 524320 | tf_op jit(solution)/shard_map/all_to_all | solution.py:186
  277.5 2.0 collective-permute-start.12
  (164 shorter events, 69.5 us)
Async XLA Ops:
  7.2 42.2 %all-gather.4.cloned.1.call-start = ((), (), s32[]{:S(2)}) async-start(), calls=%async_computation.3 | async-start | bytes 1966080 | tf_op jit(solution)/shard_map/all_gather | solution.py:55
  9.4 76.3 %copy-start.8 = (f32[2,1024]{1,0:T(2,128)S(1)}, f32[2,1024]{1,0:T(2,128)}, u32[]{:S(2)}) copy-start(f32[2,1024]{1,0:T(2,128)} %param.13) | copy-start | bytes 24580
  9.4 76.6 %all-gather.6.cloned.1.call-start = ((), (), s32[]{:S(2)}) async-start(), calls=%async_computation.4 | async-start | bytes 1310720 | tf_op jit(solution)/shard_map/all_gather | solution.py:55
  11.3 105.3 %all-gather.8.cloned.1.call-start = ((), (), s32[]{:S(2)}) async-start(), calls=%async_computation.5 | async-start | bytes 1966080 | tf_op jit(solution)/shard_map/all_gather | solution.py:55
  49.4 36.3 %collective-permute-start = (bf16[1024,768]{1,0:T(8,128)(2,1)}, bf16[1024,768]{1,0:T(8,128)(2,1)}, u32[]{:S(2)}, u32[]{:S(2)}) collective-permute-start(bf16[1024,768]{1,0:T(8,128)(2,1)} %all-gather.4.cloned.1.call-done), channel_id=1, source_target_pairs={{0,16},{16,0},{1,17},{17,1},{2,18},{18,2},{3,19},{19,3},{4,20},{20... | collective-permute-start | bytes 4718600 | tf_op jit(solution)/shard_map/ppermute | solution.py:60
  51.1 69.7 %collective-permute-start.1 = (bf16[1024,768]{1,0:T(8,128)(2,1)}, bf16[1024,768]{1,0:T(8,128)(2,1)}, u32[]{:S(2)}, u32[]{:S(2)}) collective-permute-start(bf16[1024,768]{1,0:T(8,128)(2,1)} %all-gather.4.cloned.1.call-done), channel_id=1, source_target_pairs={{0,4},{4,0},{8,12},{12,8},{1,5},{5,1},{9,13},{13,9},{2,6},{6,2},{1... | collective-permute-start | bytes 4718600 | tf_op jit(solution)/shard_map/ppermute | solution.py:65
  51.2 67.0 %copy-start.7 = (bf16[1024,768]{1,0:T(8,128)(2,1)S(1)}, bf16[1024,768]{1,0:T(8,128)(2,1)}, u32[]{:S(2)}) copy-start(bf16[1024,768]{1,0:T(8,128)(2,1)} %all-gather.4.cloned.1.call-done) | copy-start | bytes 4718596
  85.7 37.1 %collective-permute-start.2 = (bf16[1024,768]{1,0:T(8,128)(2,1)}, bf16[1024,768]{1,0:T(8,128)(2,1)}, u32[]{:S(2)}, u32[]{:S(2)}) collective-permute-start(bf16[1024,768]{1,0:T(8,128)(2,1)} %collective-permute-done), channel_id=1, source_target_pairs={{0,4},{4,0},{8,12},{12,8},{1,5},{5,1},{9,13},{13,9},{2,6},{6,2},{1... | collective-permute-start | bytes 4718600 | tf_op jit(solution)/shard_map/ppermute | solution.py:65
  86.0 48.7 %collective-permute-start.5 = (bf16[1024,512]{1,0:T(8,128)(2,1)}, bf16[1024,512]{1,0:T(8,128)(2,1)}, u32[]{:S(2)}, u32[]{:S(2)}) collective-permute-start(bf16[1024,512]{1,0:T(8,128)(2,1)} %all-gather.6.cloned.1.call-done), channel_id=1, source_target_pairs={{0,16},{16,0},{1,17},{17,1},{2,18},{18,2},{3,19},{19,3},{4,20},{20... | collective-permute-start | bytes 3145736 | tf_op jit(solution)/shard_map/ppermute | solution.py:60
  116.6 36.3 %collective-permute-start.8 = (bf16[1024,768]{1,0:T(8,128)(2,1)}, bf16[1024,768]{1,0:T(8,128)(2,1)}, u32[]{:S(2)}, u32[]{:S(2)}) collective-permute-start(bf16[1024,768]{1,0:T(8,128)(2,1)} %all-gather.8.cloned.1.call-done), channel_id=1, source_target_pairs={{0,16},{16,0},{1,17},{17,1},{2,18},{18,2},{3,19},{19,3},{4,20},{20... | collective-permute-start | bytes 4718600 | tf_op jit(solution)/shard_map/ppermute | solution.py:60
  125.9 27.0 %collective-permute-start.3 = (bf16[128,2048]{1,0:T(8,128)(2,1)}, bf16[128,2048]{1,0:T(8,128)(2,1)}, u32[]{:S(2)}, u32[]{:S(2)}) collective-permute-start(bf16[128,2048]{1,0:T(8,128)(2,1)} %get-tuple-element.81), channel_id=1, source_target_pairs={{0,4},{4,8},{8,12},{1,5},{5,9},{9,13},{2,6},{6,10},{10,14},{3,7},{... | collective-permute-start | bytes 1572872 | tf_op jit(solution)/shard_map/ppermute | solution.py:19
  128.1 25.3 %collective-permute-start.4 = (bf16[128,2048]{1,0:T(8,128)(2,1)}, bf16[128,2048]{1,0:T(8,128)(2,1)}, u32[]{:S(2)}, u32[]{:S(2)}) collective-permute-start(bf16[128,2048]{1,0:T(8,128)(2,1)} %get-tuple-element.82), channel_id=1, source_target_pairs={{4,0},{8,4},{12,8},{5,1},{9,5},{13,9},{6,2},{10,6},{14,10},{7,3},{... | collective-permute-start | bytes 1572872 | tf_op jit(solution)/shard_map/ppermute | solution.py:19
  129.8 41.7 %collective-permute-start.6 = (bf16[1024,512]{1,0:T(8,128)(2,1)}, bf16[1024,512]{1,0:T(8,128)(2,1)}, u32[]{:S(2)}, u32[]{:S(2)}) collective-permute-start(bf16[1024,512]{1,0:T(8,128)(2,1)} %all-gather.6.cloned.1.call-done), channel_id=1, source_target_pairs={{0,4},{4,0},{8,12},{12,8},{1,5},{5,1},{9,13},{13,9},{2,6},{6,2},{1... | collective-permute-start | bytes 3145736 | tf_op jit(solution)/shard_map/ppermute | solution.py:65
  134.7 43.9 %collective-permute-start.9 = (bf16[1024,768]{1,0:T(8,128)(2,1)}, bf16[1024,768]{1,0:T(8,128)(2,1)}, u32[]{:S(2)}, u32[]{:S(2)}) collective-permute-start(bf16[1024,768]{1,0:T(8,128)(2,1)} %all-gather.8.cloned.1.call-done), channel_id=1, source_target_pairs={{0,4},{4,0},{8,12},{12,8},{1,5},{5,1},{9,13},{13,9},{2,6},{6,2},{1... | collective-permute-start | bytes 4718600 | tf_op jit(solution)/shard_map/ppermute | solution.py:65
  152.9 20.0 %collective-permute-start.7 = (bf16[1024,512]{1,0:T(8,128)(2,1)}, bf16[1024,512]{1,0:T(8,128)(2,1)}, u32[]{:S(2)}, u32[]{:S(2)}) collective-permute-start(bf16[1024,512]{1,0:T(8,128)(2,1)} %collective-permute-done.5), channel_id=1, source_target_pairs={{0,4},{4,0},{8,12},{12,8},{1,5},{5,1},{9,13},{13,9},{2,6},{6,2},{1... | collective-permute-start | bytes 3145736 | tf_op jit(solution)/shard_map/ppermute | solution.py:65
  152.9 27.7 %collective-permute-start.10 = (bf16[1024,768]{1,0:T(8,128)(2,1)}, bf16[1024,768]{1,0:T(8,128)(2,1)}, u32[]{:S(2)}, u32[]{:S(2)}) collective-permute-start(bf16[1024,768]{1,0:T(8,128)(2,1)} %collective-permute-done.8), channel_id=1, source_target_pairs={{0,4},{4,0},{8,12},{12,8},{1,5},{5,1},{9,13},{13,9},{2,6},{6,2},{1... | collective-permute-start | bytes 4718600 | tf_op jit(solution)/shard_map/ppermute | solution.py:65
  224.7 8.8 %all-to-all-start = ((bf16[4,8,128]{2,1,0:T(8,128)(2,1)}), bf16[4,8,128]{2,1,0:T(8,128)(2,1)S(1)}, u32[]{:S(2)}, u32[]{:S(2)}) async-start(bf16[4,8,128]{2,1,0:T(8,128)(2,1)} %broadcast_in_dim.87), calls=%async_computation | async-start | bytes 16384 | tf_op jit(solution)/shard_map/all_to_all | solution.py:183
  252.4 16.4 %all-to-all-start.2 = ((bf16[4,2,32768]{2,1,0:T(2,128)(2,1)}), bf16[4,2,32768]{2,1,0:T(2,128)(2,1)S(1)}, u32[]{:S(2)}, u32[]{:S(2)}) async-start(bf16[4,2,32768]{2,1,0:T(2,128)(2,1)} %reshape.163), calls=%async_computation.2 | async-start | bytes 1048576 | tf_op jit(solution)/shard_map/all_to_all | solution.py:186
  277.5 5.8 %collective-permute-start.11 = (f32[4,2,1152]{2,1,0:T(2,128)S(1)}, f32[4,2,1152]{2,1,0:T(2,128)S(1)}, u32[]{:S(2)}, u32[]{:S(2)}) collective-permute-start(f32[4,2,1152]{2,1,0:T(2,128)S(1)} %get-tuple-element.85), channel_id=1, source_target_pairs={{0,1},{1,2},{2,3},{3,0},{4,5},{5,6},{6,7},{7,4},{8,9},{9,10},{10,1... | collective-permute-start | bytes 110600 | tf_op jit(solution)/shard_map/ppermute | solution.py:207
  277.5 5.7 %collective-permute-start.12 = (f32[4,2,1152]{2,1,0:T(2,128)S(1)}, f32[4,2,1152]{2,1,0:T(2,128)S(1)}, u32[]{:S(2)}, u32[]{:S(2)}) collective-permute-start(f32[4,2,1152]{2,1,0:T(2,128)S(1)} %get-tuple-element.87), channel_id=1, source_target_pairs={{0,2},{1,3},{2,0},{3,1},{4,6},{5,7},{6,4},{7,5},{8,10},{9,11},{10,... | collective-permute-start | bytes 110600 | tf_op jit(solution)/shard_map/ppermute | solution.py:207
  279.5 4.3 %collective-permute-start.13 = (f32[4,2,1152]{2,1,0:T(2,128)S(1)}, f32[4,2,1152]{2,1,0:T(2,128)S(1)}, u32[]{:S(2)}, u32[]{:S(2)}) collective-permute-start(f32[4,2,1152]{2,1,0:T(2,128)S(1)} %get-tuple-element.86), channel_id=1, source_target_pairs={{0,3},{1,0},{2,1},{3,2},{4,7},{5,4},{6,5},{7,6},{8,11},{9,8},{10,9... | collective-permute-start | bytes 110600 | tf_op jit(solution)/shard_map/ppermute | solution.py:207
  283.9 3.1 %collective-permute-start.14 = (f32[2,1152]{1,0:T(2,128)S(1)}, f32[2,1152]{1,0:T(2,128)S(1)}, u32[]{:S(2)}, u32[]{:S(2)}) collective-permute-start(f32[2,1152]{1,0:T(2,128)S(1)} %get-tuple-element.88), channel_id=1, source_target_pairs={{0,4},{4,8},{8,12},{12,0},{1,5},{5,9},{9,13},{13,1},{2,6},{6,10},{... | collective-permute-start | bytes 27656 | tf_op jit(solution)/shard_map/ppermute | solution.py:214
  284.0 3.7 %collective-permute-start.15 = (f32[2,1152]{1,0:T(2,128)S(1)}, f32[2,1152]{1,0:T(2,128)S(1)}, u32[]{:S(2)}, u32[]{:S(2)}) collective-permute-start(f32[2,1152]{1,0:T(2,128)S(1)} %get-tuple-element.90), channel_id=1, source_target_pairs={{0,8},{4,12},{8,0},{12,4},{1,9},{5,13},{9,1},{13,5},{2,10},{6,14},... | collective-permute-start | bytes 27656 | tf_op jit(solution)/shard_map/ppermute | solution.py:214
  285.5 2.8 collective-permute-start.16
  (10 other events, 125.1 us)
Sparse Core Ops, SparseCore 0:
  9.6 39.7 all-gather.3
  51.0 26.7 all-gather.5
  80.0 36.5 all-gather.7

commit v3 on v2

--- a/solution.py
+++ b/solution.py
@@ -36,15 +36,32 @@
     return jnp.dot(inputs, weight_piece, preferred_element_type=jnp.float32)
 
 
+def replica_levels():
+    levels = []
+    if lax.axis_size("groups") % 2 == 0:
+        levels.append(("groups", lax.axis_size("groups"), 1))
+    if lax.axis_size("sec") % 4 == 0:
+        levels.append(("sec", lax.axis_size("sec"), 2))
+    if lax.axis_size("sec") % 2 == 0:
+        levels.append(("sec", lax.axis_size("sec"), 1))
+    return levels
+
+
+def rotate_rows(values, axis):
+    plane_count = lax.axis_size("plane")
+    block = values.shape[axis] // plane_count
+    start = (lax.axis_index("plane") + 1) * block
+    doubled = jnp.concatenate([values, values], axis=axis)
+    return lax.dynamic_slice_in_dim(doubled, start, (plane_count - 1) * block, axis=axis)
+
+
 def gather_pieces(shards):
-    groups = lax.axis_size("groups")
-    sections = lax.axis_size("sec")
-    pair = 2 if sections % 2 == 0 else 1
-    count = groups * pair
+    levels = replica_levels()
+    count = 2 ** len(levels)
     widths = [shard.shape[1] // count for shard in shards]
-    g = lax.axis_index("groups")
-    k = lax.axis_index("sec") % pair
-    own = g * pair + k
+    own = 0
+    for bit, (axis, _, flip) in enumerate(levels):
+        own = own + ((lax.axis_index(axis) // flip) % 2) * (2 ** bit)
     mine = jnp.concatenate(
         [
             lax.dynamic_slice_in_dim(shard, own * width, width, axis=1)
@@ -52,32 +69,33 @@
         ],
         axis=1,
     )
-    first = lax.all_gather(mine, "plane", axis=0, tiled=True)
-    by_group = [(own, first)]
-    for step in range(1, groups):
-        moved = [(i, (i + step) % groups) for i in range(groups)]
-        source = lax.rem(g - step + groups, groups)
-        by_group.append((source * pair + k, lax.ppermute(first, "groups", moved)))
-    held = list(by_group)
-    if pair == 2:
-        swap = [(i, i ^ 1) for i in range(sections)]
-        for piece, block in by_group:
-            held.append((piece - k + (1 - k), lax.ppermute(block, "sec", swap)))
+    gathered = lax.all_gather(mine, "plane", axis=0, tiled=True)
+    held = [(own, rotate_rows(gathered, 0))]
+    for bit, (axis, size, flip) in enumerate(levels):
+        swap = [(i, i ^ flip) for i in range(size)]
+        held = held + [
+            (piece + (1 - 2 * ((piece // 2 ** bit) % 2)) * 2 ** bit, lax.ppermute(block, axis, swap))
+            for piece, block in held
+        ]
     results = []
     offset = 0
-    for width in widths:
-        results.append(([(piece, block[:, offset : offset + width]) for piece, block in held], width))
+    for shard, width in zip(shards, widths):
+        results.append((shard, [(piece, block[:, offset : offset + width]) for piece, block in held], width))
         offset += width
     return results
 
 
 def project(inputs, pieces):
-    held, width = pieces
-    out = jnp.zeros((inputs.shape[0], width * len(held)), jnp.float32)
+    shard, held, width = pieces
+    rows = shard.shape[0]
+    local_inputs = lax.dynamic_slice_in_dim(inputs, lax.axis_index("plane") * rows, rows, axis=1)
+    local = jnp.dot(local_inputs, shard, preferred_element_type=jnp.float32)
+    remote_inputs = rotate_rows(inputs, 1)
+    remote = jnp.zeros_like(local)
     for piece, block in held:
-        part = jnp.dot(inputs, block, preferred_element_type=jnp.float32)
-        out = lax.dynamic_update_slice_in_dim(out, part, piece * width, axis=1)
-    return out
+        part = jnp.dot(remote_inputs, block, preferred_element_type=jnp.float32)
+        remote = lax.dynamic_update_slice_in_dim(remote, part, piece * width, axis=1)
+    return local + remote
 
 
 def attend_items(pieces):
@@ -127,9 +145,8 @@
     near_valid = positions[None, :] < near_counts[:, None]
     own_valid = near_valid[1 : sec_block + 1]
     score_scale = 1.0 / math.sqrt(HEAD_DIM)
-    (cross_qkv_pieces,) = gather_pieces([cross_qkv])
-    (plane_qkv_pieces,) = gather_pieces([plane_qkv])
-    cross_out_pieces, plane_out_pieces = gather_pieces([cross_out, plane_out])
+    cross_qkv_pieces, cross_out_pieces = gather_pieces([cross_qkv, cross_out])
+    plane_qkv_pieces, plane_out_pieces = gather_pieces([plane_qkv, plane_out])
     normed = rms_norm(tokens, norm_gains[0])
     inputs = normed.reshape(-1, model_width)
     result = project(inputs, cross_qkv_pieces)

time: 297 us -> 278 us (0.936)
  waiting for transfers between devices: 137 us -> 86.8 us
  matrix products: 33.9 us -> 48.1 us
  starting transfers between devices: 24.6 us -> 34.2 us
  other arithmetic: 12.8 us -> 18.3 us
    all_gather x3 -> x2, waiting for transfers between devices: 65.3 us -> 33.2 us  [gather_pieces(): gathered = lax.all_gather(mine, 'plane', axis=0, tiled=True)]
    ppermute x9 -> x14, waiting for transfers between devices: 52.5 us -> 33.9 us  [gather_pieces(): lax.ppermute(block, axis, swap)]
    dot_general x16 -> x36, matrix products: 24.6 us -> 38.6 us  [the longest x32 35.6 us: project(): part = jnp.dot(remote_inputs, block, preferred_element_type=jnp.float32)]
    ppermute x9 -> x14, starting transfers between devices: 7.1 us -> 15.6 us  [gather_pieces(): lax.ppermute(block, axis, swap)]
    concatenate x0 -> x6, other arithmetic: none -> 6.74 us  [rotate_rows(): doubled = jnp.concatenate([values, values], axis=axis)]
    unnamed x28 -> x51, local copies, waits for them, and re-layouts: 7.47 us -> 12.8 us
    slice x2 -> x1, local copies, waits for them, and re-layouts: 3.69 us -> 0.08 us  [body(): from_below = shifted_2(own_kv[sec_block - 1], 'sec', 1)]
  transfers between devices with their start and end apart: 22 -> 26, of which waited for: 11 -> 12; matrix products, arithmetic and copies ran while one was open for 15% -> 20% of each run, Pallas kernels for 0% -> 0%
where the time goes in v3:
time: 278 us; the launch traced here: 276 us
  waiting for transfers between devices  86.8 us (31%)
  matrix products  48.1 us (17%)
  blocking collectives  41.2 us (15%)
  starting transfers between devices  34.2 us (12%)
  local copies, waits for them, and re-layouts  32.6 us (12%)
  other arithmetic  18.3 us (7%)
  between operations  15 us (5%)
    all_to_all x1, blocking collectives, body(): lax.all_to_all(heads_first, 'plane', split_axis=0, concat_axis=2, tiled=T...  41.2 us
    dot_general x32, matrix products, project(): part = jnp.dot(remote_inputs, block, preferred_element_type=jnp.float32)  35.6 us
    ppermute x14, waiting for transfers between devices, gather_pieces(): lax.ppermute(block, axis, swap)  33.9 us
    all_gather x2, waiting for transfers between devices, gather_pieces(): gathered = lax.all_gather(mine, 'plane', axis=0, tiled=True)  33.2 us
    ppermute x14, starting transfers between devices, gather_pieces(): lax.ppermute(block, axis, swap)  15.6 us
    unnamed x51, local copies, waits for them, and re-layouts  12.8 us
    all_to_all x1, waiting for transfers between devices, body(): lax.all_to_all(attended, 'plane', split_axis=2, concat_axis=0, tiled=True)  12.8 us
    squeeze x8, local copies, waits for them, and re-layouts, attend_items(): return lax.map(one_item, (packed_all[0], flags_all[0]))[None]  7.76 us
  transfers between devices with their start and end apart: 26, of which 12 were waited for; matrix products, arithmetic and copies ran while one was open for 20% of the time, Pallas kernels for 0%

profile of v3, /device:TPU:0, one launch (start us, length us, event | category | flops | bytes accessed | tf_op | source)
XLA Modules:
  0.0 276.4 jit_solution(14961034821669484474)
XLA Ops:
  14.3 26.7 %all-gather.3.cloned.1.call-done = bf16[1024,512]{1,0:T(8,128)(2,1)} async-done(((bf16[256,512]{1,0:T(8,128)(2,1)}), bf16[1024,512]{1,0:T(8,128)(2,1)}) %all-gather.3.cloned.1.call-update) | async-done | bytes 1048592 | tf_op jit(solution)/shard_map/all_gather | solution.py:72
  41.0 1.7 fusion.30
  47.1 14.9 %collective-permute-done = bf16[768,512]{1,0:T(8,128)(2,1)} collective-permute-done((bf16[768,512]{1,0:T(8,128)(2,1)S(1)}, bf16[768,512]{1,0:T(8,128)(2,1)}, u32[]{:S(2)}, u32[]{:S(2)}) %collective-permute-start) | collective-permute-done | bytes 786464 | tf_op jit(solution)/shard_map/ppermute | solution.py:77
  63.5 6.5 %all-gather.5.cloned.1.call-done = bf16[1024,512]{1,0:T(8,128)(2,1)} async-done(((bf16[256,512]{1,0:T(8,128)(2,1)}), bf16[1024,512]{1,0:T(8,128)(2,1)}) %all-gather.5.cloned.1.call-update) | async-done | bytes 1048592 | tf_op jit(solution)/shard_map/all_gather | solution.py:72
  70.1 2.6 fusion.29
  78.3 2.3 collective-permute-done.2
  83.6 8.5 %collective-permute-done.9 = bf16[768,512]{1,0:T(8,128)(2,1)} collective-permute-done((bf16[768,512]{1,0:T(8,128)(2,1)}, bf16[768,512]{1,0:T(8,128)(2,1)}, u32[]{:S(2)}, u32[]{:S(2)}) %collective-permute-start.9) | collective-permute-done | bytes 786464 | tf_op jit(solution)/shard_map/ppermute | solution.py:77
  100.2 2.1 collective-permute-start.7
  108.1 1.6 copy.57
  111.1 8.2 %collective-permute-done.11 = bf16[768,512]{1,0:T(8,128)(2,1)} collective-permute-done((bf16[768,512]{1,0:T(8,128)(2,1)}, bf16[768,512]{1,0:T(8,128)(2,1)}, u32[]{:S(2)}, u32[]{:S(2)}) %collective-permute-start.11) | collective-permute-done | bytes 786464 | tf_op jit(solution)/shard_map/ppermute | solution.py:77
  119.3 4.7 %collective-permute-start.15 = (bf16[768,512]{1,0:T(8,128)(2,1)}, bf16[768,512]{1,0:T(8,128)(2,1)S(1)}, u32[]{:S(2)}, u32[]{:S(2)}) collective-permute-start(bf16[768,512]{1,0:T(8,128)(2,1)} %collective-permute-done.11), channel_id=1, source_target_pairs={{0,4},{4,0},{8,12},{12,8},{1,5},{5,1},{9,13},{13,9},{2,6},{6,2},{1... | collective-permute-start | bytes 2359304 | tf_op jit(solution)/shard_map/ppermute | solution.py:77
  126.9 3.2 %fusion.97 = (f32[2,16,128]{2,1,0:T(8,128)S(1)}, f32[2,16,128,384]{3,2,1,0:T(8,128)S(1)}) fusion(f32[2,16,128,384]{3,2,1,0:T(8,128)S(1)} %fusion.20, pred[2,128,384]{2,1,0:T(8,128)(4,1)S(1)} %broadcast_or_fusion), kind=kOutput, calls=%fused_computation.196 | output fusion | flops 11010431 | bytes 12697600 | tf_op jit(solution)/shard_map/sub | solution.py:31
  130.1 2.0 fusion.25
  156.4 41.2 %all_to_all.45 = bf16[4,8,128,192]{2,3,1,0:T(8,128)(2,1)S(1)} all-to-all(bf16[4,8,128,192]{2,3,1,0:T(8,128)(2,1)S(1)} %bitcast.161), channel_id=1, replica_groups=mesh['groups'=2,'sec'=4,'plane'=4] {'plane'}, dimensions={0} | all-to-all | bytes 3145728 | tf_op jit(solution)/shard_map/all_to_all | solution.py:199
  198.2 3.2 %all-to-all-start = ((bf16[4,8,128]{2,1,0:T(8,128)(2,1)}), bf16[4,8,128]{2,1,0:T(8,128)(2,1)S(1)}, u32[]{:S(2)}, u32[]{:S(2)}) async-start(bf16[4,8,128]{2,1,0:T(8,128)(2,1)} %broadcast_in_dim.87), calls=%async_computation | async-start | bytes 16384 | tf_op jit(solution)/shard_map/all_to_all | solution.py:200
  201.5 2.6 copy.53
  204.1 2.9 %all-to-all-done = bf16[4,8,128]{2,1,0:T(8,128)(2,1)S(1)} async-done(((bf16[4,8,128]{2,1,0:T(8,128)(2,1)}), bf16[4,8,128]{2,1,0:T(8,128)(2,1)S(1)}, u32[]{:S(2)}, u32[]{:S(2)}) %all-to-all-start) | async-done | bytes 8224 | tf_op jit(solution)/shard_map/all_to_all | solution.py:200
  207.1 16.5 %while.11 = (s32[]{:T(128)}, bf16[8,512,64]{1,2,0:T(8,128)(2,1)S(1)}, bf16[8,512]{1,0:T(8,128)(2,1)S(1)}, bf16[8,512,192]{2,1,0:T(8,128)(2,1)}, s32[]{:T(128)}) while((s32[]{:T(128)}, bf16[8,512,64]{1,2,0:T(8,128)(2,1)S(1)}, bf16[8,512]{1,0:T(8,128)(2,1)S(1)}, bf16[8,512,192]{2,1,0:T(8,128)(2,1)}, s32[]{:T(128)}) %tuple.53), condition=%wide.region_7.8_spmd.clone, body=%wide.region_4.7_spmd.clone.sunk | while | flops 71336448 | bytes 3945545 | solution.py:131
  225.9 3.7 %all-to-all-start.2 = ((bf16[4,2,32768]{2,1,0:T(2,128)(2,1)}), bf16[4,2,32768]{2,1,0:T(2,128)(2,1)S(1)}, u32[]{:S(2)}, u32[]{:S(2)}) async-start(bf16[4,2,32768]{2,1,0:T(2,128)(2,1)} %reshape.163), calls=%async_computation.2 | async-start | bytes 1048576 | tf_op jit(solution)/shard_map/all_to_all | solution.py:203
  229.7 12.8 %all-to-all-done.2 = bf16[4,2,32768]{2,1,0:T(2,128)(2,1)S(1)} async-done(((bf16[4,2,32768]{2,1,0:T(2,128)(2,1)}), bf16[4,2,32768]{2,1,0:T(2,128)(2,1)S(1)}, u32[]{:S(2)}, u32[]{:S(2)}) %all-to-all-start.2) | async-done | bytes 524320 | tf_op jit(solution)/shard_map/all_to_all | solution.py:203
  256.9 2.0 collective-permute-start.17
  258.9 1.8 collective-permute-start.18
  260.8 1.9 collective-permute-done.16
  263.4 2.6 collective-permute-start.20
  (218 shorter events, 101.2 us)
Async XLA Ops:
  7.2 33.8 %all-gather.3.cloned.1.call-start = ((), (), s32[]{:S(2)}) async-start(), calls=%async_computation.3 | async-start | bytes 1310720 | tf_op jit(solution)/shard_map/all_gather | solution.py:72
  10.2 59.8 %all-gather.5.cloned.1.call-start = ((), (), s32[]{:S(2)}) async-start(), calls=%async_computation.4 | async-start | bytes 1310720 | tf_op jit(solution)/shard_map/all_gather | solution.py:72
  42.7 19.3 %collective-permute-start = (bf16[768,512]{1,0:T(8,128)(2,1)S(1)}, bf16[768,512]{1,0:T(8,128)(2,1)}, u32[]{:S(2)}, u32[]{:S(2)}) collective-permute-start(bf16[768,512]{1,0:T(8,128)(2,1)S(1)} %fusion.30), channel_id=1, source_target_pairs={{0,16},{16,0},{1,17},{17,1},{2,18},{18,2},{3,19},{19,3},{4,20},{20... | collective-permute-start | bytes 2359304 | tf_op jit(solution)/shard_map/ppermute | solution.py:77
  44.3 30.6 %collective-permute-start.1 = (bf16[768,512]{1,0:T(8,128)(2,1)S(1)}, bf16[768,512]{1,0:T(8,128)(2,1)}, u32[]{:S(2)}, u32[]{:S(2)}) collective-permute-start(bf16[768,512]{1,0:T(8,128)(2,1)S(1)} %fusion.30), channel_id=1, source_target_pairs={{0,8},{4,12},{8,0},{12,4},{1,9},{5,13},{9,1},{13,5},{2,10},{6,14},... | collective-permute-start | bytes 2359304 | tf_op jit(solution)/shard_map/ppermute | solution.py:77
  47.1 35.0 %collective-permute-start.3 = (bf16[768,512]{1,0:T(8,128)(2,1)S(1)}, bf16[768,512]{1,0:T(8,128)(2,1)}, u32[]{:S(2)}, u32[]{:S(2)}) collective-permute-start(bf16[768,512]{1,0:T(8,128)(2,1)S(1)} %fusion.30), channel_id=1, source_target_pairs={{0,4},{4,0},{8,12},{12,8},{1,5},{5,1},{9,13},{13,9},{2,6},{6,2},{1... | collective-permute-start | bytes 2359304 | tf_op jit(solution)/shard_map/ppermute | solution.py:77
  62.0 18.6 %collective-permute-start.2 = (bf16[768,512]{1,0:T(8,128)(2,1)}, bf16[768,512]{1,0:T(8,128)(2,1)}, u32[]{:S(2)}, u32[]{:S(2)}) collective-permute-start(bf16[768,512]{1,0:T(8,128)(2,1)} %collective-permute-done), channel_id=1, source_target_pairs={{0,8},{4,12},{8,0},{12,4},{1,9},{5,13},{9,1},{13,5},{2,10},{6,14},... | collective-permute-start | bytes 2359304 | tf_op jit(solution)/shard_map/ppermute | solution.py:77
  72.6 19.5 %collective-permute-start.9 = (bf16[768,512]{1,0:T(8,128)(2,1)}, bf16[768,512]{1,0:T(8,128)(2,1)}, u32[]{:S(2)}, u32[]{:S(2)}) collective-permute-start(bf16[768,512]{1,0:T(8,128)(2,1)} %fusion.29), channel_id=1, source_target_pairs={{0,16},{16,0},{1,17},{17,1},{2,18},{18,2},{3,19},{19,3},{4,20},{20... | collective-permute-start | bytes 2359304 | tf_op jit(solution)/shard_map/ppermute | solution.py:77
  74.8 20.2 %collective-permute-start.4 = (bf16[768,512]{1,0:T(8,128)(2,1)}, bf16[768,512]{1,0:T(8,128)(2,1)S(1)}, u32[]{:S(2)}, u32[]{:S(2)}) collective-permute-start(bf16[768,512]{1,0:T(8,128)(2,1)} %collective-permute-done), channel_id=1, source_target_pairs={{0,4},{4,0},{8,12},{12,8},{1,5},{5,1},{9,13},{13,9},{2,6},{6,2},{1... | collective-permute-start | bytes 2359304 | tf_op jit(solution)/shard_map/ppermute | solution.py:77
  74.9 20.5 %collective-permute-start.5 = (bf16[768,512]{1,0:T(8,128)(2,1)}, bf16[768,512]{1,0:T(8,128)(2,1)S(1)}, u32[]{:S(2)}, u32[]{:S(2)}) collective-permute-start(bf16[768,512]{1,0:T(8,128)(2,1)} %collective-permute-done.1), channel_id=1, source_target_pairs={{0,4},{4,0},{8,12},{12,8},{1,5},{5,1},{9,13},{13,9},{2,6},{6,2},{1... | collective-permute-start | bytes 2359304 | tf_op jit(solution)/shard_map/ppermute | solution.py:77
  80.6 15.2 %collective-permute-start.6 = (bf16[768,512]{1,0:T(8,128)(2,1)}, bf16[768,512]{1,0:T(8,128)(2,1)S(1)}, u32[]{:S(2)}, u32[]{:S(2)}) collective-permute-start(bf16[768,512]{1,0:T(8,128)(2,1)} %collective-permute-done.2), channel_id=1, source_target_pairs={{0,4},{4,0},{8,12},{12,8},{1,5},{5,1},{9,13},{13,9},{2,6},{6,2},{1... | collective-permute-start | bytes 2359304 | tf_op jit(solution)/shard_map/ppermute | solution.py:77
  82.1 28.9 %collective-permute-start.10 = (bf16[768,512]{1,0:T(8,128)(2,1)}, bf16[768,512]{1,0:T(8,128)(2,1)}, u32[]{:S(2)}, u32[]{:S(2)}) collective-permute-start(bf16[768,512]{1,0:T(8,128)(2,1)} %fusion.29), channel_id=1, source_target_pairs={{0,8},{4,12},{8,0},{12,4},{1,9},{5,13},{9,1},{13,5},{2,10},{6,14},... | collective-permute-start | bytes 2359304 | tf_op jit(solution)/shard_map/ppermute | solution.py:77
  92.1 27.2 %collective-permute-start.11 = (bf16[768,512]{1,0:T(8,128)(2,1)}, bf16[768,512]{1,0:T(8,128)(2,1)}, u32[]{:S(2)}, u32[]{:S(2)}) collective-permute-start(bf16[768,512]{1,0:T(8,128)(2,1)} %collective-permute-done.9), channel_id=1, source_target_pairs={{0,8},{4,12},{8,0},{12,4},{1,9},{5,13},{9,1},{13,5},{2,10},{6,14},... | collective-permute-start | bytes 2359304 | tf_op jit(solution)/shard_map/ppermute | solution.py:77
  100.2 19.1 %collective-permute-start.7 = (bf16[128,2048]{0,1:T(8,128)(2,1)}, bf16[128,2048]{0,1:T(8,128)(2,1)}, u32[]{:S(2)}, u32[]{:S(2)}) collective-permute-start(bf16[128,2048]{0,1:T(8,128)(2,1)} %bitcast.4), channel_id=1, source_target_pairs={{0,4},{4,8},{8,12},{1,5},{5,9},{9,13},{2,6},{6,10},{10,14},{3,7},{... | collective-permute-start | bytes 1572872 | tf_op jit(solution)/shard_map/ppermute | solution.py:19
  103.3 20.7 %collective-permute-start.8 = (bf16[128,2048]{0,1:T(8,128)(2,1)}, bf16[128,2048]{0,1:T(8,128)(2,1)}, u32[]{:S(2)}, u32[]{:S(2)}) collective-permute-start(bf16[128,2048]{0,1:T(8,128)(2,1)} %bitcast.8), channel_id=1, source_target_pairs={{4,0},{8,4},{12,8},{5,1},{9,5},{13,9},{6,2},{10,6},{14,10},{7,3},{... | collective-permute-start | bytes 1572872 | tf_op jit(solution)/shard_map/ppermute | solution.py:19
  104.9 46.2 %collective-permute-start.12 = (bf16[768,512]{1,0:T(8,128)(2,1)}, bf16[768,512]{1,0:T(8,128)(2,1)}, u32[]{:S(2)}, u32[]{:S(2)}) collective-permute-start(bf16[768,512]{1,0:T(8,128)(2,1)} %fusion.29), channel_id=1, source_target_pairs={{0,4},{4,0},{8,12},{12,8},{1,5},{5,1},{9,13},{13,9},{2,6},{6,2},{1... | collective-permute-start | bytes 2359304 | tf_op jit(solution)/shard_map/ppermute | solution.py:77
  111.0 41.6 %collective-permute-start.13 = (bf16[768,512]{1,0:T(8,128)(2,1)}, bf16[768,512]{1,0:T(8,128)(2,1)S(1)}, u32[]{:S(2)}, u32[]{:S(2)}) collective-permute-start(bf16[768,512]{1,0:T(8,128)(2,1)} %collective-permute-done.9), channel_id=1, source_target_pairs={{0,4},{4,0},{8,12},{12,8},{1,5},{5,1},{9,13},{13,9},{2,6},{6,2},{1... | collective-permute-start | bytes 2359304 | tf_op jit(solution)/shard_map/ppermute | solution.py:77
  119.2 33.8 %collective-permute-start.14 = (bf16[768,512]{1,0:T(8,128)(2,1)}, bf16[768,512]{1,0:T(8,128)(2,1)S(1)}, u32[]{:S(2)}, u32[]{:S(2)}) collective-permute-start(bf16[768,512]{1,0:T(8,128)(2,1)} %collective-permute-done.10), channel_id=1, source_target_pairs={{0,4},{4,0},{8,12},{12,8},{1,5},{5,1},{9,13},{13,9},{2,6},{6,2},{1... | collective-permute-start | bytes 2359304 | tf_op jit(solution)/shard_map/ppermute | solution.py:77
  119.3 34.2 %collective-permute-start.15 = (bf16[768,512]{1,0:T(8,128)(2,1)}, bf16[768,512]{1,0:T(8,128)(2,1)S(1)}, u32[]{:S(2)}, u32[]{:S(2)}) collective-permute-start(bf16[768,512]{1,0:T(8,128)(2,1)} %collective-permute-done.11), channel_id=1, source_target_pairs={{0,4},{4,0},{8,12},{12,8},{1,5},{5,1},{9,13},{13,9},{2,6},{6,2},{1... | collective-permute-start | bytes 2359304 | tf_op jit(solution)/shard_map/ppermute | solution.py:77
  198.2 8.8 %all-to-all-start = ((bf16[4,8,128]{2,1,0:T(8,128)(2,1)}), bf16[4,8,128]{2,1,0:T(8,128)(2,1)S(1)}, u32[]{:S(2)}, u32[]{:S(2)}) async-start(bf16[4,8,128]{2,1,0:T(8,128)(2,1)} %broadcast_in_dim.87), calls=%async_computation | async-start | bytes 16384 | tf_op jit(solution)/shard_map/all_to_all | solution.py:200
  225.9 16.6 %all-to-all-start.2 = ((bf16[4,2,32768]{2,1,0:T(2,128)(2,1)}), bf16[4,2,32768]{2,1,0:T(2,128)(2,1)S(1)}, u32[]{:S(2)}, u32[]{:S(2)}) async-start(bf16[4,2,32768]{2,1,0:T(2,128)(2,1)} %reshape.163), calls=%async_computation.2 | async-start | bytes 1048576 | tf_op jit(solution)/shard_map/all_to_all | solution.py:203
  256.9 5.8 %collective-permute-start.16 = (f32[4,2,1152]{2,1,0:T(2,128)S(1)}, f32[4,2,1152]{2,1,0:T(2,128)S(1)}, u32[]{:S(2)}, u32[]{:S(2)}) collective-permute-start(f32[4,2,1152]{2,1,0:T(2,128)S(1)} %get-tuple-element.83), channel_id=1, source_target_pairs={{0,1},{1,2},{2,3},{3,0},{4,5},{5,6},{6,7},{7,4},{8,9},{9,10},{10,1... | collective-permute-start | bytes 110600 | tf_op jit(solution)/shard_map/ppermute | solution.py:224
  256.9 5.7 %collective-permute-start.17 = (f32[4,2,1152]{2,1,0:T(2,128)S(1)}, f32[4,2,1152]{2,1,0:T(2,128)S(1)}, u32[]{:S(2)}, u32[]{:S(2)}) collective-permute-start(f32[4,2,1152]{2,1,0:T(2,128)S(1)} %get-tuple-element.85), channel_id=1, source_target_pairs={{0,2},{1,3},{2,0},{3,1},{4,6},{5,7},{6,4},{7,5},{8,10},{9,11},{10,... | collective-permute-start | bytes 110600 | tf_op jit(solution)/shard_map/ppermute | solution.py:224
  258.9 4.3 %collective-permute-start.18 = (f32[4,2,1152]{2,1,0:T(2,128)S(1)}, f32[4,2,1152]{2,1,0:T(2,128)S(1)}, u32[]{:S(2)}, u32[]{:S(2)}) collective-permute-start(f32[4,2,1152]{2,1,0:T(2,128)S(1)} %get-tuple-element.84), channel_id=1, source_target_pairs={{0,3},{1,0},{2,1},{3,2},{4,7},{5,4},{6,5},{7,6},{8,11},{9,8},{10,9... | collective-permute-start | bytes 110600 | tf_op jit(solution)/shard_map/ppermute | solution.py:224
  263.4 4.2 %collective-permute-start.20 = (f32[2,1152]{1,0:T(2,128)S(1)}, f32[2,1152]{1,0:T(2,128)S(1)}, u32[]{:S(2)}, u32[]{:S(2)}) collective-permute-start(f32[2,1152]{1,0:T(2,128)S(1)} %get-tuple-element.88), channel_id=1, source_target_pairs={{0,8},{4,12},{8,0},{12,4},{1,9},{5,13},{9,1},{13,5},{2,10},{6,14},... | collective-permute-start | bytes 27656 | tf_op jit(solution)/shard_map/ppermute | solution.py:231
  (23 other events, 214.8 us)
Sparse Core Ops, SparseCore 0:
  10.4 30.6 all-gather.2
  42.6 27.4 all-gather.4

commit v4 on v3

--- a/solution.py
+++ b/solution.py
@@ -85,50 +85,55 @@
     return results
 
 
-def project(inputs, pieces):
+def assemble(pieces):
     shard, held, width = pieces
+    remote = jnp.zeros((held[0][1].shape[0], width * len(held)), shard.dtype)
+    for piece, block in held:
+        remote = lax.dynamic_update_slice_in_dim(remote, block, piece * width, axis=1)
+    return shard, remote
+
+
+def project(inputs, weights):
+    shard, remote = weights
     rows = shard.shape[0]
     local_inputs = lax.dynamic_slice_in_dim(inputs, lax.axis_index("plane") * rows, rows, axis=1)
     local = jnp.dot(local_inputs, shard, preferred_element_type=jnp.float32)
     remote_inputs = rotate_rows(inputs, 1)
-    remote = jnp.zeros_like(local)
-    for piece, block in held:
-        part = jnp.dot(remote_inputs, block, preferred_element_type=jnp.float32)
-        remote = lax.dynamic_update_slice_in_dim(remote, part, piece * width, axis=1)
-    return local + remote
+    return local + jnp.dot(remote_inputs, remote, preferred_element_type=jnp.float32)
 
 
 def attend_items(pieces):
     packed_all, flags_all = pieces
-    seq_len = packed_all.shape[2]
-    block_len = 512
+    packed = packed_all[0]
+    items, seq_len = packed.shape[0], packed.shape[1]
+    block_len = min(seq_len, 512)
     score_scale = 1.0 / math.sqrt(HEAD_DIM)
     key_index = jnp.arange(seq_len, dtype=jnp.int32)
-
-    def one_item(item_pair):
-        packed, key_flag = item_pair
-        key_rows = packed[:, HEAD_DIM : 2 * HEAD_DIM]
-        value_rows = packed[:, 2 * HEAD_DIM :]
-        key_alive = key_flag > 0.5
-        query_blocks = packed[:, :HEAD_DIM].reshape(seq_len // block_len, block_len, HEAD_DIM)
-        block_starts = jnp.arange(seq_len // block_len, dtype=jnp.int32) * block_len
-
-        def one_block(block_pair):
-            query_rows, offset = block_pair
-            scores = (
-                jnp.einsum("qd,kd->qk", query_rows, key_rows, preferred_element_type=jnp.float32)
-                * score_scale
-            )
-            own_index = offset + jnp.arange(block_len, dtype=jnp.int32)
-            allowed = key_alive[None, :] | (key_index[None, :] == own_index[:, None])
-            attention = masked_softmax(scores, allowed)
-            return jnp.dot(attention, value_rows, preferred_element_type=jnp.float32).astype(
-                jnp.bfloat16
-            )
-
-        return lax.map(one_block, (query_blocks, block_starts)).reshape(seq_len, HEAD_DIM)
-
-    return lax.map(one_item, (packed_all[0], flags_all[0]))[None]
+    keys = packed[:, :, HEAD_DIM : 2 * HEAD_DIM]
+    values = packed[:, :, 2 * HEAD_DIM :]
+    key_alive = flags_all[0] > 0.5
+
+    def one_block(block_pair):
+        query_rows, offset = block_pair
+        scores = (
+            jnp.einsum("nqd,nkd->nqk", query_rows, keys, preferred_element_type=jnp.float32)
+            * score_scale
+        )
+        own_index = offset + jnp.arange(block_len, dtype=jnp.int32)
+        allowed = key_alive[:, None, :] | (key_index[None, None, :] == own_index[None, :, None])
+        attention = masked_softmax(scores, allowed)
+        return jnp.einsum(
+            "nqk,nkd->nqd", attention, values, preferred_element_type=jnp.float32
+        ).astype(jnp.bfloat16)
+
+    blocks = seq_len // block_len
+    queries = packed[:, :, :HEAD_DIM]
+    if blocks == 1:
+        return one_block((queries, jnp.int32(0)))[None]
+    query_blocks = jnp.transpose(queries.reshape(items, blocks, block_len, HEAD_DIM), (1, 0, 2, 3))
+    starts = jnp.arange(blocks, dtype=jnp.int32) * block_len
+    context = lax.map(one_block, (query_blocks, starts))
+    return jnp.transpose(context, (1, 0, 2, 3)).reshape(items, seq_len, HEAD_DIM)[None]
 
 
 def body(tokens, counts, region_ids, norm_gains, cross_qkv, cross_out, plane_qkv, plane_out):
@@ -145,8 +150,8 @@
     near_valid = positions[None, :] < near_counts[:, None]
     own_valid = near_valid[1 : sec_block + 1]
     score_scale = 1.0 / math.sqrt(HEAD_DIM)
-    cross_qkv_pieces, cross_out_pieces = gather_pieces([cross_qkv, cross_out])
-    plane_qkv_pieces, plane_out_pieces = gather_pieces([plane_qkv, plane_out])
+    cross_qkv_pieces, cross_out_pieces = map(assemble, gather_pieces([cross_qkv, cross_out]))
+    plane_qkv_pieces, plane_out_pieces = map(assemble, gather_pieces([plane_qkv, plane_out]))
     normed = rms_norm(tokens, norm_gains[0])
     inputs = normed.reshape(-1, model_width)
     result = project(inputs, cross_qkv_pieces)

time: 278 us -> 281 us (1.011)
  waiting for transfers between devices: 86.8 us -> 140 us
  blocking collectives: 41.2 us -> 0 us
  matrix products: 48.1 us -> 25.2 us
  local copies, waits for them, and re-layouts: 32.6 us -> 53 us
  other arithmetic: 18.3 us -> 12.4 us
    all_to_all x1 -> x0, blocking collectives: 41.2 us -> none  [body(): lax.all_to_all(heads_first, 'plane', split_axis=0, concat_axis=2, tiled=T...]
    all_to_all x0 -> x1, waiting for transfers between devices: none -> 37 us  [body(): lax.all_to_all(heads_first, 'plane', split_axis=0, concat_axis=2, tiled=T...]
    dot_general x48 -> x5, matrix products: 41.9 us -> 11.9 us  [the longest x4 6.84 us: project(): jnp.dot(remote_inputs, remote, preferred_element_type=jnp.float32)]
    dynamic_update_slice x0 -> x30, local copies, waits for them, and re-layouts: none -> 13.5 us  [assemble(): lax.dynamic_update_slice_in_dim(remote, block, piece * width, axis=1)]
    ppermute x14, waiting for transfers between devices: 33.9 us -> 42.6 us  [gather_pieces(): lax.ppermute(block, axis, swap)]
    all_gather x2, waiting for transfers between devices: 33.2 us -> 40.7 us  [gather_pieces(): gathered = lax.all_gather(mine, 'plane', axis=0, tiled=True)]
    sub x0 -> x1, matrix products: none -> 6.82 us  [masked_softmax(): expo = jnp.where(allowed, jnp.exp(shifted - top), 0.0)]
    ppermute x14, starting transfers between devices: 15.6 us -> 9.46 us  [gather_pieces(): lax.ppermute(block, axis, swap)]
  transfers between devices with their start and end apart: 26 -> 27, of which waited for: 12 -> 13; matrix products, arithmetic and copies ran while one was open for 20% -> 20% of each run, Pallas kernels for 0% -> 0%
where the time goes in v4:
time: 281 us; the launch traced here: 279 us
  waiting for transfers between devices  140 us (50%)
  local copies, waits for them, and re-layouts  53 us (19%)
  starting transfers between devices  33.4 us (12%)
  matrix products  25.2 us (9%)
  between operations  15.4 us (5%)
  other arithmetic  12.4 us (4%)
    ppermute x14, waiting for transfers between devices, gather_pieces(): lax.ppermute(block, axis, swap)  42.6 us
    all_gather x2, waiting for transfers between devices, gather_pieces(): gathered = lax.all_gather(mine, 'plane', axis=0, tiled=True)  40.7 us
    all_to_all x1, waiting for transfers between devices, body(): lax.all_to_all(heads_first, 'plane', split_axis=0, concat_axis=2, tiled=T...  37 us
    all_to_all x1, waiting for transfers between devices, body(): lax.all_to_all(attended, 'plane', split_axis=2, concat_axis=0, tiled=True)  15.7 us
    unnamed x55, local copies, waits for them, and re-layouts  14.9 us
    dynamic_update_slice x30, local copies, waits for them, and re-layouts, assemble(): lax.dynamic_update_slice_in_dim(remote, block, piece * width, axis=1)  13.5 us
    ppermute x14, starting transfers between devices, gather_pieces(): lax.ppermute(block, axis, swap)  9.46 us
    dot_general x4, matrix products, project(): jnp.dot(remote_inputs, remote, preferred_element_type=jnp.float32)  6.84 us
  transfers between devices with their start and end apart: 27, of which 13 were waited for; matrix products, arithmetic and copies ran while one was open for 20% of the time, Pallas kernels for 0%

profile of v4, /device:TPU:0, one launch (start us, length us, event | category | flops | bytes accessed | tf_op | source)
XLA Modules:
  0.0 279.4 jit_solution(11674261818513949414)
XLA Ops:
  11.7 6.3 %all-to-all-start = ((bf16[4,8,128]{2,1,0:T(8,128)(2,1)}), bf16[4,8,128]{2,1,0:T(8,128)(2,1)S(1)}, u32[]{:S(2)}, u32[]{:S(2)}) async-start(bf16[4,8,128]{2,1,0:T(8,128)(2,1)} %broadcast_in_dim.69), calls=%async_computation | async-start | bytes 16384 | tf_op jit(solution)/shard_map/all_to_all | solution.py:205
  22.4 2.3 fusion.58
  24.6 16.4 %all-gather.3.cloned.1.call-done = bf16[1024,512]{1,0:T(8,128)(2,1)} async-done(((bf16[256,512]{1,0:T(8,128)(2,1)}), bf16[1024,512]{1,0:T(8,128)(2,1)}) %all-gather.3.cloned.1.call-update) | async-done | bytes 1048592 | tf_op jit(solution)/shard_map/all_gather | solution.py:72
  45.7 24.3 %all-gather.5.cloned.1.call-done = bf16[1024,512]{1,0:T(8,128)(2,1)} async-done(((bf16[256,512]{1,0:T(8,128)(2,1)}), bf16[1024,512]{1,0:T(8,128)(2,1)}) %all-gather.5.cloned.1.call-update) | async-done | bytes 1048592 | tf_op jit(solution)/shard_map/all_gather | solution.py:72
  79.0 11.9 %collective-permute-done.9 = bf16[768,512]{1,0:T(8,128)(2,1)S(1)} collective-permute-done((bf16[768,512]{1,0:T(8,128)(2,1)S(1)}, bf16[768,512]{1,0:T(8,128)(2,1)S(1)}, u32[]{:S(2)}, u32[]{:S(2)}) %collective-permute-start.9) | collective-permute-done | bytes 786464 | tf_op jit(solution)/shard_map/ppermute | solution.py:77
  95.8 15.8 %collective-permute-done.2 = bf16[768,512]{1,0:T(8,128)(2,1)S(1)} collective-permute-done((bf16[768,512]{1,0:T(8,128)(2,1)}, bf16[768,512]{1,0:T(8,128)(2,1)S(1)}, u32[]{:S(2)}, u32[]{:S(2)}) %collective-permute-start.2) | collective-permute-done | bytes 786464 | tf_op jit(solution)/shard_map/ppermute | solution.py:77
  111.8 14.4 %collective-permute-done.11 = bf16[768,512]{1,0:T(8,128)(2,1)S(1)} collective-permute-done((bf16[768,512]{1,0:T(8,128)(2,1)S(1)}, bf16[768,512]{1,0:T(8,128)(2,1)S(1)}, u32[]{:S(2)}, u32[]{:S(2)}) %collective-permute-start.11) | collective-permute-done | bytes 786464 | tf_op jit(solution)/shard_map/ppermute | solution.py:77
  137.4 2.0 copy.59
  139.5 2.1 collective-permute-start.7
  141.5 2.1 copy.61
  157.3 3.2 %fusion.93 = (f32[2,16,128]{2,1,0:T(8,128)S(1)}, f32[2,16,128,384]{3,2,1,0:T(8,128)S(1)}) fusion(f32[2,16,128,384]{3,2,1,0:T(8,128)S(1)} %fusion.15, pred[2,128,384]{2,1,0:T(8,128)(4,1)S(1)} %broadcast_or_fusion), kind=kOutput, calls=%fused_computation.180 | output fusion | flops 11010431 | bytes 12697600 | tf_op jit(solution)/shard_map/sub | solution.py:31
  166.2 2.7 fusion.10
  170.6 1.9 reshape.172
  172.5 3.0 %copy.49 = bf16[2,16,128,3,64]{2,4,3,1,0:T(8,128)(2,1)} copy(bf16[2,16,128,3,64]{2,0,4,1,3:T(2,128)(2,1)} %bitcast.120) | data formatting | bytes 3145728 | tf_op jit(solution)/shard_map/transpose | solution.py:195
  175.5 3.8 %all-to-all-start.1 = ((bf16[4,8,128,192]{2,3,1,0:T(8,128)(2,1)}), bf16[4,8,128,192]{2,3,1,0:T(8,128)(2,1)S(1)}, u32[]{:S(2)}, u32[]{:S(2)}) async-start(bf16[4,8,128,192]{2,3,1,0:T(8,128)(2,1)} %bitcast.26), calls=%async_computation.1 | async-start | bytes 3145728 | tf_op jit(solution)/shard_map/all_to_all | solution.py:204
  179.4 37.0 %all-to-all-done.1 = bf16[4,8,128,192]{2,3,1,0:T(8,128)(2,1)S(1)} async-done(((bf16[4,8,128,192]{2,3,1,0:T(8,128)(2,1)}), bf16[4,8,128,192]{2,3,1,0:T(8,128)(2,1)S(1)}, u32[]{:S(2)}, u32[]{:S(2)}) %all-to-all-start.1) | async-done | bytes 1572896 | tf_op jit(solution)/shard_map/all_to_all | solution.py:204
  216.4 2.4 copy.50
  218.8 2.5 squeeze.41
  221.3 6.8 %fusion.94 = (f32[8,512]{1,0:T(8,128)S(1)}, f32[8,512,512]{1,2,0:T(8,128)}) fusion(pred[512,512]{0,1:T(8,128)(4,1)S(1)} %iota_compare_fusion, pred[8,512]{1,0:T(8,128)(4,1)S(1)} %compare_bitcast_fusion, bf16[8,512,192]{1,2,0:T(8,128)(2,1)S(1)} %squeeze.41), kind=kOutput, calls=%fused_computation.181 | convolution fusion | flops 283116032 | bytes 9986048 | tf_op jit(solution)/shard_map/sub | solution.py:31
  228.1 5.0 %fusion.21 = bf16[1,8,512,64]{2,3,1,0:T(8,128)(2,1)} fusion(f32[8,512,512]{1,2,0:T(8,128)} %get-tuple-element.24, f32[8,512]{1,0:T(8,128)S(1)} %get-tuple-element.23, bf16[8,512,192]{1,2,0:T(8,128)(2,1)S(1)} %squeeze.41), kind=kOutput, calls=%fused_computation.41 | convolution fusion | flops 272891904 | bytes 9453568 | tf_op jit(solution)/shard_map/nqk,nkd->nqd/dot_general | solution.py:125
  236.5 3.5 %all-to-all-start.2 = ((bf16[4,2,32768]{2,1,0:T(2,128)(2,1)}), bf16[4,2,32768]{2,1,0:T(2,128)(2,1)S(1)}, u32[]{:S(2)}, u32[]{:S(2)}) async-start(bf16[4,2,32768]{2,1,0:T(2,128)(2,1)} %reshape.180), calls=%async_computation.2 | async-start | bytes 1048576 | tf_op jit(solution)/shard_map/all_to_all | solution.py:208
  240.0 15.7 %all-to-all-done.2 = bf16[4,2,32768]{2,1,0:T(2,128)(2,1)S(1)} async-done(((bf16[4,2,32768]{2,1,0:T(2,128)(2,1)}), bf16[4,2,32768]{2,1,0:T(2,128)(2,1)S(1)}, u32[]{:S(2)}, u32[]{:S(2)}) %all-to-all-start.2) | async-done | bytes 524320 | tf_op jit(solution)/shard_map/all_to_all | solution.py:208
  261.0 2.0 collective-permute-start.17
  264.9 2.1 collective-permute-done.16
  (186 shorter events, 74.7 us)
Async XLA Ops:
  7.2 33.8 %all-gather.3.cloned.1.call-start = ((), (), s32[]{:S(2)}) async-start(), calls=%async_computation.3 | async-start | bytes 1310720 | tf_op jit(solution)/shard_map/all_gather | solution.py:72
  11.7 163.7 %all-to-all-start = ((bf16[4,8,128]{2,1,0:T(8,128)(2,1)}), bf16[4,8,128]{2,1,0:T(8,128)(2,1)S(1)}, u32[]{:S(2)}, u32[]{:S(2)}) async-start(bf16[4,8,128]{2,1,0:T(8,128)(2,1)} %broadcast_in_dim.69), calls=%async_computation | async-start | bytes 16384 | tf_op jit(solution)/shard_map/all_to_all | solution.py:205
  18.1 52.0 %all-gather.5.cloned.1.call-start = ((), (), s32[]{:S(2)}) async-start(), calls=%async_computation.4 | async-start | bytes 1310720 | tf_op jit(solution)/shard_map/all_gather | solution.py:72
  42.7 34.0 %collective-permute-start = (bf16[768,512]{1,0:T(8,128)(2,1)S(1)}, bf16[768,512]{1,0:T(8,128)(2,1)}, u32[]{:S(2)}, u32[]{:S(2)}) collective-permute-start(bf16[768,512]{1,0:T(8,128)(2,1)S(1)} %fusion.29), channel_id=1, source_target_pairs={{0,16},{16,0},{1,17},{17,1},{2,18},{18,2},{3,19},{19,3},{4,20},{20... | collective-permute-start | bytes 2359304 | tf_op jit(solution)/shard_map/ppermute | solution.py:77
  44.3 48.3 %collective-permute-start.1 = (bf16[768,512]{1,0:T(8,128)(2,1)S(1)}, bf16[768,512]{1,0:T(8,128)(2,1)}, u32[]{:S(2)}, u32[]{:S(2)}) collective-permute-start(bf16[768,512]{1,0:T(8,128)(2,1)S(1)} %fusion.29), channel_id=1, source_target_pairs={{0,8},{4,12},{8,0},{12,4},{1,9},{5,13},{9,1},{13,5},{2,10},{6,14},... | collective-permute-start | bytes 2359304 | tf_op jit(solution)/shard_map/ppermute | solution.py:77
  45.7 80.8 %collective-permute-start.3 = (bf16[768,512]{1,0:T(8,128)(2,1)S(1)}, bf16[768,512]{1,0:T(8,128)(2,1)}, u32[]{:S(2)}, u32[]{:S(2)}) collective-permute-start(bf16[768,512]{1,0:T(8,128)(2,1)S(1)} %fusion.29), channel_id=1, source_target_pairs={{0,4},{4,0},{8,12},{12,8},{1,5},{5,1},{9,13},{13,9},{2,6},{6,2},{1... | collective-permute-start | bytes 2359304 | tf_op jit(solution)/shard_map/ppermute | solution.py:77
  71.7 19.2 %collective-permute-start.9 = (bf16[768,512]{1,0:T(8,128)(2,1)S(1)}, bf16[768,512]{1,0:T(8,128)(2,1)S(1)}, u32[]{:S(2)}, u32[]{:S(2)}) collective-permute-start(bf16[768,512]{1,0:T(8,128)(2,1)S(1)} %fusion.28), channel_id=1, source_target_pairs={{0,16},{16,0},{1,17},{17,1},{2,18},{18,2},{3,19},{19,3},{4,20},{20... | collective-permute-start | bytes 2359304 | tf_op jit(solution)/shard_map/ppermute | solution.py:77
  73.3 21.7 %collective-permute-start.10 = (bf16[768,512]{1,0:T(8,128)(2,1)S(1)}, bf16[768,512]{1,0:T(8,128)(2,1)S(1)}, u32[]{:S(2)}, u32[]{:S(2)}) collective-permute-start(bf16[768,512]{1,0:T(8,128)(2,1)S(1)} %fusion.28), channel_id=1, source_target_pairs={{0,8},{4,12},{8,0},{12,4},{1,9},{5,13},{9,1},{13,5},{2,10},{6,14},... | collective-permute-start | bytes 2359304 | tf_op jit(solution)/shard_map/ppermute | solution.py:77
  76.8 51.5 %collective-permute-start.12 = (bf16[768,512]{1,0:T(8,128)(2,1)S(1)}, bf16[768,512]{1,0:T(8,128)(2,1)S(1)}, u32[]{:S(2)}, u32[]{:S(2)}) collective-permute-start(bf16[768,512]{1,0:T(8,128)(2,1)S(1)} %fusion.28), channel_id=1, source_target_pairs={{0,4},{4,0},{8,12},{12,8},{1,5},{5,1},{9,13},{13,9},{2,6},{6,2},{1... | collective-permute-start | bytes 2359304 | tf_op jit(solution)/shard_map/ppermute | solution.py:77
  90.9 20.7 %collective-permute-start.2 = (bf16[768,512]{1,0:T(8,128)(2,1)}, bf16[768,512]{1,0:T(8,128)(2,1)S(1)}, u32[]{:S(2)}, u32[]{:S(2)}) collective-permute-start(bf16[768,512]{1,0:T(8,128)(2,1)} %collective-permute-done), channel_id=1, source_target_pairs={{0,8},{4,12},{8,0},{12,4},{1,9},{5,13},{9,1},{13,5},{2,10},{6,14},... | collective-permute-start | bytes 2359304 | tf_op jit(solution)/shard_map/ppermute | solution.py:77
  92.6 36.9 %collective-permute-start.4 = (bf16[768,512]{1,0:T(8,128)(2,1)}, bf16[768,512]{1,0:T(8,128)(2,1)S(1)}, u32[]{:S(2)}, u32[]{:S(2)}) collective-permute-start(bf16[768,512]{1,0:T(8,128)(2,1)} %collective-permute-done), channel_id=1, source_target_pairs={{0,4},{4,0},{8,12},{12,8},{1,5},{5,1},{9,13},{13,9},{2,6},{6,2},{1... | collective-permute-start | bytes 2359304 | tf_op jit(solution)/shard_map/ppermute | solution.py:77
  94.9 31.3 %collective-permute-start.11 = (bf16[768,512]{1,0:T(8,128)(2,1)S(1)}, bf16[768,512]{1,0:T(8,128)(2,1)S(1)}, u32[]{:S(2)}, u32[]{:S(2)}) collective-permute-start(bf16[768,512]{1,0:T(8,128)(2,1)S(1)} %collective-permute-done.9), channel_id=1, source_target_pairs={{0,8},{4,12},{8,0},{12,4},{1,9},{5,13},{9,1},{13,5},{2,10},{6,14},... | collective-permute-start | bytes 2359304 | tf_op jit(solution)/shard_map/ppermute | solution.py:77
  111.6 19.0 %collective-permute-start.5 = (bf16[768,512]{1,0:T(8,128)(2,1)}, bf16[768,512]{1,0:T(8,128)(2,1)S(1)}, u32[]{:S(2)}, u32[]{:S(2)}) collective-permute-start(bf16[768,512]{1,0:T(8,128)(2,1)} %collective-permute-done.1), channel_id=1, source_target_pairs={{0,4},{4,0},{8,12},{12,8},{1,5},{5,1},{9,13},{13,9},{2,6},{6,2},{1... | collective-permute-start | bytes 2359304 | tf_op jit(solution)/shard_map/ppermute | solution.py:77
  126.2 4.2 %collective-permute-start.13 = (bf16[768,512]{1,0:T(8,128)(2,1)S(1)}, bf16[768,512]{1,0:T(8,128)(2,1)S(1)}, u32[]{:S(2)}, u32[]{:S(2)}) collective-permute-start(bf16[768,512]{1,0:T(8,128)(2,1)S(1)} %collective-permute-done.9), channel_id=1, source_target_pairs={{0,4},{4,0},{8,12},{12,8},{1,5},{5,1},{9,13},{13,9},{2,6},{6,2},{1... | collective-permute-start | bytes 2359304 | tf_op jit(solution)/shard_map/ppermute | solution.py:77
  126.5 4.3 %collective-permute-start.14 = (bf16[768,512]{1,0:T(8,128)(2,1)S(1)}, bf16[768,512]{1,0:T(8,128)(2,1)S(1)}, u32[]{:S(2)}, u32[]{:S(2)}) collective-permute-start(bf16[768,512]{1,0:T(8,128)(2,1)S(1)} %collective-permute-done.10), channel_id=1, source_target_pairs={{0,4},{4,0},{8,12},{12,8},{1,5},{5,1},{9,13},{13,9},{2,6},{6,2},{1... | collective-permute-start | bytes 2359304 | tf_op jit(solution)/shard_map/ppermute | solution.py:77
  139.5 14.9 %collective-permute-start.7 = (bf16[128,2048]{0,1:T(8,128)(2,1)}, bf16[128,2048]{0,1:T(8,128)(2,1)}, u32[]{:S(2)}, u32[]{:S(2)}) collective-permute-start(bf16[128,2048]{0,1:T(8,128)(2,1)} %bitcast.143), channel_id=1, source_target_pairs={{0,4},{4,8},{8,12},{1,5},{5,9},{9,13},{2,6},{6,10},{10,14},{3,7},{... | collective-permute-start | bytes 1572872 | tf_op jit(solution)/shard_map/ppermute | solution.py:19
  143.6 10.8 %collective-permute-start.8 = (bf16[128,2048]{0,1:T(8,128)(2,1)}, bf16[128,2048]{0,1:T(8,128)(2,1)}, u32[]{:S(2)}, u32[]{:S(2)}) collective-permute-start(bf16[128,2048]{0,1:T(8,128)(2,1)} %bitcast.144), channel_id=1, source_target_pairs={{4,0},{8,4},{12,8},{5,1},{9,5},{13,9},{6,2},{10,6},{14,10},{7,3},{... | collective-permute-start | bytes 1572872 | tf_op jit(solution)/shard_map/ppermute | solution.py:19
  175.5 40.9 %all-to-all-start.1 = ((bf16[4,8,128,192]{2,3,1,0:T(8,128)(2,1)}), bf16[4,8,128,192]{2,3,1,0:T(8,128)(2,1)S(1)}, u32[]{:S(2)}, u32[]{:S(2)}) async-start(bf16[4,8,128,192]{2,3,1,0:T(8,128)(2,1)} %bitcast.26), calls=%async_computation.1 | async-start | bytes 3145728 | tf_op jit(solution)/shard_map/all_to_all | solution.py:204
  236.5 19.2 %all-to-all-start.2 = ((bf16[4,2,32768]{2,1,0:T(2,128)(2,1)}), bf16[4,2,32768]{2,1,0:T(2,128)(2,1)S(1)}, u32[]{:S(2)}, u32[]{:S(2)}) async-start(bf16[4,2,32768]{2,1,0:T(2,128)(2,1)} %reshape.180), calls=%async_computation.2 | async-start | bytes 1048576 | tf_op jit(solution)/shard_map/all_to_all | solution.py:208
  261.0 6.0 %collective-permute-start.16 = (f32[4,2,1152]{2,1,0:T(2,128)S(1)}, f32[4,2,1152]{2,1,0:T(2,128)S(1)}, u32[]{:S(2)}, u32[]{:S(2)}) collective-permute-start(f32[4,2,1152]{2,1,0:T(2,128)S(1)} %get-tuple-element.6), channel_id=1, source_target_pairs={{0,1},{1,2},{2,3},{3,0},{4,5},{5,6},{6,7},{7,4},{8,9},{9,10},{10,1... | collective-permute-start | bytes 110600 | tf_op jit(solution)/shard_map/ppermute | solution.py:229
  261.0 5.9 %collective-permute-start.17 = (f32[4,2,1152]{2,1,0:T(2,128)S(1)}, f32[4,2,1152]{2,1,0:T(2,128)S(1)}, u32[]{:S(2)}, u32[]{:S(2)}) collective-permute-start(f32[4,2,1152]{2,1,0:T(2,128)S(1)} %get-tuple-element.8), channel_id=1, source_target_pairs={{0,2},{1,3},{2,0},{3,1},{4,6},{5,7},{6,4},{7,5},{8,10},{9,11},{10,... | collective-permute-start | bytes 110600 | tf_op jit(solution)/shard_map/ppermute | solution.py:229
  263.1 4.3 %collective-permute-start.18 = (f32[4,2,1152]{2,1,0:T(2,128)S(1)}, f32[4,2,1152]{2,1,0:T(2,128)S(1)}, u32[]{:S(2)}, u32[]{:S(2)}) collective-permute-start(f32[4,2,1152]{2,1,0:T(2,128)S(1)} %get-tuple-element.7), channel_id=1, source_target_pairs={{0,3},{1,0},{2,1},{3,2},{4,7},{5,4},{6,5},{7,6},{8,11},{9,8},{10,9... | collective-permute-start | bytes 110600 | tf_op jit(solution)/shard_map/ppermute | solution.py:229
  267.4 3.1 %collective-permute-start.19 = (f32[2,1152]{1,0:T(2,128)S(1)}, f32[2,1152]{1,0:T(2,128)S(1)}, u32[]{:S(2)}, u32[]{:S(2)}) collective-permute-start(f32[2,1152]{1,0:T(2,128)S(1)} %get-tuple-element.9), channel_id=1, source_target_pairs={{0,4},{4,8},{8,12},{12,0},{1,5},{5,9},{9,13},{13,1},{2,6},{6,10},{... | collective-permute-start | bytes 27656 | tf_op jit(solution)/shard_map/ppermute | solution.py:236
  267.5 3.7 %collective-permute-start.20 = (f32[2,1152]{1,0:T(2,128)S(1)}, f32[2,1152]{1,0:T(2,128)S(1)}, u32[]{:S(2)}, u32[]{:S(2)}) collective-permute-start(f32[2,1152]{1,0:T(2,128)S(1)} %get-tuple-element.11), channel_id=1, source_target_pairs={{0,8},{4,12},{8,0},{12,4},{1,9},{5,13},{9,1},{13,5},{2,10},{6,14},... | collective-permute-start | bytes 27656 | tf_op jit(solution)/shard_map/ppermute | solution.py:236
  (27 other events, 89.2 us)
Sparse Core Ops, SparseCore 0:
  10.3 30.6 all-gather.2
  42.6 27.4 all-gather.4

commit v5 on v3

--- a/solution.py
+++ b/solution.py
@@ -71,10 +71,35 @@
     )
     gathered = lax.all_gather(mine, "plane", axis=0, tiled=True)
     held = [(own, rotate_rows(gathered, 0))]
-    for bit, (axis, size, flip) in enumerate(levels):
+    direct = levels[:-1] if len(levels) > 1 else []
+    if direct:
+        axes = tuple(dict.fromkeys(axis for axis, _, _ in direct))
+        sizes = {axis: lax.axis_size(axis) for axis in axes}
+        total = 1
+        for axis in axes:
+            total *= sizes[axis]
+        first_block = held[0][1]
+        for mask in range(1, 2 ** len(direct)):
+            pairs = []
+            for linear in range(total):
+                coords = {}
+                rest = linear
+                for axis in reversed(axes):
+                    coords[axis] = rest % sizes[axis]
+                    rest //= sizes[axis]
+                for bit, (axis, _, flip) in enumerate(direct):
+                    if mask & (1 << bit):
+                        coords[axis] = coords[axis] ^ flip
+                target = 0
+                for axis in axes:
+                    target = target * sizes[axis] + coords[axis]
+                pairs.append((linear, target))
+            held.append((lax.bitwise_xor(own, mask), lax.ppermute(first_block, axes, pairs)))
+    for bit in range(len(direct), len(levels)):
+        axis, size, flip = levels[bit]
         swap = [(i, i ^ flip) for i in range(size)]
         held = held + [
-            (piece + (1 - 2 * ((piece // 2 ** bit) % 2)) * 2 ** bit, lax.ppermute(block, axis, swap))
+            (lax.bitwise_xor(piece, 2 ** bit), lax.ppermute(block, axis, swap))
             for piece, block in held
         ]
     results = []

time: 278 us -> 279 us (level)
  waiting for transfers between devices: 86.8 us -> 90.3 us
    ppermute x14 -> x8, waiting for transfers between devices: 33.9 us -> 0.02 us  [gather_pieces(): lax.ppermute(block, axis, swap)]
    ppermute x0 -> x6, waiting for transfers between devices: none -> 21.5 us  [gather_pieces(): lax.ppermute(first_block, axes, pairs)]
    all_gather x2, waiting for transfers between devices: 33.2 us -> 49.1 us  [gather_pieces(): gathered = lax.all_gather(mine, 'plane', axis=0, tiled=True)]
    ppermute x14 -> x8, starting transfers between devices: 15.6 us -> 6.07 us  [gather_pieces(): lax.ppermute(block, axis, swap)]
    ppermute x0 -> x6, starting transfers between devices: none -> 8.09 us  [gather_pieces(): lax.ppermute(first_block, axes, pairs)]
    unnamed x51 -> x53, local copies, waits for them, and re-layouts: 12.8 us -> 12.9 us
  transfers between devices with their start and end apart: 26 -> 26, of which waited for: 12 -> 10; matrix products, arithmetic and copies ran while one was open for 20% -> 20% of each run, Pallas kernels for 0% -> 0%
where the time goes in v5:
time: 279 us; the launch traced here: 277 us
  waiting for transfers between devices  90.3 us (32%)
  matrix products  47 us (17%)
  blocking collectives  40.9 us (15%)
  starting transfers between devices  32.8 us (12%)
  local copies, waits for them, and re-layouts  32.7 us (12%)
  other arithmetic  18.3 us (7%)
  between operations  15 us (5%)
    all_gather x2, waiting for transfers between devices, gather_pieces(): gathered = lax.all_gather(mine, 'plane', axis=0, tiled=True)  49.1 us
    all_to_all x1, blocking collectives, body(): lax.all_to_all(heads_first, 'plane', split_axis=0, concat_axis=2, tiled=T...  40.9 us
    dot_general x32, matrix products, project(): part = jnp.dot(remote_inputs, block, preferred_element_type=jnp.float32)  34.6 us
    ppermute x6, waiting for transfers between devices, gather_pieces(): lax.ppermute(first_block, axes, pairs)  21.5 us
    unnamed x53, local copies, waits for them, and re-layouts  12.9 us
    all_to_all x1, waiting for transfers between devices, body(): lax.all_to_all(attended, 'plane', split_axis=2, concat_axis=0, tiled=True)  12.9 us
    ppermute x6, starting transfers between devices, gather_pieces(): lax.ppermute(first_block, axes, pairs)  8.09 us
    squeeze x8, local copies, waits for them, and re-layouts, attend_items(): return lax.map(one_item, (packed_all[0], flags_all[0]))[None]  7.76 us
  transfers between devices with their start and end apart: 26, of which 10 were waited for; matrix products, arithmetic and copies ran while one was open for 20% of the time, Pallas kernels for 0%

profile of v5, /device:TPU:0, one launch (start us, length us, event | category | flops | bytes accessed | tf_op | source)
XLA Modules:
  0.0 277.4 jit_solution(453123641488444381)
XLA Ops:
  14.4 26.6 %all-gather.3.cloned.1.call-done = bf16[1024,512]{1,0:T(8,128)(2,1)} async-done(((bf16[256,512]{1,0:T(8,128)(2,1)}), bf16[1024,512]{1,0:T(8,128)(2,1)}) %all-gather.3.cloned.1.call-update) | async-done | bytes 1048592 | tf_op jit(solution)/shard_map/all_gather | solution.py:72
  41.0 1.7 fusion.30
  47.6 22.5 %all-gather.5.cloned.1.call-done = bf16[1024,512]{1,0:T(8,128)(2,1)} async-done(((bf16[256,512]{1,0:T(8,128)(2,1)}), bf16[1024,512]{1,0:T(8,128)(2,1)}) %all-gather.5.cloned.1.call-update) | async-done | bytes 1048592 | tf_op jit(solution)/shard_map/all_gather | solution.py:72
  70.1 2.6 fusion.29
  75.4 4.8 %collective-permute-done.2 = bf16[768,512]{1,0:T(8,128)(2,1)} collective-permute-done((bf16[768,512]{1,0:T(8,128)(2,1)S(1)}, bf16[768,512]{1,0:T(8,128)(2,1)}, u32[]{:S(2)}, u32[]{:S(2)}) %collective-permute-start.2) | collective-permute-done | bytes 786464 | tf_op jit(solution)/shard_map/ppermute | solution.py:97
  91.6 1.6 fusion.14
  94.3 2.6 collective-permute-start.7
  101.3 1.6 copy.57
  105.9 16.7 %collective-permute-done.11 = bf16[768,512]{1,0:T(8,128)(2,1)} collective-permute-done((bf16[768,512]{1,0:T(8,128)(2,1)}, bf16[768,512]{1,0:T(8,128)(2,1)}, u32[]{:S(2)}, u32[]{:S(2)}) %collective-permute-start.11) | collective-permute-done | bytes 786464 | tf_op jit(solution)/shard_map/ppermute | solution.py:97
  122.6 3.8 %collective-permute-start.15 = (bf16[768,512]{1,0:T(8,128)(2,1)}, bf16[768,512]{1,0:T(8,128)(2,1)S(1)}, u32[]{:S(2)}, u32[]{:S(2)}) collective-permute-start(bf16[768,512]{1,0:T(8,128)(2,1)} %collective-permute-done.11), channel_id=1, source_target_pairs={{0,4},{4,0},{8,12},{12,8},{1,5},{5,1},{9,13},{13,9},{2,6},{6,2},{1... | collective-permute-start | bytes 2359304 | tf_op jit(solution)/shard_map/ppermute | solution.py:102
  129.3 3.2 %fusion.97 = (f32[2,16,128]{2,1,0:T(8,128)S(1)}, f32[2,16,128,384]{3,2,1,0:T(8,128)S(1)}) fusion(f32[2,16,128,384]{3,2,1,0:T(8,128)S(1)} %fusion.20, pred[2,128,384]{2,1,0:T(8,128)(4,1)S(1)} %broadcast_or_fusion), kind=kOutput, calls=%fused_computation.196 | output fusion | flops 11010431 | bytes 12697600 | tf_op jit(solution)/shard_map/sub | solution.py:31
  132.6 2.0 fusion.25
  157.8 40.9 %all_to_all.45 = bf16[4,8,128,192]{2,3,1,0:T(8,128)(2,1)S(1)} all-to-all(bf16[4,8,128,192]{2,3,1,0:T(8,128)(2,1)S(1)} %bitcast.161), channel_id=1, replica_groups=mesh['groups'=2,'sec'=4,'plane'=4] {'plane'}, dimensions={0} | all-to-all | bytes 3145728 | tf_op jit(solution)/shard_map/all_to_all | solution.py:224
  199.3 3.2 %all-to-all-start = ((bf16[4,8,128]{2,1,0:T(8,128)(2,1)}), bf16[4,8,128]{2,1,0:T(8,128)(2,1)S(1)}, u32[]{:S(2)}, u32[]{:S(2)}) async-start(bf16[4,8,128]{2,1,0:T(8,128)(2,1)} %broadcast_in_dim.87), calls=%async_computation | async-start | bytes 16384 | tf_op jit(solution)/shard_map/all_to_all | solution.py:225
  202.6 2.6 copy.53
  205.2 2.9 %all-to-all-done = bf16[4,8,128]{2,1,0:T(8,128)(2,1)S(1)} async-done(((bf16[4,8,128]{2,1,0:T(8,128)(2,1)}), bf16[4,8,128]{2,1,0:T(8,128)(2,1)S(1)}, u32[]{:S(2)}, u32[]{:S(2)}) %all-to-all-start) | async-done | bytes 8224 | tf_op jit(solution)/shard_map/all_to_all | solution.py:225
  208.2 16.5 %while.11 = (s32[]{:T(128)}, bf16[8,512,64]{1,2,0:T(8,128)(2,1)S(1)}, bf16[8,512]{1,0:T(8,128)(2,1)S(1)}, bf16[8,512,192]{2,1,0:T(8,128)(2,1)}, s32[]{:T(128)}) while((s32[]{:T(128)}, bf16[8,512,64]{1,2,0:T(8,128)(2,1)S(1)}, bf16[8,512]{1,0:T(8,128)(2,1)S(1)}, bf16[8,512,192]{2,1,0:T(8,128)(2,1)}, s32[]{:T(128)}) %tuple.53), condition=%wide.region_7.8_spmd.clone, body=%wide.region_4.7_spmd.clone.sunk | while | flops 71336448 | bytes 3945545 | solution.py:156
  225.5 1.6 reshape.163
  227.0 3.7 %all-to-all-start.2 = ((bf16[4,2,32768]{2,1,0:T(2,128)(2,1)}), bf16[4,2,32768]{2,1,0:T(2,128)(2,1)S(1)}, u32[]{:S(2)}, u32[]{:S(2)}) async-start(bf16[4,2,32768]{2,1,0:T(2,128)(2,1)} %reshape.163), calls=%async_computation.2 | async-start | bytes 1048576 | tf_op jit(solution)/shard_map/all_to_all | solution.py:228
  230.8 12.9 %all-to-all-done.2 = bf16[4,2,32768]{2,1,0:T(2,128)(2,1)S(1)} async-done(((bf16[4,2,32768]{2,1,0:T(2,128)(2,1)}), bf16[4,2,32768]{2,1,0:T(2,128)(2,1)S(1)}, u32[]{:S(2)}, u32[]{:S(2)}) %all-to-all-start.2) | async-done | bytes 524320 | tf_op jit(solution)/shard_map/all_to_all | solution.py:228
  258.1 2.0 collective-permute-start.17
  260.1 1.8 collective-permute-start.18
  261.9 1.9 collective-permute-done.16
  264.5 2.4 collective-permute-start.20
  (220 shorter events, 96.3 us)
Async XLA Ops:
  7.2 33.8 %all-gather.3.cloned.1.call-start = ((), (), s32[]{:S(2)}) async-start(), calls=%async_computation.3 | async-start | bytes 1310720 | tf_op jit(solution)/shard_map/all_gather | solution.py:72
  10.2 59.8 %all-gather.5.cloned.1.call-start = ((), (), s32[]{:S(2)}) async-start(), calls=%async_computation.4 | async-start | bytes 1310720 | tf_op jit(solution)/shard_map/all_gather | solution.py:72
  42.7 32.1 %collective-permute-start = (bf16[768,512]{1,0:T(8,128)(2,1)S(1)}, bf16[768,512]{1,0:T(8,128)(2,1)}, u32[]{:S(2)}, u32[]{:S(2)}) collective-permute-start(bf16[768,512]{1,0:T(8,128)(2,1)S(1)} %fusion.30), channel_id=1, source_target_pairs={{0,16},{4,20},{8,24},{12,28},{16,0},{20,4},{24,8},{28,12},{1,17},{... | collective-permute-start | bytes 2359304 | tf_op jit(solution)/shard_map/ppermute | solution.py:97
  44.3 30.7 %collective-permute-start.1 = (bf16[768,512]{1,0:T(8,128)(2,1)S(1)}, bf16[768,512]{1,0:T(8,128)(2,1)}, u32[]{:S(2)}, u32[]{:S(2)}) collective-permute-start(bf16[768,512]{1,0:T(8,128)(2,1)S(1)} %fusion.30), channel_id=1, source_target_pairs={{0,8},{4,12},{8,0},{12,4},{16,24},{20,28},{24,16},{28,20},{1,9},{5... | collective-permute-start | bytes 2359304 | tf_op jit(solution)/shard_map/ppermute | solution.py:97
  45.7 34.4 %collective-permute-start.2 = (bf16[768,512]{1,0:T(8,128)(2,1)S(1)}, bf16[768,512]{1,0:T(8,128)(2,1)}, u32[]{:S(2)}, u32[]{:S(2)}) collective-permute-start(bf16[768,512]{1,0:T(8,128)(2,1)S(1)} %fusion.30), channel_id=1, source_target_pairs={{0,24},{4,28},{8,16},{12,20},{16,8},{20,12},{24,0},{28,4},{1,25},{... | collective-permute-start | bytes 2359304 | tf_op jit(solution)/shard_map/ppermute | solution.py:97
  47.5 37.0 %collective-permute-start.3 = (bf16[768,512]{1,0:T(8,128)(2,1)S(1)}, bf16[768,512]{1,0:T(8,128)(2,1)}, u32[]{:S(2)}, u32[]{:S(2)}) collective-permute-start(bf16[768,512]{1,0:T(8,128)(2,1)S(1)} %fusion.30), channel_id=1, source_target_pairs={{0,4},{4,0},{8,12},{12,8},{1,5},{5,1},{9,13},{13,9},{2,6},{6,2},{1... | collective-permute-start | bytes 2359304 | tf_op jit(solution)/shard_map/ppermute | solution.py:102
  72.6 31.6 %collective-permute-start.9 = (bf16[768,512]{1,0:T(8,128)(2,1)}, bf16[768,512]{1,0:T(8,128)(2,1)}, u32[]{:S(2)}, u32[]{:S(2)}) collective-permute-start(bf16[768,512]{1,0:T(8,128)(2,1)} %fusion.29), channel_id=1, source_target_pairs={{0,16},{4,20},{8,24},{12,28},{16,0},{20,4},{24,8},{28,12},{1,17},{... | collective-permute-start | bytes 2359304 | tf_op jit(solution)/shard_map/ppermute | solution.py:97
  74.8 12.6 %collective-permute-start.4 = (bf16[768,512]{1,0:T(8,128)(2,1)}, bf16[768,512]{1,0:T(8,128)(2,1)S(1)}, u32[]{:S(2)}, u32[]{:S(2)}) collective-permute-start(bf16[768,512]{1,0:T(8,128)(2,1)} %collective-permute-done), channel_id=1, source_target_pairs={{0,4},{4,0},{8,12},{12,8},{1,5},{5,1},{9,13},{13,9},{2,6},{6,2},{1... | collective-permute-start | bytes 2359304 | tf_op jit(solution)/shard_map/ppermute | solution.py:102
  74.9 14.5 %collective-permute-start.5 = (bf16[768,512]{1,0:T(8,128)(2,1)}, bf16[768,512]{1,0:T(8,128)(2,1)S(1)}, u32[]{:S(2)}, u32[]{:S(2)}) collective-permute-start(bf16[768,512]{1,0:T(8,128)(2,1)} %collective-permute-done.1), channel_id=1, source_target_pairs={{0,4},{4,0},{8,12},{12,8},{1,5},{5,1},{9,13},{13,9},{2,6},{6,2},{1... | collective-permute-start | bytes 2359304 | tf_op jit(solution)/shard_map/ppermute | solution.py:102
  80.2 9.6 %collective-permute-start.6 = (bf16[768,512]{1,0:T(8,128)(2,1)}, bf16[768,512]{1,0:T(8,128)(2,1)S(1)}, u32[]{:S(2)}, u32[]{:S(2)}) collective-permute-start(bf16[768,512]{1,0:T(8,128)(2,1)} %collective-permute-done.2), channel_id=1, source_target_pairs={{0,4},{4,0},{8,12},{12,8},{1,5},{5,1},{9,13},{13,9},{2,6},{6,2},{1... | collective-permute-start | bytes 2359304 | tf_op jit(solution)/shard_map/ppermute | solution.py:102
  84.5 21.3 %collective-permute-start.10 = (bf16[768,512]{1,0:T(8,128)(2,1)}, bf16[768,512]{1,0:T(8,128)(2,1)}, u32[]{:S(2)}, u32[]{:S(2)}) collective-permute-start(bf16[768,512]{1,0:T(8,128)(2,1)} %fusion.29), channel_id=1, source_target_pairs={{0,8},{4,12},{8,0},{12,4},{16,24},{20,28},{24,16},{28,20},{1,9},{5... | collective-permute-start | bytes 2359304 | tf_op jit(solution)/shard_map/ppermute | solution.py:97
  87.5 35.1 %collective-permute-start.11 = (bf16[768,512]{1,0:T(8,128)(2,1)}, bf16[768,512]{1,0:T(8,128)(2,1)}, u32[]{:S(2)}, u32[]{:S(2)}) collective-permute-start(bf16[768,512]{1,0:T(8,128)(2,1)} %fusion.29), channel_id=1, source_target_pairs={{0,24},{4,28},{8,16},{12,20},{16,8},{20,12},{24,0},{28,4},{1,25},{... | collective-permute-start | bytes 2359304 | tf_op jit(solution)/shard_map/ppermute | solution.py:97
  94.3 28.3 %collective-permute-start.7 = (bf16[128,2048]{0,1:T(8,128)(2,1)}, bf16[128,2048]{0,1:T(8,128)(2,1)}, u32[]{:S(2)}, u32[]{:S(2)}) collective-permute-start(bf16[128,2048]{0,1:T(8,128)(2,1)} %bitcast.4), channel_id=1, source_target_pairs={{0,4},{4,8},{8,12},{1,5},{5,9},{9,13},{2,6},{6,10},{10,14},{3,7},{... | collective-permute-start | bytes 1572872 | tf_op jit(solution)/shard_map/ppermute | solution.py:19
  97.9 28.5 %collective-permute-start.8 = (bf16[128,2048]{0,1:T(8,128)(2,1)}, bf16[128,2048]{0,1:T(8,128)(2,1)}, u32[]{:S(2)}, u32[]{:S(2)}) collective-permute-start(bf16[128,2048]{0,1:T(8,128)(2,1)} %bitcast.8), channel_id=1, source_target_pairs={{4,0},{8,4},{12,8},{5,1},{9,5},{13,9},{6,2},{10,6},{14,10},{7,3},{... | collective-permute-start | bytes 1572872 | tf_op jit(solution)/shard_map/ppermute | solution.py:19
  104.3 49.3 %collective-permute-start.12 = (bf16[768,512]{1,0:T(8,128)(2,1)}, bf16[768,512]{1,0:T(8,128)(2,1)S(1)}, u32[]{:S(2)}, u32[]{:S(2)}) collective-permute-start(bf16[768,512]{1,0:T(8,128)(2,1)} %fusion.29), channel_id=1, source_target_pairs={{0,4},{4,0},{8,12},{12,8},{1,5},{5,1},{9,13},{13,9},{2,6},{6,2},{1... | collective-permute-start | bytes 2359304 | tf_op jit(solution)/shard_map/ppermute | solution.py:102
  105.8 48.2 %collective-permute-start.13 = (bf16[768,512]{1,0:T(8,128)(2,1)}, bf16[768,512]{1,0:T(8,128)(2,1)S(1)}, u32[]{:S(2)}, u32[]{:S(2)}) collective-permute-start(bf16[768,512]{1,0:T(8,128)(2,1)} %collective-permute-done.9), channel_id=1, source_target_pairs={{0,4},{4,0},{8,12},{12,8},{1,5},{5,1},{9,13},{13,9},{2,6},{6,2},{1... | collective-permute-start | bytes 2359304 | tf_op jit(solution)/shard_map/ppermute | solution.py:102
  122.6 31.8 %collective-permute-start.14 = (bf16[768,512]{1,0:T(8,128)(2,1)}, bf16[768,512]{1,0:T(8,128)(2,1)S(1)}, u32[]{:S(2)}, u32[]{:S(2)}) collective-permute-start(bf16[768,512]{1,0:T(8,128)(2,1)} %collective-permute-done.10), channel_id=1, source_target_pairs={{0,4},{4,0},{8,12},{12,8},{1,5},{5,1},{9,13},{13,9},{2,6},{6,2},{1... | collective-permute-start | bytes 2359304 | tf_op jit(solution)/shard_map/ppermute | solution.py:102
  122.6 32.1 %collective-permute-start.15 = (bf16[768,512]{1,0:T(8,128)(2,1)}, bf16[768,512]{1,0:T(8,128)(2,1)S(1)}, u32[]{:S(2)}, u32[]{:S(2)}) collective-permute-start(bf16[768,512]{1,0:T(8,128)(2,1)} %collective-permute-done.11), channel_id=1, source_target_pairs={{0,4},{4,0},{8,12},{12,8},{1,5},{5,1},{9,13},{13,9},{2,6},{6,2},{1... | collective-permute-start | bytes 2359304 | tf_op jit(solution)/shard_map/ppermute | solution.py:102
  199.3 8.8 %all-to-all-start = ((bf16[4,8,128]{2,1,0:T(8,128)(2,1)}), bf16[4,8,128]{2,1,0:T(8,128)(2,1)S(1)}, u32[]{:S(2)}, u32[]{:S(2)}) async-start(bf16[4,8,128]{2,1,0:T(8,128)(2,1)} %broadcast_in_dim.87), calls=%async_computation | async-start | bytes 16384 | tf_op jit(solution)/shard_map/all_to_all | solution.py:225
  227.0 16.6 %all-to-all-start.2 = ((bf16[4,2,32768]{2,1,0:T(2,128)(2,1)}), bf16[4,2,32768]{2,1,0:T(2,128)(2,1)S(1)}, u32[]{:S(2)}, u32[]{:S(2)}) async-start(bf16[4,2,32768]{2,1,0:T(2,128)(2,1)} %reshape.163), calls=%async_computation.2 | async-start | bytes 1048576 | tf_op jit(solution)/shard_map/all_to_all | solution.py:228
  258.0 5.8 %collective-permute-start.16 = (f32[4,2,1152]{2,1,0:T(2,128)S(1)}, f32[4,2,1152]{2,1,0:T(2,128)S(1)}, u32[]{:S(2)}, u32[]{:S(2)}) collective-permute-start(f32[4,2,1152]{2,1,0:T(2,128)S(1)} %get-tuple-element.83), channel_id=1, source_target_pairs={{0,1},{1,2},{2,3},{3,0},{4,5},{5,6},{6,7},{7,4},{8,9},{9,10},{10,1... | collective-permute-start | bytes 110600 | tf_op jit(solution)/shard_map/ppermute | solution.py:249
  258.1 5.7 %collective-permute-start.17 = (f32[4,2,1152]{2,1,0:T(2,128)S(1)}, f32[4,2,1152]{2,1,0:T(2,128)S(1)}, u32[]{:S(2)}, u32[]{:S(2)}) collective-permute-start(f32[4,2,1152]{2,1,0:T(2,128)S(1)} %get-tuple-element.85), channel_id=1, source_target_pairs={{0,2},{1,3},{2,0},{3,1},{4,6},{5,7},{6,4},{7,5},{8,10},{9,11},{10,... | collective-permute-start | bytes 110600 | tf_op jit(solution)/shard_map/ppermute | solution.py:249
  260.1 4.3 %collective-permute-start.18 = (f32[4,2,1152]{2,1,0:T(2,128)S(1)}, f32[4,2,1152]{2,1,0:T(2,128)S(1)}, u32[]{:S(2)}, u32[]{:S(2)}) collective-permute-start(f32[4,2,1152]{2,1,0:T(2,128)S(1)} %get-tuple-element.84), channel_id=1, source_target_pairs={{0,3},{1,0},{2,1},{3,2},{4,7},{5,4},{6,5},{7,6},{8,11},{9,8},{10,9... | collective-permute-start | bytes 110600 | tf_op jit(solution)/shard_map/ppermute | solution.py:249
  264.5 4.1 %collective-permute-start.20 = (f32[2,1152]{1,0:T(2,128)S(1)}, f32[2,1152]{1,0:T(2,128)S(1)}, u32[]{:S(2)}, u32[]{:S(2)}) collective-permute-start(f32[2,1152]{1,0:T(2,128)S(1)} %get-tuple-element.88), channel_id=1, source_target_pairs={{0,8},{4,12},{8,0},{12,4},{1,9},{5,13},{9,1},{13,5},{2,10},{6,14},... | collective-permute-start | bytes 27656 | tf_op jit(solution)/shard_map/ppermute | solution.py:256
  (24 other events, 186.8 us)
Sparse Core Ops, SparseCore 0:
  10.4 30.6 all-gather.2
  42.6 27.4 all-gather.4

commit v6 on v3

--- a/solution.py
+++ b/solution.py
@@ -129,6 +129,40 @@
         return lax.map(one_block, (query_blocks, block_starts)).reshape(seq_len, HEAD_DIM)
 
     return lax.map(one_item, (packed_all[0], flags_all[0]))[None]
+
+
+def attend_by_section(projected, counts, plane_count):
+    sec_block, tok_block = projected.shape[0], projected.shape[1]
+    share = HEADS // plane_count
+    seq_len = plane_count * tok_block
+    score_scale = 1.0 / math.sqrt(HEAD_DIM)
+    key_index = jnp.arange(seq_len, dtype=jnp.int32)
+    contexts = []
+    for local in range(sec_block):
+        section = lax.axis_index("sec") * sec_block + local
+        key_alive = key_index < lax.dynamic_index_in_dim(counts, section, keepdims=False)
+        outgoing = jnp.transpose(
+            projected[local].reshape(tok_block, 3, plane_count, share, HEAD_DIM), (2, 3, 0, 1, 4)
+        ).reshape(plane_count, share, tok_block, 3 * HEAD_DIM)
+        packed = lax.all_to_all(outgoing, "plane", split_axis=0, concat_axis=2, tiled=True)[0]
+        queries = packed[:, :, :HEAD_DIM]
+        keys = packed[:, :, HEAD_DIM : 2 * HEAD_DIM]
+        values = packed[:, :, 2 * HEAD_DIM :]
+        scores = (
+            jnp.einsum("nqd,nkd->nqk", queries, keys, preferred_element_type=jnp.float32)
+            * score_scale
+        )
+        allowed = key_alive[None, None, :] | (key_index[None, None, :] == key_index[None, :, None])
+        attention = masked_softmax(scores, allowed)
+        context = jnp.einsum(
+            "nqk,nkd->nqd", attention, values, preferred_element_type=jnp.float32
+        ).astype(jnp.bfloat16)
+        homeward = jnp.transpose(
+            context.reshape(share, plane_count, tok_block, HEAD_DIM), (1, 0, 2, 3)
+        )
+        returned = lax.all_to_all(homeward, "plane", split_axis=0, concat_axis=1, tiled=True)[0]
+        contexts.append(jnp.transpose(returned, (1, 0, 2)).reshape(tok_block, HEADS * HEAD_DIM))
+    return jnp.concatenate(contexts, axis=0)
 
 
 def body(tokens, counts, region_ids, norm_gains, cross_qkv, cross_out, plane_qkv, plane_out):
@@ -186,24 +220,27 @@
     normed = rms_norm(after_cross, norm_gains[1])
     result = project(normed, plane_qkv_pieces)
     projected = result.astype(jnp.bfloat16).reshape(sec_block, tok_block, 3, HEADS, HEAD_DIM)
-    per_device = sec_block * HEADS // plane_count
-    heads_first = jnp.transpose(projected, (0, 3, 1, 2, 4)).reshape(
-        plane_count, per_device, tok_block, 3 * HEAD_DIM
-    )
-    key_flags = jnp.broadcast_to(own_valid[:, None, :], (sec_block, HEADS, tok_block)).astype(
-        jnp.bfloat16
-    )
-    key_flags = key_flags.reshape(plane_count, per_device, tok_block)
-    attended = attend_items(
-        (
-            lax.all_to_all(heads_first, "plane", split_axis=0, concat_axis=2, tiled=True),
-            lax.all_to_all(key_flags, "plane", split_axis=0, concat_axis=2, tiled=True),
-        )
-    )
-    returned = lax.all_to_all(attended, "plane", split_axis=2, concat_axis=0, tiled=True)
-    context = jnp.transpose(
-        returned.reshape(sec_block, HEADS, tok_block, HEAD_DIM), (0, 2, 1, 3)
-    ).reshape(-1, model_width)
+    if HEADS % plane_count == 0:
+        context = attend_by_section(projected, counts, plane_count)
+    else:
+        per_device = sec_block * HEADS // plane_count
+        heads_first = jnp.transpose(projected, (0, 3, 1, 2, 4)).reshape(
+            plane_count, per_device, tok_block, 3 * HEAD_DIM
+        )
+        key_flags = jnp.broadcast_to(own_valid[:, None, :], (sec_block, HEADS, tok_block)).astype(
+            jnp.bfloat16
+        )
+        key_flags = key_flags.reshape(plane_count, per_device, tok_block)
+        attended = attend_items(
+            (
+                lax.all_to_all(heads_first, "plane", split_axis=0, concat_axis=2, tiled=True),
+                lax.all_to_all(key_flags, "plane", split_axis=0, concat_axis=2, tiled=True),
+            )
+        )
+        returned = lax.all_to_all(attended, "plane", split_axis=2, concat_axis=0, tiled=True)
+        context = jnp.transpose(
+            returned.reshape(sec_block, HEADS, tok_block, HEAD_DIM), (0, 2, 1, 3)
+        ).reshape(-1, model_width)
     result = project(context, plane_out_pieces)
     encoded = (after_cross.astype(jnp.float32) + result).astype(jnp.bfloat16)
     labels = region_ids.reshape(-1)

time: 278 us -> 262 us (0.942)
  blocking collectives: 41.2 us -> 0 us
  waiting for transfers between devices: 86.8 us -> 108 us
  local copies, waits for them, and re-layouts: 32.6 us -> 21.6 us
  starting transfers between devices: 34.2 us -> 42.8 us
  matrix products: 48.1 us -> 55.1 us
    all_to_all x1 -> x0, blocking collectives: 41.2 us -> none  [body(): lax.all_to_all(heads_first, 'plane', split_axis=0, concat_axis=2, tiled=T...]
    all_to_all x2 -> x4, waiting for transfers between devices: 15.7 us -> 36.9 us  [the longest x2 28.9 us: attend_by_section(): lax.all_to_all(outgoing, 'plane', split_axis=0, concat_axis=2, tiled=True)]
    all_to_all x2 -> x4, starting transfers between devices: 6.98 us -> 16 us  [the longest x2 8.46 us: attend_by_section(): lax.all_to_all(homeward, 'plane', split_axis=0, concat_axis=1, tiled=True)]
    sub x0 -> x2, matrix products: none -> 7.91 us  [masked_softmax(): expo = jnp.where(allowed, jnp.exp(shifted - top), 0.0)]
    squeeze x8 -> x2, local copies, waits for them, and re-layouts: 7.76 us -> 0.6 us  [attend_by_section(): lax.all_to_all(outgoing, 'plane', split_axis=0, concat_axis=2, tiled=True)]
    unnamed x51 -> x42, local copies, waits for them, and re-layouts: 12.8 us -> 7.28 us
    dot_general x16 -> x2, matrix products: 6.25 us -> 5.34 us  [attend_by_section(): jnp.einsum('nqk,nkd->nqd', attention, values, preferred_element_type=jnp....]
  transfers between devices with their start and end apart: 26 -> 28, of which waited for: 12 -> 13; matrix products, arithmetic and copies ran while one was open for 20% -> 29% of each run, Pallas kernels for 0% -> 0%
where the time goes in v6:
time: 262 us; the launch traced here: 260 us
  waiting for transfers between devices  108 us (41%)
  matrix products  55.1 us (21%)
  starting transfers between devices  42.8 us (16%)
  local copies, waits for them, and re-layouts  21.6 us (8%)
  other arithmetic  17.8 us (7%)
  between operations  15 us (6%)
    dot_general x32, matrix products, project(): part = jnp.dot(remote_inputs, block, preferred_element_type=jnp.float32)  35.7 us
    ppermute x14, waiting for transfers between devices, gather_pieces(): lax.ppermute(block, axis, swap)  33.9 us
    all_gather x2, waiting for transfers between devices, gather_pieces(): gathered = lax.all_gather(mine, 'plane', axis=0, tiled=True)  33.2 us
    all_to_all x2, waiting for transfers between devices, attend_by_section(): lax.all_to_all(outgoing, 'plane', split_axis=0, concat_axis=2, tiled=True)  28.9 us
    ppermute x14, starting transfers between devices, gather_pieces(): lax.ppermute(block, axis, swap)  15.6 us
    all_to_all x2, starting transfers between devices, attend_by_section(): lax.all_to_all(homeward, 'plane', split_axis=0, concat_axis=1, tiled=True)  8.46 us
    all_to_all x2, waiting for transfers between devices, attend_by_section(): lax.all_to_all(homeward, 'plane', split_axis=0, concat_axis=1, tiled=True)  8.01 us
    sub x2, matrix products, masked_softmax(): expo = jnp.where(allowed, jnp.exp(shifted - top), 0.0)  7.91 us
  transfers between devices with their start and end apart: 28, of which 13 were waited for; matrix products, arithmetic and copies ran while one was open for 29% of the time, Pallas kernels for 0%

profile of v6, /device:TPU:0, one launch (start us, length us, event | category | flops | bytes accessed | tf_op | source)
XLA Modules:
  0.0 260.1 jit_solution(13884092929110191880)
XLA Ops:
  14.4 26.7 %all-gather.3.cloned.1.call-done = bf16[1024,512]{1,0:T(8,128)(2,1)} async-done(((bf16[256,512]{1,0:T(8,128)(2,1)}), bf16[1024,512]{1,0:T(8,128)(2,1)}) %all-gather.3.cloned.1.call-update) | async-done | bytes 1048592 | tf_op jit(solution)/shard_map/all_gather | solution.py:72
  47.1 14.9 %collective-permute-done = bf16[768,512]{1,0:T(8,128)(2,1)} collective-permute-done((bf16[768,512]{1,0:T(8,128)(2,1)S(1)}, bf16[768,512]{1,0:T(8,128)(2,1)}, u32[]{:S(2)}, u32[]{:S(2)}) %collective-permute-start) | collective-permute-done | bytes 786464 | tf_op jit(solution)/shard_map/ppermute | solution.py:77
  63.5 6.5 %all-gather.5.cloned.1.call-done = bf16[1024,512]{1,0:T(8,128)(2,1)} async-done(((bf16[256,512]{1,0:T(8,128)(2,1)}), bf16[1024,512]{1,0:T(8,128)(2,1)}) %all-gather.5.cloned.1.call-update) | async-done | bytes 1048592 | tf_op jit(solution)/shard_map/all_gather | solution.py:72
  70.1 2.6 %fusion.35 = bf16[768,512]{1,0:T(8,128)(2,1)} fusion(s32[]{:T(128)S(6)} %select_n.239, bf16[1024,512]{1,0:T(8,128)(2,1)} %all-gather.5.cloned.1.call-done), kind=kLoop, calls=%fused_computation.105 | loop fusion | flops 1572864 | bytes 1835012 | tf_op jit(solution)/shard_map/concatenate | solution.py:54
  78.3 2.3 collective-permute-done.2
  83.6 8.5 %collective-permute-done.9 = bf16[768,512]{1,0:T(8,128)(2,1)} collective-permute-done((bf16[768,512]{1,0:T(8,128)(2,1)}, bf16[768,512]{1,0:T(8,128)(2,1)}, u32[]{:S(2)}, u32[]{:S(2)}) %collective-permute-start.9) | collective-permute-done | bytes 786464 | tf_op jit(solution)/shard_map/ppermute | solution.py:77
  100.3 2.1 collective-permute-start.7
  111.1 8.2 %collective-permute-done.11 = bf16[768,512]{1,0:T(8,128)(2,1)} collective-permute-done((bf16[768,512]{1,0:T(8,128)(2,1)}, bf16[768,512]{1,0:T(8,128)(2,1)}, u32[]{:S(2)}, u32[]{:S(2)}) %collective-permute-start.11) | collective-permute-done | bytes 786464 | tf_op jit(solution)/shard_map/ppermute | solution.py:77
  119.3 4.7 %collective-permute-start.15 = (bf16[768,512]{1,0:T(8,128)(2,1)}, bf16[768,512]{1,0:T(8,128)(2,1)S(1)}, u32[]{:S(2)}, u32[]{:S(2)}) collective-permute-start(bf16[768,512]{1,0:T(8,128)(2,1)} %collective-permute-done.11), channel_id=1, source_target_pairs={{0,4},{4,0},{8,12},{12,8},{1,5},{5,1},{9,13},{13,9},{2,6},{6,2},{1... | collective-permute-start | bytes 2359304 | tf_op jit(solution)/shard_map/ppermute | solution.py:77
  126.9 3.2 %fusion.140 = (f32[2,16,128]{2,1,0:T(8,128)S(1)}, f32[2,16,128,384]{3,2,1,0:T(8,128)S(1)}) fusion(f32[2,16,128,384]{3,2,1,0:T(8,128)S(1)} %fusion.20, pred[2,128,384]{2,1,0:T(8,128)(4,1)S(1)} %broadcast_or_fusion), kind=kOutput, calls=%fused_computation.231 | output fusion | flops 11010431 | bytes 12697600 | tf_op jit(solution)/shard_map/sub | solution.py:31
  130.1 2.0 fusion.25
  155.9 3.8 %all-to-all-start.2 = ((bf16[4,4,128,192]{2,3,1,0:T(8,128)(2,1)}), bf16[4,4,128,192]{2,3,1,0:T(8,128)(2,1)S(1)}, u32[]{:S(2)}, u32[]{:S(2)}) async-start(bf16[4,4,128,192]{2,3,1,0:T(8,128)(2,1)} %bitcast.34), calls=%async_computation.2 | async-start | bytes 1572864 | tf_op jit(solution)/shard_map/all_to_all | solution.py:147
  163.1 17.5 %all-to-all-done.2 = bf16[4,4,128,192]{2,3,1,0:T(8,128)(2,1)S(1)} async-done(((bf16[4,4,128,192]{2,3,1,0:T(8,128)(2,1)}), bf16[4,4,128,192]{2,3,1,0:T(8,128)(2,1)S(1)}, u32[]{:S(2)}, u32[]{:S(2)}) %all-to-all-start.2) | async-done | bytes 786464 | tf_op jit(solution)/shard_map/all_to_all | solution.py:147
  180.6 3.8 %all-to-all-start = ((bf16[4,4,128,192]{2,3,1,0:T(8,128)(2,1)}), bf16[4,4,128,192]{2,3,1,0:T(8,128)(2,1)S(1)}, u32[]{:S(2)}, u32[]{:S(2)}) async-start(bf16[4,4,128,192]{2,3,1,0:T(8,128)(2,1)} %bitcast.24), calls=%async_computation | async-start | bytes 1572864 | tf_op jit(solution)/shard_map/all_to_all | solution.py:147
  185.5 4.0 %fusion.150 = (f32[4,512]{1,0:T(4,128)S(1)}, f32[4,512,512]{1,2,0:T(8,128)}) fusion(pred[512,512]{0,1:T(8,128)(4,1)S(1)} %fusion.33, bf16[4,512,192]{1,2,0:T(8,128)(2,1)S(1)} %squeeze.60), kind=kOutput, calls=%fused_computation.233 | convolution fusion | flops 139461120 | bytes 5251072 | tf_op jit(solution)/shard_map/sub | solution.py:31
  189.4 2.7 %fusion.29 = bf16[4,8,4,8,128]{4,3,2,1,0:T(8,128)(2,1)S(1)} fusion(f32[4,512,512]{1,2,0:T(8,128)} %get-tuple-element.29, f32[4,512]{1,0:T(4,128)S(1)} %get-tuple-element.28, bf16[4,512,192]{1,2,0:T(8,128)(2,1)S(1)} %squeeze.60), kind=kOutput, calls=%fused_computation.68 | convolution fusion | flops 136445952 | bytes 4726784 | tf_op jit(solution)/shard_map/nqk,nkd->nqd/dot_general | solution.py:157
  192.9 11.3 %all-to-all-done = bf16[4,4,128,192]{2,3,1,0:T(8,128)(2,1)S(1)} async-done(((bf16[4,4,128,192]{2,3,1,0:T(8,128)(2,1)}), bf16[4,4,128,192]{2,3,1,0:T(8,128)(2,1)S(1)}, u32[]{:S(2)}, u32[]{:S(2)}) %all-to-all-start) | async-done | bytes 786464 | tf_op jit(solution)/shard_map/all_to_all | solution.py:147
  204.2 3.4 %all-to-all-start.3 = ((bf16[4,4,128,64]{2,3,1,0:T(8,128)(2,1)}), bf16[4,4,128,64]{2,3,1,0:T(8,128)(2,1)S(1)}, u32[]{:S(2)}, u32[]{:S(2)}) async-start(bf16[4,4,128,64]{2,3,1,0:T(8,128)(2,1)} %bitcast.157), calls=%async_computation.3 | async-start | bytes 524288 | tf_op jit(solution)/shard_map/all_to_all | solution.py:163
  208.5 4.0 %fusion.141 = (f32[4,512]{1,0:T(4,128)S(1)}, f32[4,512,512]{1,2,0:T(8,128)}) fusion(pred[512,512]{0,1:T(8,128)(4,1)S(1)} %fusion.34, bf16[4,512,192]{1,2,0:T(8,128)(2,1)S(1)} %squeeze.57), kind=kOutput, calls=%fused_computation.232 | convolution fusion | flops 139461120 | bytes 5251072 | tf_op jit(solution)/shard_map/sub | solution.py:31
  212.5 2.7 %fusion.28 = bf16[4,8,4,8,128]{4,3,2,1,0:T(8,128)(2,1)S(1)} fusion(f32[4,512,512]{1,2,0:T(8,128)} %get-tuple-element.27, f32[4,512]{1,0:T(4,128)S(1)} %get-tuple-element.26, bf16[4,512,192]{1,2,0:T(8,128)(2,1)S(1)} %squeeze.57), kind=kOutput, calls=%fused_computation.67 | convolution fusion | flops 136445952 | bytes 4726784 | tf_op jit(solution)/shard_map/nqk,nkd->nqd/dot_general | solution.py:157
  215.9 5.1 %all-to-all-start.1 = ((bf16[4,4,128,64]{2,3,1,0:T(8,128)(2,1)}), bf16[4,4,128,64]{2,3,1,0:T(8,128)(2,1)S(1)}, u32[]{:S(2)}, u32[]{:S(2)}) async-start(bf16[4,4,128,64]{2,3,1,0:T(8,128)(2,1)} %bitcast.159), calls=%async_computation.1 | async-start | bytes 524288 | tf_op jit(solution)/shard_map/all_to_all | solution.py:163
  221.0 8.0 %all-to-all-done.1 = bf16[4,4,128,64]{2,3,1,0:T(8,128)(2,1)S(1)} async-done(((bf16[4,4,128,64]{2,3,1,0:T(8,128)(2,1)}), bf16[4,4,128,64]{2,3,1,0:T(8,128)(2,1)S(1)}, u32[]{:S(2)}, u32[]{:S(2)}) %all-to-all-start.1) | async-done | bytes 262176 | tf_op jit(solution)/shard_map/all_to_all | solution.py:163
  242.9 2.0 collective-permute-start.18
  247.5 2.2 collective-permute-start.20
  (181 shorter events, 93.1 us)
Async XLA Ops:
  7.2 33.8 %all-gather.3.cloned.1.call-start = ((), (), s32[]{:S(2)}) async-start(), calls=%async_computation.4 | async-start | bytes 1310720 | tf_op jit(solution)/shard_map/all_gather | solution.py:72
  10.2 59.8 %all-gather.5.cloned.1.call-start = ((), (), s32[]{:S(2)}) async-start(), calls=%async_computation.5 | async-start | bytes 1310720 | tf_op jit(solution)/shard_map/all_gather | solution.py:72
  42.7 19.3 %collective-permute-start = (bf16[768,512]{1,0:T(8,128)(2,1)S(1)}, bf16[768,512]{1,0:T(8,128)(2,1)}, u32[]{:S(2)}, u32[]{:S(2)}) collective-permute-start(bf16[768,512]{1,0:T(8,128)(2,1)S(1)} %fusion.36), channel_id=1, source_target_pairs={{0,16},{16,0},{1,17},{17,1},{2,18},{18,2},{3,19},{19,3},{4,20},{20... | collective-permute-start | bytes 2359304 | tf_op jit(solution)/shard_map/ppermute | solution.py:77
  44.3 30.7 %collective-permute-start.1 = (bf16[768,512]{1,0:T(8,128)(2,1)S(1)}, bf16[768,512]{1,0:T(8,128)(2,1)}, u32[]{:S(2)}, u32[]{:S(2)}) collective-permute-start(bf16[768,512]{1,0:T(8,128)(2,1)S(1)} %fusion.36), channel_id=1, source_target_pairs={{0,8},{4,12},{8,0},{12,4},{1,9},{5,13},{9,1},{13,5},{2,10},{6,14},... | collective-permute-start | bytes 2359304 | tf_op jit(solution)/shard_map/ppermute | solution.py:77
  47.1 35.0 %collective-permute-start.3 = (bf16[768,512]{1,0:T(8,128)(2,1)S(1)}, bf16[768,512]{1,0:T(8,128)(2,1)}, u32[]{:S(2)}, u32[]{:S(2)}) collective-permute-start(bf16[768,512]{1,0:T(8,128)(2,1)S(1)} %fusion.36), channel_id=1, source_target_pairs={{0,4},{4,0},{8,12},{12,8},{1,5},{5,1},{9,13},{13,9},{2,6},{6,2},{1... | collective-permute-start | bytes 2359304 | tf_op jit(solution)/shard_map/ppermute | solution.py:77
  62.0 18.6 %collective-permute-start.2 = (bf16[768,512]{1,0:T(8,128)(2,1)}, bf16[768,512]{1,0:T(8,128)(2,1)}, u32[]{:S(2)}, u32[]{:S(2)}) collective-permute-start(bf16[768,512]{1,0:T(8,128)(2,1)} %collective-permute-done), channel_id=1, source_target_pairs={{0,8},{4,12},{8,0},{12,4},{1,9},{5,13},{9,1},{13,5},{2,10},{6,14},... | collective-permute-start | bytes 2359304 | tf_op jit(solution)/shard_map/ppermute | solution.py:77
  72.7 19.5 %collective-permute-start.9 = (bf16[768,512]{1,0:T(8,128)(2,1)}, bf16[768,512]{1,0:T(8,128)(2,1)}, u32[]{:S(2)}, u32[]{:S(2)}) collective-permute-start(bf16[768,512]{1,0:T(8,128)(2,1)} %fusion.35), channel_id=1, source_target_pairs={{0,16},{16,0},{1,17},{17,1},{2,18},{18,2},{3,19},{19,3},{4,20},{20... | collective-permute-start | bytes 2359304 | tf_op jit(solution)/shard_map/ppermute | solution.py:77
  74.9 20.2 %collective-permute-start.4 = (bf16[768,512]{1,0:T(8,128)(2,1)}, bf16[768,512]{1,0:T(8,128)(2,1)S(1)}, u32[]{:S(2)}, u32[]{:S(2)}) collective-permute-start(bf16[768,512]{1,0:T(8,128)(2,1)} %collective-permute-done), channel_id=1, source_target_pairs={{0,4},{4,0},{8,12},{12,8},{1,5},{5,1},{9,13},{13,9},{2,6},{6,2},{1... | collective-permute-start | bytes 2359304 | tf_op jit(solution)/shard_map/ppermute | solution.py:77
  75.0 20.5 %collective-permute-start.5 = (bf16[768,512]{1,0:T(8,128)(2,1)}, bf16[768,512]{1,0:T(8,128)(2,1)S(1)}, u32[]{:S(2)}, u32[]{:S(2)}) collective-permute-start(bf16[768,512]{1,0:T(8,128)(2,1)} %collective-permute-done.1), channel_id=1, source_target_pairs={{0,4},{4,0},{8,12},{12,8},{1,5},{5,1},{9,13},{13,9},{2,6},{6,2},{1... | collective-permute-start | bytes 2359304 | tf_op jit(solution)/shard_map/ppermute | solution.py:77
  80.6 15.2 %collective-permute-start.6 = (bf16[768,512]{1,0:T(8,128)(2,1)}, bf16[768,512]{1,0:T(8,128)(2,1)S(1)}, u32[]{:S(2)}, u32[]{:S(2)}) collective-permute-start(bf16[768,512]{1,0:T(8,128)(2,1)} %collective-permute-done.2), channel_id=1, source_target_pairs={{0,4},{4,0},{8,12},{12,8},{1,5},{5,1},{9,13},{13,9},{2,6},{6,2},{1... | collective-permute-start | bytes 2359304 | tf_op jit(solution)/shard_map/ppermute | solution.py:77
  82.1 28.9 %collective-permute-start.10 = (bf16[768,512]{1,0:T(8,128)(2,1)}, bf16[768,512]{1,0:T(8,128)(2,1)}, u32[]{:S(2)}, u32[]{:S(2)}) collective-permute-start(bf16[768,512]{1,0:T(8,128)(2,1)} %fusion.35), channel_id=1, source_target_pairs={{0,8},{4,12},{8,0},{12,4},{1,9},{5,13},{9,1},{13,5},{2,10},{6,14},... | collective-permute-start | bytes 2359304 | tf_op jit(solution)/shard_map/ppermute | solution.py:77
  92.1 27.1 %collective-permute-start.11 = (bf16[768,512]{1,0:T(8,128)(2,1)}, bf16[768,512]{1,0:T(8,128)(2,1)}, u32[]{:S(2)}, u32[]{:S(2)}) collective-permute-start(bf16[768,512]{1,0:T(8,128)(2,1)} %collective-permute-done.9), channel_id=1, source_target_pairs={{0,8},{4,12},{8,0},{12,4},{1,9},{5,13},{9,1},{13,5},{2,10},{6,14},... | collective-permute-start | bytes 2359304 | tf_op jit(solution)/shard_map/ppermute | solution.py:77
  100.3 19.0 %collective-permute-start.7 = (bf16[128,2048]{0,1:T(8,128)(2,1)}, bf16[128,2048]{0,1:T(8,128)(2,1)}, u32[]{:S(2)}, u32[]{:S(2)}) collective-permute-start(bf16[128,2048]{0,1:T(8,128)(2,1)} %bitcast.4), channel_id=1, source_target_pairs={{0,4},{4,8},{8,12},{1,5},{5,9},{9,13},{2,6},{6,10},{10,14},{3,7},{... | collective-permute-start | bytes 1572872 | tf_op jit(solution)/shard_map/ppermute | solution.py:19
  103.3 20.6 %collective-permute-start.8 = (bf16[128,2048]{0,1:T(8,128)(2,1)}, bf16[128,2048]{0,1:T(8,128)(2,1)}, u32[]{:S(2)}, u32[]{:S(2)}) collective-permute-start(bf16[128,2048]{0,1:T(8,128)(2,1)} %bitcast.8), channel_id=1, source_target_pairs={{4,0},{8,4},{12,8},{5,1},{9,5},{13,9},{6,2},{10,6},{14,10},{7,3},{... | collective-permute-start | bytes 1572872 | tf_op jit(solution)/shard_map/ppermute | solution.py:19
  105.0 46.2 %collective-permute-start.12 = (bf16[768,512]{1,0:T(8,128)(2,1)}, bf16[768,512]{1,0:T(8,128)(2,1)}, u32[]{:S(2)}, u32[]{:S(2)}) collective-permute-start(bf16[768,512]{1,0:T(8,128)(2,1)} %fusion.35), channel_id=1, source_target_pairs={{0,4},{4,0},{8,12},{12,8},{1,5},{5,1},{9,13},{13,9},{2,6},{6,2},{1... | collective-permute-start | bytes 2359304 | tf_op jit(solution)/shard_map/ppermute | solution.py:77
  111.0 41.7 %collective-permute-start.13 = (bf16[768,512]{1,0:T(8,128)(2,1)}, bf16[768,512]{1,0:T(8,128)(2,1)S(1)}, u32[]{:S(2)}, u32[]{:S(2)}) collective-permute-start(bf16[768,512]{1,0:T(8,128)(2,1)} %collective-permute-done.9), channel_id=1, source_target_pairs={{0,4},{4,0},{8,12},{12,8},{1,5},{5,1},{9,13},{13,9},{2,6},{6,2},{1... | collective-permute-start | bytes 2359304 | tf_op jit(solution)/shard_map/ppermute | solution.py:77
  119.2 33.8 %collective-permute-start.14 = (bf16[768,512]{1,0:T(8,128)(2,1)}, bf16[768,512]{1,0:T(8,128)(2,1)S(1)}, u32[]{:S(2)}, u32[]{:S(2)}) collective-permute-start(bf16[768,512]{1,0:T(8,128)(2,1)} %collective-permute-done.10), channel_id=1, source_target_pairs={{0,4},{4,0},{8,12},{12,8},{1,5},{5,1},{9,13},{13,9},{2,6},{6,2},{1... | collective-permute-start | bytes 2359304 | tf_op jit(solution)/shard_map/ppermute | solution.py:77
  119.3 34.2 %collective-permute-start.15 = (bf16[768,512]{1,0:T(8,128)(2,1)}, bf16[768,512]{1,0:T(8,128)(2,1)S(1)}, u32[]{:S(2)}, u32[]{:S(2)}) collective-permute-start(bf16[768,512]{1,0:T(8,128)(2,1)} %collective-permute-done.11), channel_id=1, source_target_pairs={{0,4},{4,0},{8,12},{12,8},{1,5},{5,1},{9,13},{13,9},{2,6},{6,2},{1... | collective-permute-start | bytes 2359304 | tf_op jit(solution)/shard_map/ppermute | solution.py:77
  155.9 24.7 %all-to-all-start.2 = ((bf16[4,4,128,192]{2,3,1,0:T(8,128)(2,1)}), bf16[4,4,128,192]{2,3,1,0:T(8,128)(2,1)S(1)}, u32[]{:S(2)}, u32[]{:S(2)}) async-start(bf16[4,4,128,192]{2,3,1,0:T(8,128)(2,1)} %bitcast.34), calls=%async_computation.2 | async-start | bytes 1572864 | tf_op jit(solution)/shard_map/all_to_all | solution.py:147
  180.6 23.6 %all-to-all-start = ((bf16[4,4,128,192]{2,3,1,0:T(8,128)(2,1)}), bf16[4,4,128,192]{2,3,1,0:T(8,128)(2,1)S(1)}, u32[]{:S(2)}, u32[]{:S(2)}) async-start(bf16[4,4,128,192]{2,3,1,0:T(8,128)(2,1)} %bitcast.24), calls=%async_computation | async-start | bytes 1572864 | tf_op jit(solution)/shard_map/all_to_all | solution.py:147
  204.2 11.7 %all-to-all-start.3 = ((bf16[4,4,128,64]{2,3,1,0:T(8,128)(2,1)}), bf16[4,4,128,64]{2,3,1,0:T(8,128)(2,1)S(1)}, u32[]{:S(2)}, u32[]{:S(2)}) async-start(bf16[4,4,128,64]{2,3,1,0:T(8,128)(2,1)} %bitcast.157), calls=%async_computation.3 | async-start | bytes 524288 | tf_op jit(solution)/shard_map/all_to_all | solution.py:163
  215.9 13.1 %all-to-all-start.1 = ((bf16[4,4,128,64]{2,3,1,0:T(8,128)(2,1)}), bf16[4,4,128,64]{2,3,1,0:T(8,128)(2,1)S(1)}, u32[]{:S(2)}, u32[]{:S(2)}) async-start(bf16[4,4,128,64]{2,3,1,0:T(8,128)(2,1)} %bitcast.159), calls=%async_computation.1 | async-start | bytes 524288 | tf_op jit(solution)/shard_map/all_to_all | solution.py:163
  241.0 5.8 %collective-permute-start.16 = (f32[4,2,1152]{2,1,0:T(2,128)S(1)}, f32[4,2,1152]{2,1,0:T(2,128)S(1)}, u32[]{:S(2)}, u32[]{:S(2)}) collective-permute-start(f32[4,2,1152]{2,1,0:T(2,128)S(1)} %get-tuple-element.8), channel_id=1, source_target_pairs={{0,1},{1,2},{2,3},{3,0},{4,5},{5,6},{6,7},{7,4},{8,9},{9,10},{10,1... | collective-permute-start | bytes 110600 | tf_op jit(solution)/shard_map/ppermute | solution.py:261
  241.4 5.4 %collective-permute-start.17 = (f32[4,2,1152]{2,1,0:T(2,128)S(1)}, f32[4,2,1152]{2,1,0:T(2,128)S(1)}, u32[]{:S(2)}, u32[]{:S(2)}) collective-permute-start(f32[4,2,1152]{2,1,0:T(2,128)S(1)} %get-tuple-element.10), channel_id=1, source_target_pairs={{0,2},{1,3},{2,0},{3,1},{4,6},{5,7},{6,4},{7,5},{8,10},{9,11},{10,... | collective-permute-start | bytes 110600 | tf_op jit(solution)/shard_map/ppermute | solution.py:261
  (23 other events, 207.0 us)
Sparse Core Ops, SparseCore 0:
  10.4 30.6 all-gather.2
  42.6 27.4 all-gather.4

commit v7 on v6

--- a/solution.py
+++ b/solution.py
@@ -96,6 +96,22 @@
         part = jnp.dot(remote_inputs, block, preferred_element_type=jnp.float32)
         remote = lax.dynamic_update_slice_in_dim(remote, part, piece * width, axis=1)
     return local + remote
+
+
+def assemble(pieces):
+    shard, held, width = pieces
+    remote = jnp.zeros((held[0][1].shape[0], width * len(held)), shard.dtype)
+    for piece, block in held:
+        remote = lax.dynamic_update_slice_in_dim(remote, block, piece * width, axis=1)
+    return shard, remote
+
+
+def project_whole(inputs, weights):
+    shard, remote = weights
+    rows = shard.shape[0]
+    local_inputs = lax.dynamic_slice_in_dim(inputs, lax.axis_index("plane") * rows, rows, axis=1)
+    local = jnp.dot(local_inputs, shard, preferred_element_type=jnp.float32)
+    return local + jnp.dot(rotate_rows(inputs, 1), remote, preferred_element_type=jnp.float32)
 
 
 def attend_items(pieces):
@@ -162,7 +178,7 @@
         )
         returned = lax.all_to_all(homeward, "plane", split_axis=0, concat_axis=1, tiled=True)[0]
         contexts.append(jnp.transpose(returned, (1, 0, 2)).reshape(tok_block, HEADS * HEAD_DIM))
-    return jnp.concatenate(contexts, axis=0)
+    return contexts
 
 
 def body(tokens, counts, region_ids, norm_gains, cross_qkv, cross_out, plane_qkv, plane_out):
@@ -181,6 +197,8 @@
     score_scale = 1.0 / math.sqrt(HEAD_DIM)
     cross_qkv_pieces, cross_out_pieces = gather_pieces([cross_qkv, cross_out])
     plane_qkv_pieces, plane_out_pieces = gather_pieces([plane_qkv, plane_out])
+    cross_out_pieces = assemble(cross_out_pieces)
+    plane_out_pieces = assemble(plane_out_pieces)
     normed = rms_norm(tokens, norm_gains[0])
     inputs = normed.reshape(-1, model_width)
     result = project(inputs, cross_qkv_pieces)
@@ -213,7 +231,7 @@
         "snhqk,snkhd->snqhd", attention, stacked[:, :, :, 1], preferred_element_type=jnp.float32
     )
     context = context.astype(jnp.bfloat16).reshape(-1, model_width)
-    result = project(context, cross_out_pieces)
+    result = project_whole(context, cross_out_pieces)
     after_cross = (tokens.reshape(-1, model_width).astype(jnp.float32) + result).astype(
         jnp.bfloat16
     )
@@ -221,7 +239,7 @@
     result = project(normed, plane_qkv_pieces)
     projected = result.astype(jnp.bfloat16).reshape(sec_block, tok_block, 3, HEADS, HEAD_DIM)
     if HEADS % plane_count == 0:
-        context = attend_by_section(projected, counts, plane_count)
+        contexts = attend_by_section(projected, counts, plane_count)
     else:
         per_device = sec_block * HEADS // plane_count
         heads_first = jnp.transpose(projected, (0, 3, 1, 2, 4)).reshape(
@@ -238,17 +256,29 @@
             )
         )
         returned = lax.all_to_all(attended, "plane", split_axis=2, concat_axis=0, tiled=True)
-        context = jnp.transpose(
-            returned.reshape(sec_block, HEADS, tok_block, HEAD_DIM), (0, 2, 1, 3)
-        ).reshape(-1, model_width)
-    result = project(context, plane_out_pieces)
-    encoded = (after_cross.astype(jnp.float32) + result).astype(jnp.bfloat16)
+        contexts = [
+            jnp.transpose(
+                returned.reshape(sec_block, HEADS, tok_block, HEAD_DIM), (0, 2, 1, 3)
+            ).reshape(-1, model_width)
+        ]
     labels = region_ids.reshape(-1)
     member = (jnp.arange(regions, dtype=jnp.int32)[:, None] == labels[None, :]) & own_valid.reshape(
         -1
     )[None, :]
-    extended = jnp.concatenate([encoded, jnp.ones((encoded.shape[0], 128), jnp.bfloat16)], axis=1)
-    partial = jnp.dot(member.astype(jnp.bfloat16), extended, preferred_element_type=jnp.float32)
+    member = member.astype(jnp.bfloat16)
+    pieces_out = []
+    partial = None
+    row = 0
+    for context in contexts:
+        span = context.shape[0]
+        result = project_whole(context, plane_out_pieces)
+        piece = (after_cross[row : row + span].astype(jnp.float32) + result).astype(jnp.bfloat16)
+        pieces_out.append(piece)
+        extended = jnp.concatenate([piece, jnp.ones((span, 128), jnp.bfloat16)], axis=1)
+        term = jnp.dot(member[:, row : row + span], extended, preferred_element_type=jnp.float32)
+        partial = term if partial is None else partial + term
+        row += span
+    encoded = jnp.concatenate(pieces_out, axis=0)
     sections = lax.axis_size("sec")
     width = partial.shape[1]
     partial = partial.reshape(sections, plane_count, 2, width)

time: 262 us -> 262 us (level)
  local copies, waits for them, and re-layouts: 21.6 us -> 42.1 us
  matrix products: 55.1 us -> 40.9 us
  waiting for transfers between devices: 108 us -> 103 us
  starting transfers between devices: 42.8 us -> 40 us
    dot_general x32 -> x16, matrix products: 35.7 us -> 14.9 us  [project(): part = jnp.dot(remote_inputs, block, preferred_element_type=jnp.float32)]
    dynamic_update_slice x0 -> x16, local copies, waits for them, and re-layouts: none -> 15.4 us  [assemble(): lax.dynamic_update_slice_in_dim(remote, block, piece * width, axis=1)]
    all_gather x2, waiting for transfers between devices: 33.2 us -> 45.7 us  [gather_pieces(): gathered = lax.all_gather(mine, 'plane', axis=0, tiled=True)]
    all_to_all x2, waiting for transfers between devices: 28.9 us -> 21.1 us  [attend_by_section(): lax.all_to_all(outgoing, 'plane', split_axis=0, concat_axis=2, tiled=True)]
    dot_general x1 -> x8, matrix products: 0.2 us -> 6.68 us  [the longest x3 4.69 us: project_whole(): jnp.dot(rotate_rows(inputs, 1), remote, preferred_element_type=jnp.float32)]
    ppermute x14, waiting for transfers between devices: 33.9 us -> 27.9 us  [gather_pieces(): lax.ppermute(block, axis, swap)]
    ppermute x14, starting transfers between devices: 15.6 us -> 12.5 us  [gather_pieces(): lax.ppermute(block, axis, swap)]
    concatenate x6 -> x4, other arithmetic: 6.82 us -> 4.75 us  [rotate_rows(): doubled = jnp.concatenate([values, values], axis=axis)]
  transfers between devices with their start and end apart: 28 -> 28, of which waited for: 13 -> 8; matrix products, arithmetic and copies ran while one was open for 29% -> 34% of each run, Pallas kernels for 0% -> 0%
where the time goes in v7:
time: 262 us; the launch traced here: 260 us
  waiting for transfers between devices  103 us (39%)
  local copies, waits for them, and re-layouts  42.1 us (16%)
  matrix products  40.9 us (16%)
  starting transfers between devices  40 us (15%)
  other arithmetic  18.8 us (7%)
  between operations  15.4 us (6%)
    all_gather x2, waiting for transfers between devices, gather_pieces(): gathered = lax.all_gather(mine, 'plane', axis=0, tiled=True)  45.7 us
    ppermute x14, waiting for transfers between devices, gather_pieces(): lax.ppermute(block, axis, swap)  27.9 us
    all_to_all x2, waiting for transfers between devices, attend_by_section(): lax.all_to_all(outgoing, 'plane', split_axis=0, concat_axis=2, tiled=True)  21.1 us
    dynamic_update_slice x16, local copies, waits for them, and re-layouts, assemble(): lax.dynamic_update_slice_in_dim(remote, block, piece * width, axis=1)  15.4 us
    dot_general x16, matrix products, project(): part = jnp.dot(remote_inputs, block, preferred_element_type=jnp.float32)  14.9 us
    ppermute x14, starting transfers between devices, gather_pieces(): lax.ppermute(block, axis, swap)  12.5 us
    sub x2, matrix products, masked_softmax(): expo = jnp.where(allowed, jnp.exp(shifted - top), 0.0)  8.92 us
    all_to_all x2, starting transfers between devices, attend_by_section(): lax.all_to_all(homeward, 'plane', split_axis=0, concat_axis=1, tiled=True)  8.46 us
  transfers between devices with their start and end apart: 28, of which 8 were waited for; matrix products, arithmetic and copies ran while one was open for 34% of the time, Pallas kernels for 0%

profile of v7, /device:TPU:0, one launch (start us, length us, event | category | flops | bytes accessed | tf_op | source)
XLA Modules:
  0.0 260.4 jit_solution(5784347471574918057)
XLA Ops:
  18.3 22.0 %all-gather.3.cloned.1.call-done = bf16[1024,512]{1,0:T(8,128)(2,1)} async-done(((bf16[256,512]{1,0:T(8,128)(2,1)}), bf16[1024,512]{1,0:T(8,128)(2,1)}) %all-gather.3.cloned.1.call-update) | async-done | bytes 1048592 | tf_op jit(solution)/shard_map/all_gather | solution.py:72
  45.6 23.7 %all-gather.5.cloned.1.call-done = bf16[1024,512]{1,0:T(8,128)(2,1)} async-done(((bf16[256,512]{1,0:T(8,128)(2,1)}), bf16[1024,512]{1,0:T(8,128)(2,1)}) %all-gather.5.cloned.1.call-update) | async-done | bytes 1048592 | tf_op jit(solution)/shard_map/all_gather | solution.py:72
  69.3 2.6 fusion.34
  81.5 27.8 %collective-permute-done.2 = bf16[768,512]{1,0:T(8,128)(2,1)S(1)} collective-permute-done((bf16[768,512]{1,0:T(8,128)(2,1)}, bf16[768,512]{1,0:T(8,128)(2,1)S(1)}, u32[]{:S(2)}, u32[]{:S(2)}) %collective-permute-start.2) | collective-permute-done | bytes 786464 | tf_op jit(solution)/shard_map/ppermute | solution.py:77
  111.3 1.9 convolution_dynamic-update-slice_fusion.11
  120.0 2.9 %collective-permute-start.7 = (bf16[128,2048]{0,1:T(8,128)(2,1)}, bf16[128,2048]{0,1:T(8,128)(2,1)}, u32[]{:S(2)}, u32[]{:S(2)}) collective-permute-start(bf16[128,2048]{0,1:T(8,128)(2,1)} %bitcast.4), channel_id=1, source_target_pairs={{0,4},{4,8},{8,12},{1,5},{5,9},{9,13},{2,6},{6,10},{10,14},{3,7},{... | collective-permute-start | bytes 1572872 | tf_op jit(solution)/shard_map/ppermute | solution.py:19
  135.9 2.3 collective-permute-start.15
  141.2 3.2 %fusion.139 = (f32[2,16,128]{2,1,0:T(8,128)S(1)}, f32[2,16,128,384]{3,2,1,0:T(8,128)S(1)}) fusion(f32[2,16,128,384]{3,2,1,0:T(8,128)S(1)} %fusion.20, pred[2,128,384]{2,1,0:T(8,128)(4,1)S(1)} %copy-done.14), kind=kOutput, calls=%fused_computation.227 | output fusion | flops 11010431 | bytes 12697600 | tf_op jit(solution)/shard_map/sub | solution.py:31
  144.5 1.8 fusion.24
  161.1 3.5 %all-to-all-start = ((bf16[4,4,128,192]{2,3,1,0:T(8,128)(2,1)}), bf16[4,4,128,192]{2,3,1,0:T(8,128)(2,1)S(1)}, u32[]{:S(2)}, u32[]{:S(2)}) async-start(bf16[4,4,128,192]{2,3,1,0:T(8,128)(2,1)} %bitcast.24), calls=%async_computation | async-start | bytes 1572864 | tf_op jit(solution)/shard_map/all_to_all | solution.py:163
  173.2 12.5 %all-to-all-done = bf16[4,4,128,192]{2,3,1,0:T(8,128)(2,1)S(1)} async-done(((bf16[4,4,128,192]{2,3,1,0:T(8,128)(2,1)}), bf16[4,4,128,192]{2,3,1,0:T(8,128)(2,1)S(1)}, u32[]{:S(2)}, u32[]{:S(2)}) %all-to-all-start) | async-done | bytes 786464 | tf_op jit(solution)/shard_map/all_to_all | solution.py:163
  185.8 3.7 %all-to-all-start.2 = ((bf16[4,4,128,192]{2,3,1,0:T(8,128)(2,1)}), bf16[4,4,128,192]{2,3,1,0:T(8,128)(2,1)S(1)}, u32[]{:S(2)}, u32[]{:S(2)}) async-start(bf16[4,4,128,192]{2,3,1,0:T(8,128)(2,1)} %bitcast.156), calls=%async_computation.2 | async-start | bytes 1572864 | tf_op jit(solution)/shard_map/all_to_all | solution.py:163
  193.7 3.9 %fusion.149 = (f32[4,512]{1,0:T(4,128)S(1)}, f32[4,512,512]{1,2,0:T(8,128)}) fusion(pred[512,512]{0,1:T(8,128)(4,1)S(1)} %fusion.33, bf16[4,512,192]{1,2,0:T(8,128)(2,1)S(1)} %squeeze.57), kind=kOutput, calls=%fused_computation.229 | convolution fusion | flops 139461120 | bytes 5251072 | tf_op jit(solution)/shard_map/sub | solution.py:31
  197.6 2.7 %fusion.27 = bf16[4,8,4,8,128]{4,3,2,1,0:T(8,128)(2,1)S(1)} fusion(f32[4,512,512]{1,2,0:T(8,128)} %get-tuple-element.29, f32[4,512]{1,0:T(4,128)S(1)} %get-tuple-element.28, bf16[4,512,192]{1,2,0:T(8,128)(2,1)S(1)} %squeeze.57), kind=kOutput, calls=%fused_computation.67 | convolution fusion | flops 136445952 | bytes 4726784 | tf_op jit(solution)/shard_map/nqk,nkd->nqd/dot_general | solution.py:173
  201.1 8.6 %all-to-all-done.2 = bf16[4,4,128,192]{2,3,1,0:T(8,128)(2,1)S(1)} async-done(((bf16[4,4,128,192]{2,3,1,0:T(8,128)(2,1)}), bf16[4,4,128,192]{2,3,1,0:T(8,128)(2,1)S(1)}, u32[]{:S(2)}, u32[]{:S(2)}) %all-to-all-start.2) | async-done | bytes 786464 | tf_op jit(solution)/shard_map/all_to_all | solution.py:163
  209.6 3.4 %all-to-all-start.1 = ((bf16[4,4,128,64]{2,3,1,0:T(8,128)(2,1)}), bf16[4,4,128,64]{2,3,1,0:T(8,128)(2,1)S(1)}, u32[]{:S(2)}, u32[]{:S(2)}) async-start(bf16[4,4,128,64]{2,3,1,0:T(8,128)(2,1)} %bitcast.147), calls=%async_computation.1 | async-start | bytes 524288 | tf_op jit(solution)/shard_map/all_to_all | solution.py:179
  214.0 5.0 %fusion.140 = (f32[4,512]{1,0:T(4,128)S(1)}, f32[4,512,512]{1,2,0:T(8,128)}) fusion(pred[512,512]{0,1:T(8,128)(4,1)} %fusion.32, bf16[4,512,192]{1,2,0:T(8,128)(2,1)S(1)} %squeeze.60), kind=kOutput, calls=%fused_computation.228 | convolution fusion | flops 139461120 | bytes 5251072 | tf_op jit(solution)/shard_map/sub | solution.py:31
  219.0 2.7 %fusion.28 = bf16[4,8,4,8,128]{4,3,2,1,0:T(8,128)(2,1)S(1)} fusion(f32[4,512,512]{1,2,0:T(8,128)} %get-tuple-element.27, f32[4,512]{1,0:T(4,128)S(1)} %get-tuple-element.26, bf16[4,512,192]{1,2,0:T(8,128)(2,1)S(1)} %squeeze.60), kind=kOutput, calls=%fused_computation.68 | convolution fusion | flops 136445952 | bytes 4726784 | tf_op jit(solution)/shard_map/nqk,nkd->nqd/dot_general | solution.py:173
  222.5 5.1 %all-to-all-start.3 = ((bf16[4,4,128,64]{2,3,1,0:T(8,128)(2,1)}), bf16[4,4,128,64]{2,3,1,0:T(8,128)(2,1)S(1)}, u32[]{:S(2)}, u32[]{:S(2)}) async-start(bf16[4,4,128,64]{2,3,1,0:T(8,128)(2,1)} %bitcast.145), calls=%async_computation.3 | async-start | bytes 524288 | tf_op jit(solution)/shard_map/all_to_all | solution.py:179
  229.6 6.0 %all-to-all-done.3 = bf16[4,4,128,64]{2,3,1,0:T(8,128)(2,1)S(1)} async-done(((bf16[4,4,128,64]{2,3,1,0:T(8,128)(2,1)}), bf16[4,4,128,64]{2,3,1,0:T(8,128)(2,1)S(1)}, u32[]{:S(2)}, u32[]{:S(2)}) %all-to-all-start.3) | async-done | bytes 262176 | tf_op jit(solution)/shard_map/all_to_all | solution.py:179
  236.6 1.8 add_convert_fusion.1
  242.8 2.0 collective-permute-start.18
  244.8 1.9 collective-permute-done.16
  247.4 2.1 collective-permute-start.20
  (194 shorter events, 91.8 us)
Async XLA Ops:
  7.2 33.1 %all-gather.3.cloned.1.call-start = ((), (), s32[]{:S(2)}) async-start(), calls=%async_computation.4 | async-start | bytes 1310720 | tf_op jit(solution)/shard_map/all_gather | solution.py:72
  9.4 59.9 %all-gather.5.cloned.1.call-start = ((), (), s32[]{:S(2)}) async-start(), calls=%async_computation.5 | async-start | bytes 1310720 | tf_op jit(solution)/shard_map/all_gather | solution.py:72
  42.0 33.9 %collective-permute-start = (bf16[768,512]{1,0:T(8,128)(2,1)S(1)}, bf16[768,512]{1,0:T(8,128)(2,1)}, u32[]{:S(2)}, u32[]{:S(2)}) collective-permute-start(bf16[768,512]{1,0:T(8,128)(2,1)S(1)} %fusion.35), channel_id=1, source_target_pairs={{0,16},{16,0},{1,17},{17,1},{2,18},{18,2},{3,19},{19,3},{4,20},{20... | collective-permute-start | bytes 2359304 | tf_op jit(solution)/shard_map/ppermute | solution.py:77
  44.1 34.9 %collective-permute-start.1 = (bf16[768,512]{1,0:T(8,128)(2,1)S(1)}, bf16[768,512]{1,0:T(8,128)(2,1)}, u32[]{:S(2)}, u32[]{:S(2)}) collective-permute-start(bf16[768,512]{1,0:T(8,128)(2,1)S(1)} %fusion.35), channel_id=1, source_target_pairs={{0,8},{4,12},{8,0},{12,4},{1,9},{5,13},{9,1},{13,5},{2,10},{6,14},... | collective-permute-start | bytes 2359304 | tf_op jit(solution)/shard_map/ppermute | solution.py:77
  45.6 64.1 %collective-permute-start.3 = (bf16[768,512]{1,0:T(8,128)(2,1)S(1)}, bf16[768,512]{1,0:T(8,128)(2,1)}, u32[]{:S(2)}, u32[]{:S(2)}) collective-permute-start(bf16[768,512]{1,0:T(8,128)(2,1)S(1)} %fusion.35), channel_id=1, source_target_pairs={{0,4},{4,0},{8,12},{12,8},{1,5},{5,1},{9,13},{13,9},{2,6},{6,2},{1... | collective-permute-start | bytes 2359304 | tf_op jit(solution)/shard_map/ppermute | solution.py:77
  71.9 41.3 %collective-permute-start.9 = (bf16[768,512]{1,0:T(8,128)(2,1)}, bf16[768,512]{1,0:T(8,128)(2,1)}, u32[]{:S(2)}, u32[]{:S(2)}) collective-permute-start(bf16[768,512]{1,0:T(8,128)(2,1)} %fusion.34), channel_id=1, source_target_pairs={{0,16},{16,0},{1,17},{17,1},{2,18},{18,2},{3,19},{19,3},{4,20},{20... | collective-permute-start | bytes 2359304 | tf_op jit(solution)/shard_map/ppermute | solution.py:77
  73.4 61.3 %collective-permute-start.10 = (bf16[768,512]{1,0:T(8,128)(2,1)}, bf16[768,512]{1,0:T(8,128)(2,1)}, u32[]{:S(2)}, u32[]{:S(2)}) collective-permute-start(bf16[768,512]{1,0:T(8,128)(2,1)} %fusion.34), channel_id=1, source_target_pairs={{0,8},{4,12},{8,0},{12,4},{1,9},{5,13},{9,1},{13,5},{2,10},{6,14},... | collective-permute-start | bytes 2359304 | tf_op jit(solution)/shard_map/ppermute | solution.py:77
  75.8 33.4 %collective-permute-start.2 = (bf16[768,512]{1,0:T(8,128)(2,1)}, bf16[768,512]{1,0:T(8,128)(2,1)S(1)}, u32[]{:S(2)}, u32[]{:S(2)}) collective-permute-start(bf16[768,512]{1,0:T(8,128)(2,1)} %collective-permute-done), channel_id=1, source_target_pairs={{0,8},{4,12},{8,0},{12,4},{1,9},{5,13},{9,1},{13,5},{2,10},{6,14},... | collective-permute-start | bytes 2359304 | tf_op jit(solution)/shard_map/ppermute | solution.py:77
  78.9 34.3 %collective-permute-start.4 = (bf16[768,512]{1,0:T(8,128)(2,1)}, bf16[768,512]{1,0:T(8,128)(2,1)S(1)}, u32[]{:S(2)}, u32[]{:S(2)}) collective-permute-start(bf16[768,512]{1,0:T(8,128)(2,1)} %collective-permute-done), channel_id=1, source_target_pairs={{0,4},{4,0},{8,12},{12,8},{1,5},{5,1},{9,13},{13,9},{2,6},{6,2},{1... | collective-permute-start | bytes 2359304 | tf_op jit(solution)/shard_map/ppermute | solution.py:77
  109.3 5.9 %collective-permute-start.5 = (bf16[768,512]{1,0:T(8,128)(2,1)}, bf16[768,512]{1,0:T(8,128)(2,1)S(1)}, u32[]{:S(2)}, u32[]{:S(2)}) collective-permute-start(bf16[768,512]{1,0:T(8,128)(2,1)} %collective-permute-done.1), channel_id=1, source_target_pairs={{0,4},{4,0},{8,12},{12,8},{1,5},{5,1},{9,13},{13,9},{2,6},{6,2},{1... | collective-permute-start | bytes 2359304 | tf_op jit(solution)/shard_map/ppermute | solution.py:77
  109.8 5.8 %collective-permute-start.6 = (bf16[768,512]{1,0:T(8,128)(2,1)S(1)}, bf16[768,512]{1,0:T(8,128)(2,1)S(1)}, u32[]{:S(2)}, u32[]{:S(2)}) collective-permute-start(bf16[768,512]{1,0:T(8,128)(2,1)S(1)} %collective-permute-done.2), channel_id=1, source_target_pairs={{0,4},{4,0},{8,12},{12,8},{1,5},{5,1},{9,13},{13,9},{2,6},{6,2},{1... | collective-permute-start | bytes 2359304 | tf_op jit(solution)/shard_map/ppermute | solution.py:77
  113.2 42.2 %collective-permute-start.12 = (bf16[768,512]{1,0:T(8,128)(2,1)}, bf16[768,512]{1,0:T(8,128)(2,1)}, u32[]{:S(2)}, u32[]{:S(2)}) collective-permute-start(bf16[768,512]{1,0:T(8,128)(2,1)} %fusion.34), channel_id=1, source_target_pairs={{0,4},{4,0},{8,12},{12,8},{1,5},{5,1},{9,13},{13,9},{2,6},{6,2},{1... | collective-permute-start | bytes 2359304 | tf_op jit(solution)/shard_map/ppermute | solution.py:77
  113.3 22.6 %collective-permute-start.11 = (bf16[768,512]{1,0:T(8,128)(2,1)}, bf16[768,512]{1,0:T(8,128)(2,1)}, u32[]{:S(2)}, u32[]{:S(2)}) collective-permute-start(bf16[768,512]{1,0:T(8,128)(2,1)} %collective-permute-done.9), channel_id=1, source_target_pairs={{0,8},{4,12},{8,0},{12,4},{1,9},{5,13},{9,1},{13,5},{2,10},{6,14},... | collective-permute-start | bytes 2359304 | tf_op jit(solution)/shard_map/ppermute | solution.py:77
  120.0 15.9 %collective-permute-start.7 = (bf16[128,2048]{0,1:T(8,128)(2,1)}, bf16[128,2048]{0,1:T(8,128)(2,1)}, u32[]{:S(2)}, u32[]{:S(2)}) collective-permute-start(bf16[128,2048]{0,1:T(8,128)(2,1)} %bitcast.4), channel_id=1, source_target_pairs={{0,4},{4,8},{8,12},{1,5},{5,9},{9,13},{2,6},{6,10},{10,14},{3,7},{... | collective-permute-start | bytes 1572872 | tf_op jit(solution)/shard_map/ppermute | solution.py:19
  124.0 14.3 %collective-permute-start.8 = (bf16[128,2048]{0,1:T(8,128)(2,1)}, bf16[128,2048]{0,1:T(8,128)(2,1)}, u32[]{:S(2)}, u32[]{:S(2)}) collective-permute-start(bf16[128,2048]{0,1:T(8,128)(2,1)} %bitcast.8), channel_id=1, source_target_pairs={{4,0},{8,4},{12,8},{5,1},{9,5},{13,9},{6,2},{10,6},{14,10},{7,3},{... | collective-permute-start | bytes 1572872 | tf_op jit(solution)/shard_map/ppermute | solution.py:19
  134.7 22.2 %collective-permute-start.13 = (bf16[768,512]{1,0:T(8,128)(2,1)}, bf16[768,512]{1,0:T(8,128)(2,1)S(1)}, u32[]{:S(2)}, u32[]{:S(2)}) collective-permute-start(bf16[768,512]{1,0:T(8,128)(2,1)} %collective-permute-done.9), channel_id=1, source_target_pairs={{0,4},{4,0},{8,12},{12,8},{1,5},{5,1},{9,13},{13,9},{2,6},{6,2},{1... | collective-permute-start | bytes 2359304 | tf_op jit(solution)/shard_map/ppermute | solution.py:77
  135.9 21.4 %collective-permute-start.14 = (bf16[768,512]{1,0:T(8,128)(2,1)}, bf16[768,512]{1,0:T(8,128)(2,1)S(1)}, u32[]{:S(2)}, u32[]{:S(2)}) collective-permute-start(bf16[768,512]{1,0:T(8,128)(2,1)} %collective-permute-done.10), channel_id=1, source_target_pairs={{0,4},{4,0},{8,12},{12,8},{1,5},{5,1},{9,13},{13,9},{2,6},{6,2},{1... | collective-permute-start | bytes 2359304 | tf_op jit(solution)/shard_map/ppermute | solution.py:77
  135.9 21.7 %collective-permute-start.15 = (bf16[768,512]{1,0:T(8,128)(2,1)}, bf16[768,512]{1,0:T(8,128)(2,1)S(1)}, u32[]{:S(2)}, u32[]{:S(2)}) collective-permute-start(bf16[768,512]{1,0:T(8,128)(2,1)} %collective-permute-done.11), channel_id=1, source_target_pairs={{0,4},{4,0},{8,12},{12,8},{1,5},{5,1},{9,13},{13,9},{2,6},{6,2},{1... | collective-permute-start | bytes 2359304 | tf_op jit(solution)/shard_map/ppermute | solution.py:77
  161.1 24.7 %all-to-all-start = ((bf16[4,4,128,192]{2,3,1,0:T(8,128)(2,1)}), bf16[4,4,128,192]{2,3,1,0:T(8,128)(2,1)S(1)}, u32[]{:S(2)}, u32[]{:S(2)}) async-start(bf16[4,4,128,192]{2,3,1,0:T(8,128)(2,1)} %bitcast.24), calls=%async_computation | async-start | bytes 1572864 | tf_op jit(solution)/shard_map/all_to_all | solution.py:163
  185.8 23.9 %all-to-all-start.2 = ((bf16[4,4,128,192]{2,3,1,0:T(8,128)(2,1)}), bf16[4,4,128,192]{2,3,1,0:T(8,128)(2,1)S(1)}, u32[]{:S(2)}, u32[]{:S(2)}) async-start(bf16[4,4,128,192]{2,3,1,0:T(8,128)(2,1)} %bitcast.156), calls=%async_computation.2 | async-start | bytes 1572864 | tf_op jit(solution)/shard_map/all_to_all | solution.py:163
  209.6 12.8 %all-to-all-start.1 = ((bf16[4,4,128,64]{2,3,1,0:T(8,128)(2,1)}), bf16[4,4,128,64]{2,3,1,0:T(8,128)(2,1)S(1)}, u32[]{:S(2)}, u32[]{:S(2)}) async-start(bf16[4,4,128,64]{2,3,1,0:T(8,128)(2,1)} %bitcast.147), calls=%async_computation.1 | async-start | bytes 524288 | tf_op jit(solution)/shard_map/all_to_all | solution.py:179
  222.5 13.1 %all-to-all-start.3 = ((bf16[4,4,128,64]{2,3,1,0:T(8,128)(2,1)}), bf16[4,4,128,64]{2,3,1,0:T(8,128)(2,1)S(1)}, u32[]{:S(2)}, u32[]{:S(2)}) async-start(bf16[4,4,128,64]{2,3,1,0:T(8,128)(2,1)} %bitcast.145), calls=%async_computation.3 | async-start | bytes 524288 | tf_op jit(solution)/shard_map/all_to_all | solution.py:179
  240.9 5.8 %collective-permute-start.16 = (f32[4,2,1152]{2,1,0:T(2,128)S(1)}, f32[4,2,1152]{2,1,0:T(2,128)S(1)}, u32[]{:S(2)}, u32[]{:S(2)}) collective-permute-start(f32[4,2,1152]{2,1,0:T(2,128)S(1)} %get-tuple-element.8), channel_id=1, source_target_pairs={{0,1},{1,2},{2,3},{3,0},{4,5},{5,6},{6,7},{7,4},{8,9},{9,10},{10,1... | collective-permute-start | bytes 110600 | tf_op jit(solution)/shard_map/ppermute | solution.py:291
  241.3 5.5 %collective-permute-start.17 = (f32[4,2,1152]{2,1,0:T(2,128)S(1)}, f32[4,2,1152]{2,1,0:T(2,128)S(1)}, u32[]{:S(2)}, u32[]{:S(2)}) collective-permute-start(f32[4,2,1152]{2,1,0:T(2,128)S(1)} %get-tuple-element.10), channel_id=1, source_target_pairs={{0,2},{1,3},{2,0},{3,1},{4,6},{5,7},{6,4},{7,5},{8,10},{9,11},{10,... | collective-permute-start | bytes 110600 | tf_op jit(solution)/shard_map/ppermute | solution.py:291
  (27 other events, 196.8 us)
Sparse Core Ops, SparseCore 0:
  9.6 30.6 all-gather.2
  41.8 27.4 all-gather.4

commit v8 on v7

--- a/solution.py
+++ b/solution.py
@@ -55,8 +55,10 @@
     return lax.dynamic_slice_in_dim(doubled, start, (plane_count - 1) * block, axis=axis)
 
 
-def gather_pieces(shards):
+def gather_pieces(shards, swap_first=False):
     levels = replica_levels()
+    if swap_first and len(levels) == 3:
+        levels = [levels[1], levels[0], levels[2]]
     count = 2 ** len(levels)
     widths = [shard.shape[1] // count for shard in shards]
     own = 0
@@ -195,7 +197,7 @@
     near_valid = positions[None, :] < near_counts[:, None]
     own_valid = near_valid[1 : sec_block + 1]
     score_scale = 1.0 / math.sqrt(HEAD_DIM)
-    cross_qkv_pieces, cross_out_pieces = gather_pieces([cross_qkv, cross_out])
+    cross_qkv_pieces, cross_out_pieces = gather_pieces([cross_qkv, cross_out], swap_first=True)
     plane_qkv_pieces, plane_out_pieces = gather_pieces([plane_qkv, plane_out])
     cross_out_pieces = assemble(cross_out_pieces)
     plane_out_pieces = assemble(plane_out_pieces)

time: 262 us -> 261 us (level)
  no operation moved by 1% of the time
where the time goes in v8:
time: 261 us; the launch traced here: 259 us
  waiting for transfers between devices  103 us (39%)
  local copies, waits for them, and re-layouts  42 us (16%)
  matrix products  40.9 us (16%)
  starting transfers between devices  40 us (15%)
  other arithmetic  17.8 us (7%)
  between operations  15.7 us (6%)
    all_gather x2, waiting for transfers between devices, gather_pieces(): gathered = lax.all_gather(mine, 'plane', axis=0, tiled=True)  46.3 us
    ppermute x14, waiting for transfers between devices, gather_pieces(): lax.ppermute(block, axis, swap)  26.7 us
    all_to_all x2, waiting for transfers between devices, attend_by_section(): lax.all_to_all(outgoing, 'plane', split_axis=0, concat_axis=2, tiled=True)  21.1 us
    dynamic_update_slice x16, local copies, waits for them, and re-layouts, assemble(): lax.dynamic_update_slice_in_dim(remote, block, piece * width, axis=1)  15.4 us
    dot_general x16, matrix products, project(): part = jnp.dot(remote_inputs, block, preferred_element_type=jnp.float32)  14.9 us
    ppermute x14, starting transfers between devices, gather_pieces(): lax.ppermute(block, axis, swap)  12.5 us
    sub x2, matrix products, masked_softmax(): expo = jnp.where(allowed, jnp.exp(shifted - top), 0.0)  8.92 us
    all_to_all x2, starting transfers between devices, attend_by_section(): lax.all_to_all(homeward, 'plane', split_axis=0, concat_axis=1, tiled=True)  8.46 us
  transfers between devices with their start and end apart: 28, of which 8 were waited for; matrix products, arithmetic and copies ran while one was open for 34% of the time, Pallas kernels for 0%

profile of v8, /device:TPU:0, one launch (start us, length us, event | category | flops | bytes accessed | tf_op | source)
XLA Modules:
  0.0 259.2 jit_solution(1411169510151707761)
XLA Ops:
  17.3 23.0 %all-gather.3.cloned.1.call-done = bf16[1024,512]{1,0:T(8,128)(2,1)} async-done(((bf16[256,512]{1,0:T(8,128)(2,1)}), bf16[1024,512]{1,0:T(8,128)(2,1)}) %all-gather.3.cloned.1.call-update) | async-done | bytes 1048592 | tf_op jit(solution)/shard_map/all_gather | solution.py:74
  46.0 23.3 %all-gather.5.cloned.1.call-done = bf16[1024,512]{1,0:T(8,128)(2,1)} async-done(((bf16[256,512]{1,0:T(8,128)(2,1)}), bf16[1024,512]{1,0:T(8,128)(2,1)}) %all-gather.5.cloned.1.call-update) | async-done | bytes 1048592 | tf_op jit(solution)/shard_map/all_gather | solution.py:74
  69.3 2.6 %fusion.34 = bf16[768,512]{1,0:T(8,128)(2,1)} fusion(s32[]{:T(128)S(6)} %select_n.299, bf16[1024,512]{1,0:T(8,128)(2,1)} %all-gather.5.cloned.1.call-done), kind=kLoop, calls=%fused_computation.85 | loop fusion | flops 1572864 | bytes 1835012 | tf_op jit(solution)/shard_map/concatenate | solution.py:54
  81.5 26.6 %collective-permute-done.2 = bf16[768,512]{1,0:T(8,128)(2,1)S(1)} collective-permute-done((bf16[768,512]{1,0:T(8,128)(2,1)}, bf16[768,512]{1,0:T(8,128)(2,1)S(1)}, u32[]{:S(2)}, u32[]{:S(2)}) %collective-permute-start.2) | collective-permute-done | bytes 786464 | tf_op jit(solution)/shard_map/ppermute | solution.py:79
  110.1 1.9 convolution_dynamic-update-slice_fusion.11
  118.8 2.9 %collective-permute-start.7 = (bf16[128,2048]{0,1:T(8,128)(2,1)}, bf16[128,2048]{0,1:T(8,128)(2,1)}, u32[]{:S(2)}, u32[]{:S(2)}) collective-permute-start(bf16[128,2048]{0,1:T(8,128)(2,1)} %bitcast.4), channel_id=1, source_target_pairs={{0,4},{4,8},{8,12},{1,5},{5,9},{9,13},{2,6},{6,10},{10,14},{3,7},{... | collective-permute-start | bytes 1572872 | tf_op jit(solution)/shard_map/ppermute | solution.py:19
  134.8 2.3 collective-permute-start.15
  140.0 3.2 %fusion.139 = (f32[2,16,128]{2,1,0:T(8,128)S(1)}, f32[2,16,128,384]{3,2,1,0:T(8,128)S(1)}) fusion(f32[2,16,128,384]{3,2,1,0:T(8,128)S(1)} %fusion.20, pred[2,128,384]{2,1,0:T(8,128)(4,1)S(1)} %copy-done.14), kind=kOutput, calls=%fused_computation.227 | output fusion | flops 11010431 | bytes 12697600 | tf_op jit(solution)/shard_map/sub | solution.py:31
  143.3 1.8 fusion.24
  159.9 3.5 %all-to-all-start = ((bf16[4,4,128,192]{2,3,1,0:T(8,128)(2,1)}), bf16[4,4,128,192]{2,3,1,0:T(8,128)(2,1)S(1)}, u32[]{:S(2)}, u32[]{:S(2)}) async-start(bf16[4,4,128,192]{2,3,1,0:T(8,128)(2,1)} %bitcast.24), calls=%async_computation | async-start | bytes 1572864 | tf_op jit(solution)/shard_map/all_to_all | solution.py:165
  172.1 12.5 %all-to-all-done = bf16[4,4,128,192]{2,3,1,0:T(8,128)(2,1)S(1)} async-done(((bf16[4,4,128,192]{2,3,1,0:T(8,128)(2,1)}), bf16[4,4,128,192]{2,3,1,0:T(8,128)(2,1)S(1)}, u32[]{:S(2)}, u32[]{:S(2)}) %all-to-all-start) | async-done | bytes 786464 | tf_op jit(solution)/shard_map/all_to_all | solution.py:165
  184.6 3.7 %all-to-all-start.2 = ((bf16[4,4,128,192]{2,3,1,0:T(8,128)(2,1)}), bf16[4,4,128,192]{2,3,1,0:T(8,128)(2,1)S(1)}, u32[]{:S(2)}, u32[]{:S(2)}) async-start(bf16[4,4,128,192]{2,3,1,0:T(8,128)(2,1)} %bitcast.156), calls=%async_computation.2 | async-start | bytes 1572864 | tf_op jit(solution)/shard_map/all_to_all | solution.py:165
  192.5 3.9 %fusion.149 = (f32[4,512]{1,0:T(4,128)S(1)}, f32[4,512,512]{1,2,0:T(8,128)}) fusion(pred[512,512]{0,1:T(8,128)(4,1)S(1)} %fusion.33, bf16[4,512,192]{1,2,0:T(8,128)(2,1)S(1)} %squeeze.57), kind=kOutput, calls=%fused_computation.229 | convolution fusion | flops 139461120 | bytes 5251072 | tf_op jit(solution)/shard_map/sub | solution.py:31
  196.4 2.7 %fusion.27 = bf16[4,8,4,8,128]{4,3,2,1,0:T(8,128)(2,1)S(1)} fusion(f32[4,512,512]{1,2,0:T(8,128)} %get-tuple-element.29, f32[4,512]{1,0:T(4,128)S(1)} %get-tuple-element.28, bf16[4,512,192]{1,2,0:T(8,128)(2,1)S(1)} %squeeze.57), kind=kOutput, calls=%fused_computation.67 | convolution fusion | flops 136445952 | bytes 4726784 | tf_op jit(solution)/shard_map/nqk,nkd->nqd/dot_general | solution.py:175
  199.9 8.6 %all-to-all-done.2 = bf16[4,4,128,192]{2,3,1,0:T(8,128)(2,1)S(1)} async-done(((bf16[4,4,128,192]{2,3,1,0:T(8,128)(2,1)}), bf16[4,4,128,192]{2,3,1,0:T(8,128)(2,1)S(1)}, u32[]{:S(2)}, u32[]{:S(2)}) %all-to-all-start.2) | async-done | bytes 786464 | tf_op jit(solution)/shard_map/all_to_all | solution.py:165
  208.5 3.4 %all-to-all-start.1 = ((bf16[4,4,128,64]{2,3,1,0:T(8,128)(2,1)}), bf16[4,4,128,64]{2,3,1,0:T(8,128)(2,1)S(1)}, u32[]{:S(2)}, u32[]{:S(2)}) async-start(bf16[4,4,128,64]{2,3,1,0:T(8,128)(2,1)} %bitcast.147), calls=%async_computation.1 | async-start | bytes 524288 | tf_op jit(solution)/shard_map/all_to_all | solution.py:181
  212.8 5.0 %fusion.140 = (f32[4,512]{1,0:T(4,128)S(1)}, f32[4,512,512]{1,2,0:T(8,128)}) fusion(pred[512,512]{0,1:T(8,128)(4,1)} %fusion.32, bf16[4,512,192]{1,2,0:T(8,128)(2,1)S(1)} %squeeze.60), kind=kOutput, calls=%fused_computation.228 | convolution fusion | flops 139461120 | bytes 5251072 | tf_op jit(solution)/shard_map/sub | solution.py:31
  217.8 2.7 %fusion.28 = bf16[4,8,4,8,128]{4,3,2,1,0:T(8,128)(2,1)S(1)} fusion(f32[4,512,512]{1,2,0:T(8,128)} %get-tuple-element.27, f32[4,512]{1,0:T(4,128)S(1)} %get-tuple-element.26, bf16[4,512,192]{1,2,0:T(8,128)(2,1)S(1)} %squeeze.60), kind=kOutput, calls=%fused_computation.68 | convolution fusion | flops 136445952 | bytes 4726784 | tf_op jit(solution)/shard_map/nqk,nkd->nqd/dot_general | solution.py:175
  221.3 5.1 %all-to-all-start.3 = ((bf16[4,4,128,64]{2,3,1,0:T(8,128)(2,1)}), bf16[4,4,128,64]{2,3,1,0:T(8,128)(2,1)S(1)}, u32[]{:S(2)}, u32[]{:S(2)}) async-start(bf16[4,4,128,64]{2,3,1,0:T(8,128)(2,1)} %bitcast.145), calls=%async_computation.3 | async-start | bytes 524288 | tf_op jit(solution)/shard_map/all_to_all | solution.py:181
  228.4 6.0 %all-to-all-done.3 = bf16[4,4,128,64]{2,3,1,0:T(8,128)(2,1)S(1)} async-done(((bf16[4,4,128,64]{2,3,1,0:T(8,128)(2,1)}), bf16[4,4,128,64]{2,3,1,0:T(8,128)(2,1)S(1)}, u32[]{:S(2)}, u32[]{:S(2)}) %all-to-all-start.3) | async-done | bytes 262176 | tf_op jit(solution)/shard_map/all_to_all | solution.py:181
  235.4 1.8 add_convert_fusion.1
  241.6 2.0 collective-permute-start.18
  243.6 1.9 collective-permute-done.16
  246.2 2.1 collective-permute-start.20
  (194 shorter events, 90.8 us)
Async XLA Ops:
  7.2 33.1 %all-gather.3.cloned.1.call-start = ((), (), s32[]{:S(2)}) async-start(), calls=%async_computation.4 | async-start | bytes 1310720 | tf_op jit(solution)/shard_map/all_gather | solution.py:74
  9.4 59.9 %all-gather.5.cloned.1.call-start = ((), (), s32[]{:S(2)}) async-start(), calls=%async_computation.5 | async-start | bytes 1310720 | tf_op jit(solution)/shard_map/all_gather | solution.py:74
  42.0 33.9 %collective-permute-start = (bf16[768,512]{1,0:T(8,128)(2,1)S(1)}, bf16[768,512]{1,0:T(8,128)(2,1)}, u32[]{:S(2)}, u32[]{:S(2)}) collective-permute-start(bf16[768,512]{1,0:T(8,128)(2,1)S(1)} %fusion.35), channel_id=1, source_target_pairs={{0,8},{4,12},{8,0},{12,4},{1,9},{5,13},{9,1},{13,5},{2,10},{6,14},... | collective-permute-start | bytes 2359304 | tf_op jit(solution)/shard_map/ppermute | solution.py:79
  44.4 34.5 %collective-permute-start.1 = (bf16[768,512]{1,0:T(8,128)(2,1)S(1)}, bf16[768,512]{1,0:T(8,128)(2,1)}, u32[]{:S(2)}, u32[]{:S(2)}) collective-permute-start(bf16[768,512]{1,0:T(8,128)(2,1)S(1)} %fusion.35), channel_id=1, source_target_pairs={{0,16},{16,0},{1,17},{17,1},{2,18},{18,2},{3,19},{19,3},{4,20},{20... | collective-permute-start | bytes 2359304 | tf_op jit(solution)/shard_map/ppermute | solution.py:79
  46.0 62.6 %collective-permute-start.3 = (bf16[768,512]{1,0:T(8,128)(2,1)S(1)}, bf16[768,512]{1,0:T(8,128)(2,1)}, u32[]{:S(2)}, u32[]{:S(2)}) collective-permute-start(bf16[768,512]{1,0:T(8,128)(2,1)S(1)} %fusion.35), channel_id=1, source_target_pairs={{0,4},{4,0},{8,12},{12,8},{1,5},{5,1},{9,13},{13,9},{2,6},{6,2},{1... | collective-permute-start | bytes 2359304 | tf_op jit(solution)/shard_map/ppermute | solution.py:79
  71.9 40.1 %collective-permute-start.9 = (bf16[768,512]{1,0:T(8,128)(2,1)}, bf16[768,512]{1,0:T(8,128)(2,1)}, u32[]{:S(2)}, u32[]{:S(2)}) collective-permute-start(bf16[768,512]{1,0:T(8,128)(2,1)} %fusion.34), channel_id=1, source_target_pairs={{0,16},{16,0},{1,17},{17,1},{2,18},{18,2},{3,19},{19,3},{4,20},{20... | collective-permute-start | bytes 2359304 | tf_op jit(solution)/shard_map/ppermute | solution.py:79
  73.4 60.1 %collective-permute-start.10 = (bf16[768,512]{1,0:T(8,128)(2,1)}, bf16[768,512]{1,0:T(8,128)(2,1)}, u32[]{:S(2)}, u32[]{:S(2)}) collective-permute-start(bf16[768,512]{1,0:T(8,128)(2,1)} %fusion.34), channel_id=1, source_target_pairs={{0,8},{4,12},{8,0},{12,4},{1,9},{5,13},{9,1},{13,5},{2,10},{6,14},... | collective-permute-start | bytes 2359304 | tf_op jit(solution)/shard_map/ppermute | solution.py:79
  75.8 32.3 %collective-permute-start.2 = (bf16[768,512]{1,0:T(8,128)(2,1)}, bf16[768,512]{1,0:T(8,128)(2,1)S(1)}, u32[]{:S(2)}, u32[]{:S(2)}) collective-permute-start(bf16[768,512]{1,0:T(8,128)(2,1)} %collective-permute-done), channel_id=1, source_target_pairs={{0,16},{16,0},{1,17},{17,1},{2,18},{18,2},{3,19},{19,3},{4,20},{20... | collective-permute-start | bytes 2359304 | tf_op jit(solution)/shard_map/ppermute | solution.py:79
  78.9 33.2 %collective-permute-start.4 = (bf16[768,512]{1,0:T(8,128)(2,1)}, bf16[768,512]{1,0:T(8,128)(2,1)S(1)}, u32[]{:S(2)}, u32[]{:S(2)}) collective-permute-start(bf16[768,512]{1,0:T(8,128)(2,1)} %collective-permute-done), channel_id=1, source_target_pairs={{0,4},{4,0},{8,12},{12,8},{1,5},{5,1},{9,13},{13,9},{2,6},{6,2},{1... | collective-permute-start | bytes 2359304 | tf_op jit(solution)/shard_map/ppermute | solution.py:79
  108.1 5.9 %collective-permute-start.5 = (bf16[768,512]{1,0:T(8,128)(2,1)}, bf16[768,512]{1,0:T(8,128)(2,1)S(1)}, u32[]{:S(2)}, u32[]{:S(2)}) collective-permute-start(bf16[768,512]{1,0:T(8,128)(2,1)} %collective-permute-done.1), channel_id=1, source_target_pairs={{0,4},{4,0},{8,12},{12,8},{1,5},{5,1},{9,13},{13,9},{2,6},{6,2},{1... | collective-permute-start | bytes 2359304 | tf_op jit(solution)/shard_map/ppermute | solution.py:79
  108.6 5.8 %collective-permute-start.6 = (bf16[768,512]{1,0:T(8,128)(2,1)S(1)}, bf16[768,512]{1,0:T(8,128)(2,1)S(1)}, u32[]{:S(2)}, u32[]{:S(2)}) collective-permute-start(bf16[768,512]{1,0:T(8,128)(2,1)S(1)} %collective-permute-done.2), channel_id=1, source_target_pairs={{0,4},{4,0},{8,12},{12,8},{1,5},{5,1},{9,13},{13,9},{2,6},{6,2},{1... | collective-permute-start | bytes 2359304 | tf_op jit(solution)/shard_map/ppermute | solution.py:79
  112.0 42.2 %collective-permute-start.12 = (bf16[768,512]{1,0:T(8,128)(2,1)}, bf16[768,512]{1,0:T(8,128)(2,1)}, u32[]{:S(2)}, u32[]{:S(2)}) collective-permute-start(bf16[768,512]{1,0:T(8,128)(2,1)} %fusion.34), channel_id=1, source_target_pairs={{0,4},{4,0},{8,12},{12,8},{1,5},{5,1},{9,13},{13,9},{2,6},{6,2},{1... | collective-permute-start | bytes 2359304 | tf_op jit(solution)/shard_map/ppermute | solution.py:79
  112.1 22.6 %collective-permute-start.11 = (bf16[768,512]{1,0:T(8,128)(2,1)}, bf16[768,512]{1,0:T(8,128)(2,1)}, u32[]{:S(2)}, u32[]{:S(2)}) collective-permute-start(bf16[768,512]{1,0:T(8,128)(2,1)} %collective-permute-done.9), channel_id=1, source_target_pairs={{0,8},{4,12},{8,0},{12,4},{1,9},{5,13},{9,1},{13,5},{2,10},{6,14},... | collective-permute-start | bytes 2359304 | tf_op jit(solution)/shard_map/ppermute | solution.py:79
  118.8 15.9 %collective-permute-start.7 = (bf16[128,2048]{0,1:T(8,128)(2,1)}, bf16[128,2048]{0,1:T(8,128)(2,1)}, u32[]{:S(2)}, u32[]{:S(2)}) collective-permute-start(bf16[128,2048]{0,1:T(8,128)(2,1)} %bitcast.4), channel_id=1, source_target_pairs={{0,4},{4,8},{8,12},{1,5},{5,9},{9,13},{2,6},{6,10},{10,14},{3,7},{... | collective-permute-start | bytes 1572872 | tf_op jit(solution)/shard_map/ppermute | solution.py:19
  122.8 14.3 %collective-permute-start.8 = (bf16[128,2048]{0,1:T(8,128)(2,1)}, bf16[128,2048]{0,1:T(8,128)(2,1)}, u32[]{:S(2)}, u32[]{:S(2)}) collective-permute-start(bf16[128,2048]{0,1:T(8,128)(2,1)} %bitcast.8), channel_id=1, source_target_pairs={{4,0},{8,4},{12,8},{5,1},{9,5},{13,9},{6,2},{10,6},{14,10},{7,3},{... | collective-permute-start | bytes 1572872 | tf_op jit(solution)/shard_map/ppermute | solution.py:19
  133.5 22.1 %collective-permute-start.13 = (bf16[768,512]{1,0:T(8,128)(2,1)}, bf16[768,512]{1,0:T(8,128)(2,1)S(1)}, u32[]{:S(2)}, u32[]{:S(2)}) collective-permute-start(bf16[768,512]{1,0:T(8,128)(2,1)} %collective-permute-done.9), channel_id=1, source_target_pairs={{0,4},{4,0},{8,12},{12,8},{1,5},{5,1},{9,13},{13,9},{2,6},{6,2},{1... | collective-permute-start | bytes 2359304 | tf_op jit(solution)/shard_map/ppermute | solution.py:79
  134.7 21.4 %collective-permute-start.14 = (bf16[768,512]{1,0:T(8,128)(2,1)}, bf16[768,512]{1,0:T(8,128)(2,1)S(1)}, u32[]{:S(2)}, u32[]{:S(2)}) collective-permute-start(bf16[768,512]{1,0:T(8,128)(2,1)} %collective-permute-done.10), channel_id=1, source_target_pairs={{0,4},{4,0},{8,12},{12,8},{1,5},{5,1},{9,13},{13,9},{2,6},{6,2},{1... | collective-permute-start | bytes 2359304 | tf_op jit(solution)/shard_map/ppermute | solution.py:79
  134.8 21.7 %collective-permute-start.15 = (bf16[768,512]{1,0:T(8,128)(2,1)}, bf16[768,512]{1,0:T(8,128)(2,1)S(1)}, u32[]{:S(2)}, u32[]{:S(2)}) collective-permute-start(bf16[768,512]{1,0:T(8,128)(2,1)} %collective-permute-done.11), channel_id=1, source_target_pairs={{0,4},{4,0},{8,12},{12,8},{1,5},{5,1},{9,13},{13,9},{2,6},{6,2},{1... | collective-permute-start | bytes 2359304 | tf_op jit(solution)/shard_map/ppermute | solution.py:79
  159.9 24.7 %all-to-all-start = ((bf16[4,4,128,192]{2,3,1,0:T(8,128)(2,1)}), bf16[4,4,128,192]{2,3,1,0:T(8,128)(2,1)S(1)}, u32[]{:S(2)}, u32[]{:S(2)}) async-start(bf16[4,4,128,192]{2,3,1,0:T(8,128)(2,1)} %bitcast.24), calls=%async_computation | async-start | bytes 1572864 | tf_op jit(solution)/shard_map/all_to_all | solution.py:165
  184.6 23.9 %all-to-all-start.2 = ((bf16[4,4,128,192]{2,3,1,0:T(8,128)(2,1)}), bf16[4,4,128,192]{2,3,1,0:T(8,128)(2,1)S(1)}, u32[]{:S(2)}, u32[]{:S(2)}) async-start(bf16[4,4,128,192]{2,3,1,0:T(8,128)(2,1)} %bitcast.156), calls=%async_computation.2 | async-start | bytes 1572864 | tf_op jit(solution)/shard_map/all_to_all | solution.py:165
  208.5 12.8 %all-to-all-start.1 = ((bf16[4,4,128,64]{2,3,1,0:T(8,128)(2,1)}), bf16[4,4,128,64]{2,3,1,0:T(8,128)(2,1)S(1)}, u32[]{:S(2)}, u32[]{:S(2)}) async-start(bf16[4,4,128,64]{2,3,1,0:T(8,128)(2,1)} %bitcast.147), calls=%async_computation.1 | async-start | bytes 524288 | tf_op jit(solution)/shard_map/all_to_all | solution.py:181
  221.3 13.1 %all-to-all-start.3 = ((bf16[4,4,128,64]{2,3,1,0:T(8,128)(2,1)}), bf16[4,4,128,64]{2,3,1,0:T(8,128)(2,1)S(1)}, u32[]{:S(2)}, u32[]{:S(2)}) async-start(bf16[4,4,128,64]{2,3,1,0:T(8,128)(2,1)} %bitcast.145), calls=%async_computation.3 | async-start | bytes 524288 | tf_op jit(solution)/shard_map/all_to_all | solution.py:181
  239.7 5.8 %collective-permute-start.16 = (f32[4,2,1152]{2,1,0:T(2,128)S(1)}, f32[4,2,1152]{2,1,0:T(2,128)S(1)}, u32[]{:S(2)}, u32[]{:S(2)}) collective-permute-start(f32[4,2,1152]{2,1,0:T(2,128)S(1)} %get-tuple-element.8), channel_id=1, source_target_pairs={{0,1},{1,2},{2,3},{3,0},{4,5},{5,6},{6,7},{7,4},{8,9},{9,10},{10,1... | collective-permute-start | bytes 110600 | tf_op jit(solution)/shard_map/ppermute | solution.py:293
  240.1 5.5 %collective-permute-start.17 = (f32[4,2,1152]{2,1,0:T(2,128)S(1)}, f32[4,2,1152]{2,1,0:T(2,128)S(1)}, u32[]{:S(2)}, u32[]{:S(2)}) collective-permute-start(f32[4,2,1152]{2,1,0:T(2,128)S(1)} %get-tuple-element.10), channel_id=1, source_target_pairs={{0,2},{1,3},{2,0},{3,1},{4,6},{5,7},{6,4},{7,5},{8,10},{9,11},{10,... | collective-permute-start | bytes 110600 | tf_op jit(solution)/shard_map/ppermute | solution.py:293
  (27 other events, 191.6 us)
Sparse Core Ops, SparseCore 0:
  9.6 30.6 all-gather.2
  41.8 27.4 all-gather.4

commit v9 on v8

--- a/solution.py
+++ b/solution.py
@@ -72,17 +72,19 @@
         axis=1,
     )
     gathered = lax.all_gather(mine, "plane", axis=0, tiled=True)
-    held = [(own, rotate_rows(gathered, 0))]
+    held = [([own], rotate_rows(gathered, 0)[None])]
     for bit, (axis, size, flip) in enumerate(levels):
         swap = [(i, i ^ flip) for i in range(size)]
-        held = held + [
-            (piece + (1 - 2 * ((piece // 2 ** bit) % 2)) * 2 ** bit, lax.ppermute(block, axis, swap))
-            for piece, block in held
-        ]
+        ids = [piece for group, _ in held for piece in group]
+        stacked = held[0][1] if len(held) == 1 else jnp.concatenate([block for _, block in held], axis=0)
+        moved = lax.ppermute(stacked, axis, swap)
+        held = held + [([lax.bitwise_xor(piece, 2 ** bit) for piece in ids], moved)]
     results = []
     offset = 0
     for shard, width in zip(shards, widths):
-        results.append((shard, [(piece, block[:, offset : offset + width]) for piece, block in held], width))
+        results.append(
+            (shard, [(group, block[:, :, offset : offset + width]) for group, block in held], width)
+        )
         offset += width
     return results
 
@@ -94,17 +96,20 @@
     local = jnp.dot(local_inputs, shard, preferred_element_type=jnp.float32)
     remote_inputs = rotate_rows(inputs, 1)
     remote = jnp.zeros_like(local)
-    for piece, block in held:
-        part = jnp.dot(remote_inputs, block, preferred_element_type=jnp.float32)
-        remote = lax.dynamic_update_slice_in_dim(remote, part, piece * width, axis=1)
+    for group, block in held:
+        parts = jnp.einsum("tk,nkc->ntc", remote_inputs, block, preferred_element_type=jnp.float32)
+        for index, piece in enumerate(group):
+            remote = lax.dynamic_update_slice_in_dim(remote, parts[index], piece * width, axis=1)
     return local + remote
 
 
 def assemble(pieces):
     shard, held, width = pieces
-    remote = jnp.zeros((held[0][1].shape[0], width * len(held)), shard.dtype)
-    for piece, block in held:
-        remote = lax.dynamic_update_slice_in_dim(remote, block, piece * width, axis=1)
+    count = sum(len(group) for group, _ in held)
+    remote = jnp.zeros((held[0][1].shape[1], width * count), shard.dtype)
+    for group, block in held:
+        for index, piece in enumerate(group):
+            remote = lax.dynamic_update_slice_in_dim(remote, block[index], piece * width, axis=1)
     return shard, remote
 
 

time: 261 us -> 305 us (1.17)
  waiting for transfers between devices: 103 us -> 141 us
  other arithmetic: 17.8 us -> 32.7 us
  starting transfers between devices: 40 us -> 30.9 us
  matrix products: 40.9 us -> 37 us
  local copies, waits for them, and re-layouts: 42 us -> 45.6 us
    ppermute x14 -> x6, waiting for transfers between devices: 26.7 us -> 75.5 us  [gather_pieces(): moved = lax.ppermute(stacked, axis, swap)]
    all_gather x2, waiting for transfers between devices: 46.3 us -> 30.2 us  [gather_pieces(): gathered = lax.all_gather(mine, 'plane', axis=0, tiled=True)]
    concatenate x0 -> x4, other arithmetic: none -> 9.77 us  [gather_pieces(): jnp.concatenate([block for _, block in held], axis=0)]
    squeeze x0 -> x12, local copies, waits for them, and re-layouts: none -> 8.19 us  [assemble(): block[index]]
    dynamic_update_slice x16 -> x28, local copies, waits for them, and re-layouts: 15.4 us -> 8.44 us  [the longest x16 7.93 us: assemble(): lax.dynamic_update_slice_in_dim(remote, block[index], piece * width, axis=1)]
    ppermute x14 -> x6, starting transfers between devices: 12.5 us -> 6.02 us  [gather_pieces(): moved = lax.ppermute(stacked, axis, swap)]
    dot_general x16 -> x8, matrix products: 14.9 us -> 10.6 us  [project(): jnp.einsum('tk,nkc->ntc', remote_inputs, block, preferred_element_type=jn...]
    ppermute x3, waiting for transfers between devices: 2.49 us -> 5.64 us  [body(): gathered = gathered + lax.ppermute(block, 'plane', moved)]
  transfers between devices with their start and end apart: 28 -> 20, of which waited for: 8 -> 12; matrix products, arithmetic and copies ran while one was open for 34% -> 33% of each run, Pallas kernels for 0% -> 0%
where the time goes in v9:
time: 305 us; the launch traced here: 302 us
  waiting for transfers between devices  141 us (46%)
  local copies, waits for them, and re-layouts  45.6 us (15%)
  matrix products  37 us (12%)
  other arithmetic  32.7 us (11%)
  starting transfers between devices  30.9 us (10%)
  between operations  15.3 us (5%)
    ppermute x6, waiting for transfers between devices, gather_pieces(): moved = lax.ppermute(stacked, axis, swap)  75.5 us
    all_gather x2, waiting for transfers between devices, gather_pieces(): gathered = lax.all_gather(mine, 'plane', axis=0, tiled=True)  30.2 us
    all_to_all x2, waiting for transfers between devices, attend_by_section(): lax.all_to_all(outgoing, 'plane', split_axis=0, concat_axis=2, tiled=True)  22.3 us
    dot_general x8, matrix products, project(): jnp.einsum('tk,nkc->ntc', remote_inputs, block, preferred_element_type=jn...  10.6 us
    concatenate x4, other arithmetic, gather_pieces(): jnp.concatenate([block for _, block in held], axis=0)  9.77 us
    sub x2, matrix products, masked_softmax(): expo = jnp.where(allowed, jnp.exp(shifted - top), 0.0)  9.24 us
    all_to_all x2, starting transfers between devices, attend_by_section(): lax.all_to_all(homeward, 'plane', split_axis=0, concat_axis=1, tiled=True)  8.46 us
    squeeze x12, local copies, waits for them, and re-layouts, assemble(): block[index]  8.19 us
  transfers between devices with their start and end apart: 20, of which 12 were waited for; matrix products, arithmetic and copies ran while one was open for 33% of the time, Pallas kernels for 0%

profile of v9, /device:TPU:0, one launch (start us, length us, event | category | flops | bytes accessed | tf_op | source)
XLA Modules:
  0.0 302.1 jit_solution(1404316942874496019)
XLA Ops:
  15.2 25.8 %all-gather.3.cloned.1.call-done = bf16[1024,512]{1,0:T(8,128)(2,1)} async-done(((bf16[256,512]{1,0:T(8,128)(2,1)}), bf16[1024,512]{1,0:T(8,128)(2,1)}) %all-gather.3.cloned.1.call-update) | async-done | bytes 1048592 | tf_op jit(solution)/shard_map/all_gather | solution.py:74
  46.4 15.5 %collective-permute-done = bf16[1,768,512]{2,1,0:T(8,128)(2,1)S(1)} collective-permute-done((bf16[1,768,512]{2,1,0:T(8,128)(2,1)S(1)}, bf16[1,768,512]{2,1,0:T(8,128)(2,1)S(1)}, u32[]{:S(2)}, u32[]{:S(2)}) %collective-permute-start) | collective-permute-done | bytes 786464 | tf_op jit(solution)/shard_map/ppermute | solution.py:80
  65.6 4.4 %all-gather.5.cloned.1.call-done = bf16[1024,512]{1,0:T(8,128)(2,1)} async-done(((bf16[256,512]{1,0:T(8,128)(2,1)}), bf16[1024,512]{1,0:T(8,128)(2,1)}) %all-gather.5.cloned.1.call-update) | async-done | bytes 1048592 | tf_op jit(solution)/shard_map/all_gather | solution.py:74
  70.0 2.6 fusion.54
  79.1 21.8 %collective-permute-done.1 = bf16[2,768,512]{2,1,0:T(8,128)(2,1)} collective-permute-done((bf16[2,768,512]{2,1,0:T(8,128)(2,1)}, bf16[2,768,512]{2,1,0:T(8,128)(2,1)}, u32[]{:S(2)}, u32[]{:S(2)}) %collective-permute-start.1) | collective-permute-done | bytes 1572896 | tf_op jit(solution)/shard_map/ppermute | solution.py:80
  101.0 3.6 %pad_maximum_fusion = bf16[4,768,512]{2,1,0:T(8,128)(2,1)} fusion(bf16[2,768,512]{2,1,0:T(8,128)(2,1)} %collective-permute-done.1, bf16[1,768,512]{2,1,0:T(8,128)(2,1)} %copy-done.4, bf16[1,768,512]{2,1,0:T(8,128)(2,1)S(1)} %fusion.56), kind=kLoop, calls=%fused_computation.19 | loop fusion | flops 3145728 | bytes 6291456 | tf_op jit(solution)/shard_map/concatenate | solution.py:79
  104.6 11.0 %collective-permute-done.5 = bf16[1,768,512]{1,2,0:T(8,128)(2,1)S(1)} collective-permute-done((bf16[1,768,512]{1,2,0:T(8,128)(2,1)S(1)}, bf16[1,768,512]{1,2,0:T(8,128)(2,1)S(1)}, u32[]{:S(2)}, u32[]{:S(2)}) %collective-permute-start.5) | collective-permute-done | bytes 786464 | tf_op jit(solution)/shard_map/ppermute | solution.py:80
  125.3 27.1 %collective-permute-done.6 = bf16[2,768,512]{1,2,0:T(8,128)(2,1)} collective-permute-done((bf16[2,768,512]{1,2,0:T(8,128)(2,1)}, bf16[2,768,512]{1,2,0:T(8,128)(2,1)}, u32[]{:S(2)}, u32[]{:S(2)}) %collective-permute-start.6) | collective-permute-done | bytes 1572896 | tf_op jit(solution)/shard_map/ppermute | solution.py:80
  152.4 3.4 %pad_maximum_fusion.2 = bf16[4,768,512]{1,2,0:T(8,128)(2,1)} fusion(bf16[2,768,512]{1,2,0:T(8,128)(2,1)} %collective-permute-done.6, bf16[1,768,512]{1,2,0:T(8,128)(2,1)S(1)} %copy-done.7, bf16[1,768,512]{1,2,0:T(8,128)(2,1)S(1)} %bitcast.304), kind=kLoop, calls=%fused_computation.21 | loop fusion | flops 3145728 | bytes 6291456 | tf_op jit(solution)/shard_map/concatenate | solution.py:79
  165.5 3.2 %collective-permute-start.3 = (bf16[128,2048]{0,1:T(8,128)(2,1)}, bf16[128,2048]{0,1:T(8,128)(2,1)}, u32[]{:S(2)}, u32[]{:S(2)}) collective-permute-start(bf16[128,2048]{0,1:T(8,128)(2,1)} %bitcast.22), channel_id=1, source_target_pairs={{0,4},{4,8},{8,12},{1,5},{5,9},{9,13},{2,6},{6,10},{10,14},{3,7},{... | collective-permute-start | bytes 1572872 | tf_op jit(solution)/shard_map/ppermute | solution.py:19
  184.5 3.2 %fusion.164 = (f32[2,16,128]{2,1,0:T(8,128)S(1)}, f32[2,16,128,384]{3,2,1,0:T(8,128)S(1)}) fusion(f32[2,16,128,384]{3,2,1,0:T(8,128)S(1)} %fusion.24, pred[2,128,384]{2,1,0:T(8,128)(4,1)S(1)} %copy-done.24), kind=kOutput, calls=%fused_computation.268 | output fusion | flops 11010431 | bytes 12697600 | tf_op jit(solution)/shard_map/sub | solution.py:31
  196.0 2.6 fusion.28
  201.7 3.9 %all-to-all-start = ((bf16[4,4,128,192]{2,3,1,0:T(8,128)(2,1)}), bf16[4,4,128,192]{2,3,1,0:T(8,128)(2,1)S(1)}, u32[]{:S(2)}, u32[]{:S(2)}) async-start(bf16[4,4,128,192]{2,3,1,0:T(8,128)(2,1)} %bitcast.68), calls=%async_computation | async-start | bytes 1572864 | tf_op jit(solution)/shard_map/all_to_all | solution.py:170
  214.2 12.8 %all-to-all-done = bf16[4,4,128,192]{2,3,1,0:T(8,128)(2,1)S(1)} async-done(((bf16[4,4,128,192]{2,3,1,0:T(8,128)(2,1)}), bf16[4,4,128,192]{2,3,1,0:T(8,128)(2,1)S(1)}, u32[]{:S(2)}, u32[]{:S(2)}) %all-to-all-start) | async-done | bytes 786464 | tf_op jit(solution)/shard_map/all_to_all | solution.py:170
  227.1 3.7 %all-to-all-start.2 = ((bf16[4,4,128,192]{2,3,1,0:T(8,128)(2,1)}), bf16[4,4,128,192]{2,3,1,0:T(8,128)(2,1)S(1)}, u32[]{:S(2)}, u32[]{:S(2)}) async-start(bf16[4,4,128,192]{2,3,1,0:T(8,128)(2,1)} %bitcast.310), calls=%async_computation.2 | async-start | bytes 1572864 | tf_op jit(solution)/shard_map/all_to_all | solution.py:170
  234.1 4.0 %fusion.174 = (f32[4,512]{1,0:T(4,128)S(1)}, f32[4,512,512]{1,2,0:T(8,128)}) fusion(pred[512,512]{0,1:T(8,128)(4,1)S(1)} %copy-done.23, bf16[4,512,192]{1,2,0:T(8,128)(2,1)S(1)} %squeeze.177), kind=kOutput, calls=%fused_computation.270 | convolution fusion | flops 139461120 | bytes 5251072 | tf_op jit(solution)/shard_map/sub | solution.py:31
  238.1 2.7 fusion.47
  241.6 9.5 %all-to-all-done.2 = bf16[4,4,128,192]{2,3,1,0:T(8,128)(2,1)S(1)} async-done(((bf16[4,4,128,192]{2,3,1,0:T(8,128)(2,1)}), bf16[4,4,128,192]{2,3,1,0:T(8,128)(2,1)S(1)}, u32[]{:S(2)}, u32[]{:S(2)}) %all-to-all-start.2) | async-done | bytes 786464 | tf_op jit(solution)/shard_map/all_to_all | solution.py:170
  251.1 3.4 %all-to-all-start.1 = ((bf16[4,4,128,64]{2,3,1,0:T(8,128)(2,1)}), bf16[4,4,128,64]{2,3,1,0:T(8,128)(2,1)S(1)}, u32[]{:S(2)}, u32[]{:S(2)}) async-start(bf16[4,4,128,64]{2,3,1,0:T(8,128)(2,1)} %bitcast.296), calls=%async_computation.1 | async-start | bytes 524288 | tf_op jit(solution)/shard_map/all_to_all | solution.py:186
  255.4 5.3 %fusion.165 = (f32[4,512]{1,0:T(4,128)S(1)}, f32[4,512,512]{1,2,0:T(8,128)}) fusion(pred[512,512]{0,1:T(8,128)(4,1)} %fusion.52, bf16[4,512,192]{1,2,0:T(8,128)(2,1)S(1)} %squeeze.188), kind=kOutput, calls=%fused_computation.269 | convolution fusion | flops 139461120 | bytes 5251072 | tf_op jit(solution)/shard_map/sub | solution.py:31
  260.7 2.8 fusion.48
  264.4 5.1 %all-to-all-start.3 = ((bf16[4,4,128,64]{2,3,1,0:T(8,128)(2,1)}), bf16[4,4,128,64]{2,3,1,0:T(8,128)(2,1)S(1)}, u32[]{:S(2)}, u32[]{:S(2)}) async-start(bf16[4,4,128,64]{2,3,1,0:T(8,128)(2,1)} %bitcast.294), calls=%async_computation.3 | async-start | bytes 524288 | tf_op jit(solution)/shard_map/all_to_all | solution.py:186
  270.8 6.8 %all-to-all-done.3 = bf16[4,4,128,64]{2,3,1,0:T(8,128)(2,1)S(1)} async-done(((bf16[4,4,128,64]{2,3,1,0:T(8,128)(2,1)}), bf16[4,4,128,64]{2,3,1,0:T(8,128)(2,1)S(1)}, u32[]{:S(2)}, u32[]{:S(2)}) %all-to-all-start.3) | async-done | bytes 262176 | tf_op jit(solution)/shard_map/all_to_all | solution.py:186
  287.4 2.7 collective-permute-done.8
  (207 shorter events, 99.8 us)
Async XLA Ops:
  7.2 39.2 %copy-start.26 = (s32[2,128]{1,0:T(2,128)S(1)}, s32[2,128]{1,0:T(2,128)}, u32[]{:S(2)}) copy-start(s32[2,128]{1,0:T(2,128)} %param.10) | copy-start | bytes 3076
  7.2 33.8 %all-gather.3.cloned.1.call-start = ((), (), s32[]{:S(2)}) async-start(), calls=%async_computation.4 | async-start | bytes 1310720 | tf_op jit(solution)/shard_map/all_gather | solution.py:74
  10.2 59.8 %all-gather.5.cloned.1.call-start = ((), (), s32[]{:S(2)}) async-start(), calls=%async_computation.5 | async-start | bytes 1310720 | tf_op jit(solution)/shard_map/all_gather | solution.py:74
  12.8 52.0 %copy-start.25 = (f32[2,1024]{1,0:T(2,128)S(1)}, f32[2,1024]{1,0:T(2,128)}, u32[]{:S(2)}) copy-start(f32[2,1024]{1,0:T(2,128)} %param.11) | copy-start | bytes 24580
  42.7 19.2 %collective-permute-start = (bf16[1,768,512]{2,1,0:T(8,128)(2,1)S(1)}, bf16[1,768,512]{2,1,0:T(8,128)(2,1)S(1)}, u32[]{:S(2)}, u32[]{:S(2)}) collective-permute-start(bf16[1,768,512]{2,1,0:T(8,128)(2,1)S(1)} %fusion.56), channel_id=1, source_target_pairs={{0,8},{4,12},{8,0},{12,4},{1,9},{5,13},{9,1},{13,5},{2,10},{6,14},... | collective-permute-start | bytes 2359304 | tf_op jit(solution)/shard_map/ppermute | solution.py:80
  63.3 37.6 %collective-permute-start.1 = (bf16[2,768,512]{2,1,0:T(8,128)(2,1)}, bf16[2,768,512]{2,1,0:T(8,128)(2,1)}, u32[]{:S(2)}, u32[]{:S(2)}) collective-permute-start(bf16[2,768,512]{2,1,0:T(8,128)(2,1)} %pad_maximum_fusion.3), channel_id=1, source_target_pairs={{0,16},{16,0},{1,17},{17,1},{2,18},{18,2},{3,19},{19,3},{4,20},{20... | collective-permute-start | bytes 4718600 | tf_op jit(solution)/shard_map/ppermute | solution.py:80
  74.0 78.4 %copy-start.2 = (bf16[768,512]{0,1:T(8,128)(2,1)}, bf16[768,512]{0,1:T(8,128)(2,1)S(1)}, u32[]{:S(2)}) copy-start(bf16[768,512]{0,1:T(8,128)(2,1)S(1)} %copy.34) | copy-start | bytes 2359300
  74.0 41.6 %collective-permute-start.5 = (bf16[1,768,512]{1,2,0:T(8,128)(2,1)S(1)}, bf16[1,768,512]{1,2,0:T(8,128)(2,1)S(1)}, u32[]{:S(2)}, u32[]{:S(2)}) collective-permute-start(bf16[1,768,512]{1,2,0:T(8,128)(2,1)S(1)} %bitcast.301), channel_id=1, source_target_pairs={{0,16},{16,0},{1,17},{17,1},{2,18},{18,2},{3,19},{19,3},{4,20},{20... | collective-permute-start | bytes 2359304 | tf_op jit(solution)/shard_map/ppermute | solution.py:80
  104.6 55.6 %collective-permute-start.2 = (bf16[4,768,512]{2,1,0:T(8,128)(2,1)}, bf16[4,768,512]{2,1,0:T(8,128)(2,1)}, u32[]{:S(2)}, u32[]{:S(2)}) collective-permute-start(bf16[4,768,512]{2,1,0:T(8,128)(2,1)} %pad_maximum_fusion), channel_id=1, source_target_pairs={{0,4},{4,0},{8,12},{12,8},{1,5},{5,1},{9,13},{13,9},{2,6},{6,2},{1... | collective-permute-start | bytes 9437192 | tf_op jit(solution)/shard_map/ppermute | solution.py:80
  117.8 34.6 %collective-permute-start.6 = (bf16[2,768,512]{1,2,0:T(8,128)(2,1)}, bf16[2,768,512]{1,2,0:T(8,128)(2,1)}, u32[]{:S(2)}, u32[]{:S(2)}) collective-permute-start(bf16[2,768,512]{1,2,0:T(8,128)(2,1)} %pad_maximum_fusion.4), channel_id=1, source_target_pairs={{0,8},{4,12},{8,0},{12,4},{1,9},{5,13},{9,1},{13,5},{2,10},{6,14},... | collective-permute-start | bytes 4718600 | tf_op jit(solution)/shard_map/ppermute | solution.py:80
  124.0 28.4 %copy-start.7 = (bf16[1,768,512]{1,2,0:T(8,128)(2,1)S(1)}, bf16[1,768,512]{1,2,0:T(8,128)(2,1)}, u32[]{:S(2)}) copy-start(bf16[1,768,512]{1,2,0:T(8,128)(2,1)} %copy-done.6) | copy-start | bytes 2359300
  155.8 40.2 %collective-permute-start.7 = (bf16[4,768,512]{1,2,0:T(8,128)(2,1)}, bf16[4,768,512]{1,2,0:T(8,128)(2,1)}, u32[]{:S(2)}, u32[]{:S(2)}) collective-permute-start(bf16[4,768,512]{1,2,0:T(8,128)(2,1)} %pad_maximum_fusion.2), channel_id=1, source_target_pairs={{0,4},{4,0},{8,12},{12,8},{1,5},{5,1},{9,13},{13,9},{2,6},{6,2},{1... | collective-permute-start | bytes 9437192 | tf_op jit(solution)/shard_map/ppermute | solution.py:80
  165.5 16.0 %collective-permute-start.3 = (bf16[128,2048]{0,1:T(8,128)(2,1)}, bf16[128,2048]{0,1:T(8,128)(2,1)}, u32[]{:S(2)}, u32[]{:S(2)}) collective-permute-start(bf16[128,2048]{0,1:T(8,128)(2,1)} %bitcast.22), channel_id=1, source_target_pairs={{0,4},{4,8},{8,12},{1,5},{5,9},{9,13},{2,6},{6,10},{10,14},{3,7},{... | collective-permute-start | bytes 1572872 | tf_op jit(solution)/shard_map/ppermute | solution.py:19
  169.8 11.8 %collective-permute-start.4 = (bf16[128,2048]{0,1:T(8,128)(2,1)}, bf16[128,2048]{0,1:T(8,128)(2,1)}, u32[]{:S(2)}, u32[]{:S(2)}) collective-permute-start(bf16[128,2048]{0,1:T(8,128)(2,1)} %bitcast.26), channel_id=1, source_target_pairs={{4,0},{8,4},{12,8},{5,1},{9,5},{13,9},{6,2},{10,6},{14,10},{7,3},{... | collective-permute-start | bytes 1572872 | tf_op jit(solution)/shard_map/ppermute | solution.py:19
  201.7 25.3 %all-to-all-start = ((bf16[4,4,128,192]{2,3,1,0:T(8,128)(2,1)}), bf16[4,4,128,192]{2,3,1,0:T(8,128)(2,1)S(1)}, u32[]{:S(2)}, u32[]{:S(2)}) async-start(bf16[4,4,128,192]{2,3,1,0:T(8,128)(2,1)} %bitcast.68), calls=%async_computation | async-start | bytes 1572864 | tf_op jit(solution)/shard_map/all_to_all | solution.py:170
  227.1 24.0 %all-to-all-start.2 = ((bf16[4,4,128,192]{2,3,1,0:T(8,128)(2,1)}), bf16[4,4,128,192]{2,3,1,0:T(8,128)(2,1)S(1)}, u32[]{:S(2)}, u32[]{:S(2)}) async-start(bf16[4,4,128,192]{2,3,1,0:T(8,128)(2,1)} %bitcast.310), calls=%async_computation.2 | async-start | bytes 1572864 | tf_op jit(solution)/shard_map/all_to_all | solution.py:170
  251.1 13.3 %all-to-all-start.1 = ((bf16[4,4,128,64]{2,3,1,0:T(8,128)(2,1)}), bf16[4,4,128,64]{2,3,1,0:T(8,128)(2,1)S(1)}, u32[]{:S(2)}, u32[]{:S(2)}) async-start(bf16[4,4,128,64]{2,3,1,0:T(8,128)(2,1)} %bitcast.296), calls=%async_computation.1 | async-start | bytes 524288 | tf_op jit(solution)/shard_map/all_to_all | solution.py:186
  264.4 13.2 %all-to-all-start.3 = ((bf16[4,4,128,64]{2,3,1,0:T(8,128)(2,1)}), bf16[4,4,128,64]{2,3,1,0:T(8,128)(2,1)S(1)}, u32[]{:S(2)}, u32[]{:S(2)}) async-start(bf16[4,4,128,64]{2,3,1,0:T(8,128)(2,1)} %bitcast.294), calls=%async_computation.3 | async-start | bytes 524288 | tf_op jit(solution)/shard_map/all_to_all | solution.py:186
  282.9 4.5 %collective-permute-start.10 = (f32[4,2,1152]{2,1,0:T(2,128)S(1)}, f32[4,2,1152]{2,1,0:T(2,128)S(1)}, u32[]{:S(2)}, u32[]{:S(2)}) collective-permute-start(f32[4,2,1152]{2,1,0:T(2,128)S(1)} %get-tuple-element.15), channel_id=1, source_target_pairs={{0,3},{1,0},{2,1},{3,2},{4,7},{5,4},{6,5},{7,6},{8,11},{9,8},{10,9... | collective-permute-start | bytes 110600 | tf_op jit(solution)/shard_map/ppermute | solution.py:298
  284.2 5.9 %collective-permute-start.8 = (f32[4,2,1152]{2,1,0:T(2,128)S(1)}, f32[4,2,1152]{2,1,0:T(2,128)S(1)}, u32[]{:S(2)}, u32[]{:S(2)}) collective-permute-start(f32[4,2,1152]{2,1,0:T(2,128)S(1)} %get-tuple-element.14), channel_id=1, source_target_pairs={{0,1},{1,2},{2,3},{3,0},{4,5},{5,6},{6,7},{7,4},{8,9},{9,10},{10,1... | collective-permute-start | bytes 110600 | tf_op jit(solution)/shard_map/ppermute | solution.py:298
  284.9 5.6 %collective-permute-start.9 = (f32[4,2,1152]{2,1,0:T(2,128)S(1)}, f32[4,2,1152]{2,1,0:T(2,128)S(1)}, u32[]{:S(2)}, u32[]{:S(2)}) collective-permute-start(f32[4,2,1152]{2,1,0:T(2,128)S(1)} %get-tuple-element.16), channel_id=1, source_target_pairs={{0,2},{1,3},{2,0},{3,1},{4,6},{5,7},{6,4},{7,5},{8,10},{9,11},{10,... | collective-permute-start | bytes 110600 | tf_op jit(solution)/shard_map/ppermute | solution.py:298
  290.6 3.7 %collective-permute-start.11 = (f32[2,1152]{1,0:T(2,128)S(1)}, f32[2,1152]{1,0:T(2,128)S(1)}, u32[]{:S(2)}, u32[]{:S(2)}) collective-permute-start(f32[2,1152]{1,0:T(2,128)S(1)} %get-tuple-element.17), channel_id=1, source_target_pairs={{0,4},{4,8},{8,12},{12,0},{1,5},{5,9},{9,13},{13,1},{2,6},{6,10},{... | collective-permute-start | bytes 27656 | tf_op jit(solution)/shard_map/ppermute | solution.py:305
  290.7 3.7 %collective-permute-start.12 = (f32[2,1152]{1,0:T(2,128)S(1)}, f32[2,1152]{1,0:T(2,128)S(1)}, u32[]{:S(2)}, u32[]{:S(2)}) collective-permute-start(f32[2,1152]{1,0:T(2,128)S(1)} %get-tuple-element.19), channel_id=1, source_target_pairs={{0,8},{4,12},{8,0},{12,4},{1,9},{5,13},{9,1},{13,5},{2,10},{6,14},... | collective-permute-start | bytes 27656 | tf_op jit(solution)/shard_map/ppermute | solution.py:305
  291.2 3.2 %collective-permute-start.13 = (f32[2,1152]{1,0:T(2,128)S(1)}, f32[2,1152]{1,0:T(2,128)S(1)}, u32[]{:S(2)}, u32[]{:S(2)}) collective-permute-start(f32[2,1152]{1,0:T(2,128)S(1)} %get-tuple-element.18), channel_id=1, source_target_pairs={{0,12},{4,0},{8,4},{12,8},{1,13},{5,1},{9,5},{13,9},{2,14},{6,2},{... | collective-permute-start | bytes 27656 | tf_op jit(solution)/shard_map/ppermute | solution.py:305
  (23 other events, 103.4 us)
Sparse Core Ops, SparseCore 0:
  10.3 30.6 all-gather.2
  42.6 27.4 all-gather.4

commit v10 on v8

--- a/solution.py
+++ b/solution.py
@@ -198,7 +198,7 @@
     own_valid = near_valid[1 : sec_block + 1]
     score_scale = 1.0 / math.sqrt(HEAD_DIM)
     cross_qkv_pieces, cross_out_pieces = gather_pieces([cross_qkv, cross_out], swap_first=True)
-    plane_qkv_pieces, plane_out_pieces = gather_pieces([plane_qkv, plane_out])
+    plane_qkv_pieces, plane_out_pieces = gather_pieces([plane_qkv, plane_out], swap_first=True)
     cross_out_pieces = assemble(cross_out_pieces)
     plane_out_pieces = assemble(plane_out_pieces)
     normed = rms_norm(tokens, norm_gains[0])

time: 261 us -> 259 us (level)
  transfers between devices with their start and end apart: 28 -> 28, of which waited for: 8 -> 8; matrix products, arithmetic and copies ran while one was open for 34% -> 35% of each run, Pallas kernels for 0% -> 0%
where the time goes in v10:
time: 259 us; the launch traced here: 257 us
  waiting for transfers between devices  102 us (39%)
  local copies, waits for them, and re-layouts  42.1 us (16%)
  matrix products  40.9 us (16%)
  starting transfers between devices  37.8 us (15%)
  other arithmetic  18.8 us (7%)
  between operations  15.4 us (6%)
    all_gather x2, waiting for transfers between devices, gather_pieces(): gathered = lax.all_gather(mine, 'plane', axis=0, tiled=True)  45.7 us
    ppermute x14, waiting for transfers between devices, gather_pieces(): lax.ppermute(block, axis, swap)  27.9 us
    all_to_all x2, waiting for transfers between devices, attend_by_section(): lax.all_to_all(outgoing, 'plane', split_axis=0, concat_axis=2, tiled=True)  19.8 us
    dynamic_update_slice x16, local copies, waits for them, and re-layouts, assemble(): lax.dynamic_update_slice_in_dim(remote, block, piece * width, axis=1)  15.4 us
    dot_general x16, matrix products, project(): part = jnp.dot(remote_inputs, block, preferred_element_type=jnp.float32)  14.9 us
    ppermute x14, starting transfers between devices, gather_pieces(): lax.ppermute(block, axis, swap)  10.6 us
    sub x2, matrix products, masked_softmax(): expo = jnp.where(allowed, jnp.exp(shifted - top), 0.0)  8.92 us
    all_to_all x2, starting transfers between devices, attend_by_section(): lax.all_to_all(homeward, 'plane', split_axis=0, concat_axis=1, tiled=True)  8.46 us
  transfers between devices with their start and end apart: 28, of which 8 were waited for; matrix products, arithmetic and copies ran while one was open for 35% of the time, Pallas kernels for 0%

profile of v10, /device:TPU:0, one launch (start us, length us, event | category | flops | bytes accessed | tf_op | source)
XLA Modules:
  0.0 256.8 jit_solution(13607024868454705115)
XLA Ops:
  18.3 22.0 %all-gather.3.cloned.1.call-done = bf16[1024,512]{1,0:T(8,128)(2,1)} async-done(((bf16[256,512]{1,0:T(8,128)(2,1)}), bf16[1024,512]{1,0:T(8,128)(2,1)}) %all-gather.3.cloned.1.call-update) | async-done | bytes 1048592 | tf_op jit(solution)/shard_map/all_gather | solution.py:74
  45.6 23.7 %all-gather.5.cloned.1.call-done = bf16[1024,512]{1,0:T(8,128)(2,1)} async-done(((bf16[256,512]{1,0:T(8,128)(2,1)}), bf16[1024,512]{1,0:T(8,128)(2,1)}) %all-gather.5.cloned.1.call-update) | async-done | bytes 1048592 | tf_op jit(solution)/shard_map/all_gather | solution.py:74
  69.3 2.6 %fusion.34 = bf16[768,512]{1,0:T(8,128)(2,1)} fusion(s32[]{:T(128)S(6)} %select_n.241, bf16[1024,512]{1,0:T(8,128)(2,1)} %all-gather.5.cloned.1.call-done), kind=kLoop, calls=%fused_computation.85 | loop fusion | flops 1572864 | bytes 1835012 | tf_op jit(solution)/shard_map/concatenate | solution.py:54
  81.5 27.8 %collective-permute-done.2 = bf16[768,512]{1,0:T(8,128)(2,1)S(1)} collective-permute-done((bf16[768,512]{1,0:T(8,128)(2,1)}, bf16[768,512]{1,0:T(8,128)(2,1)S(1)}, u32[]{:S(2)}, u32[]{:S(2)}) %collective-permute-start.2) | collective-permute-done | bytes 786464 | tf_op jit(solution)/shard_map/ppermute | solution.py:79
  111.3 1.9 convolution_dynamic-update-slice_fusion.11
  120.0 2.9 %collective-permute-start.7 = (bf16[128,2048]{0,1:T(8,128)(2,1)}, bf16[128,2048]{0,1:T(8,128)(2,1)}, u32[]{:S(2)}, u32[]{:S(2)}) collective-permute-start(bf16[128,2048]{0,1:T(8,128)(2,1)} %bitcast.4), channel_id=1, source_target_pairs={{0,4},{4,8},{8,12},{1,5},{5,9},{9,13},{2,6},{6,10},{10,14},{3,7},{... | collective-permute-start | bytes 1572872 | tf_op jit(solution)/shard_map/ppermute | solution.py:19
  139.3 3.2 %fusion.139 = (f32[2,16,128]{2,1,0:T(8,128)S(1)}, f32[2,16,128,384]{3,2,1,0:T(8,128)S(1)}) fusion(f32[2,16,128,384]{3,2,1,0:T(8,128)S(1)} %fusion.20, pred[2,128,384]{2,1,0:T(8,128)(4,1)S(1)} %copy-done.14), kind=kOutput, calls=%fused_computation.227 | output fusion | flops 11010431 | bytes 12697600 | tf_op jit(solution)/shard_map/sub | solution.py:31
  142.6 1.8 fusion.24
  159.1 3.5 %all-to-all-start = ((bf16[4,4,128,192]{2,3,1,0:T(8,128)(2,1)}), bf16[4,4,128,192]{2,3,1,0:T(8,128)(2,1)S(1)}, u32[]{:S(2)}, u32[]{:S(2)}) async-start(bf16[4,4,128,192]{2,3,1,0:T(8,128)(2,1)} %bitcast.24), calls=%async_computation | async-start | bytes 1572864 | tf_op jit(solution)/shard_map/all_to_all | solution.py:165
  171.3 11.9 %all-to-all-done = bf16[4,4,128,192]{2,3,1,0:T(8,128)(2,1)S(1)} async-done(((bf16[4,4,128,192]{2,3,1,0:T(8,128)(2,1)}), bf16[4,4,128,192]{2,3,1,0:T(8,128)(2,1)S(1)}, u32[]{:S(2)}, u32[]{:S(2)}) %all-to-all-start) | async-done | bytes 786464 | tf_op jit(solution)/shard_map/all_to_all | solution.py:165
  183.2 3.7 %all-to-all-start.2 = ((bf16[4,4,128,192]{2,3,1,0:T(8,128)(2,1)}), bf16[4,4,128,192]{2,3,1,0:T(8,128)(2,1)S(1)}, u32[]{:S(2)}, u32[]{:S(2)}) async-start(bf16[4,4,128,192]{2,3,1,0:T(8,128)(2,1)} %bitcast.156), calls=%async_computation.2 | async-start | bytes 1572864 | tf_op jit(solution)/shard_map/all_to_all | solution.py:165
  191.1 3.9 %fusion.149 = (f32[4,512]{1,0:T(4,128)S(1)}, f32[4,512,512]{1,2,0:T(8,128)}) fusion(pred[512,512]{0,1:T(8,128)(4,1)S(1)} %fusion.33, bf16[4,512,192]{1,2,0:T(8,128)(2,1)S(1)} %squeeze.57), kind=kOutput, calls=%fused_computation.229 | convolution fusion | flops 139461120 | bytes 5251072 | tf_op jit(solution)/shard_map/sub | solution.py:31
  195.1 2.7 %fusion.27 = bf16[4,8,4,8,128]{4,3,2,1,0:T(8,128)(2,1)S(1)} fusion(f32[4,512,512]{1,2,0:T(8,128)} %get-tuple-element.29, f32[4,512]{1,0:T(4,128)S(1)} %get-tuple-element.28, bf16[4,512,192]{1,2,0:T(8,128)(2,1)S(1)} %squeeze.57), kind=kOutput, calls=%fused_computation.67 | convolution fusion | flops 136445952 | bytes 4726784 | tf_op jit(solution)/shard_map/nqk,nkd->nqd/dot_general | solution.py:175
  198.5 7.9 %all-to-all-done.2 = bf16[4,4,128,192]{2,3,1,0:T(8,128)(2,1)S(1)} async-done(((bf16[4,4,128,192]{2,3,1,0:T(8,128)(2,1)}), bf16[4,4,128,192]{2,3,1,0:T(8,128)(2,1)S(1)}, u32[]{:S(2)}, u32[]{:S(2)}) %all-to-all-start.2) | async-done | bytes 786464 | tf_op jit(solution)/shard_map/all_to_all | solution.py:165
  206.5 3.4 %all-to-all-start.1 = ((bf16[4,4,128,64]{2,3,1,0:T(8,128)(2,1)}), bf16[4,4,128,64]{2,3,1,0:T(8,128)(2,1)S(1)}, u32[]{:S(2)}, u32[]{:S(2)}) async-start(bf16[4,4,128,64]{2,3,1,0:T(8,128)(2,1)} %bitcast.147), calls=%async_computation.1 | async-start | bytes 524288 | tf_op jit(solution)/shard_map/all_to_all | solution.py:181
  210.8 5.0 %fusion.140 = (f32[4,512]{1,0:T(4,128)S(1)}, f32[4,512,512]{1,2,0:T(8,128)}) fusion(pred[512,512]{0,1:T(8,128)(4,1)} %fusion.32, bf16[4,512,192]{1,2,0:T(8,128)(2,1)S(1)} %squeeze.60), kind=kOutput, calls=%fused_computation.228 | convolution fusion | flops 139461120 | bytes 5251072 | tf_op jit(solution)/shard_map/sub | solution.py:31
  215.8 2.7 %fusion.28 = bf16[4,8,4,8,128]{4,3,2,1,0:T(8,128)(2,1)S(1)} fusion(f32[4,512,512]{1,2,0:T(8,128)} %get-tuple-element.27, f32[4,512]{1,0:T(4,128)S(1)} %get-tuple-element.26, bf16[4,512,192]{1,2,0:T(8,128)(2,1)S(1)} %squeeze.60), kind=kOutput, calls=%fused_computation.68 | convolution fusion | flops 136445952 | bytes 4726784 | tf_op jit(solution)/shard_map/nqk,nkd->nqd/dot_general | solution.py:175
  219.3 5.1 %all-to-all-start.3 = ((bf16[4,4,128,64]{2,3,1,0:T(8,128)(2,1)}), bf16[4,4,128,64]{2,3,1,0:T(8,128)(2,1)S(1)}, u32[]{:S(2)}, u32[]{:S(2)}) async-start(bf16[4,4,128,64]{2,3,1,0:T(8,128)(2,1)} %bitcast.145), calls=%async_computation.3 | async-start | bytes 524288 | tf_op jit(solution)/shard_map/all_to_all | solution.py:181
  226.4 5.9 %all-to-all-done.3 = bf16[4,4,128,64]{2,3,1,0:T(8,128)(2,1)S(1)} async-done(((bf16[4,4,128,64]{2,3,1,0:T(8,128)(2,1)}), bf16[4,4,128,64]{2,3,1,0:T(8,128)(2,1)S(1)}, u32[]{:S(2)}, u32[]{:S(2)}) %all-to-all-start.3) | async-done | bytes 262176 | tf_op jit(solution)/shard_map/all_to_all | solution.py:181
  233.4 1.8 add_convert_fusion.1
  239.6 2.0 collective-permute-start.18
  241.6 1.9 collective-permute-done.16
  244.2 1.8 collective-permute-start.20
  247.4 1.8 pad_maximum_fusion.3
  (194 shorter events, 90.5 us)
Async XLA Ops:
  7.2 33.1 %all-gather.3.cloned.1.call-start = ((), (), s32[]{:S(2)}) async-start(), calls=%async_computation.4 | async-start | bytes 1310720 | tf_op jit(solution)/shard_map/all_gather | solution.py:74
  9.4 59.9 %all-gather.5.cloned.1.call-start = ((), (), s32[]{:S(2)}) async-start(), calls=%async_computation.5 | async-start | bytes 1310720 | tf_op jit(solution)/shard_map/all_gather | solution.py:74
  42.0 33.9 %collective-permute-start = (bf16[768,512]{1,0:T(8,128)(2,1)S(1)}, bf16[768,512]{1,0:T(8,128)(2,1)}, u32[]{:S(2)}, u32[]{:S(2)}) collective-permute-start(bf16[768,512]{1,0:T(8,128)(2,1)S(1)} %fusion.35), channel_id=1, source_target_pairs={{0,8},{4,12},{8,0},{12,4},{1,9},{5,13},{9,1},{13,5},{2,10},{6,14},... | collective-permute-start | bytes 2359304 | tf_op jit(solution)/shard_map/ppermute | solution.py:79
  44.1 34.9 %collective-permute-start.1 = (bf16[768,512]{1,0:T(8,128)(2,1)S(1)}, bf16[768,512]{1,0:T(8,128)(2,1)}, u32[]{:S(2)}, u32[]{:S(2)}) collective-permute-start(bf16[768,512]{1,0:T(8,128)(2,1)S(1)} %fusion.35), channel_id=1, source_target_pairs={{0,16},{16,0},{1,17},{17,1},{2,18},{18,2},{3,19},{19,3},{4,20},{20... | collective-permute-start | bytes 2359304 | tf_op jit(solution)/shard_map/ppermute | solution.py:79
  45.6 64.1 %collective-permute-start.3 = (bf16[768,512]{1,0:T(8,128)(2,1)S(1)}, bf16[768,512]{1,0:T(8,128)(2,1)}, u32[]{:S(2)}, u32[]{:S(2)}) collective-permute-start(bf16[768,512]{1,0:T(8,128)(2,1)S(1)} %fusion.35), channel_id=1, source_target_pairs={{0,4},{4,0},{8,12},{12,8},{1,5},{5,1},{9,13},{13,9},{2,6},{6,2},{1... | collective-permute-start | bytes 2359304 | tf_op jit(solution)/shard_map/ppermute | solution.py:79
  71.9 41.3 %collective-permute-start.9 = (bf16[768,512]{1,0:T(8,128)(2,1)}, bf16[768,512]{1,0:T(8,128)(2,1)}, u32[]{:S(2)}, u32[]{:S(2)}) collective-permute-start(bf16[768,512]{1,0:T(8,128)(2,1)} %fusion.34), channel_id=1, source_target_pairs={{0,8},{4,12},{8,0},{12,4},{1,9},{5,13},{9,1},{13,5},{2,10},{6,14},... | collective-permute-start | bytes 2359304 | tf_op jit(solution)/shard_map/ppermute | solution.py:79
  73.4 61.3 %collective-permute-start.10 = (bf16[768,512]{1,0:T(8,128)(2,1)}, bf16[768,512]{1,0:T(8,128)(2,1)}, u32[]{:S(2)}, u32[]{:S(2)}) collective-permute-start(bf16[768,512]{1,0:T(8,128)(2,1)} %fusion.34), channel_id=1, source_target_pairs={{0,16},{16,0},{1,17},{17,1},{2,18},{18,2},{3,19},{19,3},{4,20},{20... | collective-permute-start | bytes 2359304 | tf_op jit(solution)/shard_map/ppermute | solution.py:79
  75.8 33.4 %collective-permute-start.2 = (bf16[768,512]{1,0:T(8,128)(2,1)}, bf16[768,512]{1,0:T(8,128)(2,1)S(1)}, u32[]{:S(2)}, u32[]{:S(2)}) collective-permute-start(bf16[768,512]{1,0:T(8,128)(2,1)} %collective-permute-done), channel_id=1, source_target_pairs={{0,16},{16,0},{1,17},{17,1},{2,18},{18,2},{3,19},{19,3},{4,20},{20... | collective-permute-start | bytes 2359304 | tf_op jit(solution)/shard_map/ppermute | solution.py:79
  78.9 34.3 %collective-permute-start.4 = (bf16[768,512]{1,0:T(8,128)(2,1)}, bf16[768,512]{1,0:T(8,128)(2,1)S(1)}, u32[]{:S(2)}, u32[]{:S(2)}) collective-permute-start(bf16[768,512]{1,0:T(8,128)(2,1)} %collective-permute-done), channel_id=1, source_target_pairs={{0,4},{4,0},{8,12},{12,8},{1,5},{5,1},{9,13},{13,9},{2,6},{6,2},{1... | collective-permute-start | bytes 2359304 | tf_op jit(solution)/shard_map/ppermute | solution.py:79
  109.3 5.9 %collective-permute-start.5 = (bf16[768,512]{1,0:T(8,128)(2,1)}, bf16[768,512]{1,0:T(8,128)(2,1)S(1)}, u32[]{:S(2)}, u32[]{:S(2)}) collective-permute-start(bf16[768,512]{1,0:T(8,128)(2,1)} %collective-permute-done.1), channel_id=1, source_target_pairs={{0,4},{4,0},{8,12},{12,8},{1,5},{5,1},{9,13},{13,9},{2,6},{6,2},{1... | collective-permute-start | bytes 2359304 | tf_op jit(solution)/shard_map/ppermute | solution.py:79
  109.7 5.8 %collective-permute-start.6 = (bf16[768,512]{1,0:T(8,128)(2,1)S(1)}, bf16[768,512]{1,0:T(8,128)(2,1)S(1)}, u32[]{:S(2)}, u32[]{:S(2)}) collective-permute-start(bf16[768,512]{1,0:T(8,128)(2,1)S(1)} %collective-permute-done.2), channel_id=1, source_target_pairs={{0,4},{4,0},{8,12},{12,8},{1,5},{5,1},{9,13},{13,9},{2,6},{6,2},{1... | collective-permute-start | bytes 2359304 | tf_op jit(solution)/shard_map/ppermute | solution.py:79
  113.2 40.3 %collective-permute-start.12 = (bf16[768,512]{1,0:T(8,128)(2,1)}, bf16[768,512]{1,0:T(8,128)(2,1)}, u32[]{:S(2)}, u32[]{:S(2)}) collective-permute-start(bf16[768,512]{1,0:T(8,128)(2,1)} %fusion.34), channel_id=1, source_target_pairs={{0,4},{4,0},{8,12},{12,8},{1,5},{5,1},{9,13},{13,9},{2,6},{6,2},{1... | collective-permute-start | bytes 2359304 | tf_op jit(solution)/shard_map/ppermute | solution.py:79
  113.3 22.6 %collective-permute-start.11 = (bf16[768,512]{1,0:T(8,128)(2,1)}, bf16[768,512]{1,0:T(8,128)(2,1)}, u32[]{:S(2)}, u32[]{:S(2)}) collective-permute-start(bf16[768,512]{1,0:T(8,128)(2,1)} %collective-permute-done.9), channel_id=1, source_target_pairs={{0,16},{16,0},{1,17},{17,1},{2,18},{18,2},{3,19},{19,3},{4,20},{20... | collective-permute-start | bytes 2359304 | tf_op jit(solution)/shard_map/ppermute | solution.py:79
  120.0 15.9 %collective-permute-start.7 = (bf16[128,2048]{0,1:T(8,128)(2,1)}, bf16[128,2048]{0,1:T(8,128)(2,1)}, u32[]{:S(2)}, u32[]{:S(2)}) collective-permute-start(bf16[128,2048]{0,1:T(8,128)(2,1)} %bitcast.4), channel_id=1, source_target_pairs={{0,4},{4,8},{8,12},{1,5},{5,9},{9,13},{2,6},{6,10},{10,14},{3,7},{... | collective-permute-start | bytes 1572872 | tf_op jit(solution)/shard_map/ppermute | solution.py:19
  124.0 12.4 %collective-permute-start.8 = (bf16[128,2048]{0,1:T(8,128)(2,1)}, bf16[128,2048]{0,1:T(8,128)(2,1)}, u32[]{:S(2)}, u32[]{:S(2)}) collective-permute-start(bf16[128,2048]{0,1:T(8,128)(2,1)} %bitcast.8), channel_id=1, source_target_pairs={{4,0},{8,4},{12,8},{5,1},{9,5},{13,9},{6,2},{10,6},{14,10},{7,3},{... | collective-permute-start | bytes 1572872 | tf_op jit(solution)/shard_map/ppermute | solution.py:19
  134.7 20.2 %collective-permute-start.13 = (bf16[768,512]{1,0:T(8,128)(2,1)}, bf16[768,512]{1,0:T(8,128)(2,1)S(1)}, u32[]{:S(2)}, u32[]{:S(2)}) collective-permute-start(bf16[768,512]{1,0:T(8,128)(2,1)} %collective-permute-done.9), channel_id=1, source_target_pairs={{0,4},{4,0},{8,12},{12,8},{1,5},{5,1},{9,13},{13,9},{2,6},{6,2},{1... | collective-permute-start | bytes 2359304 | tf_op jit(solution)/shard_map/ppermute | solution.py:79
  135.9 19.5 %collective-permute-start.14 = (bf16[768,512]{1,0:T(8,128)(2,1)}, bf16[768,512]{1,0:T(8,128)(2,1)S(1)}, u32[]{:S(2)}, u32[]{:S(2)}) collective-permute-start(bf16[768,512]{1,0:T(8,128)(2,1)} %collective-permute-done.10), channel_id=1, source_target_pairs={{0,4},{4,0},{8,12},{12,8},{1,5},{5,1},{9,13},{13,9},{2,6},{6,2},{1... | collective-permute-start | bytes 2359304 | tf_op jit(solution)/shard_map/ppermute | solution.py:79
  135.9 19.8 %collective-permute-start.15 = (bf16[768,512]{1,0:T(8,128)(2,1)}, bf16[768,512]{1,0:T(8,128)(2,1)S(1)}, u32[]{:S(2)}, u32[]{:S(2)}) collective-permute-start(bf16[768,512]{1,0:T(8,128)(2,1)} %collective-permute-done.11), channel_id=1, source_target_pairs={{0,4},{4,0},{8,12},{12,8},{1,5},{5,1},{9,13},{13,9},{2,6},{6,2},{1... | collective-permute-start | bytes 2359304 | tf_op jit(solution)/shard_map/ppermute | solution.py:79
  159.1 24.1 %all-to-all-start = ((bf16[4,4,128,192]{2,3,1,0:T(8,128)(2,1)}), bf16[4,4,128,192]{2,3,1,0:T(8,128)(2,1)S(1)}, u32[]{:S(2)}, u32[]{:S(2)}) async-start(bf16[4,4,128,192]{2,3,1,0:T(8,128)(2,1)} %bitcast.24), calls=%async_computation | async-start | bytes 1572864 | tf_op jit(solution)/shard_map/all_to_all | solution.py:165
  183.2 23.2 %all-to-all-start.2 = ((bf16[4,4,128,192]{2,3,1,0:T(8,128)(2,1)}), bf16[4,4,128,192]{2,3,1,0:T(8,128)(2,1)S(1)}, u32[]{:S(2)}, u32[]{:S(2)}) async-start(bf16[4,4,128,192]{2,3,1,0:T(8,128)(2,1)} %bitcast.156), calls=%async_computation.2 | async-start | bytes 1572864 | tf_op jit(solution)/shard_map/all_to_all | solution.py:165
  206.5 12.8 %all-to-all-start.1 = ((bf16[4,4,128,64]{2,3,1,0:T(8,128)(2,1)}), bf16[4,4,128,64]{2,3,1,0:T(8,128)(2,1)S(1)}, u32[]{:S(2)}, u32[]{:S(2)}) async-start(bf16[4,4,128,64]{2,3,1,0:T(8,128)(2,1)} %bitcast.147), calls=%async_computation.1 | async-start | bytes 524288 | tf_op jit(solution)/shard_map/all_to_all | solution.py:181
  219.3 13.1 %all-to-all-start.3 = ((bf16[4,4,128,64]{2,3,1,0:T(8,128)(2,1)}), bf16[4,4,128,64]{2,3,1,0:T(8,128)(2,1)S(1)}, u32[]{:S(2)}, u32[]{:S(2)}) async-start(bf16[4,4,128,64]{2,3,1,0:T(8,128)(2,1)} %bitcast.145), calls=%async_computation.3 | async-start | bytes 524288 | tf_op jit(solution)/shard_map/all_to_all | solution.py:181
  237.7 5.8 %collective-permute-start.16 = (f32[4,2,1152]{2,1,0:T(2,128)S(1)}, f32[4,2,1152]{2,1,0:T(2,128)S(1)}, u32[]{:S(2)}, u32[]{:S(2)}) collective-permute-start(f32[4,2,1152]{2,1,0:T(2,128)S(1)} %get-tuple-element.8), channel_id=1, source_target_pairs={{0,1},{1,2},{2,3},{3,0},{4,5},{5,6},{6,7},{7,4},{8,9},{9,10},{10,1... | collective-permute-start | bytes 110600 | tf_op jit(solution)/shard_map/ppermute | solution.py:293
  238.1 5.4 %collective-permute-start.17 = (f32[4,2,1152]{2,1,0:T(2,128)S(1)}, f32[4,2,1152]{2,1,0:T(2,128)S(1)}, u32[]{:S(2)}, u32[]{:S(2)}) collective-permute-start(f32[4,2,1152]{2,1,0:T(2,128)S(1)} %get-tuple-element.10), channel_id=1, source_target_pairs={{0,2},{1,3},{2,0},{3,1},{4,6},{5,7},{6,4},{7,5},{8,10},{9,11},{10,... | collective-permute-start | bytes 110600 | tf_op jit(solution)/shard_map/ppermute | solution.py:293
  (27 other events, 195.8 us)
Sparse Core Ops, SparseCore 0:
  9.6 30.6 all-gather.2
  41.8 27.4 all-gather.4

commit v11 on v10

--- a/solution.py
+++ b/solution.py
@@ -197,8 +197,10 @@
     near_valid = positions[None, :] < near_counts[:, None]
     own_valid = near_valid[1 : sec_block + 1]
     score_scale = 1.0 / math.sqrt(HEAD_DIM)
-    cross_qkv_pieces, cross_out_pieces = gather_pieces([cross_qkv, cross_out], swap_first=True)
-    plane_qkv_pieces, plane_out_pieces = gather_pieces([plane_qkv, plane_out], swap_first=True)
+    cross_qkv_pieces, cross_out_pieces, plane_out_pieces = gather_pieces(
+        [cross_qkv, cross_out, plane_out], swap_first=True
+    )
+    (plane_qkv_pieces,) = gather_pieces([plane_qkv], swap_first=True)
     cross_out_pieces = assemble(cross_out_pieces)
     plane_out_pieces = assemble(plane_out_pieces)
     normed = rms_norm(tokens, norm_gains[0])

time: 259 us -> 271 us (1.046)
  blocking collectives: 0 us -> 21.3 us
  waiting for transfers between devices: 102 us -> 95.2 us
    all_gather x0 -> x1, blocking collectives: none -> 21.3 us  [gather_pieces(): gathered = lax.all_gather(mine, 'plane', axis=0, tiled=True)]
    all_gather x2 -> x1, waiting for transfers between devices: 45.7 us -> 28.5 us  [gather_pieces(): gathered = lax.all_gather(mine, 'plane', axis=0, tiled=True)]
    dynamic_update_slice x16 -> x9, local copies, waits for them, and re-layouts: 15.4 us -> 9.03 us  [assemble(): lax.dynamic_update_slice_in_dim(remote, block, piece * width, axis=1)]
    ppermute x14, waiting for transfers between devices: 27.9 us -> 33.5 us  [gather_pieces(): lax.ppermute(block, axis, swap)]
    unnamed x50, local copies, waits for them, and re-layouts: 6.92 us -> 11.8 us
    all_to_all x2, waiting for transfers between devices: 19.8 us -> 23.7 us  [attend_by_section(): lax.all_to_all(outgoing, 'plane', split_axis=0, concat_axis=2, tiled=True)]
  transfers between devices with their start and end apart: 28 -> 27, of which waited for: 8 -> 8; matrix products, arithmetic and copies ran while one was open for 35% -> 30% of each run, Pallas kernels for 0% -> 0%
where the time goes in v11:
time: 271 us; the launch traced here: 269 us
  waiting for transfers between devices  95.2 us (35%)
  local copies, waits for them, and re-layouts  41.3 us (15%)
  starting transfers between devices  39.4 us (15%)
  matrix products  39.4 us (15%)
  blocking collectives  21.3 us (8%)
  other arithmetic  17.8 us (7%)
  between operations  14.9 us (5%)
    ppermute x14, waiting for transfers between devices, gather_pieces(): lax.ppermute(block, axis, swap)  33.5 us
    all_gather x1, waiting for transfers between devices, gather_pieces(): gathered = lax.all_gather(mine, 'plane', axis=0, tiled=True)  28.5 us
    all_to_all x2, waiting for transfers between devices, attend_by_section(): lax.all_to_all(outgoing, 'plane', split_axis=0, concat_axis=2, tiled=True)  23.7 us
    all_gather x1, blocking collectives, gather_pieces(): gathered = lax.all_gather(mine, 'plane', axis=0, tiled=True)  21.3 us
    dot_general x16, matrix products, project(): part = jnp.dot(remote_inputs, block, preferred_element_type=jnp.float32)  13.5 us
    unnamed x50, local copies, waits for them, and re-layouts  11.8 us
    ppermute x14, starting transfers between devices, gather_pieces(): lax.ppermute(block, axis, swap)  11.3 us
    dynamic_update_slice x9, local copies, waits for them, and re-layouts, assemble(): lax.dynamic_update_slice_in_dim(remote, block, piece * width, axis=1)  9.03 us
  transfers between devices with their start and end apart: 27, of which 8 were waited for; matrix products, arithmetic and copies ran while one was open for 30% of the time, Pallas kernels for 0%

profile of v11, /device:TPU:0, one launch (start us, length us, event | category | flops | bytes accessed | tf_op | source)
XLA Modules:
  0.0 269.2 jit_solution(5121392321201561869)
XLA Ops:
  8.4 21.3 %all_gather.7 = bf16[1024,384]{1,0:T(8,128)(2,1)S(1)} all-gather(bf16[256,384]{1,0:T(8,128)(2,1)S(1)} %constant_dynamic-slice_fusion.4), channel_id=1, replica_groups=mesh['groups'=2,'sec'=4,'plane'=4] {'plane'}, dimensions={0}, use_global_device_ids=true | all-gather | bytes 983040 | tf_op jit(solution)/shard_map/all_gather | solution.py:74
  29.7 2.0 fusion.35
  38.2 28.5 %all-gather.2.cloned.1.call-done = bf16[1024,640]{1,0:T(8,128)(2,1)} async-done(((bf16[256,640]{1,0:T(8,128)(2,1)}), bf16[1024,640]{1,0:T(8,128)(2,1)}) %all-gather.2.cloned.1.call-update) | async-done | bytes 1310736 | tf_op jit(solution)/shard_map/all_gather | solution.py:74
  66.7 3.0 %fusion.34 = bf16[768,640]{1,0:T(8,128)(2,1)} fusion(s32[]{:T(128)S(6)} %select_n.241, bf16[1024,640]{1,0:T(8,128)(2,1)} %all-gather.2.cloned.1.call-done), kind=kLoop, calls=%fused_computation.85 | loop fusion | flops 1966080 | bytes 2293764 | tf_op jit(solution)/shard_map/concatenate | solution.py:54
  77.5 15.3 %collective-permute-done = bf16[768,640]{1,0:T(8,128)(2,1)} collective-permute-done((bf16[768,640]{1,0:T(8,128)(2,1)}, bf16[768,640]{1,0:T(8,128)(2,1)}, u32[]{:S(2)}, u32[]{:S(2)}) %collective-permute-start) | collective-permute-done | bytes 983072 | tf_op jit(solution)/shard_map/ppermute | solution.py:79
  97.5 18.2 %collective-permute-done.2 = bf16[768,640]{1,0:T(8,128)(2,1)S(1)} collective-permute-done((bf16[768,640]{1,0:T(8,128)(2,1)}, bf16[768,640]{1,0:T(8,128)(2,1)S(1)}, u32[]{:S(2)}, u32[]{:S(2)}) %collective-permute-start.2) | collective-permute-done | bytes 983072 | tf_op jit(solution)/shard_map/ppermute | solution.py:79
  125.4 2.2 copy.34
  127.6 2.8 %collective-permute-start.7 = (bf16[128,2048]{0,1:T(8,128)(2,1)}, bf16[128,2048]{0,1:T(8,128)(2,1)}, u32[]{:S(2)}, u32[]{:S(2)}) collective-permute-start(bf16[128,2048]{0,1:T(8,128)(2,1)} %bitcast.179), channel_id=1, source_target_pairs={{0,4},{4,8},{8,12},{1,5},{5,9},{9,13},{2,6},{6,10},{10,14},{3,7},{... | collective-permute-start | bytes 1572872 | tf_op jit(solution)/shard_map/ppermute | solution.py:19
  130.4 2.1 copy.36
  148.8 3.2 %fusion.131 = (f32[2,16,128]{2,1,0:T(8,128)S(1)}, f32[2,16,128,384]{3,2,1,0:T(8,128)S(1)}) fusion(f32[2,16,128,384]{3,2,1,0:T(8,128)S(1)} %fusion.20, pred[2,128,384]{2,1,0:T(8,128)(4,1)S(1)} %copy-done.19), kind=kOutput, calls=%fused_computation.218 | output fusion | flops 11010431 | bytes 12697600 | tf_op jit(solution)/shard_map/sub | solution.py:31
  171.2 3.8 %all-to-all-start = ((bf16[4,4,128,192]{2,3,1,0:T(8,128)(2,1)}), bf16[4,4,128,192]{2,3,1,0:T(8,128)(2,1)S(1)}, u32[]{:S(2)}, u32[]{:S(2)}) async-start(bf16[4,4,128,192]{2,3,1,0:T(8,128)(2,1)} %bitcast.24), calls=%async_computation | async-start | bytes 1572864 | tf_op jit(solution)/shard_map/all_to_all | solution.py:165
  179.7 15.7 %all-to-all-done = bf16[4,4,128,192]{2,3,1,0:T(8,128)(2,1)S(1)} async-done(((bf16[4,4,128,192]{2,3,1,0:T(8,128)(2,1)}), bf16[4,4,128,192]{2,3,1,0:T(8,128)(2,1)S(1)}, u32[]{:S(2)}, u32[]{:S(2)}) %all-to-all-start) | async-done | bytes 786464 | tf_op jit(solution)/shard_map/all_to_all | solution.py:165
  195.4 3.7 %all-to-all-start.2 = ((bf16[4,4,128,192]{2,3,1,0:T(8,128)(2,1)}), bf16[4,4,128,192]{2,3,1,0:T(8,128)(2,1)S(1)}, u32[]{:S(2)}, u32[]{:S(2)}) async-start(bf16[4,4,128,192]{2,3,1,0:T(8,128)(2,1)} %bitcast.164), calls=%async_computation.2 | async-start | bytes 1572864 | tf_op jit(solution)/shard_map/all_to_all | solution.py:165
  203.1 3.9 %fusion.141 = (f32[4,512]{1,0:T(4,128)S(1)}, f32[4,512,512]{1,2,0:T(8,128)}) fusion(pred[512,512]{0,1:T(8,128)(4,1)S(1)} %fusion.33, bf16[4,512,192]{1,2,0:T(8,128)(2,1)S(1)} %squeeze.57), kind=kOutput, calls=%fused_computation.220 | convolution fusion | flops 139461120 | bytes 5251072 | tf_op jit(solution)/shard_map/sub | solution.py:31
  207.1 2.7 fusion.27
  210.5 8.0 %all-to-all-done.2 = bf16[4,4,128,192]{2,3,1,0:T(8,128)(2,1)S(1)} async-done(((bf16[4,4,128,192]{2,3,1,0:T(8,128)(2,1)}), bf16[4,4,128,192]{2,3,1,0:T(8,128)(2,1)S(1)}, u32[]{:S(2)}, u32[]{:S(2)}) %all-to-all-start.2) | async-done | bytes 786464 | tf_op jit(solution)/shard_map/all_to_all | solution.py:165
  218.5 3.4 %all-to-all-start.1 = ((bf16[4,4,128,64]{2,3,1,0:T(8,128)(2,1)}), bf16[4,4,128,64]{2,3,1,0:T(8,128)(2,1)S(1)}, u32[]{:S(2)}, u32[]{:S(2)}) async-start(bf16[4,4,128,64]{2,3,1,0:T(8,128)(2,1)} %bitcast.155), calls=%async_computation.1 | async-start | bytes 524288 | tf_op jit(solution)/shard_map/all_to_all | solution.py:181
  222.8 5.0 %fusion.132 = (f32[4,512]{1,0:T(4,128)S(1)}, f32[4,512,512]{1,2,0:T(8,128)}) fusion(pred[512,512]{0,1:T(8,128)(4,1)} %fusion.32, bf16[4,512,192]{1,2,0:T(8,128)(2,1)S(1)} %squeeze.60), kind=kOutput, calls=%fused_computation.219 | convolution fusion | flops 139461120 | bytes 5251072 | tf_op jit(solution)/shard_map/sub | solution.py:31
  227.8 2.7 %fusion.28 = bf16[4,8,4,8,128]{4,3,2,1,0:T(8,128)(2,1)S(1)} fusion(f32[4,512,512]{1,2,0:T(8,128)} %get-tuple-element.41, f32[4,512]{1,0:T(4,128)S(1)} %get-tuple-element.40, bf16[4,512,192]{1,2,0:T(8,128)(2,1)S(1)} %squeeze.60), kind=kOutput, calls=%fused_computation.68 | convolution fusion | flops 136445952 | bytes 4726784 | tf_op jit(solution)/shard_map/nqk,nkd->nqd/dot_general | solution.py:175
  231.3 5.1 %all-to-all-start.3 = ((bf16[4,4,128,64]{2,3,1,0:T(8,128)(2,1)}), bf16[4,4,128,64]{2,3,1,0:T(8,128)(2,1)S(1)}, u32[]{:S(2)}, u32[]{:S(2)}) async-start(bf16[4,4,128,64]{2,3,1,0:T(8,128)(2,1)} %bitcast.153), calls=%async_computation.3 | async-start | bytes 524288 | tf_op jit(solution)/shard_map/all_to_all | solution.py:181
  237.5 6.9 %all-to-all-done.3 = bf16[4,4,128,64]{2,3,1,0:T(8,128)(2,1)S(1)} async-done(((bf16[4,4,128,64]{2,3,1,0:T(8,128)(2,1)}), bf16[4,4,128,64]{2,3,1,0:T(8,128)(2,1)S(1)}, u32[]{:S(2)}, u32[]{:S(2)}) %all-to-all-start.3) | async-done | bytes 262176 | tf_op jit(solution)/shard_map/all_to_all | solution.py:181
  251.3 2.0 collective-permute-start.18
  253.3 1.9 collective-permute-done.16
  255.9 2.4 collective-permute-start.20
  (183 shorter events, 88.6 us)
Async XLA Ops:
  7.2 59.5 %all-gather.2.cloned.1.call-start = ((), (), s32[]{:S(2)}) async-start(), calls=%async_computation.4 | async-start | bytes 1638400 | tf_op jit(solution)/shard_map/all_gather | solution.py:74
  31.7 85.6 %collective-permute-start.9 = (bf16[768,384]{1,0:T(8,128)(2,1)}, bf16[768,384]{1,0:T(8,128)(2,1)}, u32[]{:S(2)}, u32[]{:S(2)}) collective-permute-start(bf16[768,384]{1,0:T(8,128)(2,1)} %fusion.35), channel_id=1, source_target_pairs={{0,8},{4,12},{8,0},{12,4},{1,9},{5,13},{9,1},{13,5},{2,10},{6,14},... | collective-permute-start | bytes 1769480 | tf_op jit(solution)/shard_map/ppermute | solution.py:79
  33.2 111.1 %collective-permute-start.10 = (bf16[768,384]{1,0:T(8,128)(2,1)}, bf16[768,384]{1,0:T(8,128)(2,1)}, u32[]{:S(2)}, u32[]{:S(2)}) collective-permute-start(bf16[768,384]{1,0:T(8,128)(2,1)} %fusion.35), channel_id=1, source_target_pairs={{0,16},{16,0},{1,17},{17,1},{2,18},{18,2},{3,19},{19,3},{4,20},{20... | collective-permute-start | bytes 1769480 | tf_op jit(solution)/shard_map/ppermute | solution.py:79
  69.7 23.2 %collective-permute-start = (bf16[768,640]{1,0:T(8,128)(2,1)}, bf16[768,640]{1,0:T(8,128)(2,1)}, u32[]{:S(2)}, u32[]{:S(2)}) collective-permute-start(bf16[768,640]{1,0:T(8,128)(2,1)} %fusion.34), channel_id=1, source_target_pairs={{0,8},{4,12},{8,0},{12,4},{1,9},{5,13},{9,1},{13,5},{2,10},{6,14},... | collective-permute-start | bytes 2949128 | tf_op jit(solution)/shard_map/ppermute | solution.py:79
  71.9 25.1 %collective-permute-start.1 = (bf16[768,640]{1,0:T(8,128)(2,1)}, bf16[768,640]{1,0:T(8,128)(2,1)S(1)}, u32[]{:S(2)}, u32[]{:S(2)}) collective-permute-start(bf16[768,640]{1,0:T(8,128)(2,1)} %fusion.34), channel_id=1, source_target_pairs={{0,16},{16,0},{1,17},{17,1},{2,18},{18,2},{3,19},{19,3},{4,20},{20... | collective-permute-start | bytes 2949128 | tf_op jit(solution)/shard_map/ppermute | solution.py:79
  73.3 42.9 %collective-permute-start.3 = (bf16[768,640]{1,0:T(8,128)(2,1)}, bf16[768,640]{1,0:T(8,128)(2,1)S(1)}, u32[]{:S(2)}, u32[]{:S(2)}) collective-permute-start(bf16[768,640]{1,0:T(8,128)(2,1)} %fusion.34), channel_id=1, source_target_pairs={{0,4},{4,0},{8,12},{12,8},{1,5},{5,1},{9,13},{13,9},{2,6},{6,2},{1... | collective-permute-start | bytes 2949128 | tf_op jit(solution)/shard_map/ppermute | solution.py:79
  92.8 22.8 %collective-permute-start.2 = (bf16[768,640]{1,0:T(8,128)(2,1)}, bf16[768,640]{1,0:T(8,128)(2,1)S(1)}, u32[]{:S(2)}, u32[]{:S(2)}) collective-permute-start(bf16[768,640]{1,0:T(8,128)(2,1)} %collective-permute-done), channel_id=1, source_target_pairs={{0,16},{16,0},{1,17},{17,1},{2,18},{18,2},{3,19},{19,3},{4,20},{20... | collective-permute-start | bytes 2949128 | tf_op jit(solution)/shard_map/ppermute | solution.py:79
  96.9 20.5 %collective-permute-start.4 = (bf16[768,640]{1,0:T(8,128)(2,1)}, bf16[768,640]{1,0:T(8,128)(2,1)S(1)}, u32[]{:S(2)}, u32[]{:S(2)}) collective-permute-start(bf16[768,640]{1,0:T(8,128)(2,1)} %collective-permute-done), channel_id=1, source_target_pairs={{0,4},{4,0},{8,12},{12,8},{1,5},{5,1},{9,13},{13,9},{2,6},{6,2},{1... | collective-permute-start | bytes 2949128 | tf_op jit(solution)/shard_map/ppermute | solution.py:79
  117.3 46.9 %collective-permute-start.12 = (bf16[768,384]{1,0:T(8,128)(2,1)}, bf16[768,384]{1,0:T(8,128)(2,1)}, u32[]{:S(2)}, u32[]{:S(2)}) collective-permute-start(bf16[768,384]{1,0:T(8,128)(2,1)} %fusion.35), channel_id=1, source_target_pairs={{0,4},{4,0},{8,12},{12,8},{1,5},{5,1},{9,13},{13,9},{2,6},{6,2},{1... | collective-permute-start | bytes 1769480 | tf_op jit(solution)/shard_map/ppermute | solution.py:79
  117.4 27.9 %collective-permute-start.11 = (bf16[768,384]{1,0:T(8,128)(2,1)}, bf16[768,384]{1,0:T(8,128)(2,1)}, u32[]{:S(2)}, u32[]{:S(2)}) collective-permute-start(bf16[768,384]{1,0:T(8,128)(2,1)} %collective-permute-done.9), channel_id=1, source_target_pairs={{0,16},{16,0},{1,17},{17,1},{2,18},{18,2},{3,19},{19,3},{4,20},{20... | collective-permute-start | bytes 1769480 | tf_op jit(solution)/shard_map/ppermute | solution.py:79
  127.6 17.8 %collective-permute-start.7 = (bf16[128,2048]{0,1:T(8,128)(2,1)}, bf16[128,2048]{0,1:T(8,128)(2,1)}, u32[]{:S(2)}, u32[]{:S(2)}) collective-permute-start(bf16[128,2048]{0,1:T(8,128)(2,1)} %bitcast.179), channel_id=1, source_target_pairs={{0,4},{4,8},{8,12},{1,5},{5,9},{9,13},{2,6},{6,10},{10,14},{3,7},{... | collective-permute-start | bytes 1572872 | tf_op jit(solution)/shard_map/ppermute | solution.py:19
  132.5 13.4 %collective-permute-start.8 = (bf16[128,2048]{0,1:T(8,128)(2,1)}, bf16[128,2048]{0,1:T(8,128)(2,1)}, u32[]{:S(2)}, u32[]{:S(2)}) collective-permute-start(bf16[128,2048]{0,1:T(8,128)(2,1)} %bitcast.178), channel_id=1, source_target_pairs={{4,0},{8,4},{12,8},{5,1},{9,5},{13,9},{6,2},{10,6},{14,10},{7,3},{... | collective-permute-start | bytes 1572872 | tf_op jit(solution)/shard_map/ppermute | solution.py:19
  144.2 21.5 %collective-permute-start.13 = (bf16[768,384]{1,0:T(8,128)(2,1)}, bf16[768,384]{1,0:T(8,128)(2,1)S(1)}, u32[]{:S(2)}, u32[]{:S(2)}) collective-permute-start(bf16[768,384]{1,0:T(8,128)(2,1)} %collective-permute-done.9), channel_id=1, source_target_pairs={{0,4},{4,0},{8,12},{12,8},{1,5},{5,1},{9,13},{13,9},{2,6},{6,2},{1... | collective-permute-start | bytes 1769480 | tf_op jit(solution)/shard_map/ppermute | solution.py:79
  145.3 20.8 %collective-permute-start.14 = (bf16[768,384]{1,0:T(8,128)(2,1)}, bf16[768,384]{1,0:T(8,128)(2,1)S(1)}, u32[]{:S(2)}, u32[]{:S(2)}) collective-permute-start(bf16[768,384]{1,0:T(8,128)(2,1)} %collective-permute-done.10), channel_id=1, source_target_pairs={{0,4},{4,0},{8,12},{12,8},{1,5},{5,1},{9,13},{13,9},{2,6},{6,2},{1... | collective-permute-start | bytes 1769480 | tf_op jit(solution)/shard_map/ppermute | solution.py:79
  145.4 21.1 %collective-permute-start.15 = (bf16[768,384]{1,0:T(8,128)(2,1)}, bf16[768,384]{1,0:T(8,128)(2,1)S(1)}, u32[]{:S(2)}, u32[]{:S(2)}) collective-permute-start(bf16[768,384]{1,0:T(8,128)(2,1)} %collective-permute-done.11), channel_id=1, source_target_pairs={{0,4},{4,0},{8,12},{12,8},{1,5},{5,1},{9,13},{13,9},{2,6},{6,2},{1... | collective-permute-start | bytes 1769480 | tf_op jit(solution)/shard_map/ppermute | solution.py:79
  171.2 24.2 %all-to-all-start = ((bf16[4,4,128,192]{2,3,1,0:T(8,128)(2,1)}), bf16[4,4,128,192]{2,3,1,0:T(8,128)(2,1)S(1)}, u32[]{:S(2)}, u32[]{:S(2)}) async-start(bf16[4,4,128,192]{2,3,1,0:T(8,128)(2,1)} %bitcast.24), calls=%async_computation | async-start | bytes 1572864 | tf_op jit(solution)/shard_map/all_to_all | solution.py:165
  195.4 23.1 %all-to-all-start.2 = ((bf16[4,4,128,192]{2,3,1,0:T(8,128)(2,1)}), bf16[4,4,128,192]{2,3,1,0:T(8,128)(2,1)S(1)}, u32[]{:S(2)}, u32[]{:S(2)}) async-start(bf16[4,4,128,192]{2,3,1,0:T(8,128)(2,1)} %bitcast.164), calls=%async_computation.2 | async-start | bytes 1572864 | tf_op jit(solution)/shard_map/all_to_all | solution.py:165
  218.5 12.8 %all-to-all-start.1 = ((bf16[4,4,128,64]{2,3,1,0:T(8,128)(2,1)}), bf16[4,4,128,64]{2,3,1,0:T(8,128)(2,1)S(1)}, u32[]{:S(2)}, u32[]{:S(2)}) async-start(bf16[4,4,128,64]{2,3,1,0:T(8,128)(2,1)} %bitcast.155), calls=%async_computation.1 | async-start | bytes 524288 | tf_op jit(solution)/shard_map/all_to_all | solution.py:181
  231.3 13.1 %all-to-all-start.3 = ((bf16[4,4,128,64]{2,3,1,0:T(8,128)(2,1)}), bf16[4,4,128,64]{2,3,1,0:T(8,128)(2,1)S(1)}, u32[]{:S(2)}, u32[]{:S(2)}) async-start(bf16[4,4,128,64]{2,3,1,0:T(8,128)(2,1)} %bitcast.153), calls=%async_computation.3 | async-start | bytes 524288 | tf_op jit(solution)/shard_map/all_to_all | solution.py:181
  249.4 5.8 %collective-permute-start.16 = (f32[4,2,1152]{2,1,0:T(2,128)S(1)}, f32[4,2,1152]{2,1,0:T(2,128)S(1)}, u32[]{:S(2)}, u32[]{:S(2)}) collective-permute-start(f32[4,2,1152]{2,1,0:T(2,128)S(1)} %get-tuple-element.22), channel_id=1, source_target_pairs={{0,1},{1,2},{2,3},{3,0},{4,5},{5,6},{6,7},{7,4},{8,9},{9,10},{10,1... | collective-permute-start | bytes 110600 | tf_op jit(solution)/shard_map/ppermute | solution.py:295
  249.8 5.4 %collective-permute-start.17 = (f32[4,2,1152]{2,1,0:T(2,128)S(1)}, f32[4,2,1152]{2,1,0:T(2,128)S(1)}, u32[]{:S(2)}, u32[]{:S(2)}) collective-permute-start(f32[4,2,1152]{2,1,0:T(2,128)S(1)} %get-tuple-element.24), channel_id=1, source_target_pairs={{0,2},{1,3},{2,0},{3,1},{4,6},{5,7},{6,4},{7,5},{8,10},{9,11},{10,... | collective-permute-start | bytes 110600 | tf_op jit(solution)/shard_map/ppermute | solution.py:295
  251.3 4.5 %collective-permute-start.18 = (f32[4,2,1152]{2,1,0:T(2,128)S(1)}, f32[4,2,1152]{2,1,0:T(2,128)S(1)}, u32[]{:S(2)}, u32[]{:S(2)}) collective-permute-start(f32[4,2,1152]{2,1,0:T(2,128)S(1)} %get-tuple-element.23), channel_id=1, source_target_pairs={{0,3},{1,0},{2,1},{3,2},{4,7},{5,4},{6,5},{7,6},{8,11},{9,8},{10,9... | collective-permute-start | bytes 110600 | tf_op jit(solution)/shard_map/ppermute | solution.py:295
  255.9 5.7 %collective-permute-start.19 = (f32[2,1152]{1,0:T(2,128)S(1)}, f32[2,1152]{1,0:T(2,128)S(1)}, u32[]{:S(2)}, u32[]{:S(2)}) collective-permute-start(f32[2,1152]{1,0:T(2,128)S(1)} %get-tuple-element.25), channel_id=1, source_target_pairs={{0,4},{4,8},{8,12},{12,0},{1,5},{5,9},{9,13},{13,1},{2,6},{6,10},{... | collective-permute-start | bytes 27656 | tf_op jit(solution)/shard_map/ppermute | solution.py:302
  255.9 5.6 %collective-permute-start.20 = (f32[2,1152]{1,0:T(2,128)S(1)}, f32[2,1152]{1,0:T(2,128)S(1)}, u32[]{:S(2)}, u32[]{:S(2)}) collective-permute-start(f32[2,1152]{1,0:T(2,128)S(1)} %get-tuple-element.27), channel_id=1, source_target_pairs={{0,8},{4,12},{8,0},{12,4},{1,9},{5,13},{9,1},{13,5},{2,10},{6,14},... | collective-permute-start | bytes 27656 | tf_op jit(solution)/shard_map/ppermute | solution.py:302
  (26 other events, 207.7 us)
Sparse Core Ops, SparseCore 0:
  36.5 30.1 all-gather.1

commit v12 on v10

--- a/solution.py
+++ b/solution.py
@@ -55,9 +55,11 @@
     return lax.dynamic_slice_in_dim(doubled, start, (plane_count - 1) * block, axis=axis)
 
 
-def gather_pieces(shards, swap_first=False):
+def gather_pieces(shards, swap_first=False, skip_middle=False):
     levels = replica_levels()
-    if swap_first and len(levels) == 3:
+    if skip_middle and len(levels) == 3:
+        levels = [levels[0], levels[2]]
+    elif swap_first and len(levels) == 3:
         levels = [levels[1], levels[0], levels[2]]
     count = 2 ** len(levels)
     widths = [shard.shape[1] // count for shard in shards]
@@ -198,7 +200,7 @@
     own_valid = near_valid[1 : sec_block + 1]
     score_scale = 1.0 / math.sqrt(HEAD_DIM)
     cross_qkv_pieces, cross_out_pieces = gather_pieces([cross_qkv, cross_out], swap_first=True)
-    plane_qkv_pieces, plane_out_pieces = gather_pieces([plane_qkv, plane_out], swap_first=True)
+    plane_qkv_pieces, plane_out_pieces = gather_pieces([plane_qkv, plane_out], skip_middle=True)
     cross_out_pieces = assemble(cross_out_pieces)
     plane_out_pieces = assemble(plane_out_pieces)
     normed = rms_norm(tokens, norm_gains[0])

time: 259 us -> 257 us (level)
  waiting for transfers between devices: 102 us -> 77.9 us
  matrix products: 40.9 us -> 53.1 us
  local copies, waits for them, and re-layouts: 42.1 us -> 51.7 us
    ppermute x14 -> x10, waiting for transfers between devices: 27.9 us -> 9.78 us  [gather_pieces(): lax.ppermute(block, axis, swap)]
    dot_general x16 -> x12, matrix products: 14.9 us -> 22.8 us  [project(): part = jnp.dot(remote_inputs, block, preferred_element_type=jnp.float32)]
    all_gather x2, waiting for transfers between devices: 45.7 us -> 42.4 us  [gather_pieces(): gathered = lax.all_gather(mine, 'plane', axis=0, tiled=True)]
    all_to_all x2, local copies, waits for them, and re-layouts: 2.11 us -> 5.24 us  [attend_by_section(): lax.all_to_all(outgoing, 'plane', split_axis=0, concat_axis=2, tiled=True)]
    squeeze x2, local copies, waits for them, and re-layouts: 1.95 us -> 4.72 us  [attend_by_section(): lax.all_to_all(outgoing, 'plane', split_axis=0, concat_axis=2, tiled=True)]
    ppermute x14 -> x10, starting transfers between devices: 10.6 us -> 8.5 us  [gather_pieces(): lax.ppermute(block, axis, swap)]
    dynamic_update_slice x16 -> x12, local copies, waits for them, and re-layouts: 15.4 us -> 14.1 us  [assemble(): lax.dynamic_update_slice_in_dim(remote, block, piece * width, axis=1)]
    unnamed x50 -> x40, local copies, waits for them, and re-layouts: 6.92 us -> 8.08 us
  transfers between devices with their start and end apart: 28 -> 24, of which waited for: 8 -> 8; matrix products, arithmetic and copies ran while one was open for 35% -> 44% of each run, Pallas kernels for 0% -> 0%
where the time goes in v12:
time: 257 us; the launch traced here: 254 us
  waiting for transfers between devices  77.9 us (30%)
  matrix products  53.1 us (21%)
  local copies, waits for them, and re-layouts  51.7 us (20%)
  starting transfers between devices  36.3 us (14%)
  other arithmetic  20.1 us (8%)
  between operations  15.3 us (6%)
    all_gather x2, waiting for transfers between devices, gather_pieces(): gathered = lax.all_gather(mine, 'plane', axis=0, tiled=True)  42.4 us
    dot_general x12, matrix products, project(): part = jnp.dot(remote_inputs, block, preferred_element_type=jnp.float32)  22.8 us
    all_to_all x2, waiting for transfers between devices, attend_by_section(): lax.all_to_all(outgoing, 'plane', split_axis=0, concat_axis=2, tiled=True)  18.2 us
    dynamic_update_slice x12, local copies, waits for them, and re-layouts, assemble(): lax.dynamic_update_slice_in_dim(remote, block, piece * width, axis=1)  14.1 us
    sub x2, matrix products, masked_softmax(): expo = jnp.where(allowed, jnp.exp(shifted - top), 0.0)  10.1 us
    ppermute x10, waiting for transfers between devices, gather_pieces(): lax.ppermute(block, axis, swap)  9.78 us
    all_to_all x2, starting transfers between devices, attend_by_section(): lax.all_to_all(outgoing, 'plane', split_axis=0, concat_axis=2, tiled=True)  8.61 us
    ppermute x10, starting transfers between devices, gather_pieces(): lax.ppermute(block, axis, swap)  8.5 us
  transfers between devices with their start and end apart: 24, of which 8 were waited for; matrix products, arithmetic and copies ran while one was open for 44% of the time, Pallas kernels for 0%

profile of v12, /device:TPU:0, one launch (start us, length us, event | category | flops | bytes accessed | tf_op | source)
XLA Modules:
  0.0 254.5 jit_solution(7889174731835754497)
XLA Ops:
  14.9 25.9 %all-gather.3.cloned.1.call-done = bf16[1024,512]{1,0:T(8,128)(2,1)} async-done(((bf16[256,512]{1,0:T(8,128)(2,1)}), bf16[1024,512]{1,0:T(8,128)(2,1)}) %all-gather.3.cloned.1.call-update) | async-done | bytes 1048592 | tf_op jit(solution)/shard_map/all_gather | solution.py:76
  40.8 2.6 %fusion.39 = bf16[768,512]{1,0:T(8,128)(2,1)} fusion(s32[]{:T(128)S(6)} %select_n.244, bf16[1024,512]{1,0:T(8,128)(2,1)} %all-gather.3.cloned.1.call-done), kind=kLoop, calls=%fused_computation.86 | loop fusion | flops 1572864 | bytes 1835012 | tf_op jit(solution)/shard_map/concatenate | solution.py:54
  53.1 9.8 %collective-permute-done = bf16[768,512]{1,0:T(8,128)(2,1)} collective-permute-done((bf16[768,512]{1,0:T(8,128)(2,1)}, bf16[768,512]{1,0:T(8,128)(2,1)}, u32[]{:S(2)}, u32[]{:S(2)}) %collective-permute-start) | collective-permute-done | bytes 786464 | tf_op jit(solution)/shard_map/ppermute | solution.py:81
  71.3 16.5 %all-gather.5.cloned.1.call-done = bf16[1024,1024]{1,0:T(8,128)(2,1)} async-done(((bf16[256,1024]{1,0:T(8,128)(2,1)}), bf16[1024,1024]{1,0:T(8,128)(2,1)}) %all-gather.5.cloned.1.call-update) | async-done | bytes 2097168 | tf_op jit(solution)/shard_map/all_gather | solution.py:76
  87.8 3.9 %fusion.20 = bf16[768,1024]{1,0:T(8,128)(2,1)} fusion(s32[]{:T(128)S(6)} %select_n.244, bf16[1024,1024]{1,0:T(8,128)(2,1)} %all-gather.5.cloned.1.call-done), kind=kLoop, calls=%fused_computation.37 | loop fusion | flops 3145728 | bytes 3670020 | tf_op jit(solution)/shard_map/concatenate | solution.py:54
  98.1 2.7 %convolution_dynamic-update-slice_fusion.7 = f32[256,3072]{1,0:T(8,128)} fusion(f32[256,3072]{1,0:T(8,128)} %convolution_dynamic-update-slice_fusion.8, s32[]{:T(128)S(6)} %select_n.261, bf16[256,768]{1,0:T(8,128)(2,1)S(1)} %fusion.55, bf16[768,512]{1,0:T(8,128)(2,1)} %collective-permute-done.3), kind=kOutput, calls=%fused_computation.54 | convolution fusion | flops 150994944 | bytes 1376260 | tf_op jit(solution)/shard_map/dot_general | solution.py:100
  107.2 2.6 %fusion.4 = bf16[256,3072]{1,0:T(8,128)(2,1)S(1)} fusion(f32[256,3072]{1,0:T(8,128)} %convolution_dynamic-update-slice_fusion.4, bf16[256,3072]{1,0:T(8,128)(2,1)S(1)} %copy-done.7, bf16[256,1024]{1,0:T(8,128)(2,1)} %bitcast.154, s32[]{:T(128)S(6)} %select_n.243), kind=kOutput, calls=%fused_computation.17 | convolution fusion | flops 404226048 | bytes 6422532 | tf_op jit(solution)/shard_map/dot_general | solution.py:96
  112.9 2.7 %collective-permute-start.7 = (bf16[128,2048]{0,1:T(8,128)(2,1)}, bf16[128,2048]{0,1:T(8,128)(2,1)}, u32[]{:S(2)}, u32[]{:S(2)}) collective-permute-start(bf16[128,2048]{0,1:T(8,128)(2,1)} %bitcast.165), channel_id=1, source_target_pairs={{0,4},{4,8},{8,12},{1,5},{5,9},{9,13},{2,6},{6,10},{10,14},{3,7},{... | collective-permute-start | bytes 1572872 | tf_op jit(solution)/shard_map/ppermute | solution.py:19
  131.8 3.2 %fusion.135 = (f32[2,16,128]{2,1,0:T(8,128)S(1)}, f32[2,16,128,384]{3,2,1,0:T(8,128)S(1)}) fusion(f32[2,16,128,384]{3,2,1,0:T(8,128)S(1)} %fusion.21, pred[2,128,384]{2,1,0:T(8,128)(4,1)S(1)} %copy-done.12), kind=kOutput, calls=%fused_computation.215 | output fusion | flops 11010431 | bytes 12697600 | tf_op jit(solution)/shard_map/sub | solution.py:31
  150.5 4.2 %all-to-all-start = ((bf16[4,4,128,192]{2,3,1,0:T(8,128)(2,1)}), bf16[4,4,128,192]{2,3,1,0:T(8,128)(2,1)}, u32[]{:S(2)}, u32[]{:S(2)}) async-start(bf16[4,4,128,192]{2,3,1,0:T(8,128)(2,1)} %bitcast.24), calls=%async_computation | async-start | bytes 1572864 | tf_op jit(solution)/shard_map/all_to_all | solution.py:167
  163.1 12.7 %all-to-all-done = bf16[4,4,128,192]{2,3,1,0:T(8,128)(2,1)} async-done(((bf16[4,4,128,192]{2,3,1,0:T(8,128)(2,1)}), bf16[4,4,128,192]{2,3,1,0:T(8,128)(2,1)}, u32[]{:S(2)}, u32[]{:S(2)}) %all-to-all-start) | async-done | bytes 786464 | tf_op jit(solution)/shard_map/all_to_all | solution.py:167
  175.8 4.4 %all-to-all-start.2 = ((bf16[4,4,128,192]{2,3,1,0:T(8,128)(2,1)}), bf16[4,4,128,192]{2,3,1,0:T(8,128)(2,1)}, u32[]{:S(2)}, u32[]{:S(2)}) async-start(bf16[4,4,128,192]{2,3,1,0:T(8,128)(2,1)} %bitcast.150), calls=%async_computation.2 | async-start | bytes 1572864 | tf_op jit(solution)/shard_map/all_to_all | solution.py:167
  181.2 2.6 %copy.23 = bf16[1,4,4,128,192]{3,2,4,1,0:T(4,128)(2,1)} copy(bf16[1,4,4,128,192]{3,4,1,2,0:T(8,128)(2,1)} %bitcast.26) | data formatting | bytes 1572864 | tf_op jit(solution)/shard_map/all_to_all | solution.py:167
  183.9 2.4 squeeze.57
  186.3 5.0 %fusion.145 = (f32[4,512]{1,0:T(4,128)S(1)}, f32[4,512,512]{1,2,0:T(8,128)}) fusion(pred[512,512]{0,1:T(8,128)(4,1)S(1)} %fusion.38, bf16[4,512,192]{1,2,0:T(8,128)(2,1)} %squeeze.57), kind=kOutput, calls=%fused_computation.217 | convolution fusion | flops 139461120 | bytes 5251072 | tf_op jit(solution)/shard_map/sub | solution.py:31
  191.2 2.8 %fusion.32 = bf16[4,8,4,8,128]{4,3,2,1,0:T(8,128)(2,1)S(1)} fusion(f32[4,512,512]{1,2,0:T(8,128)} %get-tuple-element.29, f32[4,512]{1,0:T(4,128)S(1)} %get-tuple-element.28, bf16[4,512,192]{1,2,0:T(8,128)(2,1)} %squeeze.57), kind=kOutput, calls=%fused_computation.68 | convolution fusion | flops 136445952 | bytes 4726784 | tf_op jit(solution)/shard_map/nqk,nkd->nqd/dot_general | solution.py:177
  194.8 5.5 %all-to-all-done.2 = bf16[4,4,128,192]{2,3,1,0:T(8,128)(2,1)} async-done(((bf16[4,4,128,192]{2,3,1,0:T(8,128)(2,1)}), bf16[4,4,128,192]{2,3,1,0:T(8,128)(2,1)}, u32[]{:S(2)}, u32[]{:S(2)}) %all-to-all-start.2) | async-done | bytes 786464 | tf_op jit(solution)/shard_map/all_to_all | solution.py:167
  200.3 3.4 %all-to-all-start.1 = ((bf16[4,4,128,64]{2,3,1,0:T(8,128)(2,1)}), bf16[4,4,128,64]{2,3,1,0:T(8,128)(2,1)S(1)}, u32[]{:S(2)}, u32[]{:S(2)}) async-start(bf16[4,4,128,64]{2,3,1,0:T(8,128)(2,1)} %bitcast.160), calls=%async_computation.1 | async-start | bytes 524288 | tf_op jit(solution)/shard_map/all_to_all | solution.py:183
  203.7 2.6 %copy.28 = bf16[1,4,4,128,192]{3,2,4,1,0:T(4,128)(2,1)} copy(bf16[1,4,4,128,192]{3,4,1,2,0:T(8,128)(2,1)} %bitcast.38) | data formatting | bytes 1572864 | tf_op jit(solution)/shard_map/all_to_all | solution.py:167
  206.3 2.3 squeeze.60
  208.7 5.1 %fusion.136 = (f32[4,512]{1,0:T(4,128)S(1)}, f32[4,512,512]{1,2,0:T(8,128)}) fusion(pred[512,512]{0,1:T(8,128)(4,1)} %fusion.37, bf16[4,512,192]{1,2,0:T(8,128)(2,1)} %squeeze.60), kind=kOutput, calls=%fused_computation.216 | convolution fusion | flops 139461120 | bytes 5251072 | tf_op jit(solution)/shard_map/sub | solution.py:31
  213.8 2.8 %fusion.33 = bf16[4,8,4,8,128]{4,3,2,1,0:T(8,128)(2,1)S(1)} fusion(f32[4,512,512]{1,2,0:T(8,128)} %get-tuple-element.27, f32[4,512]{1,0:T(4,128)S(1)} %get-tuple-element.26, bf16[4,512,192]{1,2,0:T(8,128)(2,1)} %squeeze.60), kind=kOutput, calls=%fused_computation.69 | convolution fusion | flops 136445952 | bytes 4726784 | tf_op jit(solution)/shard_map/nqk,nkd->nqd/dot_general | solution.py:177
  217.3 5.1 %all-to-all-start.3 = ((bf16[4,4,128,64]{2,3,1,0:T(8,128)(2,1)}), bf16[4,4,128,64]{2,3,1,0:T(8,128)(2,1)}, u32[]{:S(2)}, u32[]{:S(2)}) async-start(bf16[4,4,128,64]{2,3,1,0:T(8,128)(2,1)} %bitcast.161), calls=%async_computation.3 | async-start | bytes 524288 | tf_op jit(solution)/shard_map/all_to_all | solution.py:183
  225.5 5.0 %all-to-all-done.3 = bf16[4,4,128,64]{2,3,1,0:T(8,128)(2,1)} async-done(((bf16[4,4,128,64]{2,3,1,0:T(8,128)(2,1)}), bf16[4,4,128,64]{2,3,1,0:T(8,128)(2,1)}, u32[]{:S(2)}, u32[]{:S(2)}) %all-to-all-start.3) | async-done | bytes 262176 | tf_op jit(solution)/shard_map/all_to_all | solution.py:183
  (168 shorter events, 103.3 us)
Async XLA Ops:
  7.2 33.6 %all-gather.3.cloned.1.call-start = ((), (), s32[]{:S(2)}) async-start(), calls=%async_computation.4 | async-start | bytes 1310720 | tf_op jit(solution)/shard_map/all_gather | solution.py:76
  10.0 77.8 %all-gather.5.cloned.1.call-start = ((), (), s32[]{:S(2)}) async-start(), calls=%async_computation.5 | async-start | bytes 2621440 | tf_op jit(solution)/shard_map/all_gather | solution.py:76
  43.4 19.5 %collective-permute-start = (bf16[768,512]{1,0:T(8,128)(2,1)}, bf16[768,512]{1,0:T(8,128)(2,1)}, u32[]{:S(2)}, u32[]{:S(2)}) collective-permute-start(bf16[768,512]{1,0:T(8,128)(2,1)} %fusion.39), channel_id=1, source_target_pairs={{0,8},{4,12},{8,0},{12,4},{1,9},{5,13},{9,1},{13,5},{2,10},{6,14},... | collective-permute-start | bytes 2359304 | tf_op jit(solution)/shard_map/ppermute | solution.py:81
  44.9 19.5 %collective-permute-start.1 = (bf16[768,512]{1,0:T(8,128)(2,1)}, bf16[768,512]{1,0:T(8,128)(2,1)}, u32[]{:S(2)}, u32[]{:S(2)}) collective-permute-start(bf16[768,512]{1,0:T(8,128)(2,1)} %fusion.39), channel_id=1, source_target_pairs={{0,16},{16,0},{1,17},{17,1},{2,18},{18,2},{3,19},{19,3},{4,20},{20... | collective-permute-start | bytes 2359304 | tf_op jit(solution)/shard_map/ppermute | solution.py:81
  47.7 48.8 %collective-permute-start.3 = (bf16[768,512]{1,0:T(8,128)(2,1)}, bf16[768,512]{1,0:T(8,128)(2,1)}, u32[]{:S(2)}, u32[]{:S(2)}) collective-permute-start(bf16[768,512]{1,0:T(8,128)(2,1)} %fusion.39), channel_id=1, source_target_pairs={{0,4},{4,0},{8,12},{12,8},{1,5},{5,1},{9,13},{13,9},{2,6},{6,2},{1... | collective-permute-start | bytes 2359304 | tf_op jit(solution)/shard_map/ppermute | solution.py:81
  62.9 30.3 %collective-permute-start.2 = (bf16[768,512]{1,0:T(8,128)(2,1)}, bf16[768,512]{1,0:T(8,128)(2,1)}, u32[]{:S(2)}, u32[]{:S(2)}) collective-permute-start(bf16[768,512]{1,0:T(8,128)(2,1)} %collective-permute-done), channel_id=1, source_target_pairs={{0,16},{16,0},{1,17},{17,1},{2,18},{18,2},{3,19},{19,3},{4,20},{20... | collective-permute-start | bytes 2359304 | tf_op jit(solution)/shard_map/ppermute | solution.py:81
  64.3 36.4 %collective-permute-start.4 = (bf16[768,512]{1,0:T(8,128)(2,1)}, bf16[768,512]{1,0:T(8,128)(2,1)}, u32[]{:S(2)}, u32[]{:S(2)}) collective-permute-start(bf16[768,512]{1,0:T(8,128)(2,1)} %collective-permute-done), channel_id=1, source_target_pairs={{0,4},{4,0},{8,12},{12,8},{1,5},{5,1},{9,13},{13,9},{2,6},{6,2},{1... | collective-permute-start | bytes 2359304 | tf_op jit(solution)/shard_map/ppermute | solution.py:81
  64.4 38.6 %collective-permute-start.5 = (bf16[768,512]{1,0:T(8,128)(2,1)}, bf16[768,512]{1,0:T(8,128)(2,1)}, u32[]{:S(2)}, u32[]{:S(2)}) collective-permute-start(bf16[768,512]{1,0:T(8,128)(2,1)} %collective-permute-done.1), channel_id=1, source_target_pairs={{0,4},{4,0},{8,12},{12,8},{1,5},{5,1},{9,13},{13,9},{2,6},{6,2},{1... | collective-permute-start | bytes 2359304 | tf_op jit(solution)/shard_map/ppermute | solution.py:81
  91.7 46.2 %collective-permute-start.9 = (bf16[768,1024]{1,0:T(8,128)(2,1)}, bf16[768,1024]{1,0:T(8,128)(2,1)}, u32[]{:S(2)}, u32[]{:S(2)}) collective-permute-start(bf16[768,1024]{1,0:T(8,128)(2,1)} %fusion.20), channel_id=1, source_target_pairs={{0,16},{16,0},{1,17},{17,1},{2,18},{18,2},{3,19},{19,3},{4,20},{20... | collective-permute-start | bytes 4718600 | tf_op jit(solution)/shard_map/ppermute | solution.py:81
  93.2 52.0 %collective-permute-start.10 = (bf16[768,1024]{1,0:T(8,128)(2,1)}, bf16[768,1024]{1,0:T(8,128)(2,1)}, u32[]{:S(2)}, u32[]{:S(2)}) collective-permute-start(bf16[768,1024]{1,0:T(8,128)(2,1)} %fusion.20), channel_id=1, source_target_pairs={{0,4},{4,0},{8,12},{12,8},{1,5},{5,1},{9,13},{13,9},{2,6},{6,2},{1... | collective-permute-start | bytes 4718600 | tf_op jit(solution)/shard_map/ppermute | solution.py:81
  96.5 8.6 %collective-permute-start.6 = (bf16[768,512]{1,0:T(8,128)(2,1)}, bf16[768,512]{1,0:T(8,128)(2,1)S(1)}, u32[]{:S(2)}, u32[]{:S(2)}) collective-permute-start(bf16[768,512]{1,0:T(8,128)(2,1)} %collective-permute-done.2), channel_id=1, source_target_pairs={{0,4},{4,0},{8,12},{12,8},{1,5},{5,1},{9,13},{13,9},{2,6},{6,2},{1... | collective-permute-start | bytes 2359304 | tf_op jit(solution)/shard_map/ppermute | solution.py:81
  112.9 16.0 %collective-permute-start.7 = (bf16[128,2048]{0,1:T(8,128)(2,1)}, bf16[128,2048]{0,1:T(8,128)(2,1)}, u32[]{:S(2)}, u32[]{:S(2)}) collective-permute-start(bf16[128,2048]{0,1:T(8,128)(2,1)} %bitcast.165), channel_id=1, source_target_pairs={{0,4},{4,8},{8,12},{1,5},{5,9},{9,13},{2,6},{6,10},{10,14},{3,7},{... | collective-permute-start | bytes 1572872 | tf_op jit(solution)/shard_map/ppermute | solution.py:19
  117.7 11.2 %collective-permute-start.8 = (bf16[128,2048]{0,1:T(8,128)(2,1)}, bf16[128,2048]{0,1:T(8,128)(2,1)}, u32[]{:S(2)}, u32[]{:S(2)}) collective-permute-start(bf16[128,2048]{0,1:T(8,128)(2,1)} %bitcast.166), channel_id=1, source_target_pairs={{4,0},{8,4},{12,8},{5,1},{9,5},{13,9},{6,2},{10,6},{14,10},{7,3},{... | collective-permute-start | bytes 1572872 | tf_op jit(solution)/shard_map/ppermute | solution.py:19
  137.9 9.0 %collective-permute-start.11 = (bf16[768,1024]{1,0:T(8,128)(2,1)}, bf16[768,1024]{1,0:T(8,128)(2,1)S(1)}, u32[]{:S(2)}, u32[]{:S(2)}) collective-permute-start(bf16[768,1024]{1,0:T(8,128)(2,1)} %collective-permute-done.9), channel_id=1, source_target_pairs={{0,4},{4,0},{8,12},{12,8},{1,5},{5,1},{9,13},{13,9},{2,6},{6,2},{1... | collective-permute-start | bytes 4718600 | tf_op jit(solution)/shard_map/ppermute | solution.py:81
  150.5 25.3 %all-to-all-start = ((bf16[4,4,128,192]{2,3,1,0:T(8,128)(2,1)}), bf16[4,4,128,192]{2,3,1,0:T(8,128)(2,1)}, u32[]{:S(2)}, u32[]{:S(2)}) async-start(bf16[4,4,128,192]{2,3,1,0:T(8,128)(2,1)} %bitcast.24), calls=%async_computation | async-start | bytes 1572864 | tf_op jit(solution)/shard_map/all_to_all | solution.py:167
  175.8 24.5 %all-to-all-start.2 = ((bf16[4,4,128,192]{2,3,1,0:T(8,128)(2,1)}), bf16[4,4,128,192]{2,3,1,0:T(8,128)(2,1)}, u32[]{:S(2)}, u32[]{:S(2)}) async-start(bf16[4,4,128,192]{2,3,1,0:T(8,128)(2,1)} %bitcast.150), calls=%async_computation.2 | async-start | bytes 1572864 | tf_op jit(solution)/shard_map/all_to_all | solution.py:167
  200.3 17.0 %all-to-all-start.1 = ((bf16[4,4,128,64]{2,3,1,0:T(8,128)(2,1)}), bf16[4,4,128,64]{2,3,1,0:T(8,128)(2,1)S(1)}, u32[]{:S(2)}, u32[]{:S(2)}) async-start(bf16[4,4,128,64]{2,3,1,0:T(8,128)(2,1)} %bitcast.160), calls=%async_computation.1 | async-start | bytes 524288 | tf_op jit(solution)/shard_map/all_to_all | solution.py:183
  217.3 13.2 %all-to-all-start.3 = ((bf16[4,4,128,64]{2,3,1,0:T(8,128)(2,1)}), bf16[4,4,128,64]{2,3,1,0:T(8,128)(2,1)}, u32[]{:S(2)}, u32[]{:S(2)}) async-start(bf16[4,4,128,64]{2,3,1,0:T(8,128)(2,1)} %bitcast.161), calls=%async_computation.3 | async-start | bytes 524288 | tf_op jit(solution)/shard_map/all_to_all | solution.py:183
  236.1 5.8 %collective-permute-start.12 = (f32[4,2,1152]{2,1,0:T(2,128)S(1)}, f32[4,2,1152]{2,1,0:T(2,128)S(1)}, u32[]{:S(2)}, u32[]{:S(2)}) collective-permute-start(f32[4,2,1152]{2,1,0:T(2,128)S(1)} %get-tuple-element.8), channel_id=1, source_target_pairs={{0,1},{1,2},{2,3},{3,0},{4,5},{5,6},{6,7},{7,4},{8,9},{9,10},{10,1... | collective-permute-start | bytes 110600 | tf_op jit(solution)/shard_map/ppermute | solution.py:295
  236.4 5.5 %collective-permute-start.13 = (f32[4,2,1152]{2,1,0:T(2,128)S(1)}, f32[4,2,1152]{2,1,0:T(2,128)S(1)}, u32[]{:S(2)}, u32[]{:S(2)}) collective-permute-start(f32[4,2,1152]{2,1,0:T(2,128)S(1)} %get-tuple-element.10), channel_id=1, source_target_pairs={{0,2},{1,3},{2,0},{3,1},{4,6},{5,7},{6,4},{7,5},{8,10},{9,11},{10,... | collective-permute-start | bytes 110600 | tf_op jit(solution)/shard_map/ppermute | solution.py:295
  237.9 4.5 %collective-permute-start.14 = (f32[4,2,1152]{2,1,0:T(2,128)S(1)}, f32[4,2,1152]{2,1,0:T(2,128)S(1)}, u32[]{:S(2)}, u32[]{:S(2)}) collective-permute-start(f32[4,2,1152]{2,1,0:T(2,128)S(1)} %get-tuple-element.9), channel_id=1, source_target_pairs={{0,3},{1,0},{2,1},{3,2},{4,7},{5,4},{6,5},{7,6},{8,11},{9,8},{10,9... | collective-permute-start | bytes 110600 | tf_op jit(solution)/shard_map/ppermute | solution.py:295
  242.5 4.3 %collective-permute-start.15 = (f32[2,1152]{1,0:T(2,128)S(1)}, f32[2,1152]{1,0:T(2,128)S(1)}, u32[]{:S(2)}, u32[]{:S(2)}) collective-permute-start(f32[2,1152]{1,0:T(2,128)S(1)} %get-tuple-element.11), channel_id=1, source_target_pairs={{0,4},{4,8},{8,12},{12,0},{1,5},{5,9},{9,13},{13,1},{2,6},{6,10},{... | collective-permute-start | bytes 27656 | tf_op jit(solution)/shard_map/ppermute | solution.py:302
  242.6 4.2 %collective-permute-start.16 = (f32[2,1152]{1,0:T(2,128)S(1)}, f32[2,1152]{1,0:T(2,128)S(1)}, u32[]{:S(2)}, u32[]{:S(2)}) collective-permute-start(f32[2,1152]{1,0:T(2,128)S(1)} %get-tuple-element.13), channel_id=1, source_target_pairs={{0,8},{4,12},{8,0},{12,4},{1,9},{5,13},{9,1},{13,5},{2,10},{6,14},... | collective-permute-start | bytes 27656 | tf_op jit(solution)/shard_map/ppermute | solution.py:302
  243.6 3.2 %collective-permute-start.17 = (f32[2,1152]{1,0:T(2,128)S(1)}, f32[2,1152]{1,0:T(2,128)S(1)}, u32[]{:S(2)}, u32[]{:S(2)}) collective-permute-start(f32[2,1152]{1,0:T(2,128)S(1)} %get-tuple-element.12), channel_id=1, source_target_pairs={{0,12},{4,0},{8,4},{12,8},{1,13},{5,1},{9,5},{13,9},{2,14},{6,2},{... | collective-permute-start | bytes 27656 | tf_op jit(solution)/shard_map/ppermute | solution.py:302
  (18 other events, 77.8 us)
Sparse Core Ops, SparseCore 0:
  10.1 30.6 all-gather.2
  42.3 45.3 all-gather.4

commit v13 on v12

--- a/solution.py
+++ b/solution.py
@@ -152,7 +152,7 @@
 
 
 def attend_by_section(projected, counts, plane_count):
-    sec_block, tok_block = projected.shape[0], projected.shape[1]
+    sec_block, tok_block = len(projected), projected[0].shape[0]
     share = HEADS // plane_count
     seq_len = plane_count * tok_block
     score_scale = 1.0 / math.sqrt(HEAD_DIM)
@@ -240,11 +240,17 @@
         jnp.bfloat16
     )
     normed = rms_norm(after_cross, norm_gains[1])
-    result = project(normed, plane_qkv_pieces)
-    projected = result.astype(jnp.bfloat16).reshape(sec_block, tok_block, 3, HEADS, HEAD_DIM)
     if HEADS % plane_count == 0:
+        projected = [
+            project(normed[local * tok_block : (local + 1) * tok_block], plane_qkv_pieces)
+            .astype(jnp.bfloat16)
+            .reshape(tok_block, 3, HEADS, HEAD_DIM)
+            for local in range(sec_block)
+        ]
         contexts = attend_by_section(projected, counts, plane_count)
     else:
+        result = project(normed, plane_qkv_pieces)
+        projected = result.astype(jnp.bfloat16).reshape(sec_block, tok_block, 3, HEADS, HEAD_DIM)
         per_device = sec_block * HEADS // plane_count
         heads_first = jnp.transpose(projected, (0, 3, 1, 2, 4)).reshape(
             plane_count, per_device, tok_block, 3 * HEAD_DIM

time: 257 us -> 267 us (1.039)
  matrix products: 53.1 us -> 64.1 us
  waiting for transfers between devices: 77.9 us -> 70.3 us
  local copies, waits for them, and re-layouts: 51.7 us -> 57.2 us
    all_to_all x2, waiting for transfers between devices: 18.2 us -> 11.3 us  [attend_by_section(): lax.all_to_all(outgoing, 'plane', split_axis=0, concat_axis=2, tiled=True)]
    dot_general x12 -> x16, matrix products: 22.8 us -> 29.2 us  [project(): part = jnp.dot(remote_inputs, block, preferred_element_type=jnp.float32)]
    convert_element_type x0 -> x2, local copies, waits for them, and re-layouts: none -> 4.59 us  [body(): projected = [project(normed[local * tok_block:(local + 1) * tok_block], p...]
    slice x3 -> x1, local copies, waits for them, and re-layouts: 3.67 us -> 0.04 us  [body(): normed[local * tok_block:(local + 1) * tok_block]]
    dot_general x2 -> x3, matrix products: 3.2 us -> 6.49 us  [project(): local = jnp.dot(local_inputs, shard, preferred_element_type=jnp.float32)]
    unnamed x40 -> x50, local copies, waits for them, and re-layouts: 8.08 us -> 8.23 us
  transfers between devices with their start and end apart: 24 -> 24, of which waited for: 8 -> 8; matrix products, arithmetic and copies ran while one was open for 44% -> 46% of each run, Pallas kernels for 0% -> 0%
where the time goes in v13:
time: 267 us; the launch traced here: 264 us
  waiting for transfers between devices  70.3 us (26%)
  matrix products  64.1 us (24%)
  local copies, waits for them, and re-layouts  57.2 us (21%)
  starting transfers between devices  37.8 us (14%)
  other arithmetic  19.6 us (7%)
  between operations  15.3 us (6%)
    all_gather x2, waiting for transfers between devices, gather_pieces(): gathered = lax.all_gather(mine, 'plane', axis=0, tiled=True)  41.9 us
    dot_general x16, matrix products, project(): part = jnp.dot(remote_inputs, block, preferred_element_type=jnp.float32)  29.2 us
    dynamic_update_slice x12, local copies, waits for them, and re-layouts, assemble(): lax.dynamic_update_slice_in_dim(remote, block, piece * width, axis=1)  16.4 us
    all_to_all x2, waiting for transfers between devices, attend_by_section(): lax.all_to_all(outgoing, 'plane', split_axis=0, concat_axis=2, tiled=True)  11.3 us
    sub x2, matrix products, masked_softmax(): expo = jnp.where(allowed, jnp.exp(shifted - top), 0.0)  10.1 us
    ppermute x10, waiting for transfers between devices, gather_pieces(): lax.ppermute(block, axis, swap)  9.63 us
    all_to_all x2, starting transfers between devices, attend_by_section(): lax.all_to_all(outgoing, 'plane', split_axis=0, concat_axis=2, tiled=True)  8.58 us
    all_to_all x2, starting transfers between devices, attend_by_section(): lax.all_to_all(homeward, 'plane', split_axis=0, concat_axis=1, tiled=True)  8.46 us
  transfers between devices with their start and end apart: 24, of which 8 were waited for; matrix products, arithmetic and copies ran while one was open for 46% of the time, Pallas kernels for 0%

profile of v13, /device:TPU:0, one launch (start us, length us, event | category | flops | bytes accessed | tf_op | source)
XLA Modules:
  0.0 264.4 jit_solution(11935456949402057171)
XLA Ops:
  15.7 25.1 %all-gather.3.cloned.1.call-done = bf16[1024,512]{1,0:T(8,128)(2,1)} async-done(((bf16[256,512]{1,0:T(8,128)(2,1)}), bf16[1024,512]{1,0:T(8,128)(2,1)}) %all-gather.3.cloned.1.call-update) | async-done | bytes 1048592 | tf_op jit(solution)/shard_map/all_gather | solution.py:76
  52.1 9.6 %collective-permute-done = bf16[768,512]{1,0:T(8,128)(2,1)} collective-permute-done((bf16[768,512]{1,0:T(8,128)(2,1)S(1)}, bf16[768,512]{1,0:T(8,128)(2,1)}, u32[]{:S(2)}, u32[]{:S(2)}) %collective-permute-start) | collective-permute-done | bytes 786464 | tf_op jit(solution)/shard_map/ppermute | solution.py:81
  71.4 16.9 %all-gather.5.cloned.1.call-done = bf16[1024,1024]{1,0:T(8,128)(2,1)} async-done(((bf16[256,1024]{1,0:T(8,128)(2,1)}), bf16[1024,1024]{1,0:T(8,128)(2,1)}) %all-gather.5.cloned.1.call-update) | async-done | bytes 2097168 | tf_op jit(solution)/shard_map/all_gather | solution.py:76
  88.3 3.9 %fusion.21 = bf16[768,1024]{1,0:T(8,128)(2,1)} fusion(s32[]{:T(128)S(6)} %select_n.250, bf16[1024,1024]{1,0:T(8,128)(2,1)} %all-gather.5.cloned.1.call-done), kind=kLoop, calls=%fused_computation.39 | loop fusion | flops 3145728 | bytes 3670020 | tf_op jit(solution)/shard_map/concatenate | solution.py:54
  109.2 2.5 fusion.4
  114.0 2.8 %collective-permute-start.7 = (bf16[128,2048]{0,1:T(8,128)(2,1)}, bf16[128,2048]{0,1:T(8,128)(2,1)}, u32[]{:S(2)}, u32[]{:S(2)}) collective-permute-start(bf16[128,2048]{0,1:T(8,128)(2,1)} %bitcast.4), channel_id=1, source_target_pairs={{0,4},{4,8},{8,12},{1,5},{5,9},{9,13},{2,6},{6,10},{10,14},{3,7},{... | collective-permute-start | bytes 1572872 | tf_op jit(solution)/shard_map/ppermute | solution.py:19
  134.1 3.2 %fusion.143 = (f32[2,16,128]{2,1,0:T(8,128)S(1)}, f32[2,16,128,384]{3,2,1,0:T(8,128)S(1)}) fusion(f32[2,16,128,384]{3,2,1,0:T(8,128)S(1)} %fusion.22, pred[2,128,384]{2,1,0:T(8,128)(4,1)S(1)} %broadcast_or_fusion), kind=kOutput, calls=%fused_computation.230 | output fusion | flops 11010431 | bytes 12697600 | tf_op jit(solution)/shard_map/sub | solution.py:31
  140.8 2.8 %fusion.31 = (f32[256]{0:T(256)S(1)}, bf16[256,1024]{1,0:T(8,128)(2,1)S(1)}) fusion(f32[256,1024]{1,0:T(8,128)S(1)} %fusion.97, bf16[768,1024]{1,0:T(8,128)(2,1)} %slice_dynamic-update-slice_fusion.4, s32[]{:T(128)S(6)} %select_n.250, bf16[256,1024]{0,1:T(8,128)(2,1)S(1)} %bitcast.169, bf16[256,1024]{1,0:T(8,128)(2,1)S(1)} %bitcast.162), kind=kOutput, calls=%fused_computation.72 | convolution fusion | flops 405274368 | bytes 4195332 | tf_op jit(solution)/shard_map/dot_general | solution.py:118
  159.8 4.2 %all-to-all-start = ((bf16[4,4,128,192]{2,3,1,0:T(8,128)(2,1)}), bf16[4,4,128,192]{2,3,1,0:T(8,128)(2,1)}, u32[]{:S(2)}, u32[]{:S(2)}) async-start(bf16[4,4,128,192]{2,3,1,0:T(8,128)(2,1)} %bitcast.156), calls=%async_computation | async-start | bytes 1572864 | tf_op jit(solution)/shard_map/all_to_all | solution.py:167
  165.0 2.6 convolution_dynamic-update-slice_fusion.2
  171.1 2.7 %fusion.6 = bf16[128,3072]{1,0:T(8,128)(2,1)} fusion(f32[128,3072]{1,0:T(8,128)} %convolution_dynamic-update-slice_fusion, bf16[256,3072]{1,0:T(8,128)(2,1)S(1)} %copy-done, bf16[128,1024]{1,0:T(8,128)(2,1)S(1)} %get-tuple-element.7, s32[]{:T(128)S(6)} %select_n.249), kind=kOutput, calls=%fused_computation.20 | convolution fusion | flops 202113024 | bytes 3997700 | tf_op jit(solution)/shard_map/dot_general | solution.py:96
  178.3 6.3 %all-to-all-done = bf16[4,4,128,192]{2,3,1,0:T(8,128)(2,1)} async-done(((bf16[4,4,128,192]{2,3,1,0:T(8,128)(2,1)}), bf16[4,4,128,192]{2,3,1,0:T(8,128)(2,1)}, u32[]{:S(2)}, u32[]{:S(2)}) %all-to-all-start) | async-done | bytes 786464 | tf_op jit(solution)/shard_map/all_to_all | solution.py:167
  184.6 4.4 %all-to-all-start.2 = ((bf16[4,4,128,192]{2,3,1,0:T(8,128)(2,1)}), bf16[4,4,128,192]{2,3,1,0:T(8,128)(2,1)}, u32[]{:S(2)}, u32[]{:S(2)}) async-start(bf16[4,4,128,192]{2,3,1,0:T(8,128)(2,1)} %bitcast.155), calls=%async_computation.2 | async-start | bytes 1572864 | tf_op jit(solution)/shard_map/all_to_all | solution.py:167
  190.1 2.7 %copy.23 = bf16[1,4,4,128,192]{3,2,4,1,0:T(4,128)(2,1)} copy(bf16[1,4,4,128,192]{3,4,1,2,0:T(8,128)(2,1)} %bitcast.26) | data formatting | bytes 1572864 | tf_op jit(solution)/shard_map/all_to_all | solution.py:167
  195.1 5.0 %fusion.153 = (f32[4,512]{1,0:T(4,128)S(1)}, f32[4,512,512]{1,2,0:T(8,128)}) fusion(pred[512,512]{0,1:T(8,128)(4,1)S(1)} %copy-done.14, bf16[4,512,192]{1,2,0:T(8,128)(2,1)} %squeeze.57), kind=kOutput, calls=%fused_computation.232 | convolution fusion | flops 139461120 | bytes 5251072 | tf_op jit(solution)/shard_map/sub | solution.py:31
  200.1 2.8 %fusion.29 = bf16[4,8,4,8,128]{4,3,2,1,0:T(8,128)(2,1)S(1)} fusion(f32[4,512,512]{1,2,0:T(8,128)} %get-tuple-element.29, f32[4,512]{1,0:T(4,128)S(1)} %get-tuple-element.28, bf16[4,512,192]{1,2,0:T(8,128)(2,1)} %squeeze.57), kind=kOutput, calls=%fused_computation.70 | convolution fusion | flops 136445952 | bytes 4726784 | tf_op jit(solution)/shard_map/nqk,nkd->nqd/dot_general | solution.py:177
  203.7 4.9 %all-to-all-done.2 = bf16[4,4,128,192]{2,3,1,0:T(8,128)(2,1)} async-done(((bf16[4,4,128,192]{2,3,1,0:T(8,128)(2,1)}), bf16[4,4,128,192]{2,3,1,0:T(8,128)(2,1)}, u32[]{:S(2)}, u32[]{:S(2)}) %all-to-all-start.2) | async-done | bytes 786464 | tf_op jit(solution)/shard_map/all_to_all | solution.py:167
  208.6 3.4 %all-to-all-start.1 = ((bf16[4,4,128,64]{2,3,1,0:T(8,128)(2,1)}), bf16[4,4,128,64]{2,3,1,0:T(8,128)(2,1)S(1)}, u32[]{:S(2)}, u32[]{:S(2)}) async-start(bf16[4,4,128,64]{2,3,1,0:T(8,128)(2,1)} %bitcast.166), calls=%async_computation.1 | async-start | bytes 524288 | tf_op jit(solution)/shard_map/all_to_all | solution.py:183
  212.0 2.6 copy.28
  217.0 5.1 %fusion.144 = (f32[4,512]{1,0:T(4,128)S(1)}, f32[4,512,512]{1,2,0:T(8,128)}) fusion(pred[512,512]{0,1:T(8,128)(4,1)} %fusion.34, bf16[4,512,192]{1,2,0:T(8,128)(2,1)} %squeeze.60), kind=kOutput, calls=%fused_computation.231 | convolution fusion | flops 139461120 | bytes 5251072 | tf_op jit(solution)/shard_map/sub | solution.py:31
  222.1 2.8 %fusion.30 = bf16[4,8,4,8,128]{4,3,2,1,0:T(8,128)(2,1)S(1)} fusion(f32[4,512,512]{1,2,0:T(8,128)} %get-tuple-element.27, f32[4,512]{1,0:T(4,128)S(1)} %get-tuple-element.26, bf16[4,512,192]{1,2,0:T(8,128)(2,1)} %squeeze.60), kind=kOutput, calls=%fused_computation.71 | convolution fusion | flops 136445952 | bytes 4726784 | tf_op jit(solution)/shard_map/nqk,nkd->nqd/dot_general | solution.py:177
  225.7 5.1 %all-to-all-start.3 = ((bf16[4,4,128,64]{2,3,1,0:T(8,128)(2,1)}), bf16[4,4,128,64]{2,3,1,0:T(8,128)(2,1)}, u32[]{:S(2)}, u32[]{:S(2)}) async-start(bf16[4,4,128,64]{2,3,1,0:T(8,128)(2,1)} %bitcast.167), calls=%async_computation.3 | async-start | bytes 524288 | tf_op jit(solution)/shard_map/all_to_all | solution.py:183
  233.9 5.0 %all-to-all-done.3 = bf16[4,4,128,64]{2,3,1,0:T(8,128)(2,1)} async-done(((bf16[4,4,128,64]{2,3,1,0:T(8,128)(2,1)}), bf16[4,4,128,64]{2,3,1,0:T(8,128)(2,1)}, u32[]{:S(2)}, u32[]{:S(2)}) %all-to-all-start.3) | async-done | bytes 262176 | tf_op jit(solution)/shard_map/all_to_all | solution.py:183
  250.9 2.6 collective-permute-start.16
  (184 shorter events, 120.2 us)
Async XLA Ops:
  7.2 33.5 %all-gather.3.cloned.1.call-start = ((), (), s32[]{:S(2)}) async-start(), calls=%async_computation.4 | async-start | bytes 1310720 | tf_op jit(solution)/shard_map/all_gather | solution.py:76
  9.9 78.4 %all-gather.5.cloned.1.call-start = ((), (), s32[]{:S(2)}) async-start(), calls=%async_computation.5 | async-start | bytes 2621440 | tf_op jit(solution)/shard_map/all_gather | solution.py:76
  42.4 19.3 %collective-permute-start = (bf16[768,512]{1,0:T(8,128)(2,1)S(1)}, bf16[768,512]{1,0:T(8,128)(2,1)}, u32[]{:S(2)}, u32[]{:S(2)}) collective-permute-start(bf16[768,512]{1,0:T(8,128)(2,1)S(1)} %fusion.44), channel_id=1, source_target_pairs={{0,8},{4,12},{8,0},{12,4},{1,9},{5,13},{9,1},{13,5},{2,10},{6,14},... | collective-permute-start | bytes 2359304 | tf_op jit(solution)/shard_map/ppermute | solution.py:81
  43.9 19.3 %collective-permute-start.1 = (bf16[768,512]{1,0:T(8,128)(2,1)S(1)}, bf16[768,512]{1,0:T(8,128)(2,1)}, u32[]{:S(2)}, u32[]{:S(2)}) collective-permute-start(bf16[768,512]{1,0:T(8,128)(2,1)S(1)} %fusion.44), channel_id=1, source_target_pairs={{0,16},{16,0},{1,17},{17,1},{2,18},{18,2},{3,19},{19,3},{4,20},{20... | collective-permute-start | bytes 2359304 | tf_op jit(solution)/shard_map/ppermute | solution.py:81
  46.8 50.7 %collective-permute-start.3 = (bf16[768,512]{1,0:T(8,128)(2,1)S(1)}, bf16[768,512]{1,0:T(8,128)(2,1)}, u32[]{:S(2)}, u32[]{:S(2)}) collective-permute-start(bf16[768,512]{1,0:T(8,128)(2,1)S(1)} %fusion.44), channel_id=1, source_target_pairs={{0,4},{4,0},{8,12},{12,8},{1,5},{5,1},{9,13},{13,9},{2,6},{6,2},{1... | collective-permute-start | bytes 2359304 | tf_op jit(solution)/shard_map/ppermute | solution.py:81
  61.7 31.9 %collective-permute-start.2 = (bf16[768,512]{1,0:T(8,128)(2,1)}, bf16[768,512]{1,0:T(8,128)(2,1)}, u32[]{:S(2)}, u32[]{:S(2)}) collective-permute-start(bf16[768,512]{1,0:T(8,128)(2,1)} %collective-permute-done), channel_id=1, source_target_pairs={{0,16},{16,0},{1,17},{17,1},{2,18},{18,2},{3,19},{19,3},{4,20},{20... | collective-permute-start | bytes 2359304 | tf_op jit(solution)/shard_map/ppermute | solution.py:81
  63.2 36.5 %collective-permute-start.4 = (bf16[768,512]{1,0:T(8,128)(2,1)}, bf16[768,512]{1,0:T(8,128)(2,1)}, u32[]{:S(2)}, u32[]{:S(2)}) collective-permute-start(bf16[768,512]{1,0:T(8,128)(2,1)} %collective-permute-done), channel_id=1, source_target_pairs={{0,4},{4,0},{8,12},{12,8},{1,5},{5,1},{9,13},{13,9},{2,6},{6,2},{1... | collective-permute-start | bytes 2359304 | tf_op jit(solution)/shard_map/ppermute | solution.py:81
  63.2 42.6 %collective-permute-start.5 = (bf16[768,512]{1,0:T(8,128)(2,1)}, bf16[768,512]{1,0:T(8,128)(2,1)}, u32[]{:S(2)}, u32[]{:S(2)}) collective-permute-start(bf16[768,512]{1,0:T(8,128)(2,1)} %collective-permute-done.1), channel_id=1, source_target_pairs={{0,4},{4,0},{8,12},{12,8},{1,5},{5,1},{9,13},{13,9},{2,6},{6,2},{1... | collective-permute-start | bytes 2359304 | tf_op jit(solution)/shard_map/ppermute | solution.py:81
  92.2 51.4 %collective-permute-start.9 = (bf16[768,1024]{1,0:T(8,128)(2,1)}, bf16[768,1024]{1,0:T(8,128)(2,1)}, u32[]{:S(2)}, u32[]{:S(2)}) collective-permute-start(bf16[768,1024]{1,0:T(8,128)(2,1)} %fusion.21), channel_id=1, source_target_pairs={{0,16},{16,0},{1,17},{17,1},{2,18},{18,2},{3,19},{19,3},{4,20},{20... | collective-permute-start | bytes 4718600 | tf_op jit(solution)/shard_map/ppermute | solution.py:81
  93.7 57.6 %collective-permute-start.10 = (bf16[768,1024]{1,0:T(8,128)(2,1)}, bf16[768,1024]{1,0:T(8,128)(2,1)}, u32[]{:S(2)}, u32[]{:S(2)}) collective-permute-start(bf16[768,1024]{1,0:T(8,128)(2,1)} %fusion.21), channel_id=1, source_target_pairs={{0,4},{4,0},{8,12},{12,8},{1,5},{5,1},{9,13},{13,9},{2,6},{6,2},{1... | collective-permute-start | bytes 4718600 | tf_op jit(solution)/shard_map/ppermute | solution.py:81
  97.6 10.5 %collective-permute-start.6 = (bf16[768,512]{1,0:T(8,128)(2,1)}, bf16[768,512]{1,0:T(8,128)(2,1)S(1)}, u32[]{:S(2)}, u32[]{:S(2)}) collective-permute-start(bf16[768,512]{1,0:T(8,128)(2,1)} %collective-permute-done.2), channel_id=1, source_target_pairs={{0,4},{4,0},{8,12},{12,8},{1,5},{5,1},{9,13},{13,9},{2,6},{6,2},{1... | collective-permute-start | bytes 2359304 | tf_op jit(solution)/shard_map/ppermute | solution.py:81
  114.0 16.1 %collective-permute-start.7 = (bf16[128,2048]{0,1:T(8,128)(2,1)}, bf16[128,2048]{0,1:T(8,128)(2,1)}, u32[]{:S(2)}, u32[]{:S(2)}) collective-permute-start(bf16[128,2048]{0,1:T(8,128)(2,1)} %bitcast.4), channel_id=1, source_target_pairs={{0,4},{4,8},{8,12},{1,5},{5,9},{9,13},{2,6},{6,10},{10,14},{3,7},{... | collective-permute-start | bytes 1572872 | tf_op jit(solution)/shard_map/ppermute | solution.py:19
  117.8 12.3 %collective-permute-start.8 = (bf16[128,2048]{0,1:T(8,128)(2,1)}, bf16[128,2048]{0,1:T(8,128)(2,1)}, u32[]{:S(2)}, u32[]{:S(2)}) collective-permute-start(bf16[128,2048]{0,1:T(8,128)(2,1)} %bitcast.8), channel_id=1, source_target_pairs={{4,0},{8,4},{12,8},{5,1},{9,5},{13,9},{6,2},{10,6},{14,10},{7,3},{... | collective-permute-start | bytes 1572872 | tf_op jit(solution)/shard_map/ppermute | solution.py:19
  143.6 9.3 %collective-permute-start.11 = (bf16[768,1024]{1,0:T(8,128)(2,1)}, bf16[768,1024]{1,0:T(8,128)(2,1)S(1)}, u32[]{:S(2)}, u32[]{:S(2)}) collective-permute-start(bf16[768,1024]{1,0:T(8,128)(2,1)} %collective-permute-done.9), channel_id=1, source_target_pairs={{0,4},{4,0},{8,12},{12,8},{1,5},{5,1},{9,13},{13,9},{2,6},{6,2},{1... | collective-permute-start | bytes 4718600 | tf_op jit(solution)/shard_map/ppermute | solution.py:81
  159.8 24.8 %all-to-all-start = ((bf16[4,4,128,192]{2,3,1,0:T(8,128)(2,1)}), bf16[4,4,128,192]{2,3,1,0:T(8,128)(2,1)}, u32[]{:S(2)}, u32[]{:S(2)}) async-start(bf16[4,4,128,192]{2,3,1,0:T(8,128)(2,1)} %bitcast.156), calls=%async_computation | async-start | bytes 1572864 | tf_op jit(solution)/shard_map/all_to_all | solution.py:167
  184.6 24.0 %all-to-all-start.2 = ((bf16[4,4,128,192]{2,3,1,0:T(8,128)(2,1)}), bf16[4,4,128,192]{2,3,1,0:T(8,128)(2,1)}, u32[]{:S(2)}, u32[]{:S(2)}) async-start(bf16[4,4,128,192]{2,3,1,0:T(8,128)(2,1)} %bitcast.155), calls=%async_computation.2 | async-start | bytes 1572864 | tf_op jit(solution)/shard_map/all_to_all | solution.py:167
  208.6 17.1 %all-to-all-start.1 = ((bf16[4,4,128,64]{2,3,1,0:T(8,128)(2,1)}), bf16[4,4,128,64]{2,3,1,0:T(8,128)(2,1)S(1)}, u32[]{:S(2)}, u32[]{:S(2)}) async-start(bf16[4,4,128,64]{2,3,1,0:T(8,128)(2,1)} %bitcast.166), calls=%async_computation.1 | async-start | bytes 524288 | tf_op jit(solution)/shard_map/all_to_all | solution.py:183
  225.7 13.2 %all-to-all-start.3 = ((bf16[4,4,128,64]{2,3,1,0:T(8,128)(2,1)}), bf16[4,4,128,64]{2,3,1,0:T(8,128)(2,1)}, u32[]{:S(2)}, u32[]{:S(2)}) async-start(bf16[4,4,128,64]{2,3,1,0:T(8,128)(2,1)} %bitcast.167), calls=%async_computation.3 | async-start | bytes 524288 | tf_op jit(solution)/shard_map/all_to_all | solution.py:183
  244.4 5.8 %collective-permute-start.12 = (f32[4,2,1152]{2,1,0:T(2,128)S(1)}, f32[4,2,1152]{2,1,0:T(2,128)S(1)}, u32[]{:S(2)}, u32[]{:S(2)}) collective-permute-start(f32[4,2,1152]{2,1,0:T(2,128)S(1)} %get-tuple-element.8), channel_id=1, source_target_pairs={{0,1},{1,2},{2,3},{3,0},{4,5},{5,6},{6,7},{7,4},{8,9},{9,10},{10,1... | collective-permute-start | bytes 110600 | tf_op jit(solution)/shard_map/ppermute | solution.py:301
  244.8 5.4 %collective-permute-start.13 = (f32[4,2,1152]{2,1,0:T(2,128)S(1)}, f32[4,2,1152]{2,1,0:T(2,128)S(1)}, u32[]{:S(2)}, u32[]{:S(2)}) collective-permute-start(f32[4,2,1152]{2,1,0:T(2,128)S(1)} %get-tuple-element.10), channel_id=1, source_target_pairs={{0,2},{1,3},{2,0},{3,1},{4,6},{5,7},{6,4},{7,5},{8,10},{9,11},{10,... | collective-permute-start | bytes 110600 | tf_op jit(solution)/shard_map/ppermute | solution.py:301
  246.3 4.5 %collective-permute-start.14 = (f32[4,2,1152]{2,1,0:T(2,128)S(1)}, f32[4,2,1152]{2,1,0:T(2,128)S(1)}, u32[]{:S(2)}, u32[]{:S(2)}) collective-permute-start(f32[4,2,1152]{2,1,0:T(2,128)S(1)} %get-tuple-element.9), channel_id=1, source_target_pairs={{0,3},{1,0},{2,1},{3,2},{4,7},{5,4},{6,5},{7,6},{8,11},{9,8},{10,9... | collective-permute-start | bytes 110600 | tf_op jit(solution)/shard_map/ppermute | solution.py:301
  250.8 5.9 %collective-permute-start.15 = (f32[2,1152]{1,0:T(2,128)S(1)}, f32[2,1152]{1,0:T(2,128)S(1)}, u32[]{:S(2)}, u32[]{:S(2)}) collective-permute-start(f32[2,1152]{1,0:T(2,128)S(1)} %get-tuple-element.11), channel_id=1, source_target_pairs={{0,4},{4,8},{8,12},{12,0},{1,5},{5,9},{9,13},{13,1},{2,6},{6,10},{... | collective-permute-start | bytes 27656 | tf_op jit(solution)/shard_map/ppermute | solution.py:308
  250.9 5.8 %collective-permute-start.16 = (f32[2,1152]{1,0:T(2,128)S(1)}, f32[2,1152]{1,0:T(2,128)S(1)}, u32[]{:S(2)}, u32[]{:S(2)}) collective-permute-start(f32[2,1152]{1,0:T(2,128)S(1)} %get-tuple-element.13), channel_id=1, source_target_pairs={{0,8},{4,12},{8,0},{12,4},{1,9},{5,13},{9,1},{13,5},{2,10},{6,14},... | collective-permute-start | bytes 27656 | tf_op jit(solution)/shard_map/ppermute | solution.py:308
  253.5 3.2 %collective-permute-start.17 = (f32[2,1152]{1,0:T(2,128)S(1)}, f32[2,1152]{1,0:T(2,128)S(1)}, u32[]{:S(2)}, u32[]{:S(2)}) collective-permute-start(f32[2,1152]{1,0:T(2,128)S(1)} %get-tuple-element.12), channel_id=1, source_target_pairs={{0,12},{4,0},{8,4},{12,8},{1,13},{5,1},{9,5},{13,9},{2,14},{6,2},{... | collective-permute-start | bytes 27656 | tf_op jit(solution)/shard_map/ppermute | solution.py:308
  (23 other events, 69.3 us)
Sparse Core Ops, SparseCore 0:
  10.1 30.6 all-gather.2
  42.9 45.4 all-gather.4

commit v14 on v12

--- a/solution.py
+++ b/solution.py
@@ -283,23 +283,9 @@
         partial = term if partial is None else partial + term
         row += span
     encoded = jnp.concatenate(pieces_out, axis=0)
-    sections = lax.axis_size("sec")
-    width = partial.shape[1]
-    partial = partial.reshape(sections, plane_count, 2, width)
-    me_plane = lax.axis_index("plane")
-    gathered = lax.dynamic_index_in_dim(partial, me_plane, axis=1, keepdims=False)
-    for step in range(1, plane_count):
-        moved = [(i, (i + step) % plane_count) for i in range(plane_count)]
-        target = lax.rem(me_plane + step, plane_count)
-        block = lax.dynamic_index_in_dim(partial, target, axis=1, keepdims=False)
-        gathered = gathered + lax.ppermute(block, "plane", moved)
-    me_sec = lax.axis_index("sec")
-    totals = lax.dynamic_index_in_dim(gathered, me_sec, axis=0, keepdims=False)
-    for step in range(1, sections):
-        moved = [(i, (i + step) % sections) for i in range(sections)]
-        target = lax.rem(me_sec + step, sections)
-        block = lax.dynamic_index_in_dim(gathered, target, axis=0, keepdims=False)
-        totals = totals + lax.ppermute(block, "sec", moved)
+    owners = lax.axis_size("sec") * plane_count
+    arrived = lax.all_to_all(partial, ("sec", "plane"), split_axis=0, concat_axis=0, tiled=True)
+    totals = jnp.sum(arrived.reshape(owners, 2, partial.shape[1]), axis=0)
     counted = totals[:, model_width]
     pooled = totals[:, :model_width] / jnp.maximum(counted, 1.0)[:, None]
     return (encoded.reshape(sec_block, tok_block, model_width), pooled)

time: 257 us -> 258 us (level)
  waiting for transfers between devices: 77.9 us -> 81 us
  starting transfers between devices: 36.3 us -> 33.4 us
    ppermute x6 -> x0, starting transfers between devices: 6.4 us -> none  [the longest x3 3.88 us: body(): gathered = gathered + lax.ppermute(block, 'plane', moved)]
    all_to_all x0 -> x1, waiting for transfers between devices: none -> 5.66 us  [body(): lax.all_to_all(partial, ('sec', 'plane'), split_axis=0, concat_axis=0, ti...]
    all_to_all x0 -> x1, starting transfers between devices: none -> 3.51 us  [body(): lax.all_to_all(partial, ('sec', 'plane'), split_axis=0, concat_axis=0, ti...]
  transfers between devices with their start and end apart: 24 -> 19, of which waited for: 8 -> 7; matrix products, arithmetic and copies ran while one was open for 44% -> 43% of each run, Pallas kernels for 0% -> 0%
where the time goes in v14:
time: 258 us; the launch traced here: 255 us
  waiting for transfers between devices  81 us (31%)
  matrix products  53.1 us (21%)
  local copies, waits for them, and re-layouts  52.5 us (20%)
  starting transfers between devices  33.4 us (13%)
  other arithmetic  20.2 us (8%)
  between operations  15.3 us (6%)
    all_gather x2, waiting for transfers between devices, gather_pieces(): gathered = lax.all_gather(mine, 'plane', axis=0, tiled=True)  42.3 us
    dot_general x12, matrix products, project(): part = jnp.dot(remote_inputs, block, preferred_element_type=jnp.float32)  22.8 us
    all_to_all x2, waiting for transfers between devices, attend_by_section(): lax.all_to_all(outgoing, 'plane', split_axis=0, concat_axis=2, tiled=True)  18.2 us
    dynamic_update_slice x12, local copies, waits for them, and re-layouts, assemble(): lax.dynamic_update_slice_in_dim(remote, block, piece * width, axis=1)  14.1 us
    sub x2, matrix products, masked_softmax(): expo = jnp.where(allowed, jnp.exp(shifted - top), 0.0)  10 us
    ppermute x10, waiting for transfers between devices, gather_pieces(): lax.ppermute(block, axis, swap)  9.76 us
    all_to_all x2, starting transfers between devices, attend_by_section(): lax.all_to_all(outgoing, 'plane', split_axis=0, concat_axis=2, tiled=True)  8.61 us
    ppermute x10, starting transfers between devices, gather_pieces(): lax.ppermute(block, axis, swap)  8.54 us
  transfers between devices with their start and end apart: 19, of which 7 were waited for; matrix products, arithmetic and copies ran while one was open for 43% of the time, Pallas kernels for 0%

profile of v14, /device:TPU:0, one launch (start us, length us, event | category | flops | bytes accessed | tf_op | source)
XLA Modules:
  0.0 255.5 jit_solution(8428616477398599627)
XLA Ops:
  14.9 25.8 %all-gather.3.cloned.1.call-done = bf16[1024,512]{1,0:T(8,128)(2,1)} async-done(((bf16[256,512]{1,0:T(8,128)(2,1)}), bf16[1024,512]{1,0:T(8,128)(2,1)}) %all-gather.3.cloned.1.call-update) | async-done | bytes 1048592 | tf_op jit(solution)/shard_map/all_gather | solution.py:76
  40.8 2.7 %fusion.39 = bf16[768,512]{1,0:T(8,128)(2,1)} fusion(s32[]{:T(128)S(6)} %select_n.218, bf16[1024,512]{1,0:T(8,128)(2,1)} %all-gather.3.cloned.1.call-done), kind=kLoop, calls=%fused_computation.86 | loop fusion | flops 1572864 | bytes 1835012 | tf_op jit(solution)/shard_map/concatenate | solution.py:54
  53.2 9.7 %collective-permute-done = bf16[768,512]{1,0:T(8,128)(2,1)} collective-permute-done((bf16[768,512]{1,0:T(8,128)(2,1)}, bf16[768,512]{1,0:T(8,128)(2,1)}, u32[]{:S(2)}, u32[]{:S(2)}) %collective-permute-start) | collective-permute-done | bytes 786464 | tf_op jit(solution)/shard_map/ppermute | solution.py:81
  71.3 16.5 %all-gather.5.cloned.1.call-done = bf16[1024,1024]{1,0:T(8,128)(2,1)} async-done(((bf16[256,1024]{1,0:T(8,128)(2,1)}), bf16[1024,1024]{1,0:T(8,128)(2,1)}) %all-gather.5.cloned.1.call-update) | async-done | bytes 2097168 | tf_op jit(solution)/shard_map/all_gather | solution.py:76
  87.8 3.9 %fusion.20 = bf16[768,1024]{1,0:T(8,128)(2,1)} fusion(s32[]{:T(128)S(6)} %select_n.218, bf16[1024,1024]{1,0:T(8,128)(2,1)} %all-gather.5.cloned.1.call-done), kind=kLoop, calls=%fused_computation.37 | loop fusion | flops 3145728 | bytes 3670020 | tf_op jit(solution)/shard_map/concatenate | solution.py:54
  98.1 2.6 %convolution_dynamic-update-slice_fusion.7 = f32[256,3072]{1,0:T(8,128)} fusion(f32[256,3072]{1,0:T(8,128)} %convolution_dynamic-update-slice_fusion.8, s32[]{:T(128)S(6)} %select_n.235, bf16[256,768]{1,0:T(8,128)(2,1)S(1)} %fusion.55, bf16[768,512]{1,0:T(8,128)(2,1)} %collective-permute-done.3), kind=kOutput, calls=%fused_computation.54 | convolution fusion | flops 150994944 | bytes 1376260 | tf_op jit(solution)/shard_map/dot_general | solution.py:100
  107.2 2.6 %fusion.4 = bf16[256,3072]{1,0:T(8,128)(2,1)S(1)} fusion(f32[256,3072]{1,0:T(8,128)} %convolution_dynamic-update-slice_fusion.4, bf16[256,3072]{1,0:T(8,128)(2,1)S(1)} %copy-done.7, bf16[256,1024]{1,0:T(8,128)(2,1)} %bitcast.128, s32[]{:T(128)S(6)} %select_n.217), kind=kOutput, calls=%fused_computation.17 | convolution fusion | flops 404226048 | bytes 6422532 | tf_op jit(solution)/shard_map/dot_general | solution.py:96
  113.0 2.7 %collective-permute-start.7 = (bf16[128,2048]{0,1:T(8,128)(2,1)}, bf16[128,2048]{0,1:T(8,128)(2,1)}, u32[]{:S(2)}, u32[]{:S(2)}) collective-permute-start(bf16[128,2048]{0,1:T(8,128)(2,1)} %bitcast.138), channel_id=1, source_target_pairs={{0,4},{4,8},{8,12},{1,5},{5,9},{9,13},{2,6},{6,10},{10,14},{3,7},{... | collective-permute-start | bytes 1572872 | tf_op jit(solution)/shard_map/ppermute | solution.py:19
  131.9 3.2 %fusion.126 = (f32[2,16,128]{2,1,0:T(8,128)S(1)}, f32[2,16,128,384]{3,2,1,0:T(8,128)S(1)}) fusion(f32[2,16,128,384]{3,2,1,0:T(8,128)S(1)} %fusion.21, pred[2,128,384]{2,1,0:T(8,128)(4,1)S(1)} %copy-done.12), kind=kOutput, calls=%fused_computation.198 | output fusion | flops 11010431 | bytes 12697600 | tf_op jit(solution)/shard_map/sub | solution.py:31
  150.6 4.2 %all-to-all-start = ((bf16[4,4,128,192]{2,3,1,0:T(8,128)(2,1)}), bf16[4,4,128,192]{2,3,1,0:T(8,128)(2,1)}, u32[]{:S(2)}, u32[]{:S(2)}) async-start(bf16[4,4,128,192]{2,3,1,0:T(8,128)(2,1)} %bitcast.24), calls=%async_computation | async-start | bytes 1572864 | tf_op jit(solution)/shard_map/all_to_all | solution.py:167
  163.3 12.6 %all-to-all-done = bf16[4,4,128,192]{2,3,1,0:T(8,128)(2,1)} async-done(((bf16[4,4,128,192]{2,3,1,0:T(8,128)(2,1)}), bf16[4,4,128,192]{2,3,1,0:T(8,128)(2,1)}, u32[]{:S(2)}, u32[]{:S(2)}) %all-to-all-start) | async-done | bytes 786464 | tf_op jit(solution)/shard_map/all_to_all | solution.py:167
  175.9 4.4 %all-to-all-start.2 = ((bf16[4,4,128,192]{2,3,1,0:T(8,128)(2,1)}), bf16[4,4,128,192]{2,3,1,0:T(8,128)(2,1)}, u32[]{:S(2)}, u32[]{:S(2)}) async-start(bf16[4,4,128,192]{2,3,1,0:T(8,128)(2,1)} %bitcast.124), calls=%async_computation.2 | async-start | bytes 1572864 | tf_op jit(solution)/shard_map/all_to_all | solution.py:167
  181.4 2.6 %copy.23 = bf16[1,4,4,128,192]{3,2,4,1,0:T(4,128)(2,1)} copy(bf16[1,4,4,128,192]{3,4,1,2,0:T(8,128)(2,1)} %bitcast.26) | data formatting | bytes 1572864 | tf_op jit(solution)/shard_map/all_to_all | solution.py:167
  186.4 4.9 %fusion.136 = (f32[4,512]{1,0:T(4,128)S(1)}, f32[4,512,512]{1,2,0:T(8,128)}) fusion(pred[512,512]{0,1:T(8,128)(4,1)S(1)} %fusion.38, bf16[4,512,192]{1,2,0:T(8,128)(2,1)} %squeeze.31), kind=kOutput, calls=%fused_computation.200 | convolution fusion | flops 139461120 | bytes 5251072 | tf_op jit(solution)/shard_map/sub | solution.py:31
  191.3 2.8 %fusion.32 = bf16[4,8,4,8,128]{4,3,2,1,0:T(8,128)(2,1)S(1)} fusion(f32[4,512,512]{1,2,0:T(8,128)} %get-tuple-element.23, f32[4,512]{1,0:T(4,128)S(1)} %get-tuple-element.22, bf16[4,512,192]{1,2,0:T(8,128)(2,1)} %squeeze.31), kind=kOutput, calls=%fused_computation.68 | convolution fusion | flops 136445952 | bytes 4726784 | tf_op jit(solution)/shard_map/nqk,nkd->nqd/dot_general | solution.py:177
  194.8 5.6 %all-to-all-done.2 = bf16[4,4,128,192]{2,3,1,0:T(8,128)(2,1)} async-done(((bf16[4,4,128,192]{2,3,1,0:T(8,128)(2,1)}), bf16[4,4,128,192]{2,3,1,0:T(8,128)(2,1)}, u32[]{:S(2)}, u32[]{:S(2)}) %all-to-all-start.2) | async-done | bytes 786464 | tf_op jit(solution)/shard_map/all_to_all | solution.py:167
  200.4 3.4 %all-to-all-start.1 = ((bf16[4,4,128,64]{2,3,1,0:T(8,128)(2,1)}), bf16[4,4,128,64]{2,3,1,0:T(8,128)(2,1)S(1)}, u32[]{:S(2)}, u32[]{:S(2)}) async-start(bf16[4,4,128,64]{2,3,1,0:T(8,128)(2,1)} %bitcast.134), calls=%async_computation.1 | async-start | bytes 524288 | tf_op jit(solution)/shard_map/all_to_all | solution.py:183
  203.8 2.6 %copy.28 = bf16[1,4,4,128,192]{3,2,4,1,0:T(4,128)(2,1)} copy(bf16[1,4,4,128,192]{3,4,1,2,0:T(8,128)(2,1)} %bitcast.38) | data formatting | bytes 1572864 | tf_op jit(solution)/shard_map/all_to_all | solution.py:167
  208.8 5.1 %fusion.127 = (f32[4,512]{1,0:T(4,128)S(1)}, f32[4,512,512]{1,2,0:T(8,128)}) fusion(pred[512,512]{0,1:T(8,128)(4,1)} %fusion.37, bf16[4,512,192]{1,2,0:T(8,128)(2,1)} %squeeze.34), kind=kOutput, calls=%fused_computation.199 | convolution fusion | flops 139461120 | bytes 5251072 | tf_op jit(solution)/shard_map/sub | solution.py:31
  213.9 2.8 %fusion.33 = bf16[4,8,4,8,128]{4,3,2,1,0:T(8,128)(2,1)S(1)} fusion(f32[4,512,512]{1,2,0:T(8,128)} %get-tuple-element.21, f32[4,512]{1,0:T(4,128)S(1)} %get-tuple-element.20, bf16[4,512,192]{1,2,0:T(8,128)(2,1)} %squeeze.34), kind=kOutput, calls=%fused_computation.69 | convolution fusion | flops 136445952 | bytes 4726784 | tf_op jit(solution)/shard_map/nqk,nkd->nqd/dot_general | solution.py:177
  217.5 5.1 %all-to-all-start.3 = ((bf16[4,4,128,64]{2,3,1,0:T(8,128)(2,1)}), bf16[4,4,128,64]{2,3,1,0:T(8,128)(2,1)}, u32[]{:S(2)}, u32[]{:S(2)}) async-start(bf16[4,4,128,64]{2,3,1,0:T(8,128)(2,1)} %bitcast.135), calls=%async_computation.3 | async-start | bytes 524288 | tf_op jit(solution)/shard_map/all_to_all | solution.py:183
  225.7 5.0 %all-to-all-done.3 = bf16[4,4,128,64]{2,3,1,0:T(8,128)(2,1)} async-done(((bf16[4,4,128,64]{2,3,1,0:T(8,128)(2,1)}), bf16[4,4,128,64]{2,3,1,0:T(8,128)(2,1)}, u32[]{:S(2)}, u32[]{:S(2)}) %all-to-all-start.3) | async-done | bytes 262176 | tf_op jit(solution)/shard_map/all_to_all | solution.py:183
  236.8 3.5 %all-to-all-start.4 = ((f32[16,2,1152]{2,1,0:T(2,128)}), f32[16,2,1152]{2,1,0:T(2,128)S(1)}, u32[]{:S(2)}, u32[]{:S(2)}) async-start(f32[16,2,1152]{2,1,0:T(2,128)} %all_to_all.50), calls=%async_computation.4 | async-start | bytes 294912 | tf_op jit(solution)/shard_map/all_to_all | solution.py:287
  242.1 5.7 %all-to-all-done.4 = f32[16,2,1152]{2,1,0:T(2,128)S(1)} async-done(((f32[16,2,1152]{2,1,0:T(2,128)}), f32[16,2,1152]{2,1,0:T(2,128)S(1)}, u32[]{:S(2)}, u32[]{:S(2)}) %all-to-all-start.4) | async-done | bytes 147488 | tf_op jit(solution)/shard_map/all_to_all | solution.py:287
  (155 shorter events, 100.1 us)
Async XLA Ops:
  7.2 6.4 %copy-start.15 = (f32[2,1024]{1,0:T(2,128)S(1)}, f32[2,1024]{1,0:T(2,128)}, u32[]{:S(2)}) copy-start(f32[2,1024]{1,0:T(2,128)} %param.11) | copy-start | bytes 24580
  7.2 33.6 %all-gather.3.cloned.1.call-start = ((), (), s32[]{:S(2)}) async-start(), calls=%async_computation.5 | async-start | bytes 1310720 | tf_op jit(solution)/shard_map/all_gather | solution.py:76
  10.0 77.8 %all-gather.5.cloned.1.call-start = ((), (), s32[]{:S(2)}) async-start(), calls=%async_computation.6 | async-start | bytes 2621440 | tf_op jit(solution)/shard_map/all_gather | solution.py:76
  43.5 19.5 %collective-permute-start = (bf16[768,512]{1,0:T(8,128)(2,1)}, bf16[768,512]{1,0:T(8,128)(2,1)}, u32[]{:S(2)}, u32[]{:S(2)}) collective-permute-start(bf16[768,512]{1,0:T(8,128)(2,1)} %fusion.39), channel_id=1, source_target_pairs={{0,8},{4,12},{8,0},{12,4},{1,9},{5,13},{9,1},{13,5},{2,10},{6,14},... | collective-permute-start | bytes 2359304 | tf_op jit(solution)/shard_map/ppermute | solution.py:81
  44.9 19.5 %collective-permute-start.1 = (bf16[768,512]{1,0:T(8,128)(2,1)}, bf16[768,512]{1,0:T(8,128)(2,1)}, u32[]{:S(2)}, u32[]{:S(2)}) collective-permute-start(bf16[768,512]{1,0:T(8,128)(2,1)} %fusion.39), channel_id=1, source_target_pairs={{0,16},{16,0},{1,17},{17,1},{2,18},{18,2},{3,19},{19,3},{4,20},{20... | collective-permute-start | bytes 2359304 | tf_op jit(solution)/shard_map/ppermute | solution.py:81
  47.8 48.7 %collective-permute-start.3 = (bf16[768,512]{1,0:T(8,128)(2,1)}, bf16[768,512]{1,0:T(8,128)(2,1)}, u32[]{:S(2)}, u32[]{:S(2)}) collective-permute-start(bf16[768,512]{1,0:T(8,128)(2,1)} %fusion.39), channel_id=1, source_target_pairs={{0,4},{4,0},{8,12},{12,8},{1,5},{5,1},{9,13},{13,9},{2,6},{6,2},{1... | collective-permute-start | bytes 2359304 | tf_op jit(solution)/shard_map/ppermute | solution.py:81
  62.9 30.2 %collective-permute-start.2 = (bf16[768,512]{1,0:T(8,128)(2,1)}, bf16[768,512]{1,0:T(8,128)(2,1)}, u32[]{:S(2)}, u32[]{:S(2)}) collective-permute-start(bf16[768,512]{1,0:T(8,128)(2,1)} %collective-permute-done), channel_id=1, source_target_pairs={{0,16},{16,0},{1,17},{17,1},{2,18},{18,2},{3,19},{19,3},{4,20},{20... | collective-permute-start | bytes 2359304 | tf_op jit(solution)/shard_map/ppermute | solution.py:81
  64.4 36.3 %collective-permute-start.4 = (bf16[768,512]{1,0:T(8,128)(2,1)}, bf16[768,512]{1,0:T(8,128)(2,1)}, u32[]{:S(2)}, u32[]{:S(2)}) collective-permute-start(bf16[768,512]{1,0:T(8,128)(2,1)} %collective-permute-done), channel_id=1, source_target_pairs={{0,4},{4,0},{8,12},{12,8},{1,5},{5,1},{9,13},{13,9},{2,6},{6,2},{1... | collective-permute-start | bytes 2359304 | tf_op jit(solution)/shard_map/ppermute | solution.py:81
  64.4 38.5 %collective-permute-start.5 = (bf16[768,512]{1,0:T(8,128)(2,1)}, bf16[768,512]{1,0:T(8,128)(2,1)}, u32[]{:S(2)}, u32[]{:S(2)}) collective-permute-start(bf16[768,512]{1,0:T(8,128)(2,1)} %collective-permute-done.1), channel_id=1, source_target_pairs={{0,4},{4,0},{8,12},{12,8},{1,5},{5,1},{9,13},{13,9},{2,6},{6,2},{1... | collective-permute-start | bytes 2359304 | tf_op jit(solution)/shard_map/ppermute | solution.py:81
  91.7 46.3 %collective-permute-start.9 = (bf16[768,1024]{1,0:T(8,128)(2,1)}, bf16[768,1024]{1,0:T(8,128)(2,1)}, u32[]{:S(2)}, u32[]{:S(2)}) collective-permute-start(bf16[768,1024]{1,0:T(8,128)(2,1)} %fusion.20), channel_id=1, source_target_pairs={{0,16},{16,0},{1,17},{17,1},{2,18},{18,2},{3,19},{19,3},{4,20},{20... | collective-permute-start | bytes 4718600 | tf_op jit(solution)/shard_map/ppermute | solution.py:81
  93.1 52.1 %collective-permute-start.10 = (bf16[768,1024]{1,0:T(8,128)(2,1)}, bf16[768,1024]{1,0:T(8,128)(2,1)}, u32[]{:S(2)}, u32[]{:S(2)}) collective-permute-start(bf16[768,1024]{1,0:T(8,128)(2,1)} %fusion.20), channel_id=1, source_target_pairs={{0,4},{4,0},{8,12},{12,8},{1,5},{5,1},{9,13},{13,9},{2,6},{6,2},{1... | collective-permute-start | bytes 4718600 | tf_op jit(solution)/shard_map/ppermute | solution.py:81
  95.4 11.9 %copy-start.7 = (bf16[256,3072]{1,0:T(8,128)(2,1)S(1)}, bf16[256,3072]{1,0:T(8,128)(2,1)}, u32[]{:S(2)}) copy-start(bf16[256,3072]{1,0:T(8,128)(2,1)} %param.12) | copy-start | bytes 4718596
  96.5 8.7 %collective-permute-start.6 = (bf16[768,512]{1,0:T(8,128)(2,1)}, bf16[768,512]{1,0:T(8,128)(2,1)S(1)}, u32[]{:S(2)}, u32[]{:S(2)}) collective-permute-start(bf16[768,512]{1,0:T(8,128)(2,1)} %collective-permute-done.2), channel_id=1, source_target_pairs={{0,4},{4,0},{8,12},{12,8},{1,5},{5,1},{9,13},{13,9},{2,6},{6,2},{1... | collective-permute-start | bytes 2359304 | tf_op jit(solution)/shard_map/ppermute | solution.py:81
  98.1 7.1 %copy-start.8 = (bf16[768,1024]{1,0:T(8,128)(2,1)}, bf16[768,1024]{1,0:T(8,128)(2,1)S(1)}, u32[]{:S(2)}) copy-start(bf16[768,1024]{1,0:T(8,128)(2,1)S(1)} %slice_dynamic-update-slice_fusion.7) | copy-start | bytes 4718596
  113.0 16.0 %collective-permute-start.7 = (bf16[128,2048]{0,1:T(8,128)(2,1)}, bf16[128,2048]{0,1:T(8,128)(2,1)}, u32[]{:S(2)}, u32[]{:S(2)}) collective-permute-start(bf16[128,2048]{0,1:T(8,128)(2,1)} %bitcast.138), channel_id=1, source_target_pairs={{0,4},{4,8},{8,12},{1,5},{5,9},{9,13},{2,6},{6,10},{10,14},{3,7},{... | collective-permute-start | bytes 1572872 | tf_op jit(solution)/shard_map/ppermute | solution.py:19
  117.7 11.2 %collective-permute-start.8 = (bf16[128,2048]{0,1:T(8,128)(2,1)}, bf16[128,2048]{0,1:T(8,128)(2,1)}, u32[]{:S(2)}, u32[]{:S(2)}) collective-permute-start(bf16[128,2048]{0,1:T(8,128)(2,1)} %bitcast.139), channel_id=1, source_target_pairs={{4,0},{8,4},{12,8},{5,1},{9,5},{13,9},{6,2},{10,6},{14,10},{7,3},{... | collective-permute-start | bytes 1572872 | tf_op jit(solution)/shard_map/ppermute | solution.py:19
  138.0 9.0 %collective-permute-start.11 = (bf16[768,1024]{1,0:T(8,128)(2,1)}, bf16[768,1024]{1,0:T(8,128)(2,1)S(1)}, u32[]{:S(2)}, u32[]{:S(2)}) collective-permute-start(bf16[768,1024]{1,0:T(8,128)(2,1)} %collective-permute-done.9), channel_id=1, source_target_pairs={{0,4},{4,0},{8,12},{12,8},{1,5},{5,1},{9,13},{13,9},{2,6},{6,2},{1... | collective-permute-start | bytes 4718600 | tf_op jit(solution)/shard_map/ppermute | solution.py:81
  149.2 6.3 %copy-start.17 = (s32[2,128]{1,0:T(2,128)S(1)}, s32[2,128]{1,0:T(2,128)}, u32[]{:S(2)}) copy-start(s32[2,128]{1,0:T(2,128)} %param.10) | copy-start | bytes 3076
  150.6 25.3 %all-to-all-start = ((bf16[4,4,128,192]{2,3,1,0:T(8,128)(2,1)}), bf16[4,4,128,192]{2,3,1,0:T(8,128)(2,1)}, u32[]{:S(2)}, u32[]{:S(2)}) async-start(bf16[4,4,128,192]{2,3,1,0:T(8,128)(2,1)} %bitcast.24), calls=%async_computation | async-start | bytes 1572864 | tf_op jit(solution)/shard_map/all_to_all | solution.py:167
  175.9 24.5 %all-to-all-start.2 = ((bf16[4,4,128,192]{2,3,1,0:T(8,128)(2,1)}), bf16[4,4,128,192]{2,3,1,0:T(8,128)(2,1)}, u32[]{:S(2)}, u32[]{:S(2)}) async-start(bf16[4,4,128,192]{2,3,1,0:T(8,128)(2,1)} %bitcast.124), calls=%async_computation.2 | async-start | bytes 1572864 | tf_op jit(solution)/shard_map/all_to_all | solution.py:167
  200.4 17.0 %all-to-all-start.1 = ((bf16[4,4,128,64]{2,3,1,0:T(8,128)(2,1)}), bf16[4,4,128,64]{2,3,1,0:T(8,128)(2,1)S(1)}, u32[]{:S(2)}, u32[]{:S(2)}) async-start(bf16[4,4,128,64]{2,3,1,0:T(8,128)(2,1)} %bitcast.134), calls=%async_computation.1 | async-start | bytes 524288 | tf_op jit(solution)/shard_map/all_to_all | solution.py:183
  217.5 13.2 %copy-start.10 = (bf16[4,4,128,64]{2,3,1,0:T(8,128)(2,1)}, bf16[4,4,128,64]{2,3,1,0:T(8,128)(2,1)S(1)}, u32[]{:S(2)}) copy-start(bf16[4,4,128,64]{2,3,1,0:T(8,128)(2,1)S(1)} %all-to-all-done.1) | copy-start | bytes 786436
  217.5 13.2 %all-to-all-start.3 = ((bf16[4,4,128,64]{2,3,1,0:T(8,128)(2,1)}), bf16[4,4,128,64]{2,3,1,0:T(8,128)(2,1)}, u32[]{:S(2)}, u32[]{:S(2)}) async-start(bf16[4,4,128,64]{2,3,1,0:T(8,128)(2,1)} %bitcast.135), calls=%async_computation.3 | async-start | bytes 524288 | tf_op jit(solution)/shard_map/all_to_all | solution.py:183
  236.8 11.0 %all-to-all-start.4 = ((f32[16,2,1152]{2,1,0:T(2,128)}), f32[16,2,1152]{2,1,0:T(2,128)S(1)}, u32[]{:S(2)}, u32[]{:S(2)}) async-start(f32[16,2,1152]{2,1,0:T(2,128)} %all_to_all.50), calls=%async_computation.4 | async-start | bytes 294912 | tf_op jit(solution)/shard_map/all_to_all | solution.py:287
  (13 other events, 33.2 us)
Sparse Core Ops, SparseCore 0:
  10.1 30.6 all-gather.2
  42.4 45.3 all-gather.4

commit v15 on v12

--- a/solution.py
+++ b/solution.py
@@ -199,7 +199,7 @@
     near_valid = positions[None, :] < near_counts[:, None]
     own_valid = near_valid[1 : sec_block + 1]
     score_scale = 1.0 / math.sqrt(HEAD_DIM)
-    cross_qkv_pieces, cross_out_pieces = gather_pieces([cross_qkv, cross_out], swap_first=True)
+    cross_qkv_pieces, cross_out_pieces = gather_pieces([cross_qkv, cross_out])
     plane_qkv_pieces, plane_out_pieces = gather_pieces([plane_qkv, plane_out], skip_middle=True)
     cross_out_pieces = assemble(cross_out_pieces)
     plane_out_pieces = assemble(plane_out_pieces)

time: 257 us -> 257 us (level)
  no operation moved by 1% of the time
where the time goes in v15:
time: 257 us; the launch traced here: 254 us
  waiting for transfers between devices  77.9 us (30%)
  matrix products  53.1 us (21%)
  local copies, waits for them, and re-layouts  51.7 us (20%)
  starting transfers between devices  36.3 us (14%)
  other arithmetic  20.1 us (8%)
  between operations  15.4 us (6%)
    all_gather x2, waiting for transfers between devices, gather_pieces(): gathered = lax.all_gather(mine, 'plane', axis=0, tiled=True)  42.4 us
    dot_general x12, matrix products, project(): part = jnp.dot(remote_inputs, block, preferred_element_type=jnp.float32)  22.8 us
    all_to_all x2, waiting for transfers between devices, attend_by_section(): lax.all_to_all(outgoing, 'plane', split_axis=0, concat_axis=2, tiled=True)  18.2 us
    dynamic_update_slice x12, local copies, waits for them, and re-layouts, assemble(): lax.dynamic_update_slice_in_dim(remote, block, piece * width, axis=1)  14.1 us
    sub x2, matrix products, masked_softmax(): expo = jnp.where(allowed, jnp.exp(shifted - top), 0.0)  10.1 us
    ppermute x10, waiting for transfers between devices, gather_pieces(): lax.ppermute(block, axis, swap)  9.78 us
    all_to_all x2, starting transfers between devices, attend_by_section(): lax.all_to_all(outgoing, 'plane', split_axis=0, concat_axis=2, tiled=True)  8.61 us
    ppermute x10, starting transfers between devices, gather_pieces(): lax.ppermute(block, axis, swap)  8.49 us
  transfers between devices with their start and end apart: 24, of which 8 were waited for; matrix products, arithmetic and copies ran while one was open for 44% of the time, Pallas kernels for 0%

profile of v15, /device:TPU:0, one launch (start us, length us, event | category | flops | bytes accessed | tf_op | source)
XLA Modules:
  0.0 254.5 jit_solution(8493974380092549023)
XLA Ops:
  14.9 25.9 %all-gather.3.cloned.1.call-done = bf16[1024,512]{1,0:T(8,128)(2,1)} async-done(((bf16[256,512]{1,0:T(8,128)(2,1)}), bf16[1024,512]{1,0:T(8,128)(2,1)}) %all-gather.3.cloned.1.call-update) | async-done | bytes 1048592 | tf_op jit(solution)/shard_map/all_gather | solution.py:76
  40.8 2.6 %fusion.39 = bf16[768,512]{1,0:T(8,128)(2,1)} fusion(s32[]{:T(128)S(6)} %select_n.244, bf16[1024,512]{1,0:T(8,128)(2,1)} %all-gather.3.cloned.1.call-done), kind=kLoop, calls=%fused_computation.86 | loop fusion | flops 1572864 | bytes 1835012 | tf_op jit(solution)/shard_map/concatenate | solution.py:54
  53.1 9.8 %collective-permute-done = bf16[768,512]{1,0:T(8,128)(2,1)} collective-permute-done((bf16[768,512]{1,0:T(8,128)(2,1)}, bf16[768,512]{1,0:T(8,128)(2,1)}, u32[]{:S(2)}, u32[]{:S(2)}) %collective-permute-start) | collective-permute-done | bytes 786464 | tf_op jit(solution)/shard_map/ppermute | solution.py:81
  71.3 16.5 %all-gather.5.cloned.1.call-done = bf16[1024,1024]{1,0:T(8,128)(2,1)} async-done(((bf16[256,1024]{1,0:T(8,128)(2,1)}), bf16[1024,1024]{1,0:T(8,128)(2,1)}) %all-gather.5.cloned.1.call-update) | async-done | bytes 2097168 | tf_op jit(solution)/shard_map/all_gather | solution.py:76
  87.8 3.9 %fusion.20 = bf16[768,1024]{1,0:T(8,128)(2,1)} fusion(s32[]{:T(128)S(6)} %select_n.244, bf16[1024,1024]{1,0:T(8,128)(2,1)} %all-gather.5.cloned.1.call-done), kind=kLoop, calls=%fused_computation.37 | loop fusion | flops 3145728 | bytes 3670020 | tf_op jit(solution)/shard_map/concatenate | solution.py:54
  98.1 2.7 %convolution_dynamic-update-slice_fusion.7 = f32[256,3072]{1,0:T(8,128)} fusion(f32[256,3072]{1,0:T(8,128)} %convolution_dynamic-update-slice_fusion.8, s32[]{:T(128)S(6)} %select_n.261, bf16[256,768]{1,0:T(8,128)(2,1)S(1)} %fusion.55, bf16[768,512]{1,0:T(8,128)(2,1)} %collective-permute-done.3), kind=kOutput, calls=%fused_computation.54 | convolution fusion | flops 150994944 | bytes 1376260 | tf_op jit(solution)/shard_map/dot_general | solution.py:100
  107.2 2.6 %fusion.4 = bf16[256,3072]{1,0:T(8,128)(2,1)S(1)} fusion(f32[256,3072]{1,0:T(8,128)} %convolution_dynamic-update-slice_fusion.4, bf16[256,3072]{1,0:T(8,128)(2,1)S(1)} %copy-done.7, bf16[256,1024]{1,0:T(8,128)(2,1)} %bitcast.154, s32[]{:T(128)S(6)} %select_n.243), kind=kOutput, calls=%fused_computation.17 | convolution fusion | flops 404226048 | bytes 6422532 | tf_op jit(solution)/shard_map/dot_general | solution.py:96
  112.9 2.7 %collective-permute-start.7 = (bf16[128,2048]{0,1:T(8,128)(2,1)}, bf16[128,2048]{0,1:T(8,128)(2,1)}, u32[]{:S(2)}, u32[]{:S(2)}) collective-permute-start(bf16[128,2048]{0,1:T(8,128)(2,1)} %bitcast.165), channel_id=1, source_target_pairs={{0,4},{4,8},{8,12},{1,5},{5,9},{9,13},{2,6},{6,10},{10,14},{3,7},{... | collective-permute-start | bytes 1572872 | tf_op jit(solution)/shard_map/ppermute | solution.py:19
  131.8 3.2 %fusion.135 = (f32[2,16,128]{2,1,0:T(8,128)S(1)}, f32[2,16,128,384]{3,2,1,0:T(8,128)S(1)}) fusion(f32[2,16,128,384]{3,2,1,0:T(8,128)S(1)} %fusion.21, pred[2,128,384]{2,1,0:T(8,128)(4,1)S(1)} %copy-done.12), kind=kOutput, calls=%fused_computation.215 | output fusion | flops 11010431 | bytes 12697600 | tf_op jit(solution)/shard_map/sub | solution.py:31
  150.5 4.2 %all-to-all-start = ((bf16[4,4,128,192]{2,3,1,0:T(8,128)(2,1)}), bf16[4,4,128,192]{2,3,1,0:T(8,128)(2,1)}, u32[]{:S(2)}, u32[]{:S(2)}) async-start(bf16[4,4,128,192]{2,3,1,0:T(8,128)(2,1)} %bitcast.24), calls=%async_computation | async-start | bytes 1572864 | tf_op jit(solution)/shard_map/all_to_all | solution.py:167
  163.1 12.7 %all-to-all-done = bf16[4,4,128,192]{2,3,1,0:T(8,128)(2,1)} async-done(((bf16[4,4,128,192]{2,3,1,0:T(8,128)(2,1)}), bf16[4,4,128,192]{2,3,1,0:T(8,128)(2,1)}, u32[]{:S(2)}, u32[]{:S(2)}) %all-to-all-start) | async-done | bytes 786464 | tf_op jit(solution)/shard_map/all_to_all | solution.py:167
  175.8 4.4 %all-to-all-start.2 = ((bf16[4,4,128,192]{2,3,1,0:T(8,128)(2,1)}), bf16[4,4,128,192]{2,3,1,0:T(8,128)(2,1)}, u32[]{:S(2)}, u32[]{:S(2)}) async-start(bf16[4,4,128,192]{2,3,1,0:T(8,128)(2,1)} %bitcast.150), calls=%async_computation.2 | async-start | bytes 1572864 | tf_op jit(solution)/shard_map/all_to_all | solution.py:167
  181.2 2.6 %copy.23 = bf16[1,4,4,128,192]{3,2,4,1,0:T(4,128)(2,1)} copy(bf16[1,4,4,128,192]{3,4,1,2,0:T(8,128)(2,1)} %bitcast.26) | data formatting | bytes 1572864 | tf_op jit(solution)/shard_map/all_to_all | solution.py:167
  183.9 2.4 squeeze.57
  186.3 5.0 %fusion.145 = (f32[4,512]{1,0:T(4,128)S(1)}, f32[4,512,512]{1,2,0:T(8,128)}) fusion(pred[512,512]{0,1:T(8,128)(4,1)S(1)} %fusion.38, bf16[4,512,192]{1,2,0:T(8,128)(2,1)} %squeeze.57), kind=kOutput, calls=%fused_computation.217 | convolution fusion | flops 139461120 | bytes 5251072 | tf_op jit(solution)/shard_map/sub | solution.py:31
  191.2 2.8 %fusion.32 = bf16[4,8,4,8,128]{4,3,2,1,0:T(8,128)(2,1)S(1)} fusion(f32[4,512,512]{1,2,0:T(8,128)} %get-tuple-element.29, f32[4,512]{1,0:T(4,128)S(1)} %get-tuple-element.28, bf16[4,512,192]{1,2,0:T(8,128)(2,1)} %squeeze.57), kind=kOutput, calls=%fused_computation.68 | convolution fusion | flops 136445952 | bytes 4726784 | tf_op jit(solution)/shard_map/nqk,nkd->nqd/dot_general | solution.py:177
  194.8 5.5 %all-to-all-done.2 = bf16[4,4,128,192]{2,3,1,0:T(8,128)(2,1)} async-done(((bf16[4,4,128,192]{2,3,1,0:T(8,128)(2,1)}), bf16[4,4,128,192]{2,3,1,0:T(8,128)(2,1)}, u32[]{:S(2)}, u32[]{:S(2)}) %all-to-all-start.2) | async-done | bytes 786464 | tf_op jit(solution)/shard_map/all_to_all | solution.py:167
  200.3 3.4 %all-to-all-start.1 = ((bf16[4,4,128,64]{2,3,1,0:T(8,128)(2,1)}), bf16[4,4,128,64]{2,3,1,0:T(8,128)(2,1)S(1)}, u32[]{:S(2)}, u32[]{:S(2)}) async-start(bf16[4,4,128,64]{2,3,1,0:T(8,128)(2,1)} %bitcast.160), calls=%async_computation.1 | async-start | bytes 524288 | tf_op jit(solution)/shard_map/all_to_all | solution.py:183
  203.7 2.6 %copy.28 = bf16[1,4,4,128,192]{3,2,4,1,0:T(4,128)(2,1)} copy(bf16[1,4,4,128,192]{3,4,1,2,0:T(8,128)(2,1)} %bitcast.38) | data formatting | bytes 1572864 | tf_op jit(solution)/shard_map/all_to_all | solution.py:167
  206.3 2.3 squeeze.60
  208.7 5.1 %fusion.136 = (f32[4,512]{1,0:T(4,128)S(1)}, f32[4,512,512]{1,2,0:T(8,128)}) fusion(pred[512,512]{0,1:T(8,128)(4,1)} %fusion.37, bf16[4,512,192]{1,2,0:T(8,128)(2,1)} %squeeze.60), kind=kOutput, calls=%fused_computation.216 | convolution fusion | flops 139461120 | bytes 5251072 | tf_op jit(solution)/shard_map/sub | solution.py:31
  213.8 2.8 %fusion.33 = bf16[4,8,4,8,128]{4,3,2,1,0:T(8,128)(2,1)S(1)} fusion(f32[4,512,512]{1,2,0:T(8,128)} %get-tuple-element.27, f32[4,512]{1,0:T(4,128)S(1)} %get-tuple-element.26, bf16[4,512,192]{1,2,0:T(8,128)(2,1)} %squeeze.60), kind=kOutput, calls=%fused_computation.69 | convolution fusion | flops 136445952 | bytes 4726784 | tf_op jit(solution)/shard_map/nqk,nkd->nqd/dot_general | solution.py:177
  217.3 5.1 %all-to-all-start.3 = ((bf16[4,4,128,64]{2,3,1,0:T(8,128)(2,1)}), bf16[4,4,128,64]{2,3,1,0:T(8,128)(2,1)}, u32[]{:S(2)}, u32[]{:S(2)}) async-start(bf16[4,4,128,64]{2,3,1,0:T(8,128)(2,1)} %bitcast.161), calls=%async_computation.3 | async-start | bytes 524288 | tf_op jit(solution)/shard_map/all_to_all | solution.py:183
  225.5 5.0 %all-to-all-done.3 = bf16[4,4,128,64]{2,3,1,0:T(8,128)(2,1)} async-done(((bf16[4,4,128,64]{2,3,1,0:T(8,128)(2,1)}), bf16[4,4,128,64]{2,3,1,0:T(8,128)(2,1)}, u32[]{:S(2)}, u32[]{:S(2)}) %all-to-all-start.3) | async-done | bytes 262176 | tf_op jit(solution)/shard_map/all_to_all | solution.py:183
  (168 shorter events, 103.3 us)
Async XLA Ops:
  7.2 33.6 %all-gather.3.cloned.1.call-start = ((), (), s32[]{:S(2)}) async-start(), calls=%async_computation.4 | async-start | bytes 1310720 | tf_op jit(solution)/shard_map/all_gather | solution.py:76
  10.0 77.8 %all-gather.5.cloned.1.call-start = ((), (), s32[]{:S(2)}) async-start(), calls=%async_computation.5 | async-start | bytes 2621440 | tf_op jit(solution)/shard_map/all_gather | solution.py:76
  43.4 19.5 %collective-permute-start = (bf16[768,512]{1,0:T(8,128)(2,1)}, bf16[768,512]{1,0:T(8,128)(2,1)}, u32[]{:S(2)}, u32[]{:S(2)}) collective-permute-start(bf16[768,512]{1,0:T(8,128)(2,1)} %fusion.39), channel_id=1, source_target_pairs={{0,16},{16,0},{1,17},{17,1},{2,18},{18,2},{3,19},{19,3},{4,20},{20... | collective-permute-start | bytes 2359304 | tf_op jit(solution)/shard_map/ppermute | solution.py:81
  44.9 19.5 %collective-permute-start.1 = (bf16[768,512]{1,0:T(8,128)(2,1)}, bf16[768,512]{1,0:T(8,128)(2,1)}, u32[]{:S(2)}, u32[]{:S(2)}) collective-permute-start(bf16[768,512]{1,0:T(8,128)(2,1)} %fusion.39), channel_id=1, source_target_pairs={{0,8},{4,12},{8,0},{12,4},{1,9},{5,13},{9,1},{13,5},{2,10},{6,14},... | collective-permute-start | bytes 2359304 | tf_op jit(solution)/shard_map/ppermute | solution.py:81
  47.7 48.8 %collective-permute-start.3 = (bf16[768,512]{1,0:T(8,128)(2,1)}, bf16[768,512]{1,0:T(8,128)(2,1)}, u32[]{:S(2)}, u32[]{:S(2)}) collective-permute-start(bf16[768,512]{1,0:T(8,128)(2,1)} %fusion.39), channel_id=1, source_target_pairs={{0,4},{4,0},{8,12},{12,8},{1,5},{5,1},{9,13},{13,9},{2,6},{6,2},{1... | collective-permute-start | bytes 2359304 | tf_op jit(solution)/shard_map/ppermute | solution.py:81
  62.9 30.3 %collective-permute-start.2 = (bf16[768,512]{1,0:T(8,128)(2,1)}, bf16[768,512]{1,0:T(8,128)(2,1)}, u32[]{:S(2)}, u32[]{:S(2)}) collective-permute-start(bf16[768,512]{1,0:T(8,128)(2,1)} %collective-permute-done), channel_id=1, source_target_pairs={{0,8},{4,12},{8,0},{12,4},{1,9},{5,13},{9,1},{13,5},{2,10},{6,14},... | collective-permute-start | bytes 2359304 | tf_op jit(solution)/shard_map/ppermute | solution.py:81
  64.3 36.4 %collective-permute-start.4 = (bf16[768,512]{1,0:T(8,128)(2,1)}, bf16[768,512]{1,0:T(8,128)(2,1)}, u32[]{:S(2)}, u32[]{:S(2)}) collective-permute-start(bf16[768,512]{1,0:T(8,128)(2,1)} %collective-permute-done), channel_id=1, source_target_pairs={{0,4},{4,0},{8,12},{12,8},{1,5},{5,1},{9,13},{13,9},{2,6},{6,2},{1... | collective-permute-start | bytes 2359304 | tf_op jit(solution)/shard_map/ppermute | solution.py:81
  64.4 38.6 %collective-permute-start.5 = (bf16[768,512]{1,0:T(8,128)(2,1)}, bf16[768,512]{1,0:T(8,128)(2,1)}, u32[]{:S(2)}, u32[]{:S(2)}) collective-permute-start(bf16[768,512]{1,0:T(8,128)(2,1)} %collective-permute-done.1), channel_id=1, source_target_pairs={{0,4},{4,0},{8,12},{12,8},{1,5},{5,1},{9,13},{13,9},{2,6},{6,2},{1... | collective-permute-start | bytes 2359304 | tf_op jit(solution)/shard_map/ppermute | solution.py:81
  91.7 46.2 %collective-permute-start.9 = (bf16[768,1024]{1,0:T(8,128)(2,1)}, bf16[768,1024]{1,0:T(8,128)(2,1)}, u32[]{:S(2)}, u32[]{:S(2)}) collective-permute-start(bf16[768,1024]{1,0:T(8,128)(2,1)} %fusion.20), channel_id=1, source_target_pairs={{0,16},{16,0},{1,17},{17,1},{2,18},{18,2},{3,19},{19,3},{4,20},{20... | collective-permute-start | bytes 4718600 | tf_op jit(solution)/shard_map/ppermute | solution.py:81
  93.2 52.0 %collective-permute-start.10 = (bf16[768,1024]{1,0:T(8,128)(2,1)}, bf16[768,1024]{1,0:T(8,128)(2,1)}, u32[]{:S(2)}, u32[]{:S(2)}) collective-permute-start(bf16[768,1024]{1,0:T(8,128)(2,1)} %fusion.20), channel_id=1, source_target_pairs={{0,4},{4,0},{8,12},{12,8},{1,5},{5,1},{9,13},{13,9},{2,6},{6,2},{1... | collective-permute-start | bytes 4718600 | tf_op jit(solution)/shard_map/ppermute | solution.py:81
  96.5 8.6 %collective-permute-start.6 = (bf16[768,512]{1,0:T(8,128)(2,1)}, bf16[768,512]{1,0:T(8,128)(2,1)S(1)}, u32[]{:S(2)}, u32[]{:S(2)}) collective-permute-start(bf16[768,512]{1,0:T(8,128)(2,1)} %collective-permute-done.2), channel_id=1, source_target_pairs={{0,4},{4,0},{8,12},{12,8},{1,5},{5,1},{9,13},{13,9},{2,6},{6,2},{1... | collective-permute-start | bytes 2359304 | tf_op jit(solution)/shard_map/ppermute | solution.py:81
  112.9 16.0 %collective-permute-start.7 = (bf16[128,2048]{0,1:T(8,128)(2,1)}, bf16[128,2048]{0,1:T(8,128)(2,1)}, u32[]{:S(2)}, u32[]{:S(2)}) collective-permute-start(bf16[128,2048]{0,1:T(8,128)(2,1)} %bitcast.165), channel_id=1, source_target_pairs={{0,4},{4,8},{8,12},{1,5},{5,9},{9,13},{2,6},{6,10},{10,14},{3,7},{... | collective-permute-start | bytes 1572872 | tf_op jit(solution)/shard_map/ppermute | solution.py:19
  117.7 11.2 %collective-permute-start.8 = (bf16[128,2048]{0,1:T(8,128)(2,1)}, bf16[128,2048]{0,1:T(8,128)(2,1)}, u32[]{:S(2)}, u32[]{:S(2)}) collective-permute-start(bf16[128,2048]{0,1:T(8,128)(2,1)} %bitcast.166), channel_id=1, source_target_pairs={{4,0},{8,4},{12,8},{5,1},{9,5},{13,9},{6,2},{10,6},{14,10},{7,3},{... | collective-permute-start | bytes 1572872 | tf_op jit(solution)/shard_map/ppermute | solution.py:19
  137.9 9.0 %collective-permute-start.11 = (bf16[768,1024]{1,0:T(8,128)(2,1)}, bf16[768,1024]{1,0:T(8,128)(2,1)S(1)}, u32[]{:S(2)}, u32[]{:S(2)}) collective-permute-start(bf16[768,1024]{1,0:T(8,128)(2,1)} %collective-permute-done.9), channel_id=1, source_target_pairs={{0,4},{4,0},{8,12},{12,8},{1,5},{5,1},{9,13},{13,9},{2,6},{6,2},{1... | collective-permute-start | bytes 4718600 | tf_op jit(solution)/shard_map/ppermute | solution.py:81
  150.5 25.3 %all-to-all-start = ((bf16[4,4,128,192]{2,3,1,0:T(8,128)(2,1)}), bf16[4,4,128,192]{2,3,1,0:T(8,128)(2,1)}, u32[]{:S(2)}, u32[]{:S(2)}) async-start(bf16[4,4,128,192]{2,3,1,0:T(8,128)(2,1)} %bitcast.24), calls=%async_computation | async-start | bytes 1572864 | tf_op jit(solution)/shard_map/all_to_all | solution.py:167
  175.8 24.5 %all-to-all-start.2 = ((bf16[4,4,128,192]{2,3,1,0:T(8,128)(2,1)}), bf16[4,4,128,192]{2,3,1,0:T(8,128)(2,1)}, u32[]{:S(2)}, u32[]{:S(2)}) async-start(bf16[4,4,128,192]{2,3,1,0:T(8,128)(2,1)} %bitcast.150), calls=%async_computation.2 | async-start | bytes 1572864 | tf_op jit(solution)/shard_map/all_to_all | solution.py:167
  200.3 17.0 %all-to-all-start.1 = ((bf16[4,4,128,64]{2,3,1,0:T(8,128)(2,1)}), bf16[4,4,128,64]{2,3,1,0:T(8,128)(2,1)S(1)}, u32[]{:S(2)}, u32[]{:S(2)}) async-start(bf16[4,4,128,64]{2,3,1,0:T(8,128)(2,1)} %bitcast.160), calls=%async_computation.1 | async-start | bytes 524288 | tf_op jit(solution)/shard_map/all_to_all | solution.py:183
  217.3 13.2 %all-to-all-start.3 = ((bf16[4,4,128,64]{2,3,1,0:T(8,128)(2,1)}), bf16[4,4,128,64]{2,3,1,0:T(8,128)(2,1)}, u32[]{:S(2)}, u32[]{:S(2)}) async-start(bf16[4,4,128,64]{2,3,1,0:T(8,128)(2,1)} %bitcast.161), calls=%async_computation.3 | async-start | bytes 524288 | tf_op jit(solution)/shard_map/all_to_all | solution.py:183
  236.1 5.8 %collective-permute-start.12 = (f32[4,2,1152]{2,1,0:T(2,128)S(1)}, f32[4,2,1152]{2,1,0:T(2,128)S(1)}, u32[]{:S(2)}, u32[]{:S(2)}) collective-permute-start(f32[4,2,1152]{2,1,0:T(2,128)S(1)} %get-tuple-element.8), channel_id=1, source_target_pairs={{0,1},{1,2},{2,3},{3,0},{4,5},{5,6},{6,7},{7,4},{8,9},{9,10},{10,1... | collective-permute-start | bytes 110600 | tf_op jit(solution)/shard_map/ppermute | solution.py:295
  236.4 5.5 %collective-permute-start.13 = (f32[4,2,1152]{2,1,0:T(2,128)S(1)}, f32[4,2,1152]{2,1,0:T(2,128)S(1)}, u32[]{:S(2)}, u32[]{:S(2)}) collective-permute-start(f32[4,2,1152]{2,1,0:T(2,128)S(1)} %get-tuple-element.10), channel_id=1, source_target_pairs={{0,2},{1,3},{2,0},{3,1},{4,6},{5,7},{6,4},{7,5},{8,10},{9,11},{10,... | collective-permute-start | bytes 110600 | tf_op jit(solution)/shard_map/ppermute | solution.py:295
  238.0 4.5 %collective-permute-start.14 = (f32[4,2,1152]{2,1,0:T(2,128)S(1)}, f32[4,2,1152]{2,1,0:T(2,128)S(1)}, u32[]{:S(2)}, u32[]{:S(2)}) collective-permute-start(f32[4,2,1152]{2,1,0:T(2,128)S(1)} %get-tuple-element.9), channel_id=1, source_target_pairs={{0,3},{1,0},{2,1},{3,2},{4,7},{5,4},{6,5},{7,6},{8,11},{9,8},{10,9... | collective-permute-start | bytes 110600 | tf_op jit(solution)/shard_map/ppermute | solution.py:295
  242.5 4.3 %collective-permute-start.15 = (f32[2,1152]{1,0:T(2,128)S(1)}, f32[2,1152]{1,0:T(2,128)S(1)}, u32[]{:S(2)}, u32[]{:S(2)}) collective-permute-start(f32[2,1152]{1,0:T(2,128)S(1)} %get-tuple-element.11), channel_id=1, source_target_pairs={{0,4},{4,8},{8,12},{12,0},{1,5},{5,9},{9,13},{13,1},{2,6},{6,10},{... | collective-permute-start | bytes 27656 | tf_op jit(solution)/shard_map/ppermute | solution.py:302
  242.6 4.3 %collective-permute-start.16 = (f32[2,1152]{1,0:T(2,128)S(1)}, f32[2,1152]{1,0:T(2,128)S(1)}, u32[]{:S(2)}, u32[]{:S(2)}) collective-permute-start(f32[2,1152]{1,0:T(2,128)S(1)} %get-tuple-element.13), channel_id=1, source_target_pairs={{0,8},{4,12},{8,0},{12,4},{1,9},{5,13},{9,1},{13,5},{2,10},{6,14},... | collective-permute-start | bytes 27656 | tf_op jit(solution)/shard_map/ppermute | solution.py:302
  243.7 3.2 %collective-permute-start.17 = (f32[2,1152]{1,0:T(2,128)S(1)}, f32[2,1152]{1,0:T(2,128)S(1)}, u32[]{:S(2)}, u32[]{:S(2)}) collective-permute-start(f32[2,1152]{1,0:T(2,128)S(1)} %get-tuple-element.12), channel_id=1, source_target_pairs={{0,12},{4,0},{8,4},{12,8},{1,13},{5,1},{9,5},{13,9},{2,14},{6,2},{... | collective-permute-start | bytes 27656 | tf_op jit(solution)/shard_map/ppermute | solution.py:302
  (18 other events, 77.8 us)
Sparse Core Ops, SparseCore 0:
  10.1 30.6 all-gather.2
  42.3 45.3 all-gather.4

commit v16 on v15

--- a/solution.py
+++ b/solution.py
@@ -55,7 +55,7 @@
     return lax.dynamic_slice_in_dim(doubled, start, (plane_count - 1) * block, axis=axis)
 
 
-def gather_pieces(shards, swap_first=False, skip_middle=False):
+def gather_pieces(shards, swap_first=False, skip_middle=False, full_rows=False):
     levels = replica_levels()
     if skip_middle and len(levels) == 3:
         levels = [levels[0], levels[2]]
@@ -74,7 +74,7 @@
         axis=1,
     )
     gathered = lax.all_gather(mine, "plane", axis=0, tiled=True)
-    held = [(own, rotate_rows(gathered, 0))]
+    held = [(own, gathered if full_rows else rotate_rows(gathered, 0))]
     for bit, (axis, size, flip) in enumerate(levels):
         swap = [(i, i ^ flip) for i in range(size)]
         held = held + [
@@ -84,34 +84,44 @@
     results = []
     offset = 0
     for shard, width in zip(shards, widths):
-        results.append((shard, [(piece, block[:, offset : offset + width]) for piece, block in held], width))
+        results.append(
+            (
+                shard,
+                [(piece, block[:, offset : offset + width]) for piece, block in held],
+                width,
+                full_rows,
+            )
+        )
         offset += width
     return results
 
 
 def project(inputs, pieces):
-    shard, held, width = pieces
+    shard, held, width, full_rows = pieces
     rows = shard.shape[0]
-    local_inputs = lax.dynamic_slice_in_dim(inputs, lax.axis_index("plane") * rows, rows, axis=1)
-    local = jnp.dot(local_inputs, shard, preferred_element_type=jnp.float32)
-    remote_inputs = rotate_rows(inputs, 1)
-    remote = jnp.zeros_like(local)
+    out = jnp.zeros((inputs.shape[0], shard.shape[1]), jnp.float32)
+    remote_inputs = inputs if full_rows else rotate_rows(inputs, 1)
     for piece, block in held:
         part = jnp.dot(remote_inputs, block, preferred_element_type=jnp.float32)
-        remote = lax.dynamic_update_slice_in_dim(remote, part, piece * width, axis=1)
-    return local + remote
+        out = lax.dynamic_update_slice_in_dim(out, part, piece * width, axis=1)
+    if full_rows:
+        return out
+    local_inputs = lax.dynamic_slice_in_dim(inputs, lax.axis_index("plane") * rows, rows, axis=1)
+    return jnp.dot(local_inputs, shard, preferred_element_type=jnp.float32) + out
 
 
 def assemble(pieces):
-    shard, held, width = pieces
+    shard, held, width, full_rows = pieces
     remote = jnp.zeros((held[0][1].shape[0], width * len(held)), shard.dtype)
     for piece, block in held:
         remote = lax.dynamic_update_slice_in_dim(remote, block, piece * width, axis=1)
-    return shard, remote
+    return shard, remote, full_rows
 
 
 def project_whole(inputs, weights):
-    shard, remote = weights
+    shard, remote, full_rows = weights
+    if full_rows:
+        return jnp.dot(inputs, remote, preferred_element_type=jnp.float32)
     rows = shard.shape[0]
     local_inputs = lax.dynamic_slice_in_dim(inputs, lax.axis_index("plane") * rows, rows, axis=1)
     local = jnp.dot(local_inputs, shard, preferred_element_type=jnp.float32)
@@ -200,7 +210,9 @@
     own_valid = near_valid[1 : sec_block + 1]
     score_scale = 1.0 / math.sqrt(HEAD_DIM)
     cross_qkv_pieces, cross_out_pieces = gather_pieces([cross_qkv, cross_out])
-    plane_qkv_pieces, plane_out_pieces = gather_pieces([plane_qkv, plane_out], skip_middle=True)
+    plane_qkv_pieces, plane_out_pieces = gather_pieces(
+        [plane_qkv, plane_out], skip_middle=True, full_rows=True
+    )
     cross_out_pieces = assemble(cross_out_pieces)
     plane_out_pieces = assemble(plane_out_pieces)
     normed = rms_norm(tokens, norm_gains[0])

time: 257 us -> 252 us (0.981)
  waiting for transfers between devices: 77.9 us -> 97.2 us
  local copies, waits for them, and re-layouts: 51.7 us -> 40.2 us
  other arithmetic: 20.1 us -> 15 us
  matrix products: 53.1 us -> 49.4 us
  starting transfers between devices: 36.3 us -> 32.8 us
    ppermute x10, waiting for transfers between devices: 9.78 us -> 28.5 us  [gather_pieces(): lax.ppermute(block, axis, swap)]
    all_to_all x2, waiting for transfers between devices: 18.2 us -> 28.5 us  [attend_by_section(): lax.all_to_all(outgoing, 'plane', split_axis=0, concat_axis=2, tiled=True)]
    all_gather x2, waiting for transfers between devices: 42.4 us -> 32.1 us  [gather_pieces(): gathered = lax.all_gather(mine, 'plane', axis=0, tiled=True)]
    squeeze x2, local copies, waits for them, and re-layouts: 4.72 us -> 0.6 us  [attend_by_section(): lax.all_to_all(outgoing, 'plane', split_axis=0, concat_axis=2, tiled=True)]
    concatenate x4 -> x2, other arithmetic: 6.97 us -> 2.86 us  [rotate_rows(): doubled = jnp.concatenate([values, values], axis=axis)]
    all_to_all x2, local copies, waits for them, and re-layouts: 5.24 us -> 1.22 us  [attend_by_section(): lax.all_to_all(outgoing, 'plane', split_axis=0, concat_axis=2, tiled=True)]
    dot_general x2 -> x3, matrix products: 3.2 us -> 6.82 us  [the longest x2 4.28 us: project_whole(): return jnp.dot(inputs, remote, preferred_element_type=jnp.float32)]
    dot_general x3 -> x1, matrix products: 3.8 us -> 0.33 us  [project_whole(): local = jnp.dot(local_inputs, shard, preferred_element_type=jnp.float32)]
  transfers between devices with their start and end apart: 24 -> 24, of which waited for: 8 -> 13; matrix products, arithmetic and copies ran while one was open for 44% -> 34% of each run, Pallas kernels for 0% -> 0%
where the time goes in v16:
time: 252 us; the launch traced here: 250 us
  waiting for transfers between devices  97.2 us (39%)
  matrix products  49.4 us (20%)
  local copies, waits for them, and re-layouts  40.2 us (16%)
  starting transfers between devices  32.8 us (13%)
  between operations  15.2 us (6%)
  other arithmetic  15 us (6%)
    all_gather x2, waiting for transfers between devices, gather_pieces(): gathered = lax.all_gather(mine, 'plane', axis=0, tiled=True)  32.1 us
    all_to_all x2, waiting for transfers between devices, attend_by_section(): lax.all_to_all(outgoing, 'plane', split_axis=0, concat_axis=2, tiled=True)  28.5 us
    ppermute x10, waiting for transfers between devices, gather_pieces(): lax.ppermute(block, axis, swap)  28.5 us
    dot_general x12, matrix products, project(): part = jnp.dot(remote_inputs, block, preferred_element_type=jnp.float32)  23.5 us
    dynamic_update_slice x12, local copies, waits for them, and re-layouts, assemble(): lax.dynamic_update_slice_in_dim(remote, block, piece * width, axis=1)  16.8 us
    sub x2, matrix products, masked_softmax(): expo = jnp.where(allowed, jnp.exp(shifted - top), 0.0)  8.9 us
    all_to_all x2, starting transfers between devices, attend_by_section(): lax.all_to_all(homeward, 'plane', split_axis=0, concat_axis=1, tiled=True)  7.49 us
    all_to_all x2, starting transfers between devices, attend_by_section(): lax.all_to_all(outgoing, 'plane', split_axis=0, concat_axis=2, tiled=True)  7.34 us
  transfers between devices with their start and end apart: 24, of which 13 were waited for; matrix products, arithmetic and copies ran while one was open for 34% of the time, Pallas kernels for 0%

profile of v16, /device:TPU:0, one launch (start us, length us, event | category | flops | bytes accessed | tf_op | source)
XLA Modules:
  0.0 249.9 jit_solution(2289718857988038591)
XLA Ops:
  14.5 25.8 %all-gather.3.cloned.1.call-done = bf16[1024,512]{1,0:T(8,128)(2,1)} async-done(((bf16[256,512]{1,0:T(8,128)(2,1)}), bf16[1024,512]{1,0:T(8,128)(2,1)}) %all-gather.3.cloned.1.call-update) | async-done | bytes 1048592 | tf_op jit(solution)/shard_map/all_gather | solution.py:76
  40.3 2.6 %fusion.53 = bf16[768,512]{1,0:T(8,128)(2,1)} fusion(s32[]{:T(128)S(6)} %select_n.237, bf16[1024,512]{1,0:T(8,128)(2,1)} %all-gather.3.cloned.1.call-done), kind=kLoop, calls=%fused_computation.81 | loop fusion | flops 1572864 | bytes 1835012 | tf_op jit(solution)/shard_map/concatenate | solution.py:54
  49.8 2.2 convolution_dynamic-update-slice_fusion.7
  52.0 10.4 %collective-permute-done = bf16[768,512]{1,0:T(8,128)(2,1)} collective-permute-done((bf16[768,512]{1,0:T(8,128)(2,1)}, bf16[768,512]{1,0:T(8,128)(2,1)}, u32[]{:S(2)}, u32[]{:S(2)}) %collective-permute-start) | collective-permute-done | bytes 786464 | tf_op jit(solution)/shard_map/ppermute | solution.py:81
  65.4 2.2 convolution_dynamic-update-slice_fusion.6
  70.8 10.2 %collective-permute-done.2 = bf16[768,512]{1,0:T(8,128)(2,1)} collective-permute-done((bf16[768,512]{1,0:T(8,128)(2,1)}, bf16[768,512]{1,0:T(8,128)(2,1)}, u32[]{:S(2)}, u32[]{:S(2)}) %collective-permute-start.2) | collective-permute-done | bytes 786464 | tf_op jit(solution)/shard_map/ppermute | solution.py:81
  81.0 6.3 %all-gather.5.cloned.1.call-done = bf16[1024,1024]{1,0:T(8,128)(2,1)} async-done(((bf16[256,1024]{1,0:T(8,128)(2,1)}), bf16[1024,1024]{1,0:T(8,128)(2,1)}) %all-gather.5.cloned.1.call-update) | async-done | bytes 2097168 | tf_op jit(solution)/shard_map/all_gather | solution.py:76
  88.8 2.2 convolution_dynamic-update-slice_fusion.4
  93.1 2.7 %convolution_dynamic-update-slice_fusion.3 = f32[256,3072]{1,0:T(8,128)} fusion(f32[256,3072]{1,0:T(8,128)} %convolution_dynamic-update-slice_fusion.4, s32[]{:T(128)S(6)} %select_n.254, bf16[256,768]{1,0:T(8,128)(2,1)S(1)} %fusion.68, bf16[768,512]{1,0:T(8,128)(2,1)} %collective-permute-done.3), kind=kOutput, calls=%fused_computation.57 | convolution fusion | flops 150994944 | bytes 1376260 | tf_op jit(solution)/shard_map/dot_general | solution.py:105
  102.4 2.5 %fusion.4 = bf16[256,3072]{1,0:T(8,128)(2,1)S(1)} fusion(f32[256,3072]{1,0:T(8,128)} %convolution_dynamic-update-slice_fusion, bf16[256,3072]{1,0:T(8,128)(2,1)S(1)} %copy-done, bf16[256,1024]{1,0:T(8,128)(2,1)} %bitcast.150, s32[]{:T(128)S(6)} %select_n.236), kind=kOutput, calls=%fused_computation.14 | convolution fusion | flops 404226048 | bytes 6422532 | tf_op jit(solution)/shard_map/dot_general | solution.py:110
  106.0 3.2 %collective-permute-start.7 = (bf16[128,2048]{0,1:T(8,128)(2,1)}, bf16[128,2048]{0,1:T(8,128)(2,1)}, u32[]{:S(2)}, u32[]{:S(2)}) collective-permute-start(bf16[128,2048]{0,1:T(8,128)(2,1)} %bitcast.4), channel_id=1, source_target_pairs={{0,4},{4,8},{8,12},{1,5},{5,9},{9,13},{2,6},{6,10},{10,14},{3,7},{... | collective-permute-start | bytes 1572872 | tf_op jit(solution)/shard_map/ppermute | solution.py:19
  123.8 3.2 %fusion.132 = (f32[2,16,128]{2,1,0:T(8,128)S(1)}, f32[2,16,128,384]{3,2,1,0:T(8,128)S(1)}) fusion(f32[2,16,128,384]{3,2,1,0:T(8,128)S(1)} %fusion.27, pred[2,128,384]{2,1,0:T(8,128)(4,1)S(1)} %copy-done.12), kind=kOutput, calls=%fused_computation.191 | output fusion | flops 11010431 | bytes 12697600 | tf_op jit(solution)/shard_map/sub | solution.py:31
  127.1 7.9 %collective-permute-done.9 = bf16[1024,1024]{1,0:T(8,128)(2,1)} collective-permute-done((bf16[1024,1024]{1,0:T(8,128)(2,1)}, bf16[1024,1024]{1,0:T(8,128)(2,1)}, u32[]{:S(2)}, u32[]{:S(2)}) %collective-permute-start.9) | collective-permute-done | bytes 2097184 | tf_op jit(solution)/shard_map/ppermute | solution.py:81
  147.1 3.6 %all-to-all-start = ((bf16[4,4,128,192]{2,3,1,0:T(8,128)(2,1)}), bf16[4,4,128,192]{2,3,1,0:T(8,128)(2,1)S(1)}, u32[]{:S(2)}, u32[]{:S(2)}) async-start(bf16[4,4,128,192]{2,3,1,0:T(8,128)(2,1)} %bitcast.24), calls=%async_computation | async-start | bytes 1572864 | tf_op jit(solution)/shard_map/all_to_all | solution.py:177
  154.2 17.6 %all-to-all-done = bf16[4,4,128,192]{2,3,1,0:T(8,128)(2,1)S(1)} async-done(((bf16[4,4,128,192]{2,3,1,0:T(8,128)(2,1)}), bf16[4,4,128,192]{2,3,1,0:T(8,128)(2,1)S(1)}, u32[]{:S(2)}, u32[]{:S(2)}) %all-to-all-start) | async-done | bytes 786464 | tf_op jit(solution)/shard_map/all_to_all | solution.py:177
  171.8 3.7 %all-to-all-start.2 = ((bf16[4,4,128,192]{2,3,1,0:T(8,128)(2,1)}), bf16[4,4,128,192]{2,3,1,0:T(8,128)(2,1)S(1)}, u32[]{:S(2)}, u32[]{:S(2)}) async-start(bf16[4,4,128,192]{2,3,1,0:T(8,128)(2,1)} %bitcast.34), calls=%async_computation.2 | async-start | bytes 1572864 | tf_op jit(solution)/shard_map/all_to_all | solution.py:177
  184.7 10.9 %all-to-all-done.2 = bf16[4,4,128,192]{2,3,1,0:T(8,128)(2,1)S(1)} async-done(((bf16[4,4,128,192]{2,3,1,0:T(8,128)(2,1)}), bf16[4,4,128,192]{2,3,1,0:T(8,128)(2,1)S(1)}, u32[]{:S(2)}, u32[]{:S(2)}) %all-to-all-start.2) | async-done | bytes 786464 | tf_op jit(solution)/shard_map/all_to_all | solution.py:177
  196.5 5.0 %fusion.142 = (f32[4,512]{1,0:T(4,128)S(1)}, f32[4,512,512]{1,2,0:T(8,128)}) fusion(pred[512,512]{0,1:T(8,128)(4,1)} %fusion.51, bf16[4,512,192]{1,2,0:T(8,128)(2,1)S(1)} %squeeze.60), kind=kOutput, calls=%fused_computation.193 | convolution fusion | flops 139461120 | bytes 5251072 | tf_op jit(solution)/shard_map/sub | solution.py:31
  201.5 2.7 %fusion.47 = bf16[4,8,4,8,128]{4,3,2,1,0:T(8,128)(2,1)S(1)} fusion(f32[4,512,512]{1,2,0:T(8,128)} %get-tuple-element.31, f32[4,512]{1,0:T(4,128)S(1)} %get-tuple-element.30, bf16[4,512,192]{1,2,0:T(8,128)(2,1)S(1)} %squeeze.60), kind=kOutput, calls=%fused_computation.66 | convolution fusion | flops 136445952 | bytes 4726784 | tf_op jit(solution)/shard_map/nqk,nkd->nqd/dot_general | solution.py:187
  204.9 3.4 %all-to-all-start.3 = ((bf16[4,4,128,64]{2,3,1,0:T(8,128)(2,1)}), bf16[4,4,128,64]{2,3,1,0:T(8,128)(2,1)S(1)}, u32[]{:S(2)}, u32[]{:S(2)}) async-start(bf16[4,4,128,64]{2,3,1,0:T(8,128)(2,1)} %bitcast.136), calls=%async_computation.3 | async-start | bytes 524288 | tf_op jit(solution)/shard_map/all_to_all | solution.py:193
  208.3 3.9 %fusion.133 = (f32[4,512]{1,0:T(4,128)S(1)}, f32[4,512,512]{1,2,0:T(8,128)}) fusion(pred[512,512]{0,1:T(8,128)(4,1)S(1)} %fusion.52, bf16[4,512,192]{1,2,0:T(8,128)(2,1)S(1)} %squeeze.57), kind=kOutput, calls=%fused_computation.192 | convolution fusion | flops 139461120 | bytes 5251072 | tf_op jit(solution)/shard_map/sub | solution.py:31
  212.2 2.7 %fusion.46 = bf16[4,8,4,8,128]{4,3,2,1,0:T(8,128)(2,1)S(1)} fusion(f32[4,512,512]{1,2,0:T(8,128)} %get-tuple-element.29, f32[4,512]{1,0:T(4,128)S(1)} %get-tuple-element.28, bf16[4,512,192]{1,2,0:T(8,128)(2,1)S(1)} %squeeze.57), kind=kOutput, calls=%fused_computation.65 | convolution fusion | flops 136445952 | bytes 4726784 | tf_op jit(solution)/shard_map/nqk,nkd->nqd/dot_general | solution.py:187
  216.7 4.1 %all-to-all-start.1 = ((bf16[4,4,128,64]{2,3,1,0:T(8,128)(2,1)}), bf16[4,4,128,64]{2,3,1,0:T(8,128)(2,1)S(1)}, u32[]{:S(2)}, u32[]{:S(2)}) async-start(bf16[4,4,128,64]{2,3,1,0:T(8,128)(2,1)} %bitcast.138), calls=%async_computation.1 | async-start | bytes 524288 | tf_op jit(solution)/shard_map/all_to_all | solution.py:193
  224.7 4.1 %all-to-all-done.1 = bf16[4,4,128,64]{2,3,1,0:T(8,128)(2,1)S(1)} async-done(((bf16[4,4,128,64]{2,3,1,0:T(8,128)(2,1)}), bf16[4,4,128,64]{2,3,1,0:T(8,128)(2,1)S(1)}, u32[]{:S(2)}, u32[]{:S(2)}) %all-to-all-start.1) | async-done | bytes 262176 | tf_op jit(solution)/shard_map/all_to_all | solution.py:193
  (159 shorter events, 91.5 us)
Async XLA Ops:
  7.2 33.1 %all-gather.3.cloned.1.call-start = ((), (), s32[]{:S(2)}) async-start(), calls=%async_computation.4 | async-start | bytes 1310720 | tf_op jit(solution)/shard_map/all_gather | solution.py:76
  9.4 77.9 %all-gather.5.cloned.1.call-start = ((), (), s32[]{:S(2)}) async-start(), calls=%async_computation.5 | async-start | bytes 2621440 | tf_op jit(solution)/shard_map/all_gather | solution.py:76
  42.9 19.5 %collective-permute-start = (bf16[768,512]{1,0:T(8,128)(2,1)}, bf16[768,512]{1,0:T(8,128)(2,1)}, u32[]{:S(2)}, u32[]{:S(2)}) collective-permute-start(bf16[768,512]{1,0:T(8,128)(2,1)} %fusion.53), channel_id=1, source_target_pairs={{0,16},{16,0},{1,17},{17,1},{2,18},{18,2},{3,19},{19,3},{4,20},{20... | collective-permute-start | bytes 2359304 | tf_op jit(solution)/shard_map/ppermute | solution.py:81
  44.4 19.5 %collective-permute-start.1 = (bf16[768,512]{1,0:T(8,128)(2,1)}, bf16[768,512]{1,0:T(8,128)(2,1)}, u32[]{:S(2)}, u32[]{:S(2)}) collective-permute-start(bf16[768,512]{1,0:T(8,128)(2,1)} %fusion.53), channel_id=1, source_target_pairs={{0,8},{4,12},{8,0},{12,4},{1,9},{5,13},{9,1},{13,5},{2,10},{6,14},... | collective-permute-start | bytes 2359304 | tf_op jit(solution)/shard_map/ppermute | solution.py:81
  46.6 45.4 %collective-permute-start.3 = (bf16[768,512]{1,0:T(8,128)(2,1)}, bf16[768,512]{1,0:T(8,128)(2,1)}, u32[]{:S(2)}, u32[]{:S(2)}) collective-permute-start(bf16[768,512]{1,0:T(8,128)(2,1)} %fusion.53), channel_id=1, source_target_pairs={{0,4},{4,0},{8,12},{12,8},{1,5},{5,1},{9,13},{13,9},{2,6},{6,2},{1... | collective-permute-start | bytes 2359304 | tf_op jit(solution)/shard_map/ppermute | solution.py:81
  62.4 18.6 %collective-permute-start.2 = (bf16[768,512]{1,0:T(8,128)(2,1)}, bf16[768,512]{1,0:T(8,128)(2,1)}, u32[]{:S(2)}, u32[]{:S(2)}) collective-permute-start(bf16[768,512]{1,0:T(8,128)(2,1)} %collective-permute-done), channel_id=1, source_target_pairs={{0,8},{4,12},{8,0},{12,4},{1,9},{5,13},{9,1},{13,5},{2,10},{6,14},... | collective-permute-start | bytes 2359304 | tf_op jit(solution)/shard_map/ppermute | solution.py:81
  63.9 31.9 %collective-permute-start.4 = (bf16[768,512]{1,0:T(8,128)(2,1)}, bf16[768,512]{1,0:T(8,128)(2,1)}, u32[]{:S(2)}, u32[]{:S(2)}) collective-permute-start(bf16[768,512]{1,0:T(8,128)(2,1)} %collective-permute-done), channel_id=1, source_target_pairs={{0,4},{4,0},{8,12},{12,8},{1,5},{5,1},{9,13},{13,9},{2,6},{6,2},{1... | collective-permute-start | bytes 2359304 | tf_op jit(solution)/shard_map/ppermute | solution.py:81
  63.9 34.1 %collective-permute-start.5 = (bf16[768,512]{1,0:T(8,128)(2,1)}, bf16[768,512]{1,0:T(8,128)(2,1)}, u32[]{:S(2)}, u32[]{:S(2)}) collective-permute-start(bf16[768,512]{1,0:T(8,128)(2,1)} %collective-permute-done.1), channel_id=1, source_target_pairs={{0,4},{4,0},{8,12},{12,8},{1,5},{5,1},{9,13},{13,9},{2,6},{6,2},{1... | collective-permute-start | bytes 2359304 | tf_op jit(solution)/shard_map/ppermute | solution.py:81
  81.0 19.2 %collective-permute-start.6 = (bf16[768,512]{1,0:T(8,128)(2,1)}, bf16[768,512]{1,0:T(8,128)(2,1)}, u32[]{:S(2)}, u32[]{:S(2)}) collective-permute-start(bf16[768,512]{1,0:T(8,128)(2,1)} %collective-permute-done.2), channel_id=1, source_target_pairs={{0,4},{4,0},{8,12},{12,8},{1,5},{5,1},{9,13},{13,9},{2,6},{6,2},{1... | collective-permute-start | bytes 2359304 | tf_op jit(solution)/shard_map/ppermute | solution.py:81
  87.3 47.7 %collective-permute-start.9 = (bf16[1024,1024]{1,0:T(8,128)(2,1)}, bf16[1024,1024]{1,0:T(8,128)(2,1)}, u32[]{:S(2)}, u32[]{:S(2)}) collective-permute-start(bf16[1024,1024]{1,0:T(8,128)(2,1)} %all-gather.5.cloned.1.call-done), channel_id=1, source_target_pairs={{0,16},{16,0},{1,17},{17,1},{2,18},{18,2},{3,19},{19,3},{4,20},{20... | collective-permute-start | bytes 6291464 | tf_op jit(solution)/shard_map/ppermute | solution.py:81
  92.0 50.3 %collective-permute-start.10 = (bf16[1024,1024]{1,0:T(8,128)(2,1)}, bf16[1024,1024]{1,0:T(8,128)(2,1)}, u32[]{:S(2)}, u32[]{:S(2)}) collective-permute-start(bf16[1024,1024]{1,0:T(8,128)(2,1)} %all-gather.5.cloned.1.call-done), channel_id=1, source_target_pairs={{0,4},{4,0},{8,12},{12,8},{1,5},{5,1},{9,13},{13,9},{2,6},{6,2},{1... | collective-permute-start | bytes 6291464 | tf_op jit(solution)/shard_map/ppermute | solution.py:81
  106.0 14.9 %collective-permute-start.7 = (bf16[128,2048]{0,1:T(8,128)(2,1)}, bf16[128,2048]{0,1:T(8,128)(2,1)}, u32[]{:S(2)}, u32[]{:S(2)}) collective-permute-start(bf16[128,2048]{0,1:T(8,128)(2,1)} %bitcast.4), channel_id=1, source_target_pairs={{0,4},{4,8},{8,12},{1,5},{5,9},{9,13},{2,6},{6,10},{10,14},{3,7},{... | collective-permute-start | bytes 1572872 | tf_op jit(solution)/shard_map/ppermute | solution.py:19
  110.2 10.7 %collective-permute-start.8 = (bf16[128,2048]{0,1:T(8,128)(2,1)}, bf16[128,2048]{0,1:T(8,128)(2,1)}, u32[]{:S(2)}, u32[]{:S(2)}) collective-permute-start(bf16[128,2048]{0,1:T(8,128)(2,1)} %bitcast.8), channel_id=1, source_target_pairs={{4,0},{8,4},{12,8},{5,1},{9,5},{13,9},{6,2},{10,6},{14,10},{7,3},{... | collective-permute-start | bytes 1572872 | tf_op jit(solution)/shard_map/ppermute | solution.py:19
  135.0 9.3 %collective-permute-start.11 = (bf16[1024,1024]{1,0:T(8,128)(2,1)}, bf16[1024,1024]{1,0:T(8,128)(2,1)S(1)}, u32[]{:S(2)}, u32[]{:S(2)}) collective-permute-start(bf16[1024,1024]{1,0:T(8,128)(2,1)} %collective-permute-done.9), channel_id=1, source_target_pairs={{0,4},{4,0},{8,12},{12,8},{1,5},{5,1},{9,13},{13,9},{2,6},{6,2},{1... | collective-permute-start | bytes 6291464 | tf_op jit(solution)/shard_map/ppermute | solution.py:81
  147.1 24.7 %all-to-all-start = ((bf16[4,4,128,192]{2,3,1,0:T(8,128)(2,1)}), bf16[4,4,128,192]{2,3,1,0:T(8,128)(2,1)S(1)}, u32[]{:S(2)}, u32[]{:S(2)}) async-start(bf16[4,4,128,192]{2,3,1,0:T(8,128)(2,1)} %bitcast.24), calls=%async_computation | async-start | bytes 1572864 | tf_op jit(solution)/shard_map/all_to_all | solution.py:177
  171.8 23.8 %all-to-all-start.2 = ((bf16[4,4,128,192]{2,3,1,0:T(8,128)(2,1)}), bf16[4,4,128,192]{2,3,1,0:T(8,128)(2,1)S(1)}, u32[]{:S(2)}, u32[]{:S(2)}) async-start(bf16[4,4,128,192]{2,3,1,0:T(8,128)(2,1)} %bitcast.34), calls=%async_computation.2 | async-start | bytes 1572864 | tf_op jit(solution)/shard_map/all_to_all | solution.py:177
  204.9 11.8 %all-to-all-start.3 = ((bf16[4,4,128,64]{2,3,1,0:T(8,128)(2,1)}), bf16[4,4,128,64]{2,3,1,0:T(8,128)(2,1)S(1)}, u32[]{:S(2)}, u32[]{:S(2)}) async-start(bf16[4,4,128,64]{2,3,1,0:T(8,128)(2,1)} %bitcast.136), calls=%async_computation.3 | async-start | bytes 524288 | tf_op jit(solution)/shard_map/all_to_all | solution.py:193
  216.7 12.1 %all-to-all-start.1 = ((bf16[4,4,128,64]{2,3,1,0:T(8,128)(2,1)}), bf16[4,4,128,64]{2,3,1,0:T(8,128)(2,1)S(1)}, u32[]{:S(2)}, u32[]{:S(2)}) async-start(bf16[4,4,128,64]{2,3,1,0:T(8,128)(2,1)} %bitcast.138), calls=%async_computation.1 | async-start | bytes 524288 | tf_op jit(solution)/shard_map/all_to_all | solution.py:193
  231.5 5.8 %collective-permute-start.12 = (f32[4,2,1152]{2,1,0:T(2,128)S(1)}, f32[4,2,1152]{2,1,0:T(2,128)S(1)}, u32[]{:S(2)}, u32[]{:S(2)}) collective-permute-start(f32[4,2,1152]{2,1,0:T(2,128)S(1)} %get-tuple-element.10), channel_id=1, source_target_pairs={{0,1},{1,2},{2,3},{3,0},{4,5},{5,6},{6,7},{7,4},{8,9},{9,10},{10,1... | collective-permute-start | bytes 110600 | tf_op jit(solution)/shard_map/ppermute | solution.py:307
  231.9 5.5 %collective-permute-start.13 = (f32[4,2,1152]{2,1,0:T(2,128)S(1)}, f32[4,2,1152]{2,1,0:T(2,128)S(1)}, u32[]{:S(2)}, u32[]{:S(2)}) collective-permute-start(f32[4,2,1152]{2,1,0:T(2,128)S(1)} %get-tuple-element.12), channel_id=1, source_target_pairs={{0,2},{1,3},{2,0},{3,1},{4,6},{5,7},{6,4},{7,5},{8,10},{9,11},{10,... | collective-permute-start | bytes 110600 | tf_op jit(solution)/shard_map/ppermute | solution.py:307
  233.4 4.5 %collective-permute-start.14 = (f32[4,2,1152]{2,1,0:T(2,128)S(1)}, f32[4,2,1152]{2,1,0:T(2,128)S(1)}, u32[]{:S(2)}, u32[]{:S(2)}) collective-permute-start(f32[4,2,1152]{2,1,0:T(2,128)S(1)} %get-tuple-element.11), channel_id=1, source_target_pairs={{0,3},{1,0},{2,1},{3,2},{4,7},{5,4},{6,5},{7,6},{8,11},{9,8},{10,9... | collective-permute-start | bytes 110600 | tf_op jit(solution)/shard_map/ppermute | solution.py:307
  237.9 3.7 %collective-permute-start.15 = (f32[2,1152]{1,0:T(2,128)S(1)}, f32[2,1152]{1,0:T(2,128)S(1)}, u32[]{:S(2)}, u32[]{:S(2)}) collective-permute-start(f32[2,1152]{1,0:T(2,128)S(1)} %get-tuple-element.13), channel_id=1, source_target_pairs={{0,4},{4,8},{8,12},{12,0},{1,5},{5,9},{9,13},{13,1},{2,6},{6,10},{... | collective-permute-start | bytes 27656 | tf_op jit(solution)/shard_map/ppermute | solution.py:314
  238.0 3.7 %collective-permute-start.16 = (f32[2,1152]{1,0:T(2,128)S(1)}, f32[2,1152]{1,0:T(2,128)S(1)}, u32[]{:S(2)}, u32[]{:S(2)}) collective-permute-start(f32[2,1152]{1,0:T(2,128)S(1)} %get-tuple-element.15), channel_id=1, source_target_pairs={{0,8},{4,12},{8,0},{12,4},{1,9},{5,13},{9,1},{13,5},{2,10},{6,14},... | collective-permute-start | bytes 27656 | tf_op jit(solution)/shard_map/ppermute | solution.py:314
  239.4 2.8 %collective-permute-start.17 = (f32[2,1152]{1,0:T(2,128)S(1)}, f32[2,1152]{1,0:T(2,128)S(1)}, u32[]{:S(2)}, u32[]{:S(2)}) collective-permute-start(f32[2,1152]{1,0:T(2,128)S(1)} %get-tuple-element.14), channel_id=1, source_target_pairs={{0,12},{4,0},{8,4},{12,8},{1,13},{5,1},{9,5},{13,9},{2,14},{6,2},{... | collective-permute-start | bytes 27656 | tf_op jit(solution)/shard_map/ppermute | solution.py:314
  (16 other events, 97.3 us)
Sparse Core Ops, SparseCore 0:
  9.6 30.6 all-gather.2
  41.8 45.3 all-gather.4

commit v17 on v16

--- a/solution.py
+++ b/solution.py
@@ -209,7 +209,7 @@
     near_valid = positions[None, :] < near_counts[:, None]
     own_valid = near_valid[1 : sec_block + 1]
     score_scale = 1.0 / math.sqrt(HEAD_DIM)
-    cross_qkv_pieces, cross_out_pieces = gather_pieces([cross_qkv, cross_out])
+    cross_qkv_pieces, cross_out_pieces = gather_pieces([cross_qkv, cross_out], full_rows=True)
     plane_qkv_pieces, plane_out_pieces = gather_pieces(
         [plane_qkv, plane_out], skip_middle=True, full_rows=True
     )

time: 252 us -> 249 us (0.988)
  matrix products: 49.4 us -> 40.3 us
  waiting for transfers between devices: 97.2 us -> 103 us
  local copies, waits for them, and re-layouts: 40.2 us -> 44.8 us
    dot_general x12, matrix products: 23.5 us -> 17.2 us  [project(): part = jnp.dot(remote_inputs, block, preferred_element_type=jnp.float32)]
    all_gather x2, waiting for transfers between devices: 32.1 us -> 38.1 us  [gather_pieces(): gathered = lax.all_gather(mine, 'plane', axis=0, tiled=True)]
    unnamed x36 -> x20, local copies, waits for them, and re-layouts: 5.47 us -> 0.54 us
    all_to_all x2, waiting for transfers between devices: 28.5 us -> 23.7 us  [attend_by_section(): lax.all_to_all(outgoing, 'plane', split_axis=0, concat_axis=2, tiled=True)]
    dot_general x3 -> x0, matrix products: 4.21 us -> none  [the longest x1 2.55 us: project(): jnp.dot(local_inputs, shard, preferred_element_type=jnp.float32) + out]
    dynamic_update_slice x12, local copies, waits for them, and re-layouts: 16.8 us -> 20.5 us  [assemble(): lax.dynamic_update_slice_in_dim(remote, block, piece * width, axis=1)]
    slice x1 -> x2, local copies, waits for them, and re-layouts: 0.08 us -> 3.7 us  [the longest x1 2.34 us: body(): pair_win[2:sec_block + 2]]
    ppermute x3, waiting for transfers between devices: 2.49 us -> 5.5 us  [body(): gathered = gathered + lax.ppermute(block, 'plane', moved)]
  transfers between devices with their start and end apart: 24 -> 24, of which waited for: 13 -> 14; matrix products, arithmetic and copies ran while one was open for 34% -> 35% of each run, Pallas kernels for 0% -> 0%
where the time goes in v17:
time: 249 us; the launch traced here: 247 us
  waiting for transfers between devices  103 us (41%)
  local copies, waits for them, and re-layouts  44.8 us (18%)
  matrix products  40.3 us (16%)
  starting transfers between devices  30.7 us (12%)
  between operations  15.2 us (6%)
  other arithmetic  13.5 us (5%)
    all_gather x2, waiting for transfers between devices, gather_pieces(): gathered = lax.all_gather(mine, 'plane', axis=0, tiled=True)  38.1 us
    ppermute x10, waiting for transfers between devices, gather_pieces(): lax.ppermute(block, axis, swap)  29.2 us
    all_to_all x2, waiting for transfers between devices, attend_by_section(): lax.all_to_all(outgoing, 'plane', split_axis=0, concat_axis=2, tiled=True)  23.7 us
    dynamic_update_slice x12, local copies, waits for them, and re-layouts, assemble(): lax.dynamic_update_slice_in_dim(remote, block, piece * width, axis=1)  20.5 us
    dot_general x12, matrix products, project(): part = jnp.dot(remote_inputs, block, preferred_element_type=jnp.float32)  17.2 us
    all_to_all x2, starting transfers between devices, attend_by_section(): lax.all_to_all(homeward, 'plane', split_axis=0, concat_axis=1, tiled=True)  8.41 us
    sub x2, matrix products, masked_softmax(): expo = jnp.where(allowed, jnp.exp(shifted - top), 0.0)  7.84 us
    all_to_all x2, starting transfers between devices, attend_by_section(): lax.all_to_all(outgoing, 'plane', split_axis=0, concat_axis=2, tiled=True)  7.21 us
  transfers between devices with their start and end apart: 24, of which 14 were waited for; matrix products, arithmetic and copies ran while one was open for 35% of the time, Pallas kernels for 0%

profile of v17, /device:TPU:0, one launch (start us, length us, event | category | flops | bytes accessed | tf_op | source)
XLA Modules:
  0.0 247.2 jit_solution(15917008372190739685)
XLA Ops:
  14.1 26.6 %all-gather.3.cloned.1.call-done = bf16[1024,512]{1,0:T(8,128)(2,1)} async-done(((bf16[256,512]{1,0:T(8,128)(2,1)}), bf16[1024,512]{1,0:T(8,128)(2,1)}) %all-gather.3.cloned.1.call-update) | async-done | bytes 1048592 | tf_op jit(solution)/shard_map/all_gather | solution.py:76
  45.4 20.5 %collective-permute-done = bf16[1024,512]{1,0:T(8,128)(2,1)} collective-permute-done((bf16[1024,512]{1,0:T(8,128)(2,1)}, bf16[1024,512]{1,0:T(8,128)(2,1)}, u32[]{:S(2)}, u32[]{:S(2)}) %collective-permute-start) | collective-permute-done | bytes 1048608 | tf_op jit(solution)/shard_map/ppermute | solution.py:81
  76.9 11.5 %all-gather.5.cloned.1.call-done = bf16[1024,1024]{1,0:T(8,128)(2,1)} async-done(((bf16[256,1024]{1,0:T(8,128)(2,1)}), bf16[1024,1024]{1,0:T(8,128)(2,1)}) %all-gather.5.cloned.1.call-update) | async-done | bytes 2097168 | tf_op jit(solution)/shard_map/all_gather | solution.py:76
  102.5 2.7 %collective-permute-start.7 = (bf16[128,2048]{1,0:T(8,128)(2,1)}, bf16[128,2048]{1,0:T(8,128)(2,1)}, u32[]{:S(2)}, u32[]{:S(2)}) collective-permute-start(bf16[128,2048]{1,0:T(8,128)(2,1)} %get-tuple-element.4), channel_id=1, source_target_pairs={{0,4},{4,8},{8,12},{1,5},{5,9},{9,13},{2,6},{6,10},{10,14},{3,7},{... | collective-permute-start | bytes 1572872 | tf_op jit(solution)/shard_map/ppermute | solution.py:19
  114.8 2.8 %pad_maximum_fusion.2 = (bf16[2,128,2048]{2,1,0:T(8,128)(2,1)}, bf16[2,128,2048]{2,1,0:T(8,128)(2,1)}) fusion(bf16[2,128,2048]{2,1,0:T(8,128)(2,1)S(1)} %slice.245, bf16[1,128,2048]{2,1,0:T(8,128)(2,1)} %bitcast.5, bf16[1,128,2048]{2,1,0:T(8,128)(2,1)} %bitcast.9), kind=kLoop, calls=%fused_computation.66 | loop fusion | flops 1048576 | bytes 4194304 | tf_op jit(solution)/shard_map/concatenate | solution.py:225
  117.5 2.3 copy.28
  124.3 3.2 %fusion.115 = (f32[2,16,128]{2,1,0:T(8,128)S(1)}, f32[2,16,128,384]{3,2,1,0:T(8,128)S(1)}) fusion(f32[2,16,128,384]{3,2,1,0:T(8,128)S(1)} %fusion.26, pred[2,128,384]{2,1,0:T(8,128)(4,1)S(1)} %broadcast_or_fusion), kind=kOutput, calls=%fused_computation.169 | output fusion | flops 11010431 | bytes 12697600 | tf_op jit(solution)/shard_map/sub | solution.py:31
  127.6 8.5 %collective-permute-done.9 = bf16[1024,1024]{1,0:T(8,128)(2,1)} collective-permute-done((bf16[1024,1024]{1,0:T(8,128)(2,1)}, bf16[1024,1024]{1,0:T(8,128)(2,1)}, u32[]{:S(2)}, u32[]{:S(2)}) %collective-permute-start.9) | collective-permute-done | bytes 2097184 | tf_op jit(solution)/shard_map/ppermute | solution.py:81
  138.4 2.4 fusion.46
  151.4 3.5 %all-to-all-start.2 = ((bf16[4,4,128,192]{2,3,1,0:T(8,128)(2,1)}), bf16[4,4,128,192]{2,3,1,0:T(8,128)(2,1)S(1)}, u32[]{:S(2)}, u32[]{:S(2)}) async-start(bf16[4,4,128,192]{2,3,1,0:T(8,128)(2,1)} %bitcast.34), calls=%async_computation.2 | async-start | bytes 1572864 | tf_op jit(solution)/shard_map/all_to_all | solution.py:177
  162.1 13.9 %all-to-all-done.2 = bf16[4,4,128,192]{2,3,1,0:T(8,128)(2,1)S(1)} async-done(((bf16[4,4,128,192]{2,3,1,0:T(8,128)(2,1)}), bf16[4,4,128,192]{2,3,1,0:T(8,128)(2,1)S(1)}, u32[]{:S(2)}, u32[]{:S(2)}) %all-to-all-start.2) | async-done | bytes 786464 | tf_op jit(solution)/shard_map/all_to_all | solution.py:177
  176.0 3.7 %all-to-all-start = ((bf16[4,4,128,192]{2,3,1,0:T(8,128)(2,1)}), bf16[4,4,128,192]{2,3,1,0:T(8,128)(2,1)S(1)}, u32[]{:S(2)}, u32[]{:S(2)}) async-start(bf16[4,4,128,192]{2,3,1,0:T(8,128)(2,1)} %bitcast.24), calls=%async_computation | async-start | bytes 1572864 | tf_op jit(solution)/shard_map/all_to_all | solution.py:177
  182.5 3.9 %fusion.125 = (f32[4,512]{1,0:T(4,128)S(1)}, f32[4,512,512]{1,2,0:T(8,128)}) fusion(pred[512,512]{0,1:T(8,128)(4,1)S(1)} %fusion.49, bf16[4,512,192]{1,2,0:T(8,128)(2,1)S(1)} %squeeze.60), kind=kOutput, calls=%fused_computation.171 | convolution fusion | flops 139461120 | bytes 5251072 | tf_op jit(solution)/shard_map/sub | solution.py:31
  186.5 2.7 %fusion.45 = bf16[4,8,4,8,128]{4,3,2,1,0:T(8,128)(2,1)S(1)} fusion(f32[4,512,512]{1,2,0:T(8,128)} %get-tuple-element.31, f32[4,512]{1,0:T(4,128)S(1)} %get-tuple-element.30, bf16[4,512,192]{1,2,0:T(8,128)(2,1)S(1)} %squeeze.60), kind=kOutput, calls=%fused_computation.61 | convolution fusion | flops 136445952 | bytes 4726784 | tf_op jit(solution)/shard_map/nqk,nkd->nqd/dot_general | solution.py:187
  189.9 9.8 %all-to-all-done = bf16[4,4,128,192]{2,3,1,0:T(8,128)(2,1)S(1)} async-done(((bf16[4,4,128,192]{2,3,1,0:T(8,128)(2,1)}), bf16[4,4,128,192]{2,3,1,0:T(8,128)(2,1)S(1)}, u32[]{:S(2)}, u32[]{:S(2)}) %all-to-all-start) | async-done | bytes 786464 | tf_op jit(solution)/shard_map/all_to_all | solution.py:177
  199.7 3.4 %all-to-all-start.3 = ((bf16[4,4,128,64]{2,3,1,0:T(8,128)(2,1)}), bf16[4,4,128,64]{2,3,1,0:T(8,128)(2,1)S(1)}, u32[]{:S(2)}, u32[]{:S(2)}) async-start(bf16[4,4,128,64]{2,3,1,0:T(8,128)(2,1)} %bitcast.136), calls=%async_computation.3 | async-start | bytes 524288 | tf_op jit(solution)/shard_map/all_to_all | solution.py:193
  204.0 3.9 %fusion.116 = (f32[4,512]{1,0:T(4,128)S(1)}, f32[4,512,512]{1,2,0:T(8,128)}) fusion(pred[512,512]{0,1:T(8,128)(4,1)S(1)} %fusion.50, bf16[4,512,192]{1,2,0:T(8,128)(2,1)S(1)} %squeeze.57), kind=kOutput, calls=%fused_computation.170 | convolution fusion | flops 139461120 | bytes 5251072 | tf_op jit(solution)/shard_map/sub | solution.py:31
  208.0 2.7 %fusion.44 = bf16[4,8,4,8,128]{4,3,2,1,0:T(8,128)(2,1)S(1)} fusion(f32[4,512,512]{1,2,0:T(8,128)} %get-tuple-element.29, f32[4,512]{1,0:T(4,128)S(1)} %get-tuple-element.28, bf16[4,512,192]{1,2,0:T(8,128)(2,1)S(1)} %squeeze.57), kind=kOutput, calls=%fused_computation.60 | convolution fusion | flops 136445952 | bytes 4726784 | tf_op jit(solution)/shard_map/nqk,nkd->nqd/dot_general | solution.py:187
  211.5 5.0 %all-to-all-start.1 = ((bf16[4,4,128,64]{2,3,1,0:T(8,128)(2,1)}), bf16[4,4,128,64]{2,3,1,0:T(8,128)(2,1)S(1)}, u32[]{:S(2)}, u32[]{:S(2)}) async-start(bf16[4,4,128,64]{2,3,1,0:T(8,128)(2,1)} %bitcast.138), calls=%async_computation.1 | async-start | bytes 524288 | tf_op jit(solution)/shard_map/all_to_all | solution.py:193
  218.4 2.1 fusion.134
  220.5 4.0 %all-to-all-done.1 = bf16[4,4,128,64]{2,3,1,0:T(8,128)(2,1)S(1)} async-done(((bf16[4,4,128,64]{2,3,1,0:T(8,128)(2,1)}), bf16[4,4,128,64]{2,3,1,0:T(8,128)(2,1)S(1)}, u32[]{:S(2)}, u32[]{:S(2)}) %all-to-all-start.1) | async-done | bytes 262176 | tf_op jit(solution)/shard_map/all_to_all | solution.py:193
  224.5 2.2 add_convert_fusion.1
  229.3 2.1 collective-permute-done.14
  231.4 2.4 collective-permute-done.13
  (141 shorter events, 86.2 us)
Async XLA Ops:
  7.2 33.6 %all-gather.3.cloned.1.call-start = ((), (), s32[]{:S(2)}) async-start(), calls=%async_computation.4 | async-start | bytes 1310720 | tf_op jit(solution)/shard_map/all_gather | solution.py:76
  10.0 78.4 %all-gather.5.cloned.1.call-start = ((), (), s32[]{:S(2)}) async-start(), calls=%async_computation.5 | async-start | bytes 2621440 | tf_op jit(solution)/shard_map/all_gather | solution.py:76
  40.8 25.1 %collective-permute-start = (bf16[1024,512]{1,0:T(8,128)(2,1)}, bf16[1024,512]{1,0:T(8,128)(2,1)}, u32[]{:S(2)}, u32[]{:S(2)}) collective-permute-start(bf16[1024,512]{1,0:T(8,128)(2,1)} %all-gather.3.cloned.1.call-done), channel_id=1, source_target_pairs={{0,16},{16,0},{1,17},{17,1},{2,18},{18,2},{3,19},{19,3},{4,20},{20... | collective-permute-start | bytes 3145736 | tf_op jit(solution)/shard_map/ppermute | solution.py:81
  42.2 27.5 %collective-permute-start.1 = (bf16[1024,512]{1,0:T(8,128)(2,1)}, bf16[1024,512]{1,0:T(8,128)(2,1)}, u32[]{:S(2)}, u32[]{:S(2)}) collective-permute-start(bf16[1024,512]{1,0:T(8,128)(2,1)} %all-gather.3.cloned.1.call-done), channel_id=1, source_target_pairs={{0,8},{4,12},{8,0},{12,4},{1,9},{5,13},{9,1},{13,5},{2,10},{6,14},... | collective-permute-start | bytes 3145736 | tf_op jit(solution)/shard_map/ppermute | solution.py:81
  44.6 48.7 %collective-permute-start.3 = (bf16[1024,512]{1,0:T(8,128)(2,1)}, bf16[1024,512]{1,0:T(8,128)(2,1)}, u32[]{:S(2)}, u32[]{:S(2)}) collective-permute-start(bf16[1024,512]{1,0:T(8,128)(2,1)} %all-gather.3.cloned.1.call-done), channel_id=1, source_target_pairs={{0,4},{4,0},{8,12},{12,8},{1,5},{5,1},{9,13},{13,9},{2,6},{6,2},{1... | collective-permute-start | bytes 3145736 | tf_op jit(solution)/shard_map/ppermute | solution.py:81
  65.8 24.2 %collective-permute-start.2 = (bf16[1024,512]{1,0:T(8,128)(2,1)}, bf16[1024,512]{1,0:T(8,128)(2,1)}, u32[]{:S(2)}, u32[]{:S(2)}) collective-permute-start(bf16[1024,512]{1,0:T(8,128)(2,1)} %collective-permute-done), channel_id=1, source_target_pairs={{0,8},{4,12},{8,0},{12,4},{1,9},{5,13},{9,1},{13,5},{2,10},{6,14},... | collective-permute-start | bytes 3145736 | tf_op jit(solution)/shard_map/ppermute | solution.py:81
  69.8 27.4 %collective-permute-start.4 = (bf16[1024,512]{1,0:T(8,128)(2,1)}, bf16[1024,512]{1,0:T(8,128)(2,1)}, u32[]{:S(2)}, u32[]{:S(2)}) collective-permute-start(bf16[1024,512]{1,0:T(8,128)(2,1)} %collective-permute-done), channel_id=1, source_target_pairs={{0,4},{4,0},{8,12},{12,8},{1,5},{5,1},{9,13},{13,9},{2,6},{6,2},{1... | collective-permute-start | bytes 3145736 | tf_op jit(solution)/shard_map/ppermute | solution.py:81
  69.8 29.0 %collective-permute-start.5 = (bf16[1024,512]{1,0:T(8,128)(2,1)}, bf16[1024,512]{1,0:T(8,128)(2,1)}, u32[]{:S(2)}, u32[]{:S(2)}) collective-permute-start(bf16[1024,512]{1,0:T(8,128)(2,1)} %collective-permute-done.1), channel_id=1, source_target_pairs={{0,4},{4,0},{8,12},{12,8},{1,5},{5,1},{9,13},{13,9},{2,6},{6,2},{1... | collective-permute-start | bytes 3145736 | tf_op jit(solution)/shard_map/ppermute | solution.py:81
  88.4 47.7 %collective-permute-start.9 = (bf16[1024,1024]{1,0:T(8,128)(2,1)}, bf16[1024,1024]{1,0:T(8,128)(2,1)}, u32[]{:S(2)}, u32[]{:S(2)}) collective-permute-start(bf16[1024,1024]{1,0:T(8,128)(2,1)} %all-gather.5.cloned.1.call-done), channel_id=1, source_target_pairs={{0,16},{16,0},{1,17},{17,1},{2,18},{18,2},{3,19},{19,3},{4,20},{20... | collective-permute-start | bytes 6291464 | tf_op jit(solution)/shard_map/ppermute | solution.py:81
  90.0 10.4 %collective-permute-start.6 = (bf16[1024,512]{1,0:T(8,128)(2,1)}, bf16[1024,512]{1,0:T(8,128)(2,1)S(1)}, u32[]{:S(2)}, u32[]{:S(2)}) collective-permute-start(bf16[1024,512]{1,0:T(8,128)(2,1)} %collective-permute-done.2), channel_id=1, source_target_pairs={{0,4},{4,0},{8,12},{12,8},{1,5},{5,1},{9,13},{13,9},{2,6},{6,2},{1... | collective-permute-start | bytes 3145736 | tf_op jit(solution)/shard_map/ppermute | solution.py:81
  93.3 51.8 %collective-permute-start.10 = (bf16[1024,1024]{1,0:T(8,128)(2,1)}, bf16[1024,1024]{1,0:T(8,128)(2,1)}, u32[]{:S(2)}, u32[]{:S(2)}) collective-permute-start(bf16[1024,1024]{1,0:T(8,128)(2,1)} %all-gather.5.cloned.1.call-done), channel_id=1, source_target_pairs={{0,4},{4,0},{8,12},{12,8},{1,5},{5,1},{9,13},{13,9},{2,6},{6,2},{1... | collective-permute-start | bytes 6291464 | tf_op jit(solution)/shard_map/ppermute | solution.py:81
  102.5 12.3 %collective-permute-start.7 = (bf16[128,2048]{1,0:T(8,128)(2,1)}, bf16[128,2048]{1,0:T(8,128)(2,1)}, u32[]{:S(2)}, u32[]{:S(2)}) collective-permute-start(bf16[128,2048]{1,0:T(8,128)(2,1)} %get-tuple-element.4), channel_id=1, source_target_pairs={{0,4},{4,8},{8,12},{1,5},{5,9},{9,13},{2,6},{6,10},{10,14},{3,7},{... | collective-permute-start | bytes 1572872 | tf_op jit(solution)/shard_map/ppermute | solution.py:19
  105.2 9.6 %collective-permute-start.8 = (bf16[128,2048]{1,0:T(8,128)(2,1)}, bf16[128,2048]{1,0:T(8,128)(2,1)}, u32[]{:S(2)}, u32[]{:S(2)}) collective-permute-start(bf16[128,2048]{1,0:T(8,128)(2,1)} %get-tuple-element.5), channel_id=1, source_target_pairs={{4,0},{8,4},{12,8},{5,1},{9,5},{13,9},{6,2},{10,6},{14,10},{7,3},{... | collective-permute-start | bytes 1572872 | tf_op jit(solution)/shard_map/ppermute | solution.py:19
  136.0 11.1 %collective-permute-start.11 = (bf16[1024,1024]{1,0:T(8,128)(2,1)}, bf16[1024,1024]{1,0:T(8,128)(2,1)S(1)}, u32[]{:S(2)}, u32[]{:S(2)}) collective-permute-start(bf16[1024,1024]{1,0:T(8,128)(2,1)} %collective-permute-done.9), channel_id=1, source_target_pairs={{0,4},{4,0},{8,12},{12,8},{1,5},{5,1},{9,13},{13,9},{2,6},{6,2},{1... | collective-permute-start | bytes 6291464 | tf_op jit(solution)/shard_map/ppermute | solution.py:81
  151.4 24.5 %all-to-all-start.2 = ((bf16[4,4,128,192]{2,3,1,0:T(8,128)(2,1)}), bf16[4,4,128,192]{2,3,1,0:T(8,128)(2,1)S(1)}, u32[]{:S(2)}, u32[]{:S(2)}) async-start(bf16[4,4,128,192]{2,3,1,0:T(8,128)(2,1)} %bitcast.34), calls=%async_computation.2 | async-start | bytes 1572864 | tf_op jit(solution)/shard_map/all_to_all | solution.py:177
  176.0 23.7 %all-to-all-start = ((bf16[4,4,128,192]{2,3,1,0:T(8,128)(2,1)}), bf16[4,4,128,192]{2,3,1,0:T(8,128)(2,1)S(1)}, u32[]{:S(2)}, u32[]{:S(2)}) async-start(bf16[4,4,128,192]{2,3,1,0:T(8,128)(2,1)} %bitcast.24), calls=%async_computation | async-start | bytes 1572864 | tf_op jit(solution)/shard_map/all_to_all | solution.py:177
  199.7 11.8 %all-to-all-start.3 = ((bf16[4,4,128,64]{2,3,1,0:T(8,128)(2,1)}), bf16[4,4,128,64]{2,3,1,0:T(8,128)(2,1)S(1)}, u32[]{:S(2)}, u32[]{:S(2)}) async-start(bf16[4,4,128,64]{2,3,1,0:T(8,128)(2,1)} %bitcast.136), calls=%async_computation.3 | async-start | bytes 524288 | tf_op jit(solution)/shard_map/all_to_all | solution.py:193
  211.5 13.0 %all-to-all-start.1 = ((bf16[4,4,128,64]{2,3,1,0:T(8,128)(2,1)}), bf16[4,4,128,64]{2,3,1,0:T(8,128)(2,1)S(1)}, u32[]{:S(2)}, u32[]{:S(2)}) async-start(bf16[4,4,128,64]{2,3,1,0:T(8,128)(2,1)} %bitcast.138), calls=%async_computation.1 | async-start | bytes 524288 | tf_op jit(solution)/shard_map/all_to_all | solution.py:193
  227.2 4.2 %collective-permute-start.14 = (f32[4,2,1152]{2,1,0:T(2,128)S(1)}, f32[4,2,1152]{2,1,0:T(2,128)S(1)}, u32[]{:S(2)}, u32[]{:S(2)}) collective-permute-start(f32[4,2,1152]{2,1,0:T(2,128)S(1)} %get-tuple-element.11), channel_id=1, source_target_pairs={{0,3},{1,0},{2,1},{3,2},{4,7},{5,4},{6,5},{7,6},{8,11},{9,8},{10,9... | collective-permute-start | bytes 110600 | tf_op jit(solution)/shard_map/ppermute | solution.py:307
  228.5 5.3 %collective-permute-start.13 = (f32[4,2,1152]{2,1,0:T(2,128)S(1)}, f32[4,2,1152]{2,1,0:T(2,128)S(1)}, u32[]{:S(2)}, u32[]{:S(2)}) collective-permute-start(f32[4,2,1152]{2,1,0:T(2,128)S(1)} %get-tuple-element.12), channel_id=1, source_target_pairs={{0,2},{1,3},{2,0},{3,1},{4,6},{5,7},{6,4},{7,5},{8,10},{9,11},{10,... | collective-permute-start | bytes 110600 | tf_op jit(solution)/shard_map/ppermute | solution.py:307
  229.0 5.8 %collective-permute-start.12 = (f32[4,2,1152]{2,1,0:T(2,128)S(1)}, f32[4,2,1152]{2,1,0:T(2,128)S(1)}, u32[]{:S(2)}, u32[]{:S(2)}) collective-permute-start(f32[4,2,1152]{2,1,0:T(2,128)S(1)} %get-tuple-element.10), channel_id=1, source_target_pairs={{0,1},{1,2},{2,3},{3,0},{4,5},{5,6},{6,7},{7,4},{8,9},{9,10},{10,1... | collective-permute-start | bytes 110600 | tf_op jit(solution)/shard_map/ppermute | solution.py:307
  234.9 2.6 %collective-permute-start.17 = (f32[2,1152]{1,0:T(2,128)S(1)}, f32[2,1152]{1,0:T(2,128)S(1)}, u32[]{:S(2)}, u32[]{:S(2)}) collective-permute-start(f32[2,1152]{1,0:T(2,128)S(1)} %get-tuple-element.14), channel_id=1, source_target_pairs={{0,12},{4,0},{8,4},{12,8},{1,13},{5,1},{9,5},{13,9},{2,14},{6,2},{... | collective-permute-start | bytes 27656 | tf_op jit(solution)/shard_map/ppermute | solution.py:314
  234.9 3.7 %collective-permute-start.16 = (f32[2,1152]{1,0:T(2,128)S(1)}, f32[2,1152]{1,0:T(2,128)S(1)}, u32[]{:S(2)}, u32[]{:S(2)}) collective-permute-start(f32[2,1152]{1,0:T(2,128)S(1)} %get-tuple-element.15), channel_id=1, source_target_pairs={{0,8},{4,12},{8,0},{12,4},{1,9},{5,13},{9,1},{13,5},{2,10},{6,14},... | collective-permute-start | bytes 27656 | tf_op jit(solution)/shard_map/ppermute | solution.py:314
  236.4 3.1 %collective-permute-start.15 = (f32[2,1152]{1,0:T(2,128)S(1)}, f32[2,1152]{1,0:T(2,128)S(1)}, u32[]{:S(2)}, u32[]{:S(2)}) collective-permute-start(f32[2,1152]{1,0:T(2,128)S(1)} %get-tuple-element.13), channel_id=1, source_target_pairs={{0,4},{4,8},{8,12},{12,0},{1,5},{5,9},{9,13},{13,1},{2,6},{6,10},{... | collective-permute-start | bytes 27656 | tf_op jit(solution)/shard_map/ppermute | solution.py:314
  (10 other events, 46.7 us)
Sparse Core Ops, SparseCore 0:
  10.1 30.6 all-gather.2
  42.9 45.4 all-gather.4

commit v18 on v17

--- a/solution.py
+++ b/solution.py
@@ -211,7 +211,7 @@
     score_scale = 1.0 / math.sqrt(HEAD_DIM)
     cross_qkv_pieces, cross_out_pieces = gather_pieces([cross_qkv, cross_out], full_rows=True)
     plane_qkv_pieces, plane_out_pieces = gather_pieces(
-        [plane_qkv, plane_out], skip_middle=True, full_rows=True
+        [plane_qkv, plane_out], swap_first=True, full_rows=True
     )
     cross_out_pieces = assemble(cross_out_pieces)
     plane_out_pieces = assemble(plane_out_pieces)

time: 249 us -> 296 us (1.19)
  waiting for transfers between devices: 103 us -> 148 us
  local copies, waits for them, and re-layouts: 44.8 us -> 41.8 us
    ppermute x10 -> x14, waiting for transfers between devices: 29.2 us -> 65.4 us  [gather_pieces(): lax.ppermute(block, axis, swap)]
    all_gather x2, waiting for transfers between devices: 38.1 us -> 50.4 us  [gather_pieces(): gathered = lax.all_gather(mine, 'plane', axis=0, tiled=True)]
    dot_general x12 -> x16, matrix products: 17.2 us -> 21.6 us  [project(): part = jnp.dot(remote_inputs, block, preferred_element_type=jnp.float32)]
    all_to_all x2, waiting for transfers between devices: 23.7 us -> 19.9 us  [attend_by_section(): lax.all_to_all(outgoing, 'plane', split_axis=0, concat_axis=2, tiled=True)]
    ppermute x10 -> x14, starting transfers between devices: 7.02 us -> 8.62 us  [gather_pieces(): lax.ppermute(block, axis, swap)]
    dynamic_update_slice x12 -> x16, local copies, waits for them, and re-layouts: 20.5 us -> 19.3 us  [assemble(): lax.dynamic_update_slice_in_dim(remote, block, piece * width, axis=1)]
  transfers between devices with their start and end apart: 24 -> 28, of which waited for: 14 -> 13; matrix products, arithmetic and copies ran while one was open for 35% -> 30% of each run, Pallas kernels for 0% -> 0%
where the time goes in v18:
time: 296 us; the launch traced here: 294 us
  waiting for transfers between devices  148 us (50%)
  matrix products  43.1 us (15%)
  local copies, waits for them, and re-layouts  41.8 us (14%)
  starting transfers between devices  32.4 us (11%)
  between operations  14.9 us (5%)
  other arithmetic  14.7 us (5%)
    ppermute x14, waiting for transfers between devices, gather_pieces(): lax.ppermute(block, axis, swap)  65.4 us
    all_gather x2, waiting for transfers between devices, gather_pieces(): gathered = lax.all_gather(mine, 'plane', axis=0, tiled=True)  50.4 us
    dot_general x16, matrix products, project(): part = jnp.dot(remote_inputs, block, preferred_element_type=jnp.float32)  21.6 us
    all_to_all x2, waiting for transfers between devices, attend_by_section(): lax.all_to_all(outgoing, 'plane', split_axis=0, concat_axis=2, tiled=True)  19.9 us
    dynamic_update_slice x16, local copies, waits for them, and re-layouts, assemble(): lax.dynamic_update_slice_in_dim(remote, block, piece * width, axis=1)  19.3 us
    ppermute x14, starting transfers between devices, gather_pieces(): lax.ppermute(block, axis, swap)  8.62 us
    all_to_all x2, starting transfers between devices, attend_by_section(): lax.all_to_all(homeward, 'plane', split_axis=0, concat_axis=1, tiled=True)  8.45 us
    sub x2, matrix products, masked_softmax(): expo = jnp.where(allowed, jnp.exp(shifted - top), 0.0)  7.89 us
  transfers between devices with their start and end apart: 28, of which 13 were waited for; matrix products, arithmetic and copies ran while one was open for 30% of the time, Pallas kernels for 0%

profile of v18, /device:TPU:0, one launch (start us, length us, event | category | flops | bytes accessed | tf_op | source)
XLA Modules:
  0.0 294.4 jit_solution(12585021094691764726)
XLA Ops:
  16.1 24.8 %all-gather.3.cloned.1.call-done = bf16[1024,512]{1,0:T(8,128)(2,1)} async-done(((bf16[256,512]{1,0:T(8,128)(2,1)}), bf16[1024,512]{1,0:T(8,128)(2,1)}) %all-gather.3.cloned.1.call-update) | async-done | bytes 1048592 | tf_op jit(solution)/shard_map/all_gather | solution.py:76
  44.3 25.5 %all-gather.5.cloned.1.call-done = bf16[1024,512]{1,0:T(8,128)(2,1)} async-done(((bf16[256,512]{1,0:T(8,128)(2,1)}), bf16[1024,512]{1,0:T(8,128)(2,1)}) %all-gather.5.cloned.1.call-update) | async-done | bytes 1048592 | tf_op jit(solution)/shard_map/all_gather | solution.py:76
  82.4 34.9 %collective-permute-done.2 = bf16[1024,512]{1,0:T(8,128)(2,1)S(1)} collective-permute-done((bf16[1024,512]{1,0:T(8,128)(2,1)}, bf16[1024,512]{1,0:T(8,128)(2,1)S(1)}, u32[]{:S(2)}, u32[]{:S(2)}) %collective-permute-start.2) | collective-permute-done | bytes 1048608 | tf_op jit(solution)/shard_map/ppermute | solution.py:81
  125.5 2.7 collective-permute-start.7
  135.9 8.4 %collective-permute-done.10 = bf16[1024,512]{1,0:T(8,128)(2,1)} collective-permute-done((bf16[1024,512]{1,0:T(8,128)(2,1)}, bf16[1024,512]{1,0:T(8,128)(2,1)}, u32[]{:S(2)}, u32[]{:S(2)}) %collective-permute-start.10) | collective-permute-done | bytes 1048608 | tf_op jit(solution)/shard_map/ppermute | solution.py:81
  144.3 22.1 %collective-permute-done.11 = bf16[1024,512]{1,0:T(8,128)(2,1)} collective-permute-done((bf16[1024,512]{1,0:T(8,128)(2,1)}, bf16[1024,512]{1,0:T(8,128)(2,1)}, u32[]{:S(2)}, u32[]{:S(2)}) %collective-permute-start.11) | collective-permute-done | bytes 1048608 | tf_op jit(solution)/shard_map/ppermute | solution.py:81
  166.9 2.7 pad_maximum_fusion.2
  169.5 2.3 copy.28
  176.3 3.2 %fusion.112 = (f32[2,16,128]{2,1,0:T(8,128)S(1)}, f32[2,16,128,384]{3,2,1,0:T(8,128)S(1)}) fusion(f32[2,16,128,384]{3,2,1,0:T(8,128)S(1)} %fusion.18, pred[2,128,384]{2,1,0:T(8,128)(4,1)S(1)} %broadcast_or_fusion), kind=kOutput, calls=%fused_computation.182 | output fusion | flops 11010431 | bytes 12697600 | tf_op jit(solution)/shard_map/sub | solution.py:31
  199.7 3.5 %all-to-all-start.2 = ((bf16[4,4,128,192]{2,3,1,0:T(8,128)(2,1)}), bf16[4,4,128,192]{2,3,1,0:T(8,128)(2,1)S(1)}, u32[]{:S(2)}, u32[]{:S(2)}) async-start(bf16[4,4,128,192]{2,3,1,0:T(8,128)(2,1)} %bitcast.34), calls=%async_computation.2 | async-start | bytes 1572864 | tf_op jit(solution)/shard_map/all_to_all | solution.py:177
  213.2 10.5 %all-to-all-done.2 = bf16[4,4,128,192]{2,3,1,0:T(8,128)(2,1)S(1)} async-done(((bf16[4,4,128,192]{2,3,1,0:T(8,128)(2,1)}), bf16[4,4,128,192]{2,3,1,0:T(8,128)(2,1)S(1)}, u32[]{:S(2)}, u32[]{:S(2)}) %all-to-all-start.2) | async-done | bytes 786464 | tf_op jit(solution)/shard_map/all_to_all | solution.py:177
  223.7 3.7 %all-to-all-start = ((bf16[4,4,128,192]{2,3,1,0:T(8,128)(2,1)}), bf16[4,4,128,192]{2,3,1,0:T(8,128)(2,1)S(1)}, u32[]{:S(2)}, u32[]{:S(2)}) async-start(bf16[4,4,128,192]{2,3,1,0:T(8,128)(2,1)} %bitcast.24), calls=%async_computation | async-start | bytes 1572864 | tf_op jit(solution)/shard_map/all_to_all | solution.py:177
  230.2 3.9 %fusion.122 = (f32[4,512]{1,0:T(4,128)S(1)}, f32[4,512,512]{1,2,0:T(8,128)}) fusion(pred[512,512]{0,1:T(8,128)(4,1)S(1)} %copy-done.8, bf16[4,512,192]{1,2,0:T(8,128)(2,1)S(1)} %squeeze.60), kind=kOutput, calls=%fused_computation.184 | convolution fusion | flops 139461120 | bytes 5251072 | tf_op jit(solution)/shard_map/sub | solution.py:31
  234.1 2.7 fusion.25
  237.6 9.3 %all-to-all-done = bf16[4,4,128,192]{2,3,1,0:T(8,128)(2,1)S(1)} async-done(((bf16[4,4,128,192]{2,3,1,0:T(8,128)(2,1)}), bf16[4,4,128,192]{2,3,1,0:T(8,128)(2,1)S(1)}, u32[]{:S(2)}, u32[]{:S(2)}) %all-to-all-start) | async-done | bytes 786464 | tf_op jit(solution)/shard_map/all_to_all | solution.py:177
  246.9 3.4 %all-to-all-start.3 = ((bf16[4,4,128,64]{2,3,1,0:T(8,128)(2,1)}), bf16[4,4,128,64]{2,3,1,0:T(8,128)(2,1)S(1)}, u32[]{:S(2)}, u32[]{:S(2)}) async-start(bf16[4,4,128,64]{2,3,1,0:T(8,128)(2,1)} %bitcast.138), calls=%async_computation.3 | async-start | bytes 524288 | tf_op jit(solution)/shard_map/all_to_all | solution.py:193
  251.3 3.9 %fusion.113 = (f32[4,512]{1,0:T(4,128)S(1)}, f32[4,512,512]{1,2,0:T(8,128)}) fusion(pred[512,512]{0,1:T(8,128)(4,1)S(1)} %copy-done.7, bf16[4,512,192]{1,2,0:T(8,128)(2,1)S(1)} %squeeze.57), kind=kOutput, calls=%fused_computation.183 | convolution fusion | flops 139461120 | bytes 5251072 | tf_op jit(solution)/shard_map/sub | solution.py:31
  255.2 2.7 fusion.24
  258.6 5.0 %all-to-all-start.1 = ((bf16[4,4,128,64]{2,3,1,0:T(8,128)(2,1)}), bf16[4,4,128,64]{2,3,1,0:T(8,128)(2,1)S(1)}, u32[]{:S(2)}, u32[]{:S(2)}) async-start(bf16[4,4,128,64]{2,3,1,0:T(8,128)(2,1)} %bitcast.140), calls=%async_computation.1 | async-start | bytes 524288 | tf_op jit(solution)/shard_map/all_to_all | solution.py:193
  265.4 2.1 fusion.131
  267.5 4.2 %all-to-all-done.1 = bf16[4,4,128,64]{2,3,1,0:T(8,128)(2,1)S(1)} async-done(((bf16[4,4,128,64]{2,3,1,0:T(8,128)(2,1)}), bf16[4,4,128,64]{2,3,1,0:T(8,128)(2,1)S(1)}, u32[]{:S(2)}, u32[]{:S(2)}) %all-to-all-start.1) | async-done | bytes 262176 | tf_op jit(solution)/shard_map/all_to_all | solution.py:193
  271.7 2.2 add_convert_fusion.1
  276.5 2.0 collective-permute-done.18
  278.5 2.5 collective-permute-done.17
  (163 shorter events, 91.0 us)
Async XLA Ops:
  7.2 33.6 %all-gather.3.cloned.1.call-start = ((), (), s32[]{:S(2)}) async-start(), calls=%async_computation.4 | async-start | bytes 1310720 | tf_op jit(solution)/shard_map/all_gather | solution.py:76
  9.4 60.5 %all-gather.5.cloned.1.call-start = ((), (), s32[]{:S(2)}) async-start(), calls=%async_computation.5 | async-start | bytes 1310720 | tf_op jit(solution)/shard_map/all_gather | solution.py:76
  40.9 33.6 %collective-permute-start = (bf16[1024,512]{1,0:T(8,128)(2,1)}, bf16[1024,512]{1,0:T(8,128)(2,1)}, u32[]{:S(2)}, u32[]{:S(2)}) collective-permute-start(bf16[1024,512]{1,0:T(8,128)(2,1)} %all-gather.3.cloned.1.call-done), channel_id=1, source_target_pairs={{0,16},{16,0},{1,17},{17,1},{2,18},{18,2},{3,19},{19,3},{4,20},{20... | collective-permute-start | bytes 3145736 | tf_op jit(solution)/shard_map/ppermute | solution.py:81
  42.5 34.0 %collective-permute-start.1 = (bf16[1024,512]{1,0:T(8,128)(2,1)}, bf16[1024,512]{1,0:T(8,128)(2,1)}, u32[]{:S(2)}, u32[]{:S(2)}) collective-permute-start(bf16[1024,512]{1,0:T(8,128)(2,1)} %all-gather.3.cloned.1.call-done), channel_id=1, source_target_pairs={{0,8},{4,12},{8,0},{12,4},{1,9},{5,13},{9,1},{13,5},{2,10},{6,14},... | collective-permute-start | bytes 3145736 | tf_op jit(solution)/shard_map/ppermute | solution.py:81
  44.3 73.7 %collective-permute-start.3 = (bf16[1024,512]{1,0:T(8,128)(2,1)}, bf16[1024,512]{1,0:T(8,128)(2,1)}, u32[]{:S(2)}, u32[]{:S(2)}) collective-permute-start(bf16[1024,512]{1,0:T(8,128)(2,1)} %all-gather.3.cloned.1.call-done), channel_id=1, source_target_pairs={{0,4},{4,0},{8,12},{12,8},{1,5},{5,1},{9,13},{13,9},{2,6},{6,2},{1... | collective-permute-start | bytes 3145736 | tf_op jit(solution)/shard_map/ppermute | solution.py:81
  69.9 52.2 %collective-permute-start.9 = (bf16[1024,512]{1,0:T(8,128)(2,1)}, bf16[1024,512]{1,0:T(8,128)(2,1)}, u32[]{:S(2)}, u32[]{:S(2)}) collective-permute-start(bf16[1024,512]{1,0:T(8,128)(2,1)} %all-gather.5.cloned.1.call-done), channel_id=1, source_target_pairs={{0,8},{4,12},{8,0},{12,4},{1,9},{5,13},{9,1},{13,5},{2,10},{6,14},... | collective-permute-start | bytes 3145736 | tf_op jit(solution)/shard_map/ppermute | solution.py:81
  74.5 42.9 %collective-permute-start.2 = (bf16[1024,512]{1,0:T(8,128)(2,1)}, bf16[1024,512]{1,0:T(8,128)(2,1)S(1)}, u32[]{:S(2)}, u32[]{:S(2)}) collective-permute-start(bf16[1024,512]{1,0:T(8,128)(2,1)} %collective-permute-done), channel_id=1, source_target_pairs={{0,8},{4,12},{8,0},{12,4},{1,9},{5,13},{9,1},{13,5},{2,10},{6,14},... | collective-permute-start | bytes 3145736 | tf_op jit(solution)/shard_map/ppermute | solution.py:81
  76.4 46.0 %collective-permute-start.4 = (bf16[1024,512]{1,0:T(8,128)(2,1)}, bf16[1024,512]{1,0:T(8,128)(2,1)S(1)}, u32[]{:S(2)}, u32[]{:S(2)}) collective-permute-start(bf16[1024,512]{1,0:T(8,128)(2,1)} %collective-permute-done), channel_id=1, source_target_pairs={{0,4},{4,0},{8,12},{12,8},{1,5},{5,1},{9,13},{13,9},{2,6},{6,2},{1... | collective-permute-start | bytes 3145736 | tf_op jit(solution)/shard_map/ppermute | solution.py:81
  76.5 46.9 %collective-permute-start.5 = (bf16[1024,512]{1,0:T(8,128)(2,1)}, bf16[1024,512]{1,0:T(8,128)(2,1)S(1)}, u32[]{:S(2)}, u32[]{:S(2)}) collective-permute-start(bf16[1024,512]{1,0:T(8,128)(2,1)} %collective-permute-done.1), channel_id=1, source_target_pairs={{0,4},{4,0},{8,12},{12,8},{1,5},{5,1},{9,13},{13,9},{2,6},{6,2},{1... | collective-permute-start | bytes 3145736 | tf_op jit(solution)/shard_map/ppermute | solution.py:81
  117.3 6.6 %collective-permute-start.6 = (bf16[1024,512]{1,0:T(8,128)(2,1)S(1)}, bf16[1024,512]{1,0:T(8,128)(2,1)S(1)}, u32[]{:S(2)}, u32[]{:S(2)}) collective-permute-start(bf16[1024,512]{1,0:T(8,128)(2,1)S(1)} %collective-permute-done.2), channel_id=1, source_target_pairs={{0,4},{4,0},{8,12},{12,8},{1,5},{5,1},{9,13},{13,9},{2,6},{6,2},{1... | collective-permute-start | bytes 3145736 | tf_op jit(solution)/shard_map/ppermute | solution.py:81
  117.9 26.3 %collective-permute-start.10 = (bf16[1024,512]{1,0:T(8,128)(2,1)}, bf16[1024,512]{1,0:T(8,128)(2,1)}, u32[]{:S(2)}, u32[]{:S(2)}) collective-permute-start(bf16[1024,512]{1,0:T(8,128)(2,1)} %all-gather.5.cloned.1.call-done), channel_id=1, source_target_pairs={{0,16},{16,0},{1,17},{17,1},{2,18},{18,2},{3,19},{19,3},{4,20},{20... | collective-permute-start | bytes 3145736 | tf_op jit(solution)/shard_map/ppermute | solution.py:81
  122.1 67.5 %collective-permute-start.12 = (bf16[1024,512]{1,0:T(8,128)(2,1)}, bf16[1024,512]{1,0:T(8,128)(2,1)}, u32[]{:S(2)}, u32[]{:S(2)}) collective-permute-start(bf16[1024,512]{1,0:T(8,128)(2,1)} %all-gather.5.cloned.1.call-done), channel_id=1, source_target_pairs={{0,4},{4,0},{8,12},{12,8},{1,5},{5,1},{9,13},{13,9},{2,6},{6,2},{1... | collective-permute-start | bytes 3145736 | tf_op jit(solution)/shard_map/ppermute | solution.py:81
  122.4 43.9 %collective-permute-start.11 = (bf16[1024,512]{1,0:T(8,128)(2,1)}, bf16[1024,512]{1,0:T(8,128)(2,1)}, u32[]{:S(2)}, u32[]{:S(2)}) collective-permute-start(bf16[1024,512]{1,0:T(8,128)(2,1)} %collective-permute-done.9), channel_id=1, source_target_pairs={{0,16},{16,0},{1,17},{17,1},{2,18},{18,2},{3,19},{19,3},{4,20},{20... | collective-permute-start | bytes 3145736 | tf_op jit(solution)/shard_map/ppermute | solution.py:81
  125.5 40.8 %collective-permute-start.7 = (bf16[128,2048]{1,0:T(8,128)(2,1)}, bf16[128,2048]{1,0:T(8,128)(2,1)}, u32[]{:S(2)}, u32[]{:S(2)}) collective-permute-start(bf16[128,2048]{1,0:T(8,128)(2,1)} %get-tuple-element.4), channel_id=1, source_target_pairs={{0,4},{4,8},{8,12},{1,5},{5,9},{9,13},{2,6},{6,10},{10,14},{3,7},{... | collective-permute-start | bytes 1572872 | tf_op jit(solution)/shard_map/ppermute | solution.py:19
  128.2 38.6 %collective-permute-start.8 = (bf16[128,2048]{1,0:T(8,128)(2,1)}, bf16[128,2048]{1,0:T(8,128)(2,1)}, u32[]{:S(2)}, u32[]{:S(2)}) collective-permute-start(bf16[128,2048]{1,0:T(8,128)(2,1)} %get-tuple-element.5), channel_id=1, source_target_pairs={{4,0},{8,4},{12,8},{5,1},{9,5},{13,9},{6,2},{10,6},{14,10},{7,3},{... | collective-permute-start | bytes 1572872 | tf_op jit(solution)/shard_map/ppermute | solution.py:19
  144.3 47.0 %collective-permute-start.13 = (bf16[1024,512]{1,0:T(8,128)(2,1)}, bf16[1024,512]{1,0:T(8,128)(2,1)}, u32[]{:S(2)}, u32[]{:S(2)}) collective-permute-start(bf16[1024,512]{1,0:T(8,128)(2,1)} %collective-permute-done.9), channel_id=1, source_target_pairs={{0,4},{4,0},{8,12},{12,8},{1,5},{5,1},{9,13},{13,9},{2,6},{6,2},{1... | collective-permute-start | bytes 3145736 | tf_op jit(solution)/shard_map/ppermute | solution.py:81
  166.3 26.6 %collective-permute-start.14 = (bf16[1024,512]{1,0:T(8,128)(2,1)}, bf16[1024,512]{1,0:T(8,128)(2,1)}, u32[]{:S(2)}, u32[]{:S(2)}) collective-permute-start(bf16[1024,512]{1,0:T(8,128)(2,1)} %collective-permute-done.10), channel_id=1, source_target_pairs={{0,4},{4,0},{8,12},{12,8},{1,5},{5,1},{9,13},{13,9},{2,6},{6,2},{1... | collective-permute-start | bytes 3145736 | tf_op jit(solution)/shard_map/ppermute | solution.py:81
  166.3 28.2 %collective-permute-start.15 = (bf16[1024,512]{1,0:T(8,128)(2,1)}, bf16[1024,512]{1,0:T(8,128)(2,1)}, u32[]{:S(2)}, u32[]{:S(2)}) collective-permute-start(bf16[1024,512]{1,0:T(8,128)(2,1)} %collective-permute-done.11), channel_id=1, source_target_pairs={{0,4},{4,0},{8,12},{12,8},{1,5},{5,1},{9,13},{13,9},{2,6},{6,2},{1... | collective-permute-start | bytes 3145736 | tf_op jit(solution)/shard_map/ppermute | solution.py:81
  199.7 24.0 %all-to-all-start.2 = ((bf16[4,4,128,192]{2,3,1,0:T(8,128)(2,1)}), bf16[4,4,128,192]{2,3,1,0:T(8,128)(2,1)S(1)}, u32[]{:S(2)}, u32[]{:S(2)}) async-start(bf16[4,4,128,192]{2,3,1,0:T(8,128)(2,1)} %bitcast.34), calls=%async_computation.2 | async-start | bytes 1572864 | tf_op jit(solution)/shard_map/all_to_all | solution.py:177
  223.7 23.2 %all-to-all-start = ((bf16[4,4,128,192]{2,3,1,0:T(8,128)(2,1)}), bf16[4,4,128,192]{2,3,1,0:T(8,128)(2,1)S(1)}, u32[]{:S(2)}, u32[]{:S(2)}) async-start(bf16[4,4,128,192]{2,3,1,0:T(8,128)(2,1)} %bitcast.24), calls=%async_computation | async-start | bytes 1572864 | tf_op jit(solution)/shard_map/all_to_all | solution.py:177
  246.9 11.7 %all-to-all-start.3 = ((bf16[4,4,128,64]{2,3,1,0:T(8,128)(2,1)}), bf16[4,4,128,64]{2,3,1,0:T(8,128)(2,1)S(1)}, u32[]{:S(2)}, u32[]{:S(2)}) async-start(bf16[4,4,128,64]{2,3,1,0:T(8,128)(2,1)} %bitcast.138), calls=%async_computation.3 | async-start | bytes 524288 | tf_op jit(solution)/shard_map/all_to_all | solution.py:193
  258.6 13.0 %all-to-all-start.1 = ((bf16[4,4,128,64]{2,3,1,0:T(8,128)(2,1)}), bf16[4,4,128,64]{2,3,1,0:T(8,128)(2,1)S(1)}, u32[]{:S(2)}, u32[]{:S(2)}) async-start(bf16[4,4,128,64]{2,3,1,0:T(8,128)(2,1)} %bitcast.140), calls=%async_computation.1 | async-start | bytes 524288 | tf_op jit(solution)/shard_map/all_to_all | solution.py:193
  275.7 5.3 %collective-permute-start.17 = (f32[4,2,1152]{2,1,0:T(2,128)S(1)}, f32[4,2,1152]{2,1,0:T(2,128)S(1)}, u32[]{:S(2)}, u32[]{:S(2)}) collective-permute-start(f32[4,2,1152]{2,1,0:T(2,128)S(1)} %get-tuple-element.12), channel_id=1, source_target_pairs={{0,2},{1,3},{2,0},{3,1},{4,6},{5,7},{6,4},{7,5},{8,10},{9,11},{10,... | collective-permute-start | bytes 110600 | tf_op jit(solution)/shard_map/ppermute | solution.py:307
  276.2 5.8 %collective-permute-start.16 = (f32[4,2,1152]{2,1,0:T(2,128)S(1)}, f32[4,2,1152]{2,1,0:T(2,128)S(1)}, u32[]{:S(2)}, u32[]{:S(2)}) collective-permute-start(f32[4,2,1152]{2,1,0:T(2,128)S(1)} %get-tuple-element.10), channel_id=1, source_target_pairs={{0,1},{1,2},{2,3},{3,0},{4,5},{5,6},{6,7},{7,4},{8,9},{9,10},{10,1... | collective-permute-start | bytes 110600 | tf_op jit(solution)/shard_map/ppermute | solution.py:307
  (17 other events, 158.7 us)
Sparse Core Ops, SparseCore 0:
  10.2 30.6 all-gather.2
  42.4 27.4 all-gather.4
